TPU v7x, 256 devices: a whole 4x4x8 slice. The times are simulated.
256 devices in a mesh: blk: 32 (over y, x, z_hi), grp: 8 (over z_lo, core).
Axes of the slice: x: 4, y: 4, z: 8 (z_hi: 2, z_lo: 4; z = z_hi * 4 + z_lo), core: 2. Of those that a mesh axis runs over, the one named last changes fastest.
Arguments:
- x_blocks: bfloat16 [4096, 128, 128], P(('blk', 'grp')), may hold values from -0.59765625 to 0.59765625
- pair_left: int32 [32, 8, 32, 12], P('blk', 'grp'), may hold values from 0 to 127
- pair_right: int32 [32, 8, 32, 12], P('blk', 'grp'), may hold values from 0 to 127
- pair_target: int32 [32, 8, 32, 12], P('blk', 'grp'), may hold values from 0 to 3
Outputs:
- c_blocks: bfloat16 [32, 8, 4, 128, 128], P('blk', 'grp')
All inputs are finite; a program needn't handle non-finite values.
Results may differ from a plain program's by a relative error of at most 0.001.
Values may be sent and summed in bfloat16 or wider, within the bound.
No kernel may reach another device: no remote copies, remote signals or barrier semaphores. Data moves between devices by JAX's collectives and lax.ppermute only.
A program may use at most 64 MiB of HBM per device.

v0:
```python
import jax
import jax.numpy as jnp
from jax import lax
from jax.sharding import PartitionSpec as P

CS = 4


def from_behind(block, axis, distance):
    devices = range(lax.axis_size(axis))
    route = [((i - distance) % len(devices), i) for i in devices]
    return lax.ppermute(block, axis, route)


def per_device(x_blocks, pair_left, pair_right, pair_target):
    gathered = lax.all_gather(x_blocks, "grp", axis=0, tiled=True)
    group_count = lax.axis_size("blk")
    left_all = pair_left[0, 0]
    right_all = pair_right[0, 0]
    target_all = pair_target[0, 0]
    block_order = x_blocks.shape[1]
    panel_count = gathered.shape[0]
    pair_count = left_all.shape[1]
    flat_panel = gathered.reshape(panel_count, block_order * block_order)

    def partial_value(turn_index):
        left_index = lax.dynamic_index_in_dim(left_all, turn_index, 0, keepdims=False)
        right_index = lax.dynamic_index_in_dim(right_all, turn_index, 0, keepdims=False)
        target_index = lax.dynamic_index_in_dim(target_all, turn_index, 0, keepdims=False)
        both_index = jnp.concatenate([left_index, right_index])
        one_hot = (both_index[:, None] == jnp.arange(panel_count, dtype=jnp.int32)[None, :]).astype(
            jnp.bfloat16
        )
        picked = jnp.dot(one_hot, flat_panel, preferred_element_type=jnp.float32).astype(
            jnp.bfloat16
        )
        picked = picked.reshape(2 * pair_count, block_order, block_order)
        left_tiles = picked[:pair_count]
        right_tiles = picked[pair_count:]
        product = jnp.einsum(
            "pxy,pxz->pyz", left_tiles, right_tiles, preferred_element_type=jnp.float32
        )
        selector = (target_index[:, None] == jnp.arange(CS, dtype=jnp.int32)[None, :]).astype(
            jnp.float32
        )
        return jnp.einsum("pc,pyz->cyz", selector, product, precision=lax.Precision.HIGHEST)

    def advance(turn_index, carried):
        arrived = from_behind(carried, "blk", 1)
        return arrived + partial_value(turn_index)

    summed = lax.fori_loop(1, group_count, advance, partial_value(0))
    return summed.astype(jnp.bfloat16).reshape(1, 1, CS, block_order, block_order)


def solution(mesh):
    return jax.shard_map(
        per_device,
        mesh=mesh,
        in_specs=(
            P(("blk", "grp"), None, None),
            P("blk", "grp", None, None),
            P("blk", "grp", None, None),
            P("blk", "grp", None, None),
        ),
        out_specs=P("blk", "grp", None, None, None),
        check_vma=False,
    )
```

profile of v0, /device:TPU:120, one launch (start us, length us, event | category | flops | bytes accessed | tf_op | source)
XLA Modules:
  0.0 671.8 jit_solution(15409390500098320005)
XLA Ops:
  11.9 50.7 %all-gather.2.cloned.1.call-done = bf16[128,128,128]{2,1,0:T(8,128)(2,1)} async-done(((bf16[16,128,128]{2,1,0:T(8,128)(2,1)}), bf16[128,128,128]{2,1,0:T(8,128)(2,1)}) %all-gather.2.cloned.1.call-update) | async-done | bytes 4194320 | tf_op jit(solution)/shard_map/all_gather | solution.py:16
  62.6 7.8 %copy.37 = bf16[16,8,128,128]{3,1,2,0:T(8,128)(2,1)} copy(bf16[16,8,128,128]{3,2,1,0:T(8,128)(2,1)} %bitcast.57) | data formatting | bytes 8388608
  74.3 589.9 %while.15 = (s32[]{:T(128)}, f32[4,128,128]{2,0,1:T(4,128)S(1)}, s32[32,12]{1,0:T(8,128)S(1)}, s32[32,12]{1,0:T(8,128)S(1)}, s32[32,12]{1,0:T(8,128)S(1)}, /*ind...) while((s32[]{:T(128)}, f32[4,128,128]{2,0,1:T(4,128)S(1)}, s32[32,12]{1,0:T(8,128)S(1)}, ...), condition=%wide.region_1.2_spmd, body=%wide.region_0.1_spmd.sunk | while | flops 160894032 | bytes 12583719 | solution.py:52
  80.0 11.3 %collective-permute-done = f32[4,128,128]{2,0,1:T(4,128)S(1)} collective-permute-done((f32[4,128,128]{2,0,1:T(4,128)S(1)}, f32[4,128,128]{2,0,1:T(4,128)S(1)}, u32[]{:S(2)}, u32[]{:S(2)}) %collective-permute-start) | collective-permute-done | bytes 262176 | tf_op jit(solution)/shard_map/while/body/eval_jaxpr/ppermute | solution.py:12
  92.4 2.9 convolution_convert_fusion.3
  96.0 15.9 %collective-permute-done = f32[4,128,128]{2,0,1:T(4,128)S(1)} collective-permute-done((f32[4,128,128]{2,0,1:T(4,128)S(1)}, f32[4,128,128]{2,0,1:T(4,128)S(1)}, u32[]{:S(2)}, u32[]{:S(2)}) %collective-permute-start) | collective-permute-done | bytes 262176 | tf_op jit(solution)/shard_map/while/body/eval_jaxpr/ppermute | solution.py:12
  113.0 2.9 convolution_convert_fusion.3
  116.6 16.1 %collective-permute-done = f32[4,128,128]{2,0,1:T(4,128)S(1)} collective-permute-done((f32[4,128,128]{2,0,1:T(4,128)S(1)}, f32[4,128,128]{2,0,1:T(4,128)S(1)}, u32[]{:S(2)}, u32[]{:S(2)}) %collective-permute-start) | collective-permute-done | bytes 262176 | tf_op jit(solution)/shard_map/while/body/eval_jaxpr/ppermute | solution.py:12
  133.8 2.9 convolution_convert_fusion.3
  137.3 12.8 %collective-permute-done = f32[4,128,128]{2,0,1:T(4,128)S(1)} collective-permute-done((f32[4,128,128]{2,0,1:T(4,128)S(1)}, f32[4,128,128]{2,0,1:T(4,128)S(1)}, u32[]{:S(2)}, u32[]{:S(2)}) %collective-permute-start) | collective-permute-done | bytes 262176 | tf_op jit(solution)/shard_map/while/body/eval_jaxpr/ppermute | solution.py:12
  151.3 2.9 convolution_convert_fusion.3
  154.8 17.2 %collective-permute-done = f32[4,128,128]{2,0,1:T(4,128)S(1)} collective-permute-done((f32[4,128,128]{2,0,1:T(4,128)S(1)}, f32[4,128,128]{2,0,1:T(4,128)S(1)}, u32[]{:S(2)}, u32[]{:S(2)}) %collective-permute-start) | collective-permute-done | bytes 262176 | tf_op jit(solution)/shard_map/while/body/eval_jaxpr/ppermute | solution.py:12
  173.1 2.9 convolution_convert_fusion.3
  176.6 15.8 %collective-permute-done = f32[4,128,128]{2,0,1:T(4,128)S(1)} collective-permute-done((f32[4,128,128]{2,0,1:T(4,128)S(1)}, f32[4,128,128]{2,0,1:T(4,128)S(1)}, u32[]{:S(2)}, u32[]{:S(2)}) %collective-permute-start) | collective-permute-done | bytes 262176 | tf_op jit(solution)/shard_map/while/body/eval_jaxpr/ppermute | solution.py:12
  193.6 2.9 convolution_convert_fusion.3
  197.2 12.8 %collective-permute-done = f32[4,128,128]{2,0,1:T(4,128)S(1)} collective-permute-done((f32[4,128,128]{2,0,1:T(4,128)S(1)}, f32[4,128,128]{2,0,1:T(4,128)S(1)}, u32[]{:S(2)}, u32[]{:S(2)}) %collective-permute-start) | collective-permute-done | bytes 262176 | tf_op jit(solution)/shard_map/while/body/eval_jaxpr/ppermute | solution.py:12
  216.1 15.8 %collective-permute-done = f32[4,128,128]{2,0,1:T(4,128)S(1)} collective-permute-done((f32[4,128,128]{2,0,1:T(4,128)S(1)}, f32[4,128,128]{2,0,1:T(4,128)S(1)}, u32[]{:S(2)}, u32[]{:S(2)}) %collective-permute-start) | collective-permute-done | bytes 262176 | tf_op jit(solution)/shard_map/while/body/eval_jaxpr/ppermute | solution.py:12
  233.0 2.9 convolution_convert_fusion.3
  236.5 15.7 %collective-permute-done = f32[4,128,128]{2,0,1:T(4,128)S(1)} collective-permute-done((f32[4,128,128]{2,0,1:T(4,128)S(1)}, f32[4,128,128]{2,0,1:T(4,128)S(1)}, u32[]{:S(2)}, u32[]{:S(2)}) %collective-permute-start) | collective-permute-done | bytes 262176 | tf_op jit(solution)/shard_map/while/body/eval_jaxpr/ppermute | solution.py:12
  253.4 2.9 convolution_convert_fusion.3
  257.0 12.8 %collective-permute-done = f32[4,128,128]{2,0,1:T(4,128)S(1)} collective-permute-done((f32[4,128,128]{2,0,1:T(4,128)S(1)}, f32[4,128,128]{2,0,1:T(4,128)S(1)}, u32[]{:S(2)}, u32[]{:S(2)}) %collective-permute-start) | collective-permute-done | bytes 262176 | tf_op jit(solution)/shard_map/while/body/eval_jaxpr/ppermute | solution.py:12
  270.9 2.9 convolution_convert_fusion.3
  274.4 17.2 %collective-permute-done = f32[4,128,128]{2,0,1:T(4,128)S(1)} collective-permute-done((f32[4,128,128]{2,0,1:T(4,128)S(1)}, f32[4,128,128]{2,0,1:T(4,128)S(1)}, u32[]{:S(2)}, u32[]{:S(2)}) %collective-permute-start) | collective-permute-done | bytes 262176 | tf_op jit(solution)/shard_map/while/body/eval_jaxpr/ppermute | solution.py:12
  292.7 2.9 convolution_convert_fusion.3
  296.3 15.9 %collective-permute-done = f32[4,128,128]{2,0,1:T(4,128)S(1)} collective-permute-done((f32[4,128,128]{2,0,1:T(4,128)S(1)}, f32[4,128,128]{2,0,1:T(4,128)S(1)}, u32[]{:S(2)}, u32[]{:S(2)}) %collective-permute-start) | collective-permute-done | bytes 262176 | tf_op jit(solution)/shard_map/while/body/eval_jaxpr/ppermute | solution.py:12
  313.3 2.9 convolution_convert_fusion.3
  316.9 12.7 %collective-permute-done = f32[4,128,128]{2,0,1:T(4,128)S(1)} collective-permute-done((f32[4,128,128]{2,0,1:T(4,128)S(1)}, f32[4,128,128]{2,0,1:T(4,128)S(1)}, u32[]{:S(2)}, u32[]{:S(2)}) %collective-permute-start) | collective-permute-done | bytes 262176 | tf_op jit(solution)/shard_map/while/body/eval_jaxpr/ppermute | solution.py:12
  330.7 2.9 convolution_convert_fusion.3
  334.2 17.2 %collective-permute-done = f32[4,128,128]{2,0,1:T(4,128)S(1)} collective-permute-done((f32[4,128,128]{2,0,1:T(4,128)S(1)}, f32[4,128,128]{2,0,1:T(4,128)S(1)}, u32[]{:S(2)}, u32[]{:S(2)}) %collective-permute-start) | collective-permute-done | bytes 262176 | tf_op jit(solution)/shard_map/while/body/eval_jaxpr/ppermute | solution.py:12
  356.1 16.5 %collective-permute-done = f32[4,128,128]{2,0,1:T(4,128)S(1)} collective-permute-done((f32[4,128,128]{2,0,1:T(4,128)S(1)}, f32[4,128,128]{2,0,1:T(4,128)S(1)}, u32[]{:S(2)}, u32[]{:S(2)}) %collective-permute-start) | collective-permute-done | bytes 262176 | tf_op jit(solution)/shard_map/while/body/eval_jaxpr/ppermute | solution.py:12
  377.3 13.3 %collective-permute-done = f32[4,128,128]{2,0,1:T(4,128)S(1)} collective-permute-done((f32[4,128,128]{2,0,1:T(4,128)S(1)}, f32[4,128,128]{2,0,1:T(4,128)S(1)}, u32[]{:S(2)}, u32[]{:S(2)}) %collective-permute-start) | collective-permute-done | bytes 262176 | tf_op jit(solution)/shard_map/while/body/eval_jaxpr/ppermute | solution.py:12
  395.3 17.2 %collective-permute-done = f32[4,128,128]{2,0,1:T(4,128)S(1)} collective-permute-done((f32[4,128,128]{2,0,1:T(4,128)S(1)}, f32[4,128,128]{2,0,1:T(4,128)S(1)}, u32[]{:S(2)}, u32[]{:S(2)}) %collective-permute-start) | collective-permute-done | bytes 262176 | tf_op jit(solution)/shard_map/while/body/eval_jaxpr/ppermute | solution.py:12
  417.2 16.6 %collective-permute-done = f32[4,128,128]{2,0,1:T(4,128)S(1)} collective-permute-done((f32[4,128,128]{2,0,1:T(4,128)S(1)}, f32[4,128,128]{2,0,1:T(4,128)S(1)}, u32[]{:S(2)}, u32[]{:S(2)}) %collective-permute-start) | collective-permute-done | bytes 262176 | tf_op jit(solution)/shard_map/while/body/eval_jaxpr/ppermute | solution.py:12
  438.5 12.8 %collective-permute-done = f32[4,128,128]{2,0,1:T(4,128)S(1)} collective-permute-done((f32[4,128,128]{2,0,1:T(4,128)S(1)}, f32[4,128,128]{2,0,1:T(4,128)S(1)}, u32[]{:S(2)}, u32[]{:S(2)}) %collective-permute-start) | collective-permute-done | bytes 262176 | tf_op jit(solution)/shard_map/while/body/eval_jaxpr/ppermute | solution.py:12
  455.9 16.8 %collective-permute-done = f32[4,128,128]{2,0,1:T(4,128)S(1)} collective-permute-done((f32[4,128,128]{2,0,1:T(4,128)S(1)}, f32[4,128,128]{2,0,1:T(4,128)S(1)}, u32[]{:S(2)}, u32[]{:S(2)}) %collective-permute-start) | collective-permute-done | bytes 262176 | tf_op jit(solution)/shard_map/while/body/eval_jaxpr/ppermute | solution.py:12
  477.4 15.0 %collective-permute-done = f32[4,128,128]{2,0,1:T(4,128)S(1)} collective-permute-done((f32[4,128,128]{2,0,1:T(4,128)S(1)}, f32[4,128,128]{2,0,1:T(4,128)S(1)}, u32[]{:S(2)}, u32[]{:S(2)}) %collective-permute-start) | collective-permute-done | bytes 262176 | tf_op jit(solution)/shard_map/while/body/eval_jaxpr/ppermute | solution.py:12
  497.1 16.7 %collective-permute-done = f32[4,128,128]{2,0,1:T(4,128)S(1)} collective-permute-done((f32[4,128,128]{2,0,1:T(4,128)S(1)}, f32[4,128,128]{2,0,1:T(4,128)S(1)}, u32[]{:S(2)}, u32[]{:S(2)}) %collective-permute-start) | collective-permute-done | bytes 262176 | tf_op jit(solution)/shard_map/while/body/eval_jaxpr/ppermute | solution.py:12
  518.5 16.6 %collective-permute-done = f32[4,128,128]{2,0,1:T(4,128)S(1)} collective-permute-done((f32[4,128,128]{2,0,1:T(4,128)S(1)}, f32[4,128,128]{2,0,1:T(4,128)S(1)}, u32[]{:S(2)}, u32[]{:S(2)}) %collective-permute-start) | collective-permute-done | bytes 262176 | tf_op jit(solution)/shard_map/while/body/eval_jaxpr/ppermute | solution.py:12
  539.9 12.9 %collective-permute-done = f32[4,128,128]{2,0,1:T(4,128)S(1)} collective-permute-done((f32[4,128,128]{2,0,1:T(4,128)S(1)}, f32[4,128,128]{2,0,1:T(4,128)S(1)}, u32[]{:S(2)}, u32[]{:S(2)}) %collective-permute-start) | collective-permute-done | bytes 262176 | tf_op jit(solution)/shard_map/while/body/eval_jaxpr/ppermute | solution.py:12
  557.4 11.7 %collective-permute-done = f32[4,128,128]{2,0,1:T(4,128)S(1)} collective-permute-done((f32[4,128,128]{2,0,1:T(4,128)S(1)}, f32[4,128,128]{2,0,1:T(4,128)S(1)}, u32[]{:S(2)}, u32[]{:S(2)}) %collective-permute-start) | collective-permute-done | bytes 262176 | tf_op jit(solution)/shard_map/while/body/eval_jaxpr/ppermute | solution.py:12
  573.8 11.2 %collective-permute-done = f32[4,128,128]{2,0,1:T(4,128)S(1)} collective-permute-done((f32[4,128,128]{2,0,1:T(4,128)S(1)}, f32[4,128,128]{2,0,1:T(4,128)S(1)}, u32[]{:S(2)}, u32[]{:S(2)}) %collective-permute-start) | collective-permute-done | bytes 262176 | tf_op jit(solution)/shard_map/while/body/eval_jaxpr/ppermute | solution.py:12
  589.7 11.2 %collective-permute-done = f32[4,128,128]{2,0,1:T(4,128)S(1)} collective-permute-done((f32[4,128,128]{2,0,1:T(4,128)S(1)}, f32[4,128,128]{2,0,1:T(4,128)S(1)}, u32[]{:S(2)}, u32[]{:S(2)}) %collective-permute-start) | collective-permute-done | bytes 262176 | tf_op jit(solution)/shard_map/while/body/eval_jaxpr/ppermute | solution.py:12
  602.1 2.9 convolution_convert_fusion.3
  605.6 11.4 %collective-permute-done = f32[4,128,128]{2,0,1:T(4,128)S(1)} collective-permute-done((f32[4,128,128]{2,0,1:T(4,128)S(1)}, f32[4,128,128]{2,0,1:T(4,128)S(1)}, u32[]{:S(2)}, u32[]{:S(2)}) %collective-permute-start) | collective-permute-done | bytes 262176 | tf_op jit(solution)/shard_map/while/body/eval_jaxpr/ppermute | solution.py:12
  618.1 2.9 convolution_convert_fusion.3
  621.6 11.4 %collective-permute-done = f32[4,128,128]{2,0,1:T(4,128)S(1)} collective-permute-done((f32[4,128,128]{2,0,1:T(4,128)S(1)}, f32[4,128,128]{2,0,1:T(4,128)S(1)}, u32[]{:S(2)}, u32[]{:S(2)}) %collective-permute-start) | collective-permute-done | bytes 262176 | tf_op jit(solution)/shard_map/while/body/eval_jaxpr/ppermute | solution.py:12
  637.7 11.4 %collective-permute-done = f32[4,128,128]{2,0,1:T(4,128)S(1)} collective-permute-done((f32[4,128,128]{2,0,1:T(4,128)S(1)}, f32[4,128,128]{2,0,1:T(4,128)S(1)}, u32[]{:S(2)}, u32[]{:S(2)}) %collective-permute-start) | collective-permute-done | bytes 262176 | tf_op jit(solution)/shard_map/while/body/eval_jaxpr/ppermute | solution.py:12
  653.7 9.6 %collective-permute-done = f32[4,128,128]{2,0,1:T(4,128)S(1)} collective-permute-done((f32[4,128,128]{2,0,1:T(4,128)S(1)}, f32[4,128,128]{2,0,1:T(4,128)S(1)}, u32[]{:S(2)}, u32[]{:S(2)}) %collective-permute-start) | collective-permute-done | bytes 262176 | tf_op jit(solution)/shard_map/while/body/eval_jaxpr/ppermute | solution.py:12
  (313 shorter events, 115.4 us)
Async XLA Ops:
  6.5 56.0 %all-gather.2.cloned.1.call-start = ((), (), s32[]{:S(2)}) async-start(), calls=%async_computation | async-start | bytes 4718592 | tf_op jit(solution)/shard_map/all_gather | solution.py:16
  62.6 7.8 %copy-start = (bf16[128,128,128]{2,1,0:T(8,128)(2,1)S(1)}, bf16[128,128,128]{2,1,0:T(8,128)(2,1)}, u32[]{:S(2)}) copy-start(bf16[128,128,128]{2,1,0:T(8,128)(2,1)} %all-gather.2.cloned.1.call-done) | copy-start | bytes 12582916
  74.3 17.0 %collective-permute-start = (f32[4,128,128]{2,0,1:T(4,128)S(1)}, f32[4,128,128]{2,0,1:T(4,128)S(1)}, u32[]{:S(2)}, u32[]{:S(2)}) collective-permute-start(f32[4,128,128]{2,0,1:T(4,128)S(1)} %get-tuple-element.235), channel_id=1, source_target_pairs={{248,0},{0,8},{8,16},{16,24},{24,32},{32,40},{40,48},{48,56},{56,6... | collective-permute-start | bytes 786440 | tf_op jit(solution)/shard_map/while/body/eval_jaxpr/ppermute | solution.py:12
  92.2 19.7 %collective-permute-start = (f32[4,128,128]{2,0,1:T(4,128)S(1)}, f32[4,128,128]{2,0,1:T(4,128)S(1)}, u32[]{:S(2)}, u32[]{:S(2)}) collective-permute-start(f32[4,128,128]{2,0,1:T(4,128)S(1)} %get-tuple-element.235), channel_id=1, source_target_pairs={{248,0},{0,8},{8,16},{16,24},{24,32},{32,40},{40,48},{48,56},{56,6... | collective-permute-start | bytes 786440 | tf_op jit(solution)/shard_map/while/body/eval_jaxpr/ppermute | solution.py:12
  112.8 19.8 %collective-permute-start = (f32[4,128,128]{2,0,1:T(4,128)S(1)}, f32[4,128,128]{2,0,1:T(4,128)S(1)}, u32[]{:S(2)}, u32[]{:S(2)}) collective-permute-start(f32[4,128,128]{2,0,1:T(4,128)S(1)} %get-tuple-element.235), channel_id=1, source_target_pairs={{248,0},{0,8},{8,16},{16,24},{24,32},{32,40},{40,48},{48,56},{56,6... | collective-permute-start | bytes 786440 | tf_op jit(solution)/shard_map/while/body/eval_jaxpr/ppermute | solution.py:12
  133.6 16.6 %collective-permute-start = (f32[4,128,128]{2,0,1:T(4,128)S(1)}, f32[4,128,128]{2,0,1:T(4,128)S(1)}, u32[]{:S(2)}, u32[]{:S(2)}) collective-permute-start(f32[4,128,128]{2,0,1:T(4,128)S(1)} %get-tuple-element.235), channel_id=1, source_target_pairs={{248,0},{0,8},{8,16},{16,24},{24,32},{32,40},{40,48},{48,56},{56,6... | collective-permute-start | bytes 786440 | tf_op jit(solution)/shard_map/while/body/eval_jaxpr/ppermute | solution.py:12
  151.0 20.9 %collective-permute-start = (f32[4,128,128]{2,0,1:T(4,128)S(1)}, f32[4,128,128]{2,0,1:T(4,128)S(1)}, u32[]{:S(2)}, u32[]{:S(2)}) collective-permute-start(f32[4,128,128]{2,0,1:T(4,128)S(1)} %get-tuple-element.235), channel_id=1, source_target_pairs={{248,0},{0,8},{8,16},{16,24},{24,32},{32,40},{40,48},{48,56},{56,6... | collective-permute-start | bytes 786440 | tf_op jit(solution)/shard_map/while/body/eval_jaxpr/ppermute | solution.py:12
  172.9 19.6 %collective-permute-start = (f32[4,128,128]{2,0,1:T(4,128)S(1)}, f32[4,128,128]{2,0,1:T(4,128)S(1)}, u32[]{:S(2)}, u32[]{:S(2)}) collective-permute-start(f32[4,128,128]{2,0,1:T(4,128)S(1)} %get-tuple-element.235), channel_id=1, source_target_pairs={{248,0},{0,8},{8,16},{16,24},{24,32},{32,40},{40,48},{48,56},{56,6... | collective-permute-start | bytes 786440 | tf_op jit(solution)/shard_map/while/body/eval_jaxpr/ppermute | solution.py:12
  193.4 16.5 %collective-permute-start = (f32[4,128,128]{2,0,1:T(4,128)S(1)}, f32[4,128,128]{2,0,1:T(4,128)S(1)}, u32[]{:S(2)}, u32[]{:S(2)}) collective-permute-start(f32[4,128,128]{2,0,1:T(4,128)S(1)} %get-tuple-element.235), channel_id=1, source_target_pairs={{248,0},{0,8},{8,16},{16,24},{24,32},{32,40},{40,48},{48,56},{56,6... | collective-permute-start | bytes 786440 | tf_op jit(solution)/shard_map/while/body/eval_jaxpr/ppermute | solution.py:12
  210.9 21.0 %collective-permute-start = (f32[4,128,128]{2,0,1:T(4,128)S(1)}, f32[4,128,128]{2,0,1:T(4,128)S(1)}, u32[]{:S(2)}, u32[]{:S(2)}) collective-permute-start(f32[4,128,128]{2,0,1:T(4,128)S(1)} %get-tuple-element.235), channel_id=1, source_target_pairs={{248,0},{0,8},{8,16},{16,24},{24,32},{32,40},{40,48},{48,56},{56,6... | collective-permute-start | bytes 786440 | tf_op jit(solution)/shard_map/while/body/eval_jaxpr/ppermute | solution.py:12
  232.8 19.5 %collective-permute-start = (f32[4,128,128]{2,0,1:T(4,128)S(1)}, f32[4,128,128]{2,0,1:T(4,128)S(1)}, u32[]{:S(2)}, u32[]{:S(2)}) collective-permute-start(f32[4,128,128]{2,0,1:T(4,128)S(1)} %get-tuple-element.235), channel_id=1, source_target_pairs={{248,0},{0,8},{8,16},{16,24},{24,32},{32,40},{40,48},{48,56},{56,6... | collective-permute-start | bytes 786440 | tf_op jit(solution)/shard_map/while/body/eval_jaxpr/ppermute | solution.py:12
  253.2 16.5 %collective-permute-start = (f32[4,128,128]{2,0,1:T(4,128)S(1)}, f32[4,128,128]{2,0,1:T(4,128)S(1)}, u32[]{:S(2)}, u32[]{:S(2)}) collective-permute-start(f32[4,128,128]{2,0,1:T(4,128)S(1)} %get-tuple-element.235), channel_id=1, source_target_pairs={{248,0},{0,8},{8,16},{16,24},{24,32},{32,40},{40,48},{48,56},{56,6... | collective-permute-start | bytes 786440 | tf_op jit(solution)/shard_map/while/body/eval_jaxpr/ppermute | solution.py:12
  270.7 20.9 %collective-permute-start = (f32[4,128,128]{2,0,1:T(4,128)S(1)}, f32[4,128,128]{2,0,1:T(4,128)S(1)}, u32[]{:S(2)}, u32[]{:S(2)}) collective-permute-start(f32[4,128,128]{2,0,1:T(4,128)S(1)} %get-tuple-element.235), channel_id=1, source_target_pairs={{248,0},{0,8},{8,16},{16,24},{24,32},{32,40},{40,48},{48,56},{56,6... | collective-permute-start | bytes 786440 | tf_op jit(solution)/shard_map/while/body/eval_jaxpr/ppermute | solution.py:12
  292.5 19.7 %collective-permute-start = (f32[4,128,128]{2,0,1:T(4,128)S(1)}, f32[4,128,128]{2,0,1:T(4,128)S(1)}, u32[]{:S(2)}, u32[]{:S(2)}) collective-permute-start(f32[4,128,128]{2,0,1:T(4,128)S(1)} %get-tuple-element.235), channel_id=1, source_target_pairs={{248,0},{0,8},{8,16},{16,24},{24,32},{32,40},{40,48},{48,56},{56,6... | collective-permute-start | bytes 786440 | tf_op jit(solution)/shard_map/while/body/eval_jaxpr/ppermute | solution.py:12
  313.1 16.5 %collective-permute-start = (f32[4,128,128]{2,0,1:T(4,128)S(1)}, f32[4,128,128]{2,0,1:T(4,128)S(1)}, u32[]{:S(2)}, u32[]{:S(2)}) collective-permute-start(f32[4,128,128]{2,0,1:T(4,128)S(1)} %get-tuple-element.235), channel_id=1, source_target_pairs={{248,0},{0,8},{8,16},{16,24},{24,32},{32,40},{40,48},{48,56},{56,6... | collective-permute-start | bytes 786440 | tf_op jit(solution)/shard_map/while/body/eval_jaxpr/ppermute | solution.py:12
  330.5 20.9 %collective-permute-start = (f32[4,128,128]{2,0,1:T(4,128)S(1)}, f32[4,128,128]{2,0,1:T(4,128)S(1)}, u32[]{:S(2)}, u32[]{:S(2)}) collective-permute-start(f32[4,128,128]{2,0,1:T(4,128)S(1)} %get-tuple-element.235), channel_id=1, source_target_pairs={{248,0},{0,8},{8,16},{16,24},{24,32},{32,40},{40,48},{48,56},{56,6... | collective-permute-start | bytes 786440 | tf_op jit(solution)/shard_map/while/body/eval_jaxpr/ppermute | solution.py:12
  352.4 20.3 %collective-permute-start = (f32[4,128,128]{2,0,1:T(4,128)S(1)}, f32[4,128,128]{2,0,1:T(4,128)S(1)}, u32[]{:S(2)}, u32[]{:S(2)}) collective-permute-start(f32[4,128,128]{2,0,1:T(4,128)S(1)} %get-tuple-element.235), channel_id=1, source_target_pairs={{248,0},{0,8},{8,16},{16,24},{24,32},{32,40},{40,48},{48,56},{56,6... | collective-permute-start | bytes 786440 | tf_op jit(solution)/shard_map/while/body/eval_jaxpr/ppermute | solution.py:12
  373.6 17.1 %collective-permute-start = (f32[4,128,128]{2,0,1:T(4,128)S(1)}, f32[4,128,128]{2,0,1:T(4,128)S(1)}, u32[]{:S(2)}, u32[]{:S(2)}) collective-permute-start(f32[4,128,128]{2,0,1:T(4,128)S(1)} %get-tuple-element.235), channel_id=1, source_target_pairs={{248,0},{0,8},{8,16},{16,24},{24,32},{32,40},{40,48},{48,56},{56,6... | collective-permute-start | bytes 786440 | tf_op jit(solution)/shard_map/while/body/eval_jaxpr/ppermute | solution.py:12
  391.6 20.9 %collective-permute-start = (f32[4,128,128]{2,0,1:T(4,128)S(1)}, f32[4,128,128]{2,0,1:T(4,128)S(1)}, u32[]{:S(2)}, u32[]{:S(2)}) collective-permute-start(f32[4,128,128]{2,0,1:T(4,128)S(1)} %get-tuple-element.235), channel_id=1, source_target_pairs={{248,0},{0,8},{8,16},{16,24},{24,32},{32,40},{40,48},{48,56},{56,6... | collective-permute-start | bytes 786440 | tf_op jit(solution)/shard_map/while/body/eval_jaxpr/ppermute | solution.py:12
  413.4 20.4 %collective-permute-start = (f32[4,128,128]{2,0,1:T(4,128)S(1)}, f32[4,128,128]{2,0,1:T(4,128)S(1)}, u32[]{:S(2)}, u32[]{:S(2)}) collective-permute-start(f32[4,128,128]{2,0,1:T(4,128)S(1)} %get-tuple-element.235), channel_id=1, source_target_pairs={{248,0},{0,8},{8,16},{16,24},{24,32},{32,40},{40,48},{48,56},{56,6... | collective-permute-start | bytes 786440 | tf_op jit(solution)/shard_map/while/body/eval_jaxpr/ppermute | solution.py:12
  434.7 16.5 %collective-permute-start = (f32[4,128,128]{2,0,1:T(4,128)S(1)}, f32[4,128,128]{2,0,1:T(4,128)S(1)}, u32[]{:S(2)}, u32[]{:S(2)}) collective-permute-start(f32[4,128,128]{2,0,1:T(4,128)S(1)} %get-tuple-element.235), channel_id=1, source_target_pairs={{248,0},{0,8},{8,16},{16,24},{24,32},{32,40},{40,48},{48,56},{56,6... | collective-permute-start | bytes 786440 | tf_op jit(solution)/shard_map/while/body/eval_jaxpr/ppermute | solution.py:12
  452.2 20.6 %collective-permute-start = (f32[4,128,128]{2,0,1:T(4,128)S(1)}, f32[4,128,128]{2,0,1:T(4,128)S(1)}, u32[]{:S(2)}, u32[]{:S(2)}) collective-permute-start(f32[4,128,128]{2,0,1:T(4,128)S(1)} %get-tuple-element.235), channel_id=1, source_target_pairs={{248,0},{0,8},{8,16},{16,24},{24,32},{32,40},{40,48},{48,56},{56,6... | collective-permute-start | bytes 786440 | tf_op jit(solution)/shard_map/while/body/eval_jaxpr/ppermute | solution.py:12
  473.7 18.8 %collective-permute-start = (f32[4,128,128]{2,0,1:T(4,128)S(1)}, f32[4,128,128]{2,0,1:T(4,128)S(1)}, u32[]{:S(2)}, u32[]{:S(2)}) collective-permute-start(f32[4,128,128]{2,0,1:T(4,128)S(1)} %get-tuple-element.235), channel_id=1, source_target_pairs={{248,0},{0,8},{8,16},{16,24},{24,32},{32,40},{40,48},{48,56},{56,6... | collective-permute-start | bytes 786440 | tf_op jit(solution)/shard_map/while/body/eval_jaxpr/ppermute | solution.py:12
  493.3 20.5 %collective-permute-start = (f32[4,128,128]{2,0,1:T(4,128)S(1)}, f32[4,128,128]{2,0,1:T(4,128)S(1)}, u32[]{:S(2)}, u32[]{:S(2)}) collective-permute-start(f32[4,128,128]{2,0,1:T(4,128)S(1)} %get-tuple-element.235), channel_id=1, source_target_pairs={{248,0},{0,8},{8,16},{16,24},{24,32},{32,40},{40,48},{48,56},{56,6... | collective-permute-start | bytes 786440 | tf_op jit(solution)/shard_map/while/body/eval_jaxpr/ppermute | solution.py:12
  514.8 20.4 %collective-permute-start = (f32[4,128,128]{2,0,1:T(4,128)S(1)}, f32[4,128,128]{2,0,1:T(4,128)S(1)}, u32[]{:S(2)}, u32[]{:S(2)}) collective-permute-start(f32[4,128,128]{2,0,1:T(4,128)S(1)} %get-tuple-element.235), channel_id=1, source_target_pairs={{248,0},{0,8},{8,16},{16,24},{24,32},{32,40},{40,48},{48,56},{56,6... | collective-permute-start | bytes 786440 | tf_op jit(solution)/shard_map/while/body/eval_jaxpr/ppermute | solution.py:12
  536.1 16.7 %collective-permute-start = (f32[4,128,128]{2,0,1:T(4,128)S(1)}, f32[4,128,128]{2,0,1:T(4,128)S(1)}, u32[]{:S(2)}, u32[]{:S(2)}) collective-permute-start(f32[4,128,128]{2,0,1:T(4,128)S(1)} %get-tuple-element.235), channel_id=1, source_target_pairs={{248,0},{0,8},{8,16},{16,24},{24,32},{32,40},{40,48},{48,56},{56,6... | collective-permute-start | bytes 786440 | tf_op jit(solution)/shard_map/while/body/eval_jaxpr/ppermute | solution.py:12
  553.7 15.5 %collective-permute-start = (f32[4,128,128]{2,0,1:T(4,128)S(1)}, f32[4,128,128]{2,0,1:T(4,128)S(1)}, u32[]{:S(2)}, u32[]{:S(2)}) collective-permute-start(f32[4,128,128]{2,0,1:T(4,128)S(1)} %get-tuple-element.235), channel_id=1, source_target_pairs={{248,0},{0,8},{8,16},{16,24},{24,32},{32,40},{40,48},{48,56},{56,6... | collective-permute-start | bytes 786440 | tf_op jit(solution)/shard_map/while/body/eval_jaxpr/ppermute | solution.py:12
  570.1 15.0 %collective-permute-start = (f32[4,128,128]{2,0,1:T(4,128)S(1)}, f32[4,128,128]{2,0,1:T(4,128)S(1)}, u32[]{:S(2)}, u32[]{:S(2)}) collective-permute-start(f32[4,128,128]{2,0,1:T(4,128)S(1)} %get-tuple-element.235), channel_id=1, source_target_pairs={{248,0},{0,8},{8,16},{16,24},{24,32},{32,40},{40,48},{48,56},{56,6... | collective-permute-start | bytes 786440 | tf_op jit(solution)/shard_map/while/body/eval_jaxpr/ppermute | solution.py:12
  586.0 15.0 %collective-permute-start = (f32[4,128,128]{2,0,1:T(4,128)S(1)}, f32[4,128,128]{2,0,1:T(4,128)S(1)}, u32[]{:S(2)}, u32[]{:S(2)}) collective-permute-start(f32[4,128,128]{2,0,1:T(4,128)S(1)} %get-tuple-element.235), channel_id=1, source_target_pairs={{248,0},{0,8},{8,16},{16,24},{24,32},{32,40},{40,48},{48,56},{56,6... | collective-permute-start | bytes 786440 | tf_op jit(solution)/shard_map/while/body/eval_jaxpr/ppermute | solution.py:12
  601.8 15.1 %collective-permute-start = (f32[4,128,128]{2,0,1:T(4,128)S(1)}, f32[4,128,128]{2,0,1:T(4,128)S(1)}, u32[]{:S(2)}, u32[]{:S(2)}) collective-permute-start(f32[4,128,128]{2,0,1:T(4,128)S(1)} %get-tuple-element.235), channel_id=1, source_target_pairs={{248,0},{0,8},{8,16},{16,24},{24,32},{32,40},{40,48},{48,56},{56,6... | collective-permute-start | bytes 786440 | tf_op jit(solution)/shard_map/while/body/eval_jaxpr/ppermute | solution.py:12
  617.9 15.1 %collective-permute-start = (f32[4,128,128]{2,0,1:T(4,128)S(1)}, f32[4,128,128]{2,0,1:T(4,128)S(1)}, u32[]{:S(2)}, u32[]{:S(2)}) collective-permute-start(f32[4,128,128]{2,0,1:T(4,128)S(1)} %get-tuple-element.235), channel_id=1, source_target_pairs={{248,0},{0,8},{8,16},{16,24},{24,32},{32,40},{40,48},{48,56},{56,6... | collective-permute-start | bytes 786440 | tf_op jit(solution)/shard_map/while/body/eval_jaxpr/ppermute | solution.py:12
  633.9 15.1 %collective-permute-start = (f32[4,128,128]{2,0,1:T(4,128)S(1)}, f32[4,128,128]{2,0,1:T(4,128)S(1)}, u32[]{:S(2)}, u32[]{:S(2)}) collective-permute-start(f32[4,128,128]{2,0,1:T(4,128)S(1)} %get-tuple-element.235), channel_id=1, source_target_pairs={{248,0},{0,8},{8,16},{16,24},{24,32},{32,40},{40,48},{48,56},{56,6... | collective-permute-start | bytes 786440 | tf_op jit(solution)/shard_map/while/body/eval_jaxpr/ppermute | solution.py:12
  650.0 13.4 %collective-permute-start = (f32[4,128,128]{2,0,1:T(4,128)S(1)}, f32[4,128,128]{2,0,1:T(4,128)S(1)}, u32[]{:S(2)}, u32[]{:S(2)}) collective-permute-start(f32[4,128,128]{2,0,1:T(4,128)S(1)} %get-tuple-element.235), channel_id=1, source_target_pairs={{248,0},{0,8},{8,16},{16,24},{24,32},{32,40},{40,48},{48,56},{56,6... | collective-permute-start | bytes 786440 | tf_op jit(solution)/shard_map/while/body/eval_jaxpr/ppermute | solution.py:12
Sparse Core Ops, SparseCore 0:
  9.1 53.4 all-gather.1
where the time goes:
time: 673 us; the launch traced here: 672 us
  waiting for transfers between devices  493 us (73%)
  matrix products  131 us (19%)
  local copies, waits for them, and re-layouts  23.7 us (4%)
  between operations  13.4 us (2%)
    ppermute x31, waiting for transfers between devices, from_behind(): return lax.ppermute(block, axis, route)  441 us
    dot_general x32, matrix products, partial_value(): jnp.dot(one_hot, flat_panel, preferred_element_type=jnp.float32)  91.8 us
    all_gather x1, waiting for transfers between devices, per_device(): gathered = lax.all_gather(x_blocks, 'grp', axis=0, tiled=True)  50.7 us
    dot_general x32, matrix products, partial_value(): jnp.einsum('pc,pyz->cyz', selector, product, precision=lax.Precision.HIGH...  28.9 us
  transfers between devices with their start and end apart: 32, of which 32 were waited for; matrix products, arithmetic and copies ran while one was open for 17% of the time, Pallas kernels for 0%

commit v1 on v0

v1 whole, which is shorter than its diff:
```python
import jax
import jax.numpy as jnp
from jax import lax
from jax.experimental import pallas as pl
from jax.experimental.pallas import tpu as pltpu
from jax.sharding import PartitionSpec as P

CS = 4
OWNERS_PER_STEP = 4


def _products_kernel(left_ref, right_ref, target_ref, x_ref, out_ref):
    step = pl.program_id(0)
    pair_count = left_ref.shape[0] // (pl.num_programs(0) * OWNERS_PER_STEP)
    out_ref[...] = jnp.zeros_like(out_ref)

    def body(j, carry):
        k = j // pair_count
        flat = step * OWNERS_PER_STEP * pair_count + j
        l = left_ref[flat]
        r = right_ref[flat]
        t = target_ref[flat]
        prod = lax.dot_general(
            x_ref[l], x_ref[r], (((0,), (0,)), ((), ())), preferred_element_type=jnp.float32
        )
        out_ref[k, t] += prod
        return carry

    lax.fori_loop(0, OWNERS_PER_STEP * pair_count, body, 0, unroll=4)


def owner_partials(gathered, left, right, target):
    owners, pair_count = left.shape
    block = gathered.shape[1]
    steps = owners // OWNERS_PER_STEP
    flops = 2 * owners * pair_count * block * block * block
    return pl.pallas_call(
        _products_kernel,
        out_shape=jax.ShapeDtypeStruct((owners, CS, block, block), jnp.float32),
        grid_spec=pltpu.PrefetchScalarGridSpec(
            num_scalar_prefetch=3,
            grid=(steps,),
            in_specs=[
                pl.BlockSpec(
                    gathered.shape,
                    lambda i, *_: (0, 0, 0),
                    pipeline_mode=pl.Buffered(1),
                )
            ],
            out_specs=pl.BlockSpec(
                (OWNERS_PER_STEP, CS, block, block), lambda i, *_: (i, 0, 0, 0)
            ),
        ),
        compiler_params=pltpu.CompilerParams(
            dimension_semantics=("arbitrary",), vmem_limit_bytes=48 * 1024 * 1024
        ),
        cost_estimate=pl.CostEstimate(
            flops=flops,
            transcendentals=0,
            bytes_accessed=gathered.size * 2 + owners * CS * block * block * 4,
        ),
    )(left.reshape(-1), right.reshape(-1), target.reshape(-1), gathered)


def per_device(x_blocks, pair_left, pair_right, pair_target):
    gathered = lax.all_gather(x_blocks, "grp", axis=0, tiled=True)
    group_count = lax.axis_size("blk")
    me = lax.axis_index("blk")
    visit = (me - 1 - jnp.arange(group_count, dtype=jnp.int32)) % group_count
    left = jnp.take(pair_left[0, 0], visit, axis=0)
    right = jnp.take(pair_right[0, 0], visit, axis=0)
    target = jnp.take(pair_target[0, 0], visit, axis=0)
    partials = owner_partials(gathered, left, right, target)
    summed = lax.psum_scatter(partials, "blk", scatter_dimension=0, tiled=True)
    block = x_blocks.shape[1]
    return summed.astype(jnp.bfloat16).reshape(1, 1, CS, block, block)


def solution(mesh):
    return jax.shard_map(
        per_device,
        mesh=mesh,
        in_specs=(
            P(("blk", "grp"), None, None),
            P("blk", "grp", None, None),
            P("blk", "grp", None, None),
            P("blk", "grp", None, None),
        ),
        out_specs=P("blk", "grp", None, None, None),
        check_vma=False,
    )
```

time: 673 us -> 484 us (0.72)
  the two profiles are of different devices: /device:TPU:120 before, /device:TPU:0 now
where the time goes in v1:
time: 484 us
  waiting for transfers between devices  439 us (91%)
  Pallas kernels  23.9 us (5%)
  between operations  13.4 us (3%)
  local copies, waits for them, and re-layouts  6.54 us (1%)
    reduce_scatter x1, waiting for transfers between devices, per_device(): summed = lax.psum_scatter(partials, 'blk', scatter_dimension=0, tiled=True)  385 us
    all_gather x1, waiting for transfers between devices, per_device(): gathered = lax.all_gather(x_blocks, 'grp', axis=0, tiled=True)  53.2 us
    pallas_call x1, Pallas kernels, owner_partials(): pl.pallas_call(_products_kernel, out_shape=jax.ShapeDtypeStruct((owners,...  23.9 us
  transfers between devices with their start and end apart: 2, of which 2 were waited for; matrix products, arithmetic and copies ran while one was open for 1% of the time, Pallas kernels for 0%

profile of v1, /device:TPU:0, one launch (start us, length us, event | category | flops | bytes accessed | tf_op | source)
XLA Modules:
  0.0 484.1 jit_solution(6773645160751019706)
XLA Ops:
  6.5 0.0 all-gather.2.cloned.1.call-start
  6.5 0.7 all-gather.2.cloned.1.call-update
  7.3 0.0 reduce-scatter.2.cloned.1.call-start
  7.3 0.8 copy.11
  8.1 0.8 copy.12
  8.9 0.6 gather_fusion
  9.4 0.6 gather_fusion.1
  10.0 0.8 copy.13
  10.8 0.6 gather_fusion.2
  11.4 0.1 broadcast_select_fusion
  11.5 0.1 reshape.19.target_ref
  11.6 0.1 reshape.18.right_ref
  11.7 0.1 reshape.17.left_ref
  11.8 53.2 %all-gather.2.cloned.1.call-done.x_ref = bf16[128,128,128]{2,1,0:T(8,128)(2,1)} async-done(((bf16[16,128,128]{2,1,0:T(8,128)(2,1)}), bf16[128,128,128]{2,1,0:T(8,128)(2,1)}) %all-gather.2.cloned.1.call-update) | async-done | bytes 4194320 | tf_op jit(solution)/shard_map/all_gather | solution.py:66
  64.9 0.0 copy-start
  64.9 2.2 copy-done
  67.1 23.9 %shard_map.46 = f32[32,4,128,128]{3,2,1,0:T(8,128)} custom-call(s32[384]{0:T(512)S(1)} %reshape.17.left_ref, s32[384]{0:T(512)S(1)} %reshape.18.right_ref, s32[384]{0:T(512)S(1)} %reshape.19.target_ref, bf16[128,128,128]{2,1,0:T(8,128)(2,1)S(1)} %copy-done), custom_call_target="tpu_custom_call" | custom-call | flops 1610612736 | bytes 12582912 | tf_op jit(solution)/shard_map/pallas_call | solution.py:37
  91.0 0.0 reduce-scatter.2.cloned.1.call-update
  91.0 384.6 %reduce-scatter.2.cloned.1.call-done = f32[1,4,128,128]{3,2,1,0:T(8,128)} async-done(((f32[32,4,128,128]{3,2,1,0:T(8,128)}), f32[1,4,128,128]{3,2,1,0:T(8,128)}) %reduce-scatter.2.cloned.1.call-update) | async-done | bytes 262160 | tf_op jit(solution)/shard_map/reduce_scatter | solution.py:74
  475.7 1.6 convert_bitcast_fusion
  (3 shorter events, 0.0 us)
Async XLA Ops:
  6.5 58.4 %all-gather.2.cloned.1.call-start = ((), (), s32[]{:S(2)}) async-start(), calls=%async_computation.1 | async-start | bytes 4718592 | tf_op jit(solution)/shard_map/all_gather | solution.py:66
  7.3 468.4 %reduce-scatter.2.cloned.1.call-start = ((), (), s32[]{:S(2)}) async-start(), calls=%async_computation.2 | async-start | bytes 8650752 | tf_op jit(solution)/shard_map/reduce_scatter | solution.py:74
  64.9 2.2 copy-start
Sparse Core Ops, SparseCore 0:
  9.1 55.7 all-gather.1
  91.1 384.4 reduce-scatter.1

commit v2 on v1

--- a/solution.py
+++ b/solution.py
@@ -23,7 +23,7 @@
         prod = lax.dot_general(
             x_ref[l], x_ref[r], (((0,), (0,)), ((), ())), preferred_element_type=jnp.float32
         )
-        out_ref[k, t] += prod
+        out_ref[t, k] += prod
         return carry
 
     lax.fori_loop(0, OWNERS_PER_STEP * pair_count, body, 0, unroll=4)
@@ -36,7 +36,7 @@
     flops = 2 * owners * pair_count * block * block * block
     return pl.pallas_call(
         _products_kernel,
-        out_shape=jax.ShapeDtypeStruct((owners, CS, block, block), jnp.float32),
+        out_shape=jax.ShapeDtypeStruct((CS, owners, block, block), jnp.float32),
         grid_spec=pltpu.PrefetchScalarGridSpec(
             num_scalar_prefetch=3,
             grid=(steps,),
@@ -48,7 +48,7 @@
                 )
             ],
             out_specs=pl.BlockSpec(
-                (OWNERS_PER_STEP, CS, block, block), lambda i, *_: (i, 0, 0, 0)
+                (CS, OWNERS_PER_STEP, block, block), lambda i, *_: (0, i, 0, 0)
             ),
         ),
         compiler_params=pltpu.CompilerParams(
@@ -62,17 +62,81 @@
     )(left.reshape(-1), right.reshape(-1), target.reshape(-1), gathered)
 
 
+BLK_DIMS = (4, 4, 2)
+
+
+def _blk_coords(index):
+    coords = []
+    for size in reversed(BLK_DIMS):
+        coords.append(index % size)
+        index = index // size
+    return tuple(reversed(coords))
+
+
+def _blk_index(coords):
+    index = 0
+    for c, size in zip(coords, BLK_DIMS):
+        index = index * size + c
+    return index
+
+
+def _shift_route(dim, step):
+    route = []
+    for b in range(_blk_index(tuple(s - 1 for s in BLK_DIMS)) + 1):
+        coords = list(_blk_coords(b))
+        coords[dim] = (coords[dim] + step) % BLK_DIMS[dim]
+        route.append((b, _blk_index(tuple(coords))))
+    return route
+
+
+def ring_reduce_scatter(data, axis, dim, direction, coord):
+    size = BLK_DIMS[dim]
+    route = _shift_route(dim, direction)
+
+    def piece(k):
+        return lax.dynamic_index_in_dim(
+            data, (coord - direction * (1 + k)) % size, axis, keepdims=False
+        )
+
+    send = piece(0)
+    for k in range(size - 1):
+        arrived = lax.ppermute(send, "blk", route)
+        send = arrived + piece(k + 1)
+    return send
+
+
+def pair_reduce_scatter(data, dim, coord):
+    route = _shift_route(dim, 1)
+    other = lax.dynamic_index_in_dim(data, 1 - coord, 0, keepdims=False)
+    mine = lax.dynamic_index_in_dim(data, coord, 0, keepdims=False)
+    return lax.ppermute(other, "blk", route) + mine
+
+
 def per_device(x_blocks, pair_left, pair_right, pair_target):
     gathered = lax.all_gather(x_blocks, "grp", axis=0, tiled=True)
     group_count = lax.axis_size("blk")
+    assert group_count == BLK_DIMS[0] * BLK_DIMS[1] * BLK_DIMS[2]
     me = lax.axis_index("blk")
     visit = (me - 1 - jnp.arange(group_count, dtype=jnp.int32)) % group_count
     left = jnp.take(pair_left[0, 0], visit, axis=0)
     right = jnp.take(pair_right[0, 0], visit, axis=0)
     target = jnp.take(pair_target[0, 0], visit, axis=0)
     partials = owner_partials(gathered, left, right, target)
-    summed = lax.psum_scatter(partials, "blk", scatter_dimension=0, tiled=True)
     block = x_blocks.shape[1]
+    partials = partials.reshape((CS,) + BLK_DIMS + (block, block))
+    my_y, my_x, my_z = _blk_coords(me)
+    results = []
+    for c in range(CS):
+        data = partials[c]
+        direction = 1 if c % 2 == 0 else -1
+        if c < 2:
+            data = ring_reduce_scatter(data, 1, 1, direction, my_x)
+            data = ring_reduce_scatter(data, 0, 0, direction, my_y)
+        else:
+            data = ring_reduce_scatter(data, 0, 0, direction, my_y)
+            data = ring_reduce_scatter(data, 0, 1, direction, my_x)
+        results.append(pair_reduce_scatter(data, 2, my_z))
+    summed = jnp.stack(results)
     return summed.astype(jnp.bfloat16).reshape(1, 1, CS, block, block)
 
 

time: 484 us -> 194 us (0.40)
  the two profiles are of different devices: /device:TPU:0 before, /device:TPU:32 now
where the time goes in v2:
time: 194 us; the launch traced here: 193 us
  waiting for transfers between devices  80.1 us (41%)
  starting transfers between devices  53.5 us (28%)
  Pallas kernels  23.9 us (12%)
  local copies, waits for them, and re-layouts  18.4 us (9%)
  between operations  13.8 us (7%)
  other arithmetic  2.85 us (1%)
    all_gather x1, waiting for transfers between devices, per_device(): gathered = lax.all_gather(x_blocks, 'grp', axis=0, tiled=True)  50.5 us
    ppermute x24, starting transfers between devices, ring_reduce_scatter(): arrived = lax.ppermute(send, 'blk', route)  42.1 us
    ppermute x24, waiting for transfers between devices, ring_reduce_scatter(): arrived = lax.ppermute(send, 'blk', route)  24 us
    pallas_call x1, Pallas kernels, owner_partials(): pl.pallas_call(_products_kernel, out_shape=jax.ShapeDtypeStruct((CS, owne...  23.9 us
    ppermute x4, starting transfers between devices, pair_reduce_scatter(): return lax.ppermute(other, 'blk', route) + mine  11.3 us
    slice x1, local copies, waits for them, and re-layouts, per_device(): data = partials[c]  6.45 us
    unnamed x13, local copies, waits for them, and re-layouts  5.86 us
    ppermute x4, waiting for transfers between devices, pair_reduce_scatter(): return lax.ppermute(other, 'blk', route) + mine  4.9 us
  transfers between devices with their start and end apart: 29, of which 12 were waited for; matrix products, arithmetic and copies ran while one was open for 5% of the time, Pallas kernels for 0%

profile of v2, /device:TPU:32, one launch (start us, length us, event | category | flops | bytes accessed | tf_op | source)
XLA Modules:
  0.0 192.6 jit_solution(7111963111390675640)
XLA Ops:
  6.5 0.7 all-gather.2.cloned.1.call-update
  7.3 0.8 copy.13
  8.1 0.8 copy.12
  8.9 0.6 gather_fusion.2
  9.5 0.6 gather_fusion.1
  10.0 0.8 copy.11
  10.8 0.6 gather_fusion
  11.5 0.1 reshape.87.left_ref
  11.6 0.1 reshape.88.right_ref
  11.8 50.5 %all-gather.2.cloned.1.call-done.x_ref = bf16[128,128,128]{2,1,0:T(8,128)(2,1)} async-done(((bf16[16,128,128]{2,1,0:T(8,128)(2,1)}), bf16[128,128,128]{2,1,0:T(8,128)(2,1)}) %all-gather.2.cloned.1.call-update) | async-done | bytes 4194320 | tf_op jit(solution)/shard_map/all_gather | solution.py:116
  62.3 2.2 %copy-done = bf16[128,128,128]{2,1,0:T(8,128)(2,1)S(1)} copy-done((bf16[128,128,128]{2,1,0:T(8,128)(2,1)S(1)}, bf16[128,128,128]{2,1,0:T(8,128)(2,1)}, u32[]{:S(2)}) %copy-start) | copy-done | bytes 4194328
  64.5 23.9 %shard_map.46 = f32[4,32,128,128]{3,2,1,0:T(8,128)} custom-call(s32[384]{0:T(512)S(1)} %reshape.87.left_ref, s32[384]{0:T(512)S(1)} %reshape.88.right_ref, s32[384]{0:T(512)S(1)} %reshape.89.target_ref, bf16[128,128,128]{2,1,0:T(8,128)(2,1)S(1)} %copy-done), custom_call_target="tpu_custom_call" | custom-call | flops 1610612736 | bytes 12582912 | tf_op jit(solution)/shard_map/pallas_call | solution.py:37
  88.4 6.4 %fusion.9 = (f32[1,32,128,128]{3,2,1,0:T(8,128)S(1)}, f32[1,32,128,128]{3,2,1,0:T(8,128)S(1)}, f32[1,32,128,128]{3,2,1,0:T(8,128)}, f32[1,32,128,128]{3,2,1,0:T(8,128)}) fusion(f32[4,32,128,128]{3,2,1,0:T(8,128)} %shard_map.46), kind=kLoop, calls=%fused_computation.62 | loop fusion | bytes 16777216 | tf_op jit(solution)/shard_map/slice | solution.py:130
  94.9 1.4 copy-done.3
  96.2 0.8 dynamic-slice_bitcast_fusion
  97.0 3.2 %collective-permute-start.21 = (f32[4,2,128,128]{3,2,1,0:T(8,128)}, f32[4,2,128,128]{3,2,1,0:T(8,128)S(1)}, u32[]{:S(2)}, u32[]{:S(2)}) collective-permute-start(f32[4,2,128,128]{3,2,1,0:T(8,128)} %dynamic-slice_bitcast_fusion), channel_id=1, source_target_pairs={{0,192},{8,200},{16,208},{24,216},{32,224},{40,232},{48,240},{56,2... | collective-permute-start | bytes 1572872 | tf_op jit(solution)/shard_map/ppermute | solution.py:103
  100.2 1.9 dynamic-slice_bitcast_fusion.1
  102.1 1.2 dynamic-slice_bitcast_fusion.2
  103.3 2.8 %collective-permute-start.7 = (f32[4,2,128,128]{3,2,1,0:T(8,128)S(1)}, f32[4,2,128,128]{3,2,1,0:T(8,128)S(1)}, u32[]{:S(2)}, u32[]{:S(2)}) collective-permute-start(f32[4,2,128,128]{3,2,1,0:T(8,128)S(1)} %dynamic-slice_bitcast_fusion.2), channel_id=1, source_target_pairs={{0,48},{8,56},{16,0},{24,8},{32,16},{40,24},{48,32},{56,40},{64,11... | collective-permute-start | bytes 1572872 | tf_op jit(solution)/shard_map/ppermute | solution.py:103
  106.2 5.6 %collective-permute-done.21 = f32[4,2,128,128]{3,2,1,0:T(8,128)S(1)} collective-permute-done((f32[4,2,128,128]{3,2,1,0:T(8,128)}, f32[4,2,128,128]{3,2,1,0:T(8,128)S(1)}, u32[]{:S(2)}, u32[]{:S(2)}) %collective-permute-start.21) | collective-permute-done | bytes 524320 | tf_op jit(solution)/shard_map/ppermute | solution.py:103
  111.8 1.1 bitcast_add_fusion.2
  112.9 3.7 %collective-permute-start.22 = (f32[4,2,128,128]{3,2,1,0:T(8,128)S(1)}, f32[4,2,128,128]{3,2,1,0:T(8,128)S(1)}, u32[]{:S(2)}, u32[]{:S(2)}) collective-permute-start(f32[4,2,128,128]{3,2,1,0:T(8,128)S(1)} %bitcast_add_fusion.2), channel_id=1, source_target_pairs={{0,192},{8,200},{16,208},{24,216},{32,224},{40,232},{48,240},{56,2... | collective-permute-start | bytes 1572872 | tf_op jit(solution)/shard_map/ppermute | solution.py:103
  116.6 1.0 collective-permute-done.14
  117.8 3.7 %collective-permute-start.8 = (f32[4,2,128,128]{3,2,1,0:T(8,128)S(1)}, f32[4,2,128,128]{3,2,1,0:T(8,128)S(1)}, u32[]{:S(2)}, u32[]{:S(2)}) collective-permute-start(f32[4,2,128,128]{3,2,1,0:T(8,128)S(1)} %bitcast_add_fusion.8), channel_id=1, source_target_pairs={{0,48},{8,56},{16,0},{24,8},{32,16},{40,24},{48,32},{56,40},{64,11... | collective-permute-start | bytes 1572872 | tf_op jit(solution)/shard_map/ppermute | solution.py:103
  121.5 0.3 collective-permute-done
  121.9 6.8 %collective-permute-done.22 = f32[4,2,128,128]{3,2,1,0:T(8,128)S(1)} collective-permute-done((f32[4,2,128,128]{3,2,1,0:T(8,128)S(1)}, f32[4,2,128,128]{3,2,1,0:T(8,128)S(1)}, u32[]{:S(2)}, u32[]{:S(2)}) %collective-permute-start.22) | collective-permute-done | bytes 524320 | tf_op jit(solution)/shard_map/ppermute | solution.py:103
  128.8 3.8 %collective-permute-start.23 = (f32[4,2,128,128]{3,2,1,0:T(8,128)S(1)}, f32[4,2,128,128]{3,2,1,0:T(8,128)S(1)}, u32[]{:S(2)}, u32[]{:S(2)}) collective-permute-start(f32[4,2,128,128]{3,2,1,0:T(8,128)S(1)} %bitcast_add_fusion.1), channel_id=1, source_target_pairs={{0,192},{8,200},{16,208},{24,216},{32,224},{40,232},{48,240},{56,2... | collective-permute-start | bytes 1572872 | tf_op jit(solution)/shard_map/ppermute | solution.py:103
  132.5 1.1 collective-permute-done.15
  133.8 3.4 %collective-permute-start.9 = (f32[4,2,128,128]{3,2,1,0:T(8,128)S(1)}, f32[4,2,128,128]{3,2,1,0:T(8,128)S(1)}, u32[]{:S(2)}, u32[]{:S(2)}) collective-permute-start(f32[4,2,128,128]{3,2,1,0:T(8,128)S(1)} %bitcast_add_fusion.7), channel_id=1, source_target_pairs={{0,48},{8,56},{16,0},{24,8},{32,16},{40,24},{48,32},{56,40},{64,11... | collective-permute-start | bytes 1572872 | tf_op jit(solution)/shard_map/ppermute | solution.py:103
  137.4 6.8 %collective-permute-done.23 = f32[4,2,128,128]{3,2,1,0:T(8,128)S(1)} collective-permute-done((f32[4,2,128,128]{3,2,1,0:T(8,128)S(1)}, f32[4,2,128,128]{3,2,1,0:T(8,128)S(1)}, u32[]{:S(2)}, u32[]{:S(2)}) %collective-permute-start.23) | collective-permute-done | bytes 524320 | tf_op jit(solution)/shard_map/ppermute | solution.py:103
  144.3 2.9 %collective-permute-start.24 = (f32[2,128,128]{2,1,0:T(8,128)S(1)}, f32[2,128,128]{2,1,0:T(8,128)S(1)}, u32[]{:S(2)}, u32[]{:S(2)}) collective-permute-start(f32[2,128,128]{2,1,0:T(8,128)S(1)} %dynamic-slice_bitcast_fusion.4), channel_id=1, source_target_pairs={{0,48},{8,56},{16,0},{24,8},{32,16},{40,24},{48,32},{56,40},{64,11... | collective-permute-start | bytes 393224 | tf_op jit(solution)/shard_map/ppermute | solution.py:103
  147.2 1.6 collective-permute-done.16
  148.9 1.0 collective-permute-start.17
  149.9 3.3 %collective-permute-start.10 = (f32[2,128,128]{2,1,0:T(8,128)S(1)}, f32[2,128,128]{2,1,0:T(8,128)S(1)}, u32[]{:S(2)}, u32[]{:S(2)}) collective-permute-start(f32[2,128,128]{2,1,0:T(8,128)S(1)} %dynamic-slice_bitcast_fusion.6), channel_id=1, source_target_pairs={{0,192},{8,200},{16,208},{24,216},{32,224},{40,232},{48,240},{56,2... | collective-permute-start | bytes 393224 | tf_op jit(solution)/shard_map/ppermute | solution.py:103
  153.3 0.7 collective-permute-start.3
  154.0 3.2 %collective-permute-start.25 = (f32[2,128,128]{2,1,0:T(8,128)S(1)}, f32[2,128,128]{2,1,0:T(8,128)S(1)}, u32[]{:S(2)}, u32[]{:S(2)}) collective-permute-start(f32[2,128,128]{2,1,0:T(8,128)S(1)} %bitcast_add_fusion.14), channel_id=1, source_target_pairs={{0,48},{8,56},{16,0},{24,8},{32,16},{40,24},{48,32},{56,40},{64,11... | collective-permute-start | bytes 393224 | tf_op jit(solution)/shard_map/ppermute | solution.py:103
  157.4 3.3 %collective-permute-start.11 = (f32[2,128,128]{2,1,0:T(8,128)S(1)}, f32[2,128,128]{2,1,0:T(8,128)S(1)}, u32[]{:S(2)}, u32[]{:S(2)}) collective-permute-start(f32[2,128,128]{2,1,0:T(8,128)S(1)} %bitcast_add_fusion.20), channel_id=1, source_target_pairs={{0,192},{8,200},{16,208},{24,216},{32,224},{40,232},{48,240},{56,2... | collective-permute-start | bytes 393224 | tf_op jit(solution)/shard_map/ppermute | solution.py:103
  160.8 3.3 %collective-permute-start.26 = (f32[2,128,128]{2,1,0:T(8,128)S(1)}, f32[2,128,128]{2,1,0:T(8,128)S(1)}, u32[]{:S(2)}, u32[]{:S(2)}) collective-permute-start(f32[2,128,128]{2,1,0:T(8,128)S(1)} %bitcast_add_fusion.13), channel_id=1, source_target_pairs={{0,48},{8,56},{16,0},{24,8},{32,16},{40,24},{48,32},{56,40},{64,11... | collective-permute-start | bytes 393224 | tf_op jit(solution)/shard_map/ppermute | solution.py:103
  164.3 3.3 %collective-permute-start.12 = (f32[2,128,128]{2,1,0:T(8,128)S(1)}, f32[2,128,128]{2,1,0:T(8,128)S(1)}, u32[]{:S(2)}, u32[]{:S(2)}) collective-permute-start(f32[2,128,128]{2,1,0:T(8,128)S(1)} %bitcast_add_fusion.19), channel_id=1, source_target_pairs={{0,192},{8,200},{16,208},{24,216},{32,224},{40,232},{48,240},{56,2... | collective-permute-start | bytes 393224 | tf_op jit(solution)/shard_map/ppermute | solution.py:103
  167.7 1.8 collective-permute-start.27
  169.5 0.9 collective-permute-done.19
  170.4 3.4 %collective-permute-start.20 = (f32[128,128]{1,0:T(8,128)S(1)}, f32[128,128]{1,0:T(8,128)S(1)}, u32[]{:S(2)}, u32[]{:S(2)}) collective-permute-start(f32[128,128]{1,0:T(8,128)S(1)} %dynamic-slice_bitcast_fusion.9), channel_id=1, source_target_pairs={{0,8},{8,0},{16,24},{24,16},{32,40},{40,32},{48,56},{56,48},{64,72... | collective-permute-start | bytes 196616 | tf_op jit(solution)/shard_map/ppermute | solution.py:112
  173.9 2.7 %collective-permute-start.13 = (f32[128,128]{1,0:T(8,128)S(1)}, f32[128,128]{1,0:T(8,128)S(1)}, u32[]{:S(2)}, u32[]{:S(2)}) collective-permute-start(f32[128,128]{1,0:T(8,128)S(1)} %dynamic-slice_bitcast_fusion.10), channel_id=1, source_target_pairs={{0,8},{8,0},{16,24},{24,16},{32,40},{40,32},{48,56},{56,48},{64,72... | collective-permute-start | bytes 196616 | tf_op jit(solution)/shard_map/ppermute | solution.py:112
  176.6 3.4 %collective-permute-start.6 = (f32[128,128]{1,0:T(8,128)S(1)}, f32[128,128]{1,0:T(8,128)S(1)}, u32[]{:S(2)}, u32[]{:S(2)}) collective-permute-start(f32[128,128]{1,0:T(8,128)S(1)} %dynamic-slice_bitcast_fusion.11), channel_id=1, source_target_pairs={{0,8},{8,0},{16,24},{24,16},{32,40},{40,32},{48,56},{56,48},{64,72... | collective-permute-start | bytes 196616 | tf_op jit(solution)/shard_map/ppermute | solution.py:112
  180.1 0.4 collective-permute-done.20
  180.5 1.8 collective-permute-done.13
  182.3 2.7 %collective-permute-done.6 = f32[128,128]{1,0:T(8,128)S(1)} collective-permute-done((f32[128,128]{1,0:T(8,128)S(1)}, f32[128,128]{1,0:T(8,128)S(1)}, u32[]{:S(2)}, u32[]{:S(2)}) %collective-permute-start.6) | collective-permute-done | bytes 65568 | tf_op jit(solution)/shard_map/ppermute | solution.py:112
  185.0 0.7 pad_maximum_fusion
  (77 shorter events, 2.2 us)
Async XLA Ops:
  6.5 55.8 %all-gather.2.cloned.1.call-start = ((), (), s32[]{:S(2)}) async-start(), calls=%async_computation | async-start | bytes 4718592 | tf_op jit(solution)/shard_map/all_gather | solution.py:116
  62.3 2.2 %copy-start = (bf16[128,128,128]{2,1,0:T(8,128)(2,1)S(1)}, bf16[128,128,128]{2,1,0:T(8,128)(2,1)}, u32[]{:S(2)}) copy-start(bf16[128,128,128]{2,1,0:T(8,128)(2,1)} %all-gather.2.cloned.1.call-done.x_ref) | copy-start | bytes 12582916
  94.9 1.4 copy-start.3
  97.0 14.8 %collective-permute-start.21 = (f32[4,2,128,128]{3,2,1,0:T(8,128)}, f32[4,2,128,128]{3,2,1,0:T(8,128)S(1)}, u32[]{:S(2)}, u32[]{:S(2)}) collective-permute-start(f32[4,2,128,128]{3,2,1,0:T(8,128)} %dynamic-slice_bitcast_fusion), channel_id=1, source_target_pairs={{0,192},{8,200},{16,208},{24,216},{32,224},{40,232},{48,240},{56,2... | collective-permute-start | bytes 1572872 | tf_op jit(solution)/shard_map/ppermute | solution.py:103
  102.1 15.5 %collective-permute-start.14 = (f32[4,2,128,128]{3,2,1,0:T(8,128)}, f32[4,2,128,128]{3,2,1,0:T(8,128)S(1)}, u32[]{:S(2)}, u32[]{:S(2)}) collective-permute-start(f32[4,2,128,128]{3,2,1,0:T(8,128)} %dynamic-slice_bitcast_fusion.1), channel_id=1, source_target_pairs={{0,64},{8,72},{16,80},{24,88},{32,96},{40,104},{48,112},{56,120},{... | collective-permute-start | bytes 1572872 | tf_op jit(solution)/shard_map/ppermute | solution.py:103
  102.1 15.5 %copy-start.2 = (f32[1,32,128,128]{3,2,1,0:T(8,128)S(1)}, f32[1,32,128,128]{3,2,1,0:T(8,128)}, u32[]{:S(2)}) copy-start(f32[1,32,128,128]{3,2,1,0:T(8,128)} %get-tuple-element.8) | copy-start | bytes 6291460
  103.3 14.4 %collective-permute-start.7 = (f32[4,2,128,128]{3,2,1,0:T(8,128)S(1)}, f32[4,2,128,128]{3,2,1,0:T(8,128)S(1)}, u32[]{:S(2)}, u32[]{:S(2)}) collective-permute-start(f32[4,2,128,128]{3,2,1,0:T(8,128)S(1)} %dynamic-slice_bitcast_fusion.2), channel_id=1, source_target_pairs={{0,48},{8,56},{16,0},{24,8},{32,16},{40,24},{48,32},{56,40},{64,11... | collective-permute-start | bytes 1572872 | tf_op jit(solution)/shard_map/ppermute | solution.py:103
  106.1 11.6 %copy-start.1 = (f32[1,32,128,128]{3,2,1,0:T(8,128)S(1)}, f32[1,32,128,128]{3,2,1,0:T(8,128)}, u32[]{:S(2)}) copy-start(f32[1,32,128,128]{3,2,1,0:T(8,128)} %get-tuple-element.9) | copy-start | bytes 6291460
  106.1 15.6 %collective-permute-start = (f32[4,2,128,128]{3,2,1,0:T(8,128)S(1)}, f32[4,2,128,128]{3,2,1,0:T(8,128)S(1)}, u32[]{:S(2)}, u32[]{:S(2)}) collective-permute-start(f32[4,2,128,128]{3,2,1,0:T(8,128)S(1)} %dynamic-slice_bitcast_fusion.3), channel_id=1, source_target_pairs={{0,16},{8,24},{16,32},{24,40},{32,48},{40,56},{48,0},{56,8},{64,80... | collective-permute-start | bytes 1572872 | tf_op jit(solution)/shard_map/ppermute | solution.py:103
  112.9 15.8 %copy-start.4 = (f32[1,32,128,128]{3,2,1,0:T(8,128)S(1)}, f32[1,32,128,128]{3,2,1,0:T(8,128)}, u32[]{:S(2)}) copy-start(f32[1,32,128,128]{3,2,1,0:T(8,128)} %copy-done.3) | copy-start | bytes 6291460
  112.9 15.8 %collective-permute-start.22 = (f32[4,2,128,128]{3,2,1,0:T(8,128)S(1)}, f32[4,2,128,128]{3,2,1,0:T(8,128)S(1)}, u32[]{:S(2)}, u32[]{:S(2)}) collective-permute-start(f32[4,2,128,128]{3,2,1,0:T(8,128)S(1)} %bitcast_add_fusion.2), channel_id=1, source_target_pairs={{0,192},{8,200},{16,208},{24,216},{32,224},{40,232},{48,240},{56,2... | collective-permute-start | bytes 1572872 | tf_op jit(solution)/shard_map/ppermute | solution.py:103
  117.6 16.0 %collective-permute-start.15 = (f32[4,2,128,128]{3,2,1,0:T(8,128)S(1)}, f32[4,2,128,128]{3,2,1,0:T(8,128)S(1)}, u32[]{:S(2)}, u32[]{:S(2)}) collective-permute-start(f32[4,2,128,128]{3,2,1,0:T(8,128)S(1)} %bitcast_add_fusion.5), channel_id=1, source_target_pairs={{0,64},{8,72},{16,80},{24,88},{32,96},{40,104},{48,112},{56,120},{... | collective-permute-start | bytes 1572872 | tf_op jit(solution)/shard_map/ppermute | solution.py:103
  117.8 16.0 %collective-permute-start.8 = (f32[4,2,128,128]{3,2,1,0:T(8,128)S(1)}, f32[4,2,128,128]{3,2,1,0:T(8,128)S(1)}, u32[]{:S(2)}, u32[]{:S(2)}) collective-permute-start(f32[4,2,128,128]{3,2,1,0:T(8,128)S(1)} %bitcast_add_fusion.8), channel_id=1, source_target_pairs={{0,48},{8,56},{16,0},{24,8},{32,16},{40,24},{48,32},{56,40},{64,11... | collective-permute-start | bytes 1572872 | tf_op jit(solution)/shard_map/ppermute | solution.py:103
  121.8 15.4 %collective-permute-start.1 = (f32[4,2,128,128]{3,2,1,0:T(8,128)S(1)}, f32[4,2,128,128]{3,2,1,0:T(8,128)S(1)}, u32[]{:S(2)}, u32[]{:S(2)}) collective-permute-start(f32[4,2,128,128]{3,2,1,0:T(8,128)S(1)} %bitcast_add_fusion.11), channel_id=1, source_target_pairs={{0,16},{8,24},{16,32},{24,40},{32,48},{40,56},{48,0},{56,8},{64,80... | collective-permute-start | bytes 1572872 | tf_op jit(solution)/shard_map/ppermute | solution.py:103
  128.8 15.4 %collective-permute-start.23 = (f32[4,2,128,128]{3,2,1,0:T(8,128)S(1)}, f32[4,2,128,128]{3,2,1,0:T(8,128)S(1)}, u32[]{:S(2)}, u32[]{:S(2)}) collective-permute-start(f32[4,2,128,128]{3,2,1,0:T(8,128)S(1)} %bitcast_add_fusion.1), channel_id=1, source_target_pairs={{0,192},{8,200},{16,208},{24,216},{32,224},{40,232},{48,240},{56,2... | collective-permute-start | bytes 1572872 | tf_op jit(solution)/shard_map/ppermute | solution.py:103
  133.7 15.1 %collective-permute-start.16 = (f32[4,2,128,128]{3,2,1,0:T(8,128)S(1)}, f32[4,2,128,128]{3,2,1,0:T(8,128)S(1)}, u32[]{:S(2)}, u32[]{:S(2)}) collective-permute-start(f32[4,2,128,128]{3,2,1,0:T(8,128)S(1)} %bitcast_add_fusion.4), channel_id=1, source_target_pairs={{0,64},{8,72},{16,80},{24,88},{32,96},{40,104},{48,112},{56,120},{... | collective-permute-start | bytes 1572872 | tf_op jit(solution)/shard_map/ppermute | solution.py:103
  133.8 16.0 %collective-permute-start.9 = (f32[4,2,128,128]{3,2,1,0:T(8,128)S(1)}, f32[4,2,128,128]{3,2,1,0:T(8,128)S(1)}, u32[]{:S(2)}, u32[]{:S(2)}) collective-permute-start(f32[4,2,128,128]{3,2,1,0:T(8,128)S(1)} %bitcast_add_fusion.7), channel_id=1, source_target_pairs={{0,48},{8,56},{16,0},{24,8},{32,16},{40,24},{48,32},{56,40},{64,11... | collective-permute-start | bytes 1572872 | tf_op jit(solution)/shard_map/ppermute | solution.py:103
  137.3 15.9 %collective-permute-start.2 = (f32[4,2,128,128]{3,2,1,0:T(8,128)S(1)}, f32[4,2,128,128]{3,2,1,0:T(8,128)S(1)}, u32[]{:S(2)}, u32[]{:S(2)}) collective-permute-start(f32[4,2,128,128]{3,2,1,0:T(8,128)S(1)} %bitcast_add_fusion.10), channel_id=1, source_target_pairs={{0,16},{8,24},{16,32},{24,40},{32,48},{40,56},{48,0},{56,8},{64,80... | collective-permute-start | bytes 1572872 | tf_op jit(solution)/shard_map/ppermute | solution.py:103
  144.3 9.7 %collective-permute-start.24 = (f32[2,128,128]{2,1,0:T(8,128)S(1)}, f32[2,128,128]{2,1,0:T(8,128)S(1)}, u32[]{:S(2)}, u32[]{:S(2)}) collective-permute-start(f32[2,128,128]{2,1,0:T(8,128)S(1)} %dynamic-slice_bitcast_fusion.4), channel_id=1, source_target_pairs={{0,48},{8,56},{16,0},{24,8},{32,16},{40,24},{48,32},{56,40},{64,11... | collective-permute-start | bytes 393224 | tf_op jit(solution)/shard_map/ppermute | solution.py:103
  148.9 8.4 %collective-permute-start.17 = (f32[2,128,128]{2,1,0:T(8,128)S(1)}, f32[2,128,128]{2,1,0:T(8,128)S(1)}, u32[]{:S(2)}, u32[]{:S(2)}) collective-permute-start(f32[2,128,128]{2,1,0:T(8,128)S(1)} %dynamic-slice_bitcast_fusion.5), channel_id=1, source_target_pairs={{0,16},{8,24},{16,32},{24,40},{32,48},{40,56},{48,0},{56,8},{64,80... | collective-permute-start | bytes 393224 | tf_op jit(solution)/shard_map/ppermute | solution.py:103
  149.9 7.4 %collective-permute-start.10 = (f32[2,128,128]{2,1,0:T(8,128)S(1)}, f32[2,128,128]{2,1,0:T(8,128)S(1)}, u32[]{:S(2)}, u32[]{:S(2)}) collective-permute-start(f32[2,128,128]{2,1,0:T(8,128)S(1)} %dynamic-slice_bitcast_fusion.6), channel_id=1, source_target_pairs={{0,192},{8,200},{16,208},{24,216},{32,224},{40,232},{48,240},{56,2... | collective-permute-start | bytes 393224 | tf_op jit(solution)/shard_map/ppermute | solution.py:103
  153.3 7.3 %collective-permute-start.3 = (f32[2,128,128]{2,1,0:T(8,128)S(1)}, f32[2,128,128]{2,1,0:T(8,128)S(1)}, u32[]{:S(2)}, u32[]{:S(2)}) collective-permute-start(f32[2,128,128]{2,1,0:T(8,128)S(1)} %dynamic-slice_bitcast_fusion.7), channel_id=1, source_target_pairs={{0,64},{8,72},{16,80},{24,88},{32,96},{40,104},{48,112},{56,120},{... | collective-permute-start | bytes 393224 | tf_op jit(solution)/shard_map/ppermute | solution.py:103
  154.0 6.8 %collective-permute-start.25 = (f32[2,128,128]{2,1,0:T(8,128)S(1)}, f32[2,128,128]{2,1,0:T(8,128)S(1)}, u32[]{:S(2)}, u32[]{:S(2)}) collective-permute-start(f32[2,128,128]{2,1,0:T(8,128)S(1)} %bitcast_add_fusion.14), channel_id=1, source_target_pairs={{0,48},{8,56},{16,0},{24,8},{32,16},{40,24},{48,32},{56,40},{64,11... | collective-permute-start | bytes 393224 | tf_op jit(solution)/shard_map/ppermute | solution.py:103
  157.3 6.9 %collective-permute-start.18 = (f32[2,128,128]{2,1,0:T(8,128)S(1)}, f32[2,128,128]{2,1,0:T(8,128)S(1)}, u32[]{:S(2)}, u32[]{:S(2)}) collective-permute-start(f32[2,128,128]{2,1,0:T(8,128)S(1)} %bitcast_add_fusion.17), channel_id=1, source_target_pairs={{0,16},{8,24},{16,32},{24,40},{32,48},{40,56},{48,0},{56,8},{64,80... | collective-permute-start | bytes 393224 | tf_op jit(solution)/shard_map/ppermute | solution.py:103
  157.4 6.8 %collective-permute-start.11 = (f32[2,128,128]{2,1,0:T(8,128)S(1)}, f32[2,128,128]{2,1,0:T(8,128)S(1)}, u32[]{:S(2)}, u32[]{:S(2)}) collective-permute-start(f32[2,128,128]{2,1,0:T(8,128)S(1)} %bitcast_add_fusion.20), channel_id=1, source_target_pairs={{0,192},{8,200},{16,208},{24,216},{32,224},{40,232},{48,240},{56,2... | collective-permute-start | bytes 393224 | tf_op jit(solution)/shard_map/ppermute | solution.py:103
  160.7 6.9 %collective-permute-start.4 = (f32[2,128,128]{2,1,0:T(8,128)S(1)}, f32[2,128,128]{2,1,0:T(8,128)S(1)}, u32[]{:S(2)}, u32[]{:S(2)}) collective-permute-start(f32[2,128,128]{2,1,0:T(8,128)S(1)} %bitcast_add_fusion.23), channel_id=1, source_target_pairs={{0,64},{8,72},{16,80},{24,88},{32,96},{40,104},{48,112},{56,120},{... | collective-permute-start | bytes 393224 | tf_op jit(solution)/shard_map/ppermute | solution.py:103
  160.8 6.8 %collective-permute-start.26 = (f32[2,128,128]{2,1,0:T(8,128)S(1)}, f32[2,128,128]{2,1,0:T(8,128)S(1)}, u32[]{:S(2)}, u32[]{:S(2)}) collective-permute-start(f32[2,128,128]{2,1,0:T(8,128)S(1)} %bitcast_add_fusion.13), channel_id=1, source_target_pairs={{0,48},{8,56},{16,0},{24,8},{32,16},{40,24},{48,32},{56,40},{64,11... | collective-permute-start | bytes 393224 | tf_op jit(solution)/shard_map/ppermute | solution.py:103
  164.1 6.3 %collective-permute-start.19 = (f32[2,128,128]{2,1,0:T(8,128)S(1)}, f32[2,128,128]{2,1,0:T(8,128)S(1)}, u32[]{:S(2)}, u32[]{:S(2)}) collective-permute-start(f32[2,128,128]{2,1,0:T(8,128)S(1)} %bitcast_add_fusion.16), channel_id=1, source_target_pairs={{0,16},{8,24},{16,32},{24,40},{32,48},{40,56},{48,0},{56,8},{64,80... | collective-permute-start | bytes 393224 | tf_op jit(solution)/shard_map/ppermute | solution.py:103
  164.3 9.6 %collective-permute-start.12 = (f32[2,128,128]{2,1,0:T(8,128)S(1)}, f32[2,128,128]{2,1,0:T(8,128)S(1)}, u32[]{:S(2)}, u32[]{:S(2)}) collective-permute-start(f32[2,128,128]{2,1,0:T(8,128)S(1)} %bitcast_add_fusion.19), channel_id=1, source_target_pairs={{0,192},{8,200},{16,208},{24,216},{32,224},{40,232},{48,240},{56,2... | collective-permute-start | bytes 393224 | tf_op jit(solution)/shard_map/ppermute | solution.py:103
  167.6 9.0 %collective-permute-start.5 = (f32[2,128,128]{2,1,0:T(8,128)S(1)}, f32[2,128,128]{2,1,0:T(8,128)S(1)}, u32[]{:S(2)}, u32[]{:S(2)}) collective-permute-start(f32[2,128,128]{2,1,0:T(8,128)S(1)} %bitcast_add_fusion.22), channel_id=1, source_target_pairs={{0,64},{8,72},{16,80},{24,88},{32,96},{40,104},{48,112},{56,120},{... | collective-permute-start | bytes 393224 | tf_op jit(solution)/shard_map/ppermute | solution.py:103
  167.7 12.4 %collective-permute-start.27 = (f32[128,128]{1,0:T(8,128)S(1)}, f32[128,128]{1,0:T(8,128)S(1)}, u32[]{:S(2)}, u32[]{:S(2)}) collective-permute-start(f32[128,128]{1,0:T(8,128)S(1)} %dynamic-slice_bitcast_fusion.8), channel_id=1, source_target_pairs={{0,8},{8,0},{16,24},{24,16},{32,40},{40,32},{48,56},{56,48},{64,72... | collective-permute-start | bytes 196616 | tf_op jit(solution)/shard_map/ppermute | solution.py:112
  170.4 10.0 %collective-permute-start.20 = (f32[128,128]{1,0:T(8,128)S(1)}, f32[128,128]{1,0:T(8,128)S(1)}, u32[]{:S(2)}, u32[]{:S(2)}) collective-permute-start(f32[128,128]{1,0:T(8,128)S(1)} %dynamic-slice_bitcast_fusion.9), channel_id=1, source_target_pairs={{0,8},{8,0},{16,24},{24,16},{32,40},{40,32},{48,56},{56,48},{64,72... | collective-permute-start | bytes 196616 | tf_op jit(solution)/shard_map/ppermute | solution.py:112
  173.9 8.3 %collective-permute-start.13 = (f32[128,128]{1,0:T(8,128)S(1)}, f32[128,128]{1,0:T(8,128)S(1)}, u32[]{:S(2)}, u32[]{:S(2)}) collective-permute-start(f32[128,128]{1,0:T(8,128)S(1)} %dynamic-slice_bitcast_fusion.10), channel_id=1, source_target_pairs={{0,8},{8,0},{16,24},{24,16},{32,40},{40,32},{48,56},{56,48},{64,72... | collective-permute-start | bytes 196616 | tf_op jit(solution)/shard_map/ppermute | solution.py:112
  176.6 8.4 %collective-permute-start.6 = (f32[128,128]{1,0:T(8,128)S(1)}, f32[128,128]{1,0:T(8,128)S(1)}, u32[]{:S(2)}, u32[]{:S(2)}) collective-permute-start(f32[128,128]{1,0:T(8,128)S(1)} %dynamic-slice_bitcast_fusion.11), channel_id=1, source_target_pairs={{0,8},{8,0},{16,24},{24,16},{32,40},{40,32},{48,56},{56,48},{64,72... | collective-permute-start | bytes 196616 | tf_op jit(solution)/shard_map/ppermute | solution.py:112
Sparse Core Ops, SparseCore 0:
  9.1 53.1 all-gather.1

commit v3 on v2

--- a/solution.py
+++ b/solution.py
@@ -80,18 +80,20 @@
     return index
 
 
-def _shift_route(dim, step):
+def _shift_route(dim, step, members):
     route = []
     for b in range(_blk_index(tuple(s - 1 for s in BLK_DIMS)) + 1):
-        coords = list(_blk_coords(b))
-        coords[dim] = (coords[dim] + step) % BLK_DIMS[dim]
-        route.append((b, _blk_index(tuple(coords))))
+        for g in range(members):
+            coords = list(_blk_coords(b))
+            move = step if g % 2 == 0 else -step
+            coords[dim] = (coords[dim] + move) % BLK_DIMS[dim]
+            route.append((b * members + g, _blk_index(tuple(coords)) * members + g))
     return route
 
 
-def ring_reduce_scatter(data, axis, dim, direction, coord):
+def ring_reduce_scatter(data, axis, dim, direction, coord, members):
     size = BLK_DIMS[dim]
-    route = _shift_route(dim, direction)
+    route = _shift_route(dim, 1, members)
 
     def piece(k):
         return lax.dynamic_index_in_dim(
@@ -100,21 +102,22 @@
 
     send = piece(0)
     for k in range(size - 1):
-        arrived = lax.ppermute(send, "blk", route)
+        arrived = lax.ppermute(send, ("blk", "grp"), route)
         send = arrived + piece(k + 1)
     return send
 
 
-def pair_reduce_scatter(data, dim, coord):
-    route = _shift_route(dim, 1)
-    other = lax.dynamic_index_in_dim(data, 1 - coord, 0, keepdims=False)
-    mine = lax.dynamic_index_in_dim(data, coord, 0, keepdims=False)
-    return lax.ppermute(other, "blk", route) + mine
+def pair_reduce_scatter(data, axis, dim, coord, members):
+    route = _shift_route(dim, 1, members)
+    other = lax.dynamic_index_in_dim(data, 1 - coord, axis, keepdims=False)
+    mine = lax.dynamic_index_in_dim(data, coord, axis, keepdims=False)
+    return lax.ppermute(other, ("blk", "grp"), route) + mine
 
 
 def per_device(x_blocks, pair_left, pair_right, pair_target):
     gathered = lax.all_gather(x_blocks, "grp", axis=0, tiled=True)
     group_count = lax.axis_size("blk")
+    members = lax.axis_size("grp")
     assert group_count == BLK_DIMS[0] * BLK_DIMS[1] * BLK_DIMS[2]
     me = lax.axis_index("blk")
     visit = (me - 1 - jnp.arange(group_count, dtype=jnp.int32)) % group_count
@@ -125,18 +128,14 @@
     block = x_blocks.shape[1]
     partials = partials.reshape((CS,) + BLK_DIMS + (block, block))
     my_y, my_x, my_z = _blk_coords(me)
-    results = []
-    for c in range(CS):
-        data = partials[c]
-        direction = 1 if c % 2 == 0 else -1
-        if c < 2:
-            data = ring_reduce_scatter(data, 1, 1, direction, my_x)
-            data = ring_reduce_scatter(data, 0, 0, direction, my_y)
-        else:
-            data = ring_reduce_scatter(data, 0, 0, direction, my_y)
-            data = ring_reduce_scatter(data, 0, 1, direction, my_x)
-        results.append(pair_reduce_scatter(data, 2, my_z))
-    summed = jnp.stack(results)
+    direction = 1 - 2 * (lax.axis_index("grp") % 2)
+    half = CS // 2
+    first = ring_reduce_scatter(partials[:half], 2, 1, direction, my_x, members)
+    first = ring_reduce_scatter(first, 1, 0, direction, my_y, members)
+    second = ring_reduce_scatter(partials[half:], 1, 0, direction, my_y, members)
+    second = ring_reduce_scatter(second, 1, 1, direction, my_x, members)
+    both = jnp.concatenate([first, second], axis=0)
+    summed = pair_reduce_scatter(both, 1, 2, my_z, members)
     return summed.astype(jnp.bfloat16).reshape(1, 1, CS, block, block)
 
 

time: 194 us -> 202 us (1.041)
  waiting for transfers between devices: 80.1 us -> 119 us
  starting transfers between devices: 53.5 us -> 15.4 us
  other arithmetic: 2.85 us -> 11.6 us
    ppermute x28 -> x13, waiting for transfers between devices: 28.9 us -> 67.4 us  [the longest x12 60.2 us: ring_reduce_scatter(): arrived = lax.ppermute(send, ('blk', 'grp'), route)]
    ppermute x28 -> x13, starting transfers between devices: 53.4 us -> 15.4 us  [the longest x12 9.16 us: ring_reduce_scatter(): arrived = lax.ppermute(send, ('blk', 'grp'), route)]
    add x24 -> x12, other arithmetic: 2.02 us -> 10.8 us  [ring_reduce_scatter(): send = arrived + piece(k + 1)]
    squeeze x8 -> x2, local copies, waits for them, and re-layouts: 4.04 us -> 1.38 us  [piece(): lax.dynamic_index_in_dim(data, (coord - direction * (1 + k)) % size, axis...]
    unnamed x13 -> x7, local copies, waits for them, and re-layouts: 5.86 us -> 6.44 us
  transfers between devices with their start and end apart: 29 -> 14, of which waited for: 12 -> 13; matrix products, arithmetic and copies ran while one was open for 5% -> 8% of each run, Pallas kernels for 0% -> 0%
where the time goes in v3:
time: 202 us; the launch traced here: 200 us
  waiting for transfers between devices  119 us (59%)
  Pallas kernels  23.9 us (12%)
  local copies, waits for them, and re-layouts  16.4 us (8%)
  starting transfers between devices  15.4 us (8%)
  between operations  13.7 us (7%)
  other arithmetic  11.6 us (6%)
    ppermute x12, waiting for transfers between devices, ring_reduce_scatter(): arrived = lax.ppermute(send, ('blk', 'grp'), route)  60.2 us
    all_gather x1, waiting for transfers between devices, per_device(): gathered = lax.all_gather(x_blocks, 'grp', axis=0, tiled=True)  50.5 us
    pallas_call x1, Pallas kernels, owner_partials(): pl.pallas_call(_products_kernel, out_shape=jax.ShapeDtypeStruct((CS, owne...  23.9 us
    add x12, other arithmetic, ring_reduce_scatter(): send = arrived + piece(k + 1)  10.8 us
    ppermute x12, starting transfers between devices, ring_reduce_scatter(): arrived = lax.ppermute(send, ('blk', 'grp'), route)  9.16 us
    ppermute x1, waiting for transfers between devices, pair_reduce_scatter(): return lax.ppermute(other, ('blk', 'grp'), route) + mine  7.21 us
    unnamed x7, local copies, waits for them, and re-layouts  6.44 us
    slice x1, local copies, waits for them, and re-layouts, per_device(): partials[half:]  6.29 us
  transfers between devices with their start and end apart: 14, of which 13 were waited for; matrix products, arithmetic and copies ran while one was open for 8% of the time, Pallas kernels for 0%

profile of v3, /device:TPU:32, one launch (start us, length us, event | category | flops | bytes accessed | tf_op | source)
XLA Modules:
  0.0 199.7 jit_solution(6448213169852533541)
XLA Ops:
  6.5 0.7 all-gather.2.cloned.1.call-update
  7.3 0.8 copy.27
  8.1 0.8 copy.28
  8.9 0.6 gather_fusion
  9.5 0.6 gather_fusion.1
  10.1 0.8 copy.29
  10.8 0.6 gather_fusion.2
  11.5 0.1 reshape.20.left_ref
  11.6 0.1 reshape.21.right_ref
  11.7 0.1 reshape.22.target_ref
  11.8 50.5 %all-gather.2.cloned.1.call-done.x_ref = bf16[128,128,128]{2,1,0:T(8,128)(2,1)} async-done(((bf16[16,128,128]{2,1,0:T(8,128)(2,1)}), bf16[128,128,128]{2,1,0:T(8,128)(2,1)}) %all-gather.2.cloned.1.call-update) | async-done | bytes 4194320 | tf_op jit(solution)/shard_map/all_gather | solution.py:118
  62.3 2.2 %copy-done = bf16[128,128,128]{2,1,0:T(8,128)(2,1)S(1)} copy-done((bf16[128,128,128]{2,1,0:T(8,128)(2,1)S(1)}, bf16[128,128,128]{2,1,0:T(8,128)(2,1)}, u32[]{:S(2)}) %copy-start) | copy-done | bytes 4194328
  64.5 23.9 %shard_map.46 = f32[4,32,128,128]{3,2,1,0:T(8,128)} custom-call(s32[384]{0:T(512)S(1)} %reshape.20.left_ref, s32[384]{0:T(512)S(1)} %reshape.21.right_ref, s32[384]{0:T(512)S(1)} %reshape.22.target_ref, bf16[128,128,128]{2,1,0:T(8,128)(2,1)S(1)} %copy-done), custom_call_target="tpu_custom_call" | custom-call | flops 1610612736 | bytes 12582912 | tf_op jit(solution)/shard_map/pallas_call | solution.py:37
  88.4 6.3 %fusion.8 = (f32[2,32,128,128]{3,2,1,0:T(8,128)S(1)}, f32[2,32,128,128]{3,2,1,0:T(8,128)}) fusion(f32[4,32,128,128]{3,2,1,0:T(8,128)} %shard_map.46), kind=kLoop, calls=%fused_computation.48 | loop fusion | bytes 16777216 | tf_op jit(solution)/shard_map/slice | solution.py:135
  94.7 1.9 copy-done.1
  96.6 0.1 dynamic-slice_bitcast_fusion
  96.7 2.0 collective-permute-start.6
  98.7 1.3 dynamic-slice_bitcast_fusion.1
  100.0 1.5 collective-permute-start
  101.6 11.3 %collective-permute-done.6 = f32[2,4,2,128,128]{4,3,2,1,0:T(8,128)S(1)} collective-permute-done((f32[2,4,2,128,128]{4,3,2,1,0:T(8,128)S(1)}, f32[2,4,2,128,128]{4,3,2,1,0:T(8,128)S(1)}, u32[]{:S(2)}, u32[]{:S(2)}) %collective-permute-start.6) | collective-permute-done | bytes 1048608 | tf_op jit(solution)/shard_map/ppermute | solution.py:105
  112.8 1.3 bitcast_add_fusion.2
  114.2 0.8 collective-permute-start.7
  114.9 1.3 collective-permute-done
  116.2 2.6 %bitcast_add_fusion.5 = f32[2,4,2,128,128]{4,3,2,1,0:T(8,128)} fusion(f32[2,4,2,128,128]{4,3,2,1,0:T(8,128)} %collective-permute-done, f32[2,4,4,2,128,128]{5,4,3,2,1,0:T(8,128)} %bitcast.52, s32[]{:T(128)S(6)} %select_n.136), kind=kLoop, calls=%fused_computation.8 | loop fusion | flops 262144 | bytes 3145732 | tf_op jit(solution)/shard_map/add | solution.py:106
  118.9 0.3 collective-permute-start.1
  119.1 11.1 %collective-permute-done.7 = f32[2,4,2,128,128]{4,3,2,1,0:T(8,128)S(1)} collective-permute-done((f32[2,4,2,128,128]{4,3,2,1,0:T(8,128)S(1)}, f32[2,4,2,128,128]{4,3,2,1,0:T(8,128)S(1)}, u32[]{:S(2)}, u32[]{:S(2)}) %collective-permute-start.7) | collective-permute-done | bytes 1048608 | tf_op jit(solution)/shard_map/ppermute | solution.py:105
  130.3 1.3 bitcast_add_fusion.1
  131.6 0.1 collective-permute-start.8
  131.7 3.5 %collective-permute-done.1 = f32[2,4,2,128,128]{4,3,2,1,0:T(8,128)} collective-permute-done((f32[2,4,2,128,128]{4,3,2,1,0:T(8,128)}, f32[2,4,2,128,128]{4,3,2,1,0:T(8,128)}, u32[]{:S(2)}, u32[]{:S(2)}) %collective-permute-start.1) | collective-permute-done | bytes 1048608 | tf_op jit(solution)/shard_map/ppermute | solution.py:105
  135.2 2.6 %bitcast_add_fusion.4 = f32[2,4,2,128,128]{4,3,2,1,0:T(8,128)} fusion(f32[2,4,2,128,128]{4,3,2,1,0:T(8,128)} %collective-permute-done.1, f32[2,4,4,2,128,128]{5,4,3,2,1,0:T(8,128)} %bitcast.53, s32[]{:T(128)S(6)} %select_n.138), kind=kLoop, calls=%fused_computation.7 | loop fusion | flops 262144 | bytes 3145732 | tf_op jit(solution)/shard_map/add | solution.py:106
  137.8 9.8 %collective-permute-done.8 = f32[2,4,2,128,128]{4,3,2,1,0:T(8,128)S(1)} collective-permute-done((f32[2,4,2,128,128]{4,3,2,1,0:T(8,128)S(1)}, f32[2,4,2,128,128]{4,3,2,1,0:T(8,128)S(1)}, u32[]{:S(2)}, u32[]{:S(2)}) %collective-permute-start.8) | collective-permute-done | bytes 1048608 | tf_op jit(solution)/shard_map/ppermute | solution.py:105
  147.7 1.3 bitcast_add_fusion
  149.0 0.1 constant_dynamic-slice_fusion
  149.2 2.0 collective-permute-start.9
  151.1 2.9 %collective-permute-done.2 = f32[2,4,2,128,128]{4,3,2,1,0:T(8,128)S(1)} collective-permute-done((f32[2,4,2,128,128]{4,3,2,1,0:T(8,128)}, f32[2,4,2,128,128]{4,3,2,1,0:T(8,128)S(1)}, u32[]{:S(2)}, u32[]{:S(2)}) %collective-permute-start.2) | collective-permute-done | bytes 1048608 | tf_op jit(solution)/shard_map/ppermute | solution.py:105
  154.1 1.3 bitcast_add_fusion.3
  155.4 0.1 constant_dynamic-slice_fusion.4
  155.5 1.6 collective-permute-start.3
  157.1 0.5 collective-permute-start.10
  157.6 5.6 %collective-permute-done.3 = f32[2,2,128,128]{3,2,0,1:T(8,128)S(1)} collective-permute-done((f32[2,2,128,128]{3,2,0,1:T(8,128)S(1)}, f32[2,2,128,128]{3,2,0,1:T(8,128)S(1)}, u32[]{:S(2)}, u32[]{:S(2)}) %collective-permute-start.3) | collective-permute-done | bytes 262176 | tf_op jit(solution)/shard_map/ppermute | solution.py:105
  163.2 0.3 collective-permute-start.4
  163.6 1.2 collective-permute-done.10
  164.9 6.0 %collective-permute-done.4 = f32[2,2,128,128]{3,2,0,1:T(8,128)S(1)} collective-permute-done((f32[2,2,128,128]{3,2,0,1:T(8,128)S(1)}, f32[2,2,128,128]{3,2,0,1:T(8,128)S(1)}, u32[]{:S(2)}, u32[]{:S(2)}) %collective-permute-start.4) | collective-permute-done | bytes 262176 | tf_op jit(solution)/shard_map/ppermute | solution.py:105
  171.0 1.5 collective-permute-done.11
  172.5 6.1 %collective-permute-done.5 = f32[2,2,128,128]{3,2,0,1:T(8,128)S(1)} collective-permute-done((f32[2,2,128,128]{3,2,0,1:T(8,128)S(1)}, f32[2,2,128,128]{3,2,0,1:T(8,128)S(1)}, u32[]{:S(2)}, u32[]{:S(2)}) %collective-permute-start.5) | collective-permute-done | bytes 262176 | tf_op jit(solution)/shard_map/ppermute | solution.py:105
  178.6 6.3 %collective-permute-start.12 = (f32[4,128,128]{2,1,0:T(8,128)S(1)}, f32[4,128,128]{2,1,0:T(8,128)S(1)}, u32[]{:S(2)}, u32[]{:S(2)}) collective-permute-start(f32[4,128,128]{2,1,0:T(8,128)S(1)} %fusion.5), channel_id=1, source_target_pairs={{0,8},{1,9},{2,10},{3,11},{4,12},{5,13},{6,14},{7,15},{8,0},{9,1},... | collective-permute-start | bytes 786440 | tf_op jit(solution)/shard_map/ppermute | solution.py:114
  184.9 7.2 %collective-permute-done.12 = f32[4,128,128]{2,1,0:T(8,128)S(1)} collective-permute-done((f32[4,128,128]{2,1,0:T(8,128)S(1)}, f32[4,128,128]{2,1,0:T(8,128)S(1)}, u32[]{:S(2)}, u32[]{:S(2)}) %collective-permute-start.12) | collective-permute-done | bytes 262176 | tf_op jit(solution)/shard_map/ppermute | solution.py:114
  192.1 0.7 fusion.6
  (20 shorter events, 0.5 us)
Async XLA Ops:
  6.5 55.8 %all-gather.2.cloned.1.call-start = ((), (), s32[]{:S(2)}) async-start(), calls=%async_computation | async-start | bytes 4718592 | tf_op jit(solution)/shard_map/all_gather | solution.py:118
  62.3 2.2 %copy-start = (bf16[128,128,128]{2,1,0:T(8,128)(2,1)S(1)}, bf16[128,128,128]{2,1,0:T(8,128)(2,1)}, u32[]{:S(2)}) copy-start(bf16[128,128,128]{2,1,0:T(8,128)(2,1)} %all-gather.2.cloned.1.call-done.x_ref) | copy-start | bytes 12582916
  94.7 1.9 copy-start.1
  96.7 16.1 %collective-permute-start.6 = (f32[2,4,2,128,128]{4,3,2,1,0:T(8,128)S(1)}, f32[2,4,2,128,128]{4,3,2,1,0:T(8,128)S(1)}, u32[]{:S(2)}, u32[]{:S(2)}) collective-permute-start(f32[2,4,2,128,128]{4,3,2,1,0:T(8,128)S(1)} %dynamic-slice_bitcast_fusion), channel_id=1, source_target_pairs={{0,64},{1,193},{2,66},{3,195},{4,68},{5,197},{6,70},{7,199},{8,72}... | collective-permute-start | bytes 3145736 | tf_op jit(solution)/shard_map/ppermute | solution.py:105
  100.0 16.2 %collective-permute-start = (f32[2,4,2,128,128]{4,3,2,1,0:T(8,128)S(1)}, f32[2,4,2,128,128]{4,3,2,1,0:T(8,128)}, u32[]{:S(2)}, u32[]{:S(2)}) collective-permute-start(f32[2,4,2,128,128]{4,3,2,1,0:T(8,128)S(1)} %dynamic-slice_bitcast_fusion.1), channel_id=1, source_target_pairs={{0,16},{1,49},{2,18},{3,51},{4,20},{5,53},{6,22},{7,55},{8,24},{9,... | collective-permute-start | bytes 3145736 | tf_op jit(solution)/shard_map/ppermute | solution.py:105
  114.2 16.1 %collective-permute-start.7 = (f32[2,4,2,128,128]{4,3,2,1,0:T(8,128)S(1)}, f32[2,4,2,128,128]{4,3,2,1,0:T(8,128)S(1)}, u32[]{:S(2)}, u32[]{:S(2)}) collective-permute-start(f32[2,4,2,128,128]{4,3,2,1,0:T(8,128)S(1)} %bitcast_add_fusion.2), channel_id=1, source_target_pairs={{0,64},{1,193},{2,66},{3,195},{4,68},{5,197},{6,70},{7,199},{8,72}... | collective-permute-start | bytes 3145736 | tf_op jit(solution)/shard_map/ppermute | solution.py:105
  118.9 16.3 %collective-permute-start.1 = (f32[2,4,2,128,128]{4,3,2,1,0:T(8,128)}, f32[2,4,2,128,128]{4,3,2,1,0:T(8,128)}, u32[]{:S(2)}, u32[]{:S(2)}) collective-permute-start(f32[2,4,2,128,128]{4,3,2,1,0:T(8,128)} %bitcast_add_fusion.5), channel_id=1, source_target_pairs={{0,16},{1,49},{2,18},{3,51},{4,20},{5,53},{6,22},{7,55},{8,24},{9,... | collective-permute-start | bytes 3145736 | tf_op jit(solution)/shard_map/ppermute | solution.py:105
  131.6 16.1 %collective-permute-start.8 = (f32[2,4,2,128,128]{4,3,2,1,0:T(8,128)S(1)}, f32[2,4,2,128,128]{4,3,2,1,0:T(8,128)S(1)}, u32[]{:S(2)}, u32[]{:S(2)}) collective-permute-start(f32[2,4,2,128,128]{4,3,2,1,0:T(8,128)S(1)} %bitcast_add_fusion.1), channel_id=1, source_target_pairs={{0,64},{1,193},{2,66},{3,195},{4,68},{5,197},{6,70},{7,199},{8,72}... | collective-permute-start | bytes 3145736 | tf_op jit(solution)/shard_map/ppermute | solution.py:105
  137.8 16.2 %collective-permute-start.2 = (f32[2,4,2,128,128]{4,3,2,1,0:T(8,128)}, f32[2,4,2,128,128]{4,3,2,1,0:T(8,128)S(1)}, u32[]{:S(2)}, u32[]{:S(2)}) collective-permute-start(f32[2,4,2,128,128]{4,3,2,1,0:T(8,128)} %bitcast_add_fusion.4), channel_id=1, source_target_pairs={{0,16},{1,49},{2,18},{3,51},{4,20},{5,53},{6,22},{7,55},{8,24},{9,... | collective-permute-start | bytes 3145736 | tf_op jit(solution)/shard_map/ppermute | solution.py:105
  149.2 7.9 %collective-permute-start.9 = (f32[2,2,128,128]{3,2,0,1:T(8,128)S(1)}, f32[2,2,128,128]{3,2,0,1:T(8,128)S(1)}, u32[]{:S(2)}, u32[]{:S(2)}) collective-permute-start(f32[2,2,128,128]{3,2,0,1:T(8,128)S(1)} %bitcast.62), channel_id=1, source_target_pairs={{0,16},{1,49},{2,18},{3,51},{4,20},{5,53},{6,22},{7,55},{8,24},{9,... | collective-permute-start | bytes 786440 | tf_op jit(solution)/shard_map/ppermute | solution.py:105
  155.5 7.7 %collective-permute-start.3 = (f32[2,2,128,128]{3,2,0,1:T(8,128)S(1)}, f32[2,2,128,128]{3,2,0,1:T(8,128)S(1)}, u32[]{:S(2)}, u32[]{:S(2)}) collective-permute-start(f32[2,2,128,128]{3,2,0,1:T(8,128)S(1)} %bitcast.63), channel_id=1, source_target_pairs={{0,64},{1,193},{2,66},{3,195},{4,68},{5,197},{6,70},{7,199},{8,72}... | collective-permute-start | bytes 786440 | tf_op jit(solution)/shard_map/ppermute | solution.py:105
  157.1 7.7 %collective-permute-start.10 = (f32[2,2,128,128]{3,2,0,1:T(8,128)S(1)}, f32[2,2,128,128]{3,2,0,1:T(8,128)S(1)}, u32[]{:S(2)}, u32[]{:S(2)}) collective-permute-start(f32[2,2,128,128]{3,2,0,1:T(8,128)S(1)} %bitcast_add_fusion.8), channel_id=1, source_target_pairs={{0,16},{1,49},{2,18},{3,51},{4,20},{5,53},{6,22},{7,55},{8,24},{9,... | collective-permute-start | bytes 786440 | tf_op jit(solution)/shard_map/ppermute | solution.py:105
  163.2 7.7 %collective-permute-start.4 = (f32[2,2,128,128]{3,2,0,1:T(8,128)S(1)}, f32[2,2,128,128]{3,2,0,1:T(8,128)S(1)}, u32[]{:S(2)}, u32[]{:S(2)}) collective-permute-start(f32[2,2,128,128]{3,2,0,1:T(8,128)S(1)} %bitcast_add_fusion.11), channel_id=1, source_target_pairs={{0,64},{1,193},{2,66},{3,195},{4,68},{5,197},{6,70},{7,199},{8,72}... | collective-permute-start | bytes 786440 | tf_op jit(solution)/shard_map/ppermute | solution.py:105
  164.8 7.7 %collective-permute-start.11 = (f32[2,2,128,128]{3,2,0,1:T(8,128)S(1)}, f32[2,2,128,128]{3,2,0,1:T(8,128)S(1)}, u32[]{:S(2)}, u32[]{:S(2)}) collective-permute-start(f32[2,2,128,128]{3,2,0,1:T(8,128)S(1)} %bitcast_add_fusion.7), channel_id=1, source_target_pairs={{0,16},{1,49},{2,18},{3,51},{4,20},{5,53},{6,22},{7,55},{8,24},{9,... | collective-permute-start | bytes 786440 | tf_op jit(solution)/shard_map/ppermute | solution.py:105
  170.9 7.7 %collective-permute-start.5 = (f32[2,2,128,128]{3,2,0,1:T(8,128)S(1)}, f32[2,2,128,128]{3,2,0,1:T(8,128)S(1)}, u32[]{:S(2)}, u32[]{:S(2)}) collective-permute-start(f32[2,2,128,128]{3,2,0,1:T(8,128)S(1)} %bitcast_add_fusion.10), channel_id=1, source_target_pairs={{0,64},{1,193},{2,66},{3,195},{4,68},{5,197},{6,70},{7,199},{8,72}... | collective-permute-start | bytes 786440 | tf_op jit(solution)/shard_map/ppermute | solution.py:105
  178.6 13.5 %collective-permute-start.12 = (f32[4,128,128]{2,1,0:T(8,128)S(1)}, f32[4,128,128]{2,1,0:T(8,128)S(1)}, u32[]{:S(2)}, u32[]{:S(2)}) collective-permute-start(f32[4,128,128]{2,1,0:T(8,128)S(1)} %fusion.5), channel_id=1, source_target_pairs={{0,8},{1,9},{2,10},{3,11},{4,12},{5,13},{6,14},{7,15},{8,0},{9,1},... | collective-permute-start | bytes 786440 | tf_op jit(solution)/shard_map/ppermute | solution.py:114
Sparse Core Ops, SparseCore 0:
  9.1 53.1 all-gather.1

commit v4 on v2

--- a/solution.py
+++ b/solution.py
@@ -9,10 +9,11 @@
 OWNERS_PER_STEP = 4
 
 
-def _products_kernel(left_ref, right_ref, target_ref, x_ref, out_ref):
+def _products_kernel(left_ref, right_ref, target_ref, x_ref, *out_refs):
     step = pl.program_id(0)
     pair_count = left_ref.shape[0] // (pl.num_programs(0) * OWNERS_PER_STEP)
-    out_ref[...] = jnp.zeros_like(out_ref)
+    for out_ref in out_refs:
+        out_ref[...] = jnp.zeros_like(out_ref)
 
     def body(j, carry):
         k = j // pair_count
@@ -23,7 +24,12 @@
         prod = lax.dot_general(
             x_ref[l], x_ref[r], (((0,), (0,)), ((), ())), preferred_element_type=jnp.float32
         )
-        out_ref[t, k] += prod
+        for c, out_ref in enumerate(out_refs):
+
+            @pl.when(t == c)
+            def _(out_ref=out_ref):
+                out_ref[k] += prod
+
         return carry
 
     lax.fori_loop(0, OWNERS_PER_STEP * pair_count, body, 0, unroll=4)
@@ -36,7 +42,7 @@
     flops = 2 * owners * pair_count * block * block * block
     return pl.pallas_call(
         _products_kernel,
-        out_shape=jax.ShapeDtypeStruct((CS, owners, block, block), jnp.float32),
+        out_shape=[jax.ShapeDtypeStruct((owners, block, block), jnp.float32)] * CS,
         grid_spec=pltpu.PrefetchScalarGridSpec(
             num_scalar_prefetch=3,
             grid=(steps,),
@@ -47,9 +53,10 @@
                     pipeline_mode=pl.Buffered(1),
                 )
             ],
-            out_specs=pl.BlockSpec(
-                (CS, OWNERS_PER_STEP, block, block), lambda i, *_: (0, i, 0, 0)
-            ),
+            out_specs=[
+                pl.BlockSpec((OWNERS_PER_STEP, block, block), lambda i, *_: (i, 0, 0))
+            ]
+            * CS,
         ),
         compiler_params=pltpu.CompilerParams(
             dimension_semantics=("arbitrary",), vmem_limit_bytes=48 * 1024 * 1024
@@ -112,8 +119,47 @@
     return lax.ppermute(other, "blk", route) + mine
 
 
+LINE, CORES = 4, 2
+
+
+def line_all_gather(own):
+    z = lax.axis_index("grp") // CORES
+    core = lax.axis_index("grp") % CORES
+    members = LINE * CORES
+    up = [(g, g + CORES) for g in range(members) if g // CORES < LINE - 1]
+    down = [(g, g - CORES) for g in range(members) if g // CORES > 0]
+    below, above = [], []
+    send_up, send_down = own, own
+    for _ in range(LINE - 1):
+        send_up = lax.ppermute(send_up, "grp", up)
+        send_down = lax.ppermute(send_down, "grp", down)
+        below.append(send_up)
+        above.append(send_down)
+    below = jnp.stack(below)
+    above = jnp.stack(above)
+    mine = []
+    for spot in range(LINE):
+        from_below = lax.dynamic_index_in_dim(
+            below, jnp.clip(z - 1 - spot, 0, LINE - 2), 0, keepdims=False
+        )
+        from_above = lax.dynamic_index_in_dim(
+            above, jnp.clip(spot - z - 1, 0, LINE - 2), 0, keepdims=False
+        )
+        mine.append(
+            jnp.where(spot == z, own, jnp.where(spot < z, from_below, from_above))
+        )
+    mine = jnp.stack(mine)
+    sibling = [(g, g ^ 1) for g in range(members)]
+    theirs = lax.ppermute(mine, "grp", sibling)
+    first = jnp.where(core == 0, mine, theirs)
+    second = jnp.where(core == 0, theirs, mine)
+    gathered = jnp.stack([first, second], axis=1)
+    return gathered.reshape((members * own.shape[0],) + own.shape[1:])
+
+
 def per_device(x_blocks, pair_left, pair_right, pair_target):
-    gathered = lax.all_gather(x_blocks, "grp", axis=0, tiled=True)
+    assert lax.axis_size("grp") == LINE * CORES
+    gathered = line_all_gather(x_blocks)
     group_count = lax.axis_size("blk")
     assert group_count == BLK_DIMS[0] * BLK_DIMS[1] * BLK_DIMS[2]
     me = lax.axis_index("blk")
@@ -123,11 +169,10 @@
     target = jnp.take(pair_target[0, 0], visit, axis=0)
     partials = owner_partials(gathered, left, right, target)
     block = x_blocks.shape[1]
-    partials = partials.reshape((CS,) + BLK_DIMS + (block, block))
     my_y, my_x, my_z = _blk_coords(me)
     results = []
     for c in range(CS):
-        data = partials[c]
+        data = partials[c].reshape(BLK_DIMS + (block, block))
         direction = 1 if c % 2 == 0 else -1
         if c < 2:
             data = ring_reduce_scatter(data, 1, 1, direction, my_x)

time: 194 us -> 231 us (1.19)
  Pallas kernels: 23.9 us -> 79.8 us
  waiting for transfers between devices: 80.1 us -> 58.9 us
  starting transfers between devices: 53.5 us -> 72.1 us
  between operations: 13.8 us -> 0.6 us
  local copies, waits for them, and re-layouts: 18.4 us -> 11.1 us
  other arithmetic: 2.85 us -> 7.19 us
    pallas_call x1, Pallas kernels: 23.9 us -> 79.8 us  [owner_partials(): pl.pallas_call(_products_kernel, out_shape=[jax.ShapeDtypeStruct((owners,...]
    all_gather x1 -> x0, waiting for transfers between devices: 50.5 us -> none  [per_device(): gathered = lax.all_gather(x_blocks, 'grp', axis=0, tiled=True)]
    ppermute x0 -> x7, waiting for transfers between devices: none -> 31.2 us  [the longest x3 27.2 us: line_all_gather(): send_down = lax.ppermute(send_down, 'grp', down)]
    ppermute x0 -> x7, starting transfers between devices: none -> 17.5 us  [the longest x3 9.59 us: line_all_gather(): send_up = lax.ppermute(send_up, 'grp', up)]
    slice x1 -> x0, local copies, waits for them, and re-layouts: 6.45 us -> none  [per_device(): data = partials[c]]
    another operation x0 -> x6, other arithmetic: none -> 4.34 us  [the longest x2 2.14 us: line_all_gather(): gathered = jnp.stack([first, second], axis=1)]
    unnamed x13 -> x19, local copies, waits for them, and re-layouts: 5.86 us -> 1.64 us
    ppermute x24, waiting for transfers between devices: 24 us -> 21.2 us  [ring_reduce_scatter(): arrived = lax.ppermute(send, 'blk', route)]
  transfers between devices with their start and end apart: 29 -> 35, of which waited for: 12 -> 17; matrix products, arithmetic and copies ran while one was open for 5% -> 3% of each run, Pallas kernels for 0% -> 0%
where the time goes in v4:
time: 231 us; the launch traced here: 230 us
  Pallas kernels  79.8 us (35%)
  starting transfers between devices  72.1 us (31%)
  waiting for transfers between devices  58.9 us (25%)
  local copies, waits for them, and re-layouts  11.1 us (5%)
  other arithmetic  7.19 us (3%)
    pallas_call x1, Pallas kernels, owner_partials(): pl.pallas_call(_products_kernel, out_shape=[jax.ShapeDtypeStruct((owners,...  79.8 us
    ppermute x24, starting transfers between devices, ring_reduce_scatter(): arrived = lax.ppermute(send, 'blk', route)  40.6 us
    ppermute x3, waiting for transfers between devices, line_all_gather(): send_down = lax.ppermute(send_down, 'grp', down)  27.2 us
    ppermute x24, waiting for transfers between devices, ring_reduce_scatter(): arrived = lax.ppermute(send, 'blk', route)  21.2 us
    ppermute x4, starting transfers between devices, pair_reduce_scatter(): return lax.ppermute(other, 'blk', route) + mine  14 us
    ppermute x3, starting transfers between devices, line_all_gather(): send_up = lax.ppermute(send_up, 'grp', up)  9.59 us
    ppermute x3, starting transfers between devices, line_all_gather(): send_down = lax.ppermute(send_down, 'grp', down)  7.91 us
    ppermute x4, waiting for transfers between devices, pair_reduce_scatter(): return lax.ppermute(other, 'blk', route) + mine  6.57 us
  transfers between devices with their start and end apart: 35, of which 17 were waited for; matrix products, arithmetic and copies ran while one was open for 3% of the time, Pallas kernels for 0%

profile of v4, /device:TPU:32, one launch (start us, length us, event | category | flops | bytes accessed | tf_op | source)
XLA Modules:
  0.0 229.7 jit_solution(1820041808923494840)
XLA Ops:
  0.0 3.7 %collective-permute-start.3 = (bf16[16,128,128]{2,1,0:T(8,128)(2,1)}, bf16[16,128,128]{2,1,0:T(8,128)(2,1)S(1)}, u32[]{:S(2)}, u32[]{:S(2)}) collective-permute-start(bf16[16,128,128]{2,1,0:T(8,128)(2,1)} %param.6), channel_id=1, source_target_pairs={{2,0},{3,1},{4,2},{5,3},{6,4},{7,5},{10,8},{11,9},{12,10},{13,11},... | collective-permute-start | bytes 1572872 | tf_op jit(solution)/shard_map/ppermute | solution.py:135
  3.7 2.1 collective-permute-start
  5.9 10.1 %collective-permute-done.3 = bf16[16,128,128]{2,1,0:T(8,128)(2,1)S(1)} collective-permute-done((bf16[16,128,128]{2,1,0:T(8,128)(2,1)}, bf16[16,128,128]{2,1,0:T(8,128)(2,1)S(1)}, u32[]{:S(2)}, u32[]{:S(2)}) %collective-permute-start.3) | collective-permute-done | bytes 524320 | tf_op jit(solution)/shard_map/ppermute | solution.py:135
  15.9 2.0 collective-permute-start.4
  18.0 3.8 %collective-permute-start.1 = (bf16[16,128,128]{2,1,0:T(8,128)(2,1)S(1)}, bf16[16,128,128]{2,1,0:T(8,128)(2,1)S(1)}, u32[]{:S(2)}, u32[]{:S(2)}) collective-permute-start(bf16[16,128,128]{2,1,0:T(8,128)(2,1)S(1)} %collective-permute-done), channel_id=1, source_target_pairs={{0,2},{1,3},{2,4},{3,5},{4,6},{5,7},{8,10},{9,11},{10,12},{11,13},... | collective-permute-start | bytes 1572872 | tf_op jit(solution)/shard_map/ppermute | solution.py:134
  21.8 9.0 %collective-permute-done.4 = bf16[16,128,128]{2,1,0:T(8,128)(2,1)S(1)} collective-permute-done((bf16[16,128,128]{2,1,0:T(8,128)(2,1)S(1)}, bf16[16,128,128]{2,1,0:T(8,128)(2,1)S(1)}, u32[]{:S(2)}, u32[]{:S(2)}) %collective-permute-start.4) | collective-permute-done | bytes 524320 | tf_op jit(solution)/shard_map/ppermute | solution.py:135
  30.8 2.2 collective-permute-start.5
  33.0 3.6 %collective-permute-start.2 = (bf16[16,128,128]{2,1,0:T(8,128)(2,1)S(1)}, bf16[16,128,128]{2,1,0:T(8,128)(2,1)S(1)}, u32[]{:S(2)}, u32[]{:S(2)}) collective-permute-start(bf16[16,128,128]{2,1,0:T(8,128)(2,1)S(1)} %collective-permute-done.1), channel_id=1, source_target_pairs={{0,2},{1,3},{2,4},{3,5},{4,6},{5,7},{8,10},{9,11},{10,12},{11,13},... | collective-permute-start | bytes 1572872 | tf_op jit(solution)/shard_map/ppermute | solution.py:134
  36.7 8.1 %collective-permute-done.5 = bf16[16,128,128]{2,1,0:T(8,128)(2,1)S(1)} collective-permute-done((bf16[16,128,128]{2,1,0:T(8,128)(2,1)S(1)}, bf16[16,128,128]{2,1,0:T(8,128)(2,1)S(1)}, u32[]{:S(2)}, u32[]{:S(2)}) %collective-permute-start.5) | collective-permute-done | bytes 524320 | tf_op jit(solution)/shard_map/ppermute | solution.py:135
  45.0 1.9 collective-permute-done.2
  47.4 1.6 pad_maximum_fusion.1
  49.2 0.6 gather_fusion.2
  51.5 2.0 collective-permute-done.6
  53.5 1.8 select_bitcast_fusion.1
  55.7 2.3 copy.12
  58.0 79.8 %shard_map.46 = (f32[32,128,128]{2,1,0:T(8,128)S(1)}, f32[32,128,128]{2,1,0:T(8,128)S(1)}, f32[32,128,128]{2,1,0:T(8,128)}, f32[32,128,128]{2,1,0:T(8,128)}) custom-call(s32[384]{0:T(512)S(1)} %reshape.101.left_ref, s32[384]{0:T(512)S(1)} %reshape.102.right_ref, s32[384]{0:T(512)S(1)} %reshape.103.target_ref, bf16[128,128,128]{2,1,0:T(8,128)(2,1)} %bitcast.154), custom_call_target="tpu_custom_call" | custom-call | flops 1610612736 | bytes 12582912 | tf_op jit(solution)/shard_map/pallas_call | solution.py:43
  137.7 1.3 copy-done
  139.1 1.9 dynamic-slice_bitcast_fusion
  140.9 3.0 %collective-permute-start.28 = (f32[4,2,128,128]{3,2,1,0:T(8,128)}, f32[4,2,128,128]{3,2,1,0:T(8,128)S(1)}, u32[]{:S(2)}, u32[]{:S(2)}) collective-permute-start(f32[4,2,128,128]{3,2,1,0:T(8,128)} %dynamic-slice_bitcast_fusion), channel_id=1, source_target_pairs={{0,192},{8,200},{16,208},{24,216},{32,224},{40,232},{48,240},{56,2... | collective-permute-start | bytes 1572872 | tf_op jit(solution)/shard_map/ppermute | solution.py:110
  144.0 1.9 dynamic-slice_bitcast_fusion.1
  145.9 1.2 dynamic-slice_bitcast_fusion.2
  147.1 2.9 %collective-permute-start.14 = (f32[4,2,128,128]{3,2,1,0:T(8,128)S(1)}, f32[4,2,128,128]{3,2,1,0:T(8,128)S(1)}, u32[]{:S(2)}, u32[]{:S(2)}) collective-permute-start(f32[4,2,128,128]{3,2,1,0:T(8,128)S(1)} %dynamic-slice_bitcast_fusion.2), channel_id=1, source_target_pairs={{0,48},{8,56},{16,0},{24,8},{32,16},{40,24},{48,32},{56,40},{64,11... | collective-permute-start | bytes 1572872 | tf_op jit(solution)/shard_map/ppermute | solution.py:110
  150.1 5.7 %collective-permute-done.28 = f32[4,2,128,128]{3,2,1,0:T(8,128)S(1)} collective-permute-done((f32[4,2,128,128]{3,2,1,0:T(8,128)}, f32[4,2,128,128]{3,2,1,0:T(8,128)S(1)}, u32[]{:S(2)}, u32[]{:S(2)}) %collective-permute-start.28) | collective-permute-done | bytes 524320 | tf_op jit(solution)/shard_map/ppermute | solution.py:110
  155.8 1.1 bitcast_add_fusion.2
  156.9 3.7 %collective-permute-start.29 = (f32[4,2,128,128]{3,2,1,0:T(8,128)S(1)}, f32[4,2,128,128]{3,2,1,0:T(8,128)S(1)}, u32[]{:S(2)}, u32[]{:S(2)}) collective-permute-start(f32[4,2,128,128]{3,2,1,0:T(8,128)S(1)} %bitcast_add_fusion.2), channel_id=1, source_target_pairs={{0,192},{8,200},{16,208},{24,216},{32,224},{40,232},{48,240},{56,2... | collective-permute-start | bytes 1572872 | tf_op jit(solution)/shard_map/ppermute | solution.py:110
  161.3 3.8 %collective-permute-start.15 = (f32[4,2,128,128]{3,2,1,0:T(8,128)S(1)}, f32[4,2,128,128]{3,2,1,0:T(8,128)S(1)}, u32[]{:S(2)}, u32[]{:S(2)}) collective-permute-start(f32[4,2,128,128]{3,2,1,0:T(8,128)S(1)} %bitcast_add_fusion.8), channel_id=1, source_target_pairs={{0,48},{8,56},{16,0},{24,8},{32,16},{40,24},{48,32},{56,40},{64,11... | collective-permute-start | bytes 1572872 | tf_op jit(solution)/shard_map/ppermute | solution.py:110
  165.2 6.1 %collective-permute-done.29 = f32[4,2,128,128]{3,2,1,0:T(8,128)S(1)} collective-permute-done((f32[4,2,128,128]{3,2,1,0:T(8,128)S(1)}, f32[4,2,128,128]{3,2,1,0:T(8,128)S(1)}, u32[]{:S(2)}, u32[]{:S(2)}) %collective-permute-start.29) | collective-permute-done | bytes 524320 | tf_op jit(solution)/shard_map/ppermute | solution.py:110
  171.3 3.8 %collective-permute-start.30 = (f32[4,2,128,128]{3,2,1,0:T(8,128)S(1)}, f32[4,2,128,128]{3,2,1,0:T(8,128)S(1)}, u32[]{:S(2)}, u32[]{:S(2)}) collective-permute-start(f32[4,2,128,128]{3,2,1,0:T(8,128)S(1)} %bitcast_add_fusion.1), channel_id=1, source_target_pairs={{0,192},{8,200},{16,208},{24,216},{32,224},{40,232},{48,240},{56,2... | collective-permute-start | bytes 1572872 | tf_op jit(solution)/shard_map/ppermute | solution.py:110
  175.7 3.6 %collective-permute-start.16 = (f32[4,2,128,128]{3,2,1,0:T(8,128)S(1)}, f32[4,2,128,128]{3,2,1,0:T(8,128)S(1)}, u32[]{:S(2)}, u32[]{:S(2)}) collective-permute-start(f32[4,2,128,128]{3,2,1,0:T(8,128)S(1)} %bitcast_add_fusion.7), channel_id=1, source_target_pairs={{0,48},{8,56},{16,0},{24,8},{32,16},{40,24},{48,32},{56,40},{64,11... | collective-permute-start | bytes 1572872 | tf_op jit(solution)/shard_map/ppermute | solution.py:110
  179.4 5.5 %collective-permute-done.30 = f32[4,2,128,128]{3,2,1,0:T(8,128)S(1)} collective-permute-done((f32[4,2,128,128]{3,2,1,0:T(8,128)S(1)}, f32[4,2,128,128]{3,2,1,0:T(8,128)S(1)}, u32[]{:S(2)}, u32[]{:S(2)}) %collective-permute-start.30) | collective-permute-done | bytes 524320 | tf_op jit(solution)/shard_map/ppermute | solution.py:110
  185.0 2.8 %collective-permute-start.31 = (f32[2,128,128]{2,1,0:T(8,128)S(1)}, f32[2,128,128]{2,1,0:T(8,128)S(1)}, u32[]{:S(2)}, u32[]{:S(2)}) collective-permute-start(f32[2,128,128]{2,1,0:T(8,128)S(1)} %dynamic-slice_bitcast_fusion.4), channel_id=1, source_target_pairs={{0,48},{8,56},{16,0},{24,8},{32,16},{40,24},{48,32},{56,40},{64,11... | collective-permute-start | bytes 393224 | tf_op jit(solution)/shard_map/ppermute | solution.py:110
  187.8 1.0 collective-permute-done.23
  188.9 1.5 collective-permute-start.24
  190.5 2.2 collective-permute-start.17
  192.7 1.0 collective-permute-done.9
  194.0 2.8 %collective-permute-start.32 = (f32[2,128,128]{2,1,0:T(8,128)S(1)}, f32[2,128,128]{2,1,0:T(8,128)S(1)}, u32[]{:S(2)}, u32[]{:S(2)}) collective-permute-start(f32[2,128,128]{2,1,0:T(8,128)S(1)} %bitcast_add_fusion.14), channel_id=1, source_target_pairs={{0,48},{8,56},{16,0},{24,8},{32,16},{40,24},{48,32},{56,40},{64,11... | collective-permute-start | bytes 393224 | tf_op jit(solution)/shard_map/ppermute | solution.py:110
  196.9 3.3 %collective-permute-start.18 = (f32[2,128,128]{2,1,0:T(8,128)S(1)}, f32[2,128,128]{2,1,0:T(8,128)S(1)}, u32[]{:S(2)}, u32[]{:S(2)}) collective-permute-start(f32[2,128,128]{2,1,0:T(8,128)S(1)} %bitcast_add_fusion.20), channel_id=1, source_target_pairs={{0,192},{8,200},{16,208},{24,216},{32,224},{40,232},{48,240},{56,2... | collective-permute-start | bytes 393224 | tf_op jit(solution)/shard_map/ppermute | solution.py:110
  200.8 2.8 %collective-permute-start.33 = (f32[2,128,128]{2,1,0:T(8,128)S(1)}, f32[2,128,128]{2,1,0:T(8,128)S(1)}, u32[]{:S(2)}, u32[]{:S(2)}) collective-permute-start(f32[2,128,128]{2,1,0:T(8,128)S(1)} %bitcast_add_fusion.13), channel_id=1, source_target_pairs={{0,48},{8,56},{16,0},{24,8},{32,16},{40,24},{48,32},{56,40},{64,11... | collective-permute-start | bytes 393224 | tf_op jit(solution)/shard_map/ppermute | solution.py:110
  203.7 3.5 %collective-permute-start.19 = (f32[2,128,128]{2,1,0:T(8,128)S(1)}, f32[2,128,128]{2,1,0:T(8,128)S(1)}, u32[]{:S(2)}, u32[]{:S(2)}) collective-permute-start(f32[2,128,128]{2,1,0:T(8,128)S(1)} %bitcast_add_fusion.19), channel_id=1, source_target_pairs={{0,192},{8,200},{16,208},{24,216},{32,224},{40,232},{48,240},{56,2... | collective-permute-start | bytes 393224 | tf_op jit(solution)/shard_map/ppermute | solution.py:110
  207.3 0.9 collective-permute-done.11
  208.3 6.2 %collective-permute-start.34 = (f32[128,128]{1,0:T(8,128)S(1)}, f32[128,128]{1,0:T(8,128)S(1)}, u32[]{:S(2)}, u32[]{:S(2)}) collective-permute-start(f32[128,128]{1,0:T(8,128)S(1)} %dynamic-slice_bitcast_fusion.8), channel_id=1, source_target_pairs={{0,8},{8,0},{16,24},{24,16},{32,40},{40,32},{48,56},{56,48},{64,72... | collective-permute-start | bytes 196616 | tf_op jit(solution)/shard_map/ppermute | solution.py:119
  214.5 1.6 collective-permute-start.27
  216.2 4.5 %collective-permute-start.20 = (f32[128,128]{1,0:T(8,128)S(1)}, f32[128,128]{1,0:T(8,128)S(1)}, u32[]{:S(2)}, u32[]{:S(2)}) collective-permute-start(f32[128,128]{1,0:T(8,128)S(1)} %dynamic-slice_bitcast_fusion.10), channel_id=1, source_target_pairs={{0,8},{8,0},{16,24},{24,16},{32,40},{40,32},{48,56},{56,48},{64,72... | collective-permute-start | bytes 196616 | tf_op jit(solution)/shard_map/ppermute | solution.py:119
  220.7 1.6 collective-permute-start.13
  222.4 0.6 collective-permute-done.27
  223.1 1.8 collective-permute-done.20
  224.9 4.1 %collective-permute-done.13 = f32[128,128]{1,0:T(8,128)S(1)} collective-permute-done((f32[128,128]{1,0:T(8,128)S(1)}, f32[128,128]{1,0:T(8,128)S(1)}, u32[]{:S(2)}, u32[]{:S(2)}) %collective-permute-start.13) | collective-permute-done | bytes 65568 | tf_op jit(solution)/shard_map/ppermute | solution.py:119
  229.0 0.7 pad_maximum_fusion.4
  (100 shorter events, 6.1 us)
Async XLA Ops:
  0.0 15.9 %collective-permute-start.3 = (bf16[16,128,128]{2,1,0:T(8,128)(2,1)}, bf16[16,128,128]{2,1,0:T(8,128)(2,1)S(1)}, u32[]{:S(2)}, u32[]{:S(2)}) collective-permute-start(bf16[16,128,128]{2,1,0:T(8,128)(2,1)} %param.6), channel_id=1, source_target_pairs={{2,0},{3,1},{4,2},{5,3},{6,4},{7,5},{10,8},{11,9},{12,10},{13,11},... | collective-permute-start | bytes 1572872 | tf_op jit(solution)/shard_map/ppermute | solution.py:135
  3.7 14.2 %collective-permute-start = (bf16[16,128,128]{2,1,0:T(8,128)(2,1)}, bf16[16,128,128]{2,1,0:T(8,128)(2,1)S(1)}, u32[]{:S(2)}, u32[]{:S(2)}) collective-permute-start(bf16[16,128,128]{2,1,0:T(8,128)(2,1)} %param.6), channel_id=1, source_target_pairs={{0,2},{1,3},{2,4},{3,5},{4,6},{5,7},{8,10},{9,11},{10,12},{11,13},... | collective-permute-start | bytes 1572872 | tf_op jit(solution)/shard_map/ppermute | solution.py:134
  15.9 14.9 %collective-permute-start.4 = (bf16[16,128,128]{2,1,0:T(8,128)(2,1)S(1)}, bf16[16,128,128]{2,1,0:T(8,128)(2,1)S(1)}, u32[]{:S(2)}, u32[]{:S(2)}) collective-permute-start(bf16[16,128,128]{2,1,0:T(8,128)(2,1)S(1)} %collective-permute-done.3), channel_id=1, source_target_pairs={{2,0},{3,1},{4,2},{5,3},{6,4},{7,5},{10,8},{11,9},{12,10},{13,11},... | collective-permute-start | bytes 1572872 | tf_op jit(solution)/shard_map/ppermute | solution.py:135
  18.0 15.0 %collective-permute-start.1 = (bf16[16,128,128]{2,1,0:T(8,128)(2,1)S(1)}, bf16[16,128,128]{2,1,0:T(8,128)(2,1)S(1)}, u32[]{:S(2)}, u32[]{:S(2)}) collective-permute-start(bf16[16,128,128]{2,1,0:T(8,128)(2,1)S(1)} %collective-permute-done), channel_id=1, source_target_pairs={{0,2},{1,3},{2,4},{3,5},{4,6},{5,7},{8,10},{9,11},{10,12},{11,13},... | collective-permute-start | bytes 1572872 | tf_op jit(solution)/shard_map/ppermute | solution.py:134
  30.8 14.0 %collective-permute-start.5 = (bf16[16,128,128]{2,1,0:T(8,128)(2,1)S(1)}, bf16[16,128,128]{2,1,0:T(8,128)(2,1)S(1)}, u32[]{:S(2)}, u32[]{:S(2)}) collective-permute-start(bf16[16,128,128]{2,1,0:T(8,128)(2,1)S(1)} %collective-permute-done.4), channel_id=1, source_target_pairs={{2,0},{3,1},{4,2},{5,3},{6,4},{7,5},{10,8},{11,9},{12,10},{13,11},... | collective-permute-start | bytes 1572872 | tf_op jit(solution)/shard_map/ppermute | solution.py:135
  33.0 13.9 %collective-permute-start.2 = (bf16[16,128,128]{2,1,0:T(8,128)(2,1)S(1)}, bf16[16,128,128]{2,1,0:T(8,128)(2,1)S(1)}, u32[]{:S(2)}, u32[]{:S(2)}) collective-permute-start(bf16[16,128,128]{2,1,0:T(8,128)(2,1)S(1)} %collective-permute-done.1), channel_id=1, source_target_pairs={{0,2},{1,3},{2,4},{3,5},{4,6},{5,7},{8,10},{9,11},{10,12},{11,13},... | collective-permute-start | bytes 1572872 | tf_op jit(solution)/shard_map/ppermute | solution.py:134
  45.0 2.1 copy-start.4
  47.4 1.7 copy-start.5
  47.4 1.7 copy-start.6
  47.4 3.0 %copy-start.7 = (s32[1,1,32,12]{2,1,3,0:T(1,128)S(1)}, s32[1,1,32,12]{2,1,3,0:T(1,128)}, u32[]{:S(2)}) copy-start(s32[1,1,32,12]{2,1,3,0:T(1,128)} %param.7) | copy-start | bytes 4612
  49.0 4.5 %collective-permute-start.6 = (bf16[4,16,128,128]{3,2,1,0:T(8,128)(2,1)}, bf16[4,16,128,128]{3,2,1,0:T(8,128)(2,1)}, u32[]{:S(2)}, u32[]{:S(2)}) collective-permute-start(bf16[4,16,128,128]{3,2,1,0:T(8,128)(2,1)} %pad_maximum_fusion.1), channel_id=1, source_target_pairs={{0,1},{1,0},{2,3},{3,2},{4,5},{5,4},{6,7},{7,6},{8,9},{9,8},{10,11... | collective-permute-start | bytes 6291464 | tf_op jit(solution)/shard_map/ppermute | solution.py:153
  137.7 1.3 copy-start
  140.9 14.9 %collective-permute-start.28 = (f32[4,2,128,128]{3,2,1,0:T(8,128)}, f32[4,2,128,128]{3,2,1,0:T(8,128)S(1)}, u32[]{:S(2)}, u32[]{:S(2)}) collective-permute-start(f32[4,2,128,128]{3,2,1,0:T(8,128)} %dynamic-slice_bitcast_fusion), channel_id=1, source_target_pairs={{0,192},{8,200},{16,208},{24,216},{32,224},{40,232},{48,240},{56,2... | collective-permute-start | bytes 1572872 | tf_op jit(solution)/shard_map/ppermute | solution.py:110
  145.9 15.2 %collective-permute-start.21 = (f32[4,2,128,128]{3,2,1,0:T(8,128)}, f32[4,2,128,128]{3,2,1,0:T(8,128)S(1)}, u32[]{:S(2)}, u32[]{:S(2)}) collective-permute-start(f32[4,2,128,128]{3,2,1,0:T(8,128)} %dynamic-slice_bitcast_fusion.1), channel_id=1, source_target_pairs={{0,64},{8,72},{16,80},{24,88},{32,96},{40,104},{48,112},{56,120},{... | collective-permute-start | bytes 1572872 | tf_op jit(solution)/shard_map/ppermute | solution.py:110
  145.9 15.1 %copy-start.2 = (f32[32,128,128]{2,1,0:T(8,128)S(1)}, f32[32,128,128]{2,1,0:T(8,128)}, u32[]{:S(2)}) copy-start(f32[32,128,128]{2,1,0:T(8,128)} %get-tuple-element.12) | copy-start | bytes 6291460
  147.1 14.1 %collective-permute-start.14 = (f32[4,2,128,128]{3,2,1,0:T(8,128)S(1)}, f32[4,2,128,128]{3,2,1,0:T(8,128)S(1)}, u32[]{:S(2)}, u32[]{:S(2)}) collective-permute-start(f32[4,2,128,128]{3,2,1,0:T(8,128)S(1)} %dynamic-slice_bitcast_fusion.2), channel_id=1, source_target_pairs={{0,48},{8,56},{16,0},{24,8},{32,16},{40,24},{48,32},{56,40},{64,11... | collective-permute-start | bytes 1572872 | tf_op jit(solution)/shard_map/ppermute | solution.py:110
  150.0 11.2 %copy-start.1 = (f32[32,128,128]{2,1,0:T(8,128)S(1)}, f32[32,128,128]{2,1,0:T(8,128)}, u32[]{:S(2)}) copy-start(f32[32,128,128]{2,1,0:T(8,128)} %copy-done) | copy-start | bytes 6291460
  150.0 15.0 %collective-permute-start.7 = (f32[4,2,128,128]{3,2,1,0:T(8,128)S(1)}, f32[4,2,128,128]{3,2,1,0:T(8,128)S(1)}, u32[]{:S(2)}, u32[]{:S(2)}) collective-permute-start(f32[4,2,128,128]{3,2,1,0:T(8,128)S(1)} %dynamic-slice_bitcast_fusion.3), channel_id=1, source_target_pairs={{0,16},{8,24},{16,32},{24,40},{32,48},{40,56},{48,0},{56,8},{64,80... | collective-permute-start | bytes 1572872 | tf_op jit(solution)/shard_map/ppermute | solution.py:110
  156.9 14.3 %copy-start.3 = (f32[32,128,128]{2,1,0:T(8,128)S(1)}, f32[32,128,128]{2,1,0:T(8,128)}, u32[]{:S(2)}) copy-start(f32[32,128,128]{2,1,0:T(8,128)} %get-tuple-element.13) | copy-start | bytes 6291460
  156.9 14.3 %collective-permute-start.29 = (f32[4,2,128,128]{3,2,1,0:T(8,128)S(1)}, f32[4,2,128,128]{3,2,1,0:T(8,128)S(1)}, u32[]{:S(2)}, u32[]{:S(2)}) collective-permute-start(f32[4,2,128,128]{3,2,1,0:T(8,128)S(1)} %bitcast_add_fusion.2), channel_id=1, source_target_pairs={{0,192},{8,200},{16,208},{24,216},{32,224},{40,232},{48,240},{56,2... | collective-permute-start | bytes 1572872 | tf_op jit(solution)/shard_map/ppermute | solution.py:110
  161.1 14.2 %collective-permute-start.22 = (f32[4,2,128,128]{3,2,1,0:T(8,128)S(1)}, f32[4,2,128,128]{3,2,1,0:T(8,128)S(1)}, u32[]{:S(2)}, u32[]{:S(2)}) collective-permute-start(f32[4,2,128,128]{3,2,1,0:T(8,128)S(1)} %bitcast_add_fusion.5), channel_id=1, source_target_pairs={{0,64},{8,72},{16,80},{24,88},{32,96},{40,104},{48,112},{56,120},{... | collective-permute-start | bytes 1572872 | tf_op jit(solution)/shard_map/ppermute | solution.py:110
  161.3 14.3 %collective-permute-start.15 = (f32[4,2,128,128]{3,2,1,0:T(8,128)S(1)}, f32[4,2,128,128]{3,2,1,0:T(8,128)S(1)}, u32[]{:S(2)}, u32[]{:S(2)}) collective-permute-start(f32[4,2,128,128]{3,2,1,0:T(8,128)S(1)} %bitcast_add_fusion.8), channel_id=1, source_target_pairs={{0,48},{8,56},{16,0},{24,8},{32,16},{40,24},{48,32},{56,40},{64,11... | collective-permute-start | bytes 1572872 | tf_op jit(solution)/shard_map/ppermute | solution.py:110
  165.1 14.1 %collective-permute-start.8 = (f32[4,2,128,128]{3,2,1,0:T(8,128)S(1)}, f32[4,2,128,128]{3,2,1,0:T(8,128)S(1)}, u32[]{:S(2)}, u32[]{:S(2)}) collective-permute-start(f32[4,2,128,128]{3,2,1,0:T(8,128)S(1)} %bitcast_add_fusion.11), channel_id=1, source_target_pairs={{0,16},{8,24},{16,32},{24,40},{32,48},{40,56},{48,0},{56,8},{64,80... | collective-permute-start | bytes 1572872 | tf_op jit(solution)/shard_map/ppermute | solution.py:110
  171.3 13.6 %collective-permute-start.30 = (f32[4,2,128,128]{3,2,1,0:T(8,128)S(1)}, f32[4,2,128,128]{3,2,1,0:T(8,128)S(1)}, u32[]{:S(2)}, u32[]{:S(2)}) collective-permute-start(f32[4,2,128,128]{3,2,1,0:T(8,128)S(1)} %bitcast_add_fusion.1), channel_id=1, source_target_pairs={{0,192},{8,200},{16,208},{24,216},{32,224},{40,232},{48,240},{56,2... | collective-permute-start | bytes 1572872 | tf_op jit(solution)/shard_map/ppermute | solution.py:110
  175.3 13.5 %collective-permute-start.23 = (f32[4,2,128,128]{3,2,1,0:T(8,128)S(1)}, f32[4,2,128,128]{3,2,1,0:T(8,128)S(1)}, u32[]{:S(2)}, u32[]{:S(2)}) collective-permute-start(f32[4,2,128,128]{3,2,1,0:T(8,128)S(1)} %bitcast_add_fusion.4), channel_id=1, source_target_pairs={{0,64},{8,72},{16,80},{24,88},{32,96},{40,104},{48,112},{56,120},{... | collective-permute-start | bytes 1572872 | tf_op jit(solution)/shard_map/ppermute | solution.py:110
  175.7 14.8 %collective-permute-start.16 = (f32[4,2,128,128]{3,2,1,0:T(8,128)S(1)}, f32[4,2,128,128]{3,2,1,0:T(8,128)S(1)}, u32[]{:S(2)}, u32[]{:S(2)}) collective-permute-start(f32[4,2,128,128]{3,2,1,0:T(8,128)S(1)} %bitcast_add_fusion.7), channel_id=1, source_target_pairs={{0,48},{8,56},{16,0},{24,8},{32,16},{40,24},{48,32},{56,40},{64,11... | collective-permute-start | bytes 1572872 | tf_op jit(solution)/shard_map/ppermute | solution.py:110
  179.3 14.4 %collective-permute-start.9 = (f32[4,2,128,128]{3,2,1,0:T(8,128)S(1)}, f32[4,2,128,128]{3,2,1,0:T(8,128)S(1)}, u32[]{:S(2)}, u32[]{:S(2)}) collective-permute-start(f32[4,2,128,128]{3,2,1,0:T(8,128)S(1)} %bitcast_add_fusion.10), channel_id=1, source_target_pairs={{0,16},{8,24},{16,32},{24,40},{32,48},{40,56},{48,0},{56,8},{64,80... | collective-permute-start | bytes 1572872 | tf_op jit(solution)/shard_map/ppermute | solution.py:110
  185.0 8.9 %collective-permute-start.31 = (f32[2,128,128]{2,1,0:T(8,128)S(1)}, f32[2,128,128]{2,1,0:T(8,128)S(1)}, u32[]{:S(2)}, u32[]{:S(2)}) collective-permute-start(f32[2,128,128]{2,1,0:T(8,128)S(1)} %dynamic-slice_bitcast_fusion.4), channel_id=1, source_target_pairs={{0,48},{8,56},{16,0},{24,8},{32,16},{40,24},{48,32},{56,40},{64,11... | collective-permute-start | bytes 393224 | tf_op jit(solution)/shard_map/ppermute | solution.py:110
  188.9 7.8 %collective-permute-start.24 = (f32[2,128,128]{2,1,0:T(8,128)S(1)}, f32[2,128,128]{2,1,0:T(8,128)S(1)}, u32[]{:S(2)}, u32[]{:S(2)}) collective-permute-start(f32[2,128,128]{2,1,0:T(8,128)S(1)} %dynamic-slice_bitcast_fusion.5), channel_id=1, source_target_pairs={{0,16},{8,24},{16,32},{24,40},{32,48},{40,56},{48,0},{56,8},{64,80... | collective-permute-start | bytes 393224 | tf_op jit(solution)/shard_map/ppermute | solution.py:110
  190.5 6.3 %collective-permute-start.17 = (f32[2,128,128]{2,1,0:T(8,128)S(1)}, f32[2,128,128]{2,1,0:T(8,128)S(1)}, u32[]{:S(2)}, u32[]{:S(2)}) collective-permute-start(f32[2,128,128]{2,1,0:T(8,128)S(1)} %dynamic-slice_bitcast_fusion.6), channel_id=1, source_target_pairs={{0,192},{8,200},{16,208},{24,216},{32,224},{40,232},{48,240},{56,2... | collective-permute-start | bytes 393224 | tf_op jit(solution)/shard_map/ppermute | solution.py:110
  193.8 6.8 %collective-permute-start.10 = (f32[2,128,128]{2,1,0:T(8,128)S(1)}, f32[2,128,128]{2,1,0:T(8,128)S(1)}, u32[]{:S(2)}, u32[]{:S(2)}) collective-permute-start(f32[2,128,128]{2,1,0:T(8,128)S(1)} %dynamic-slice_bitcast_fusion.7), channel_id=1, source_target_pairs={{0,64},{8,72},{16,80},{24,88},{32,96},{40,104},{48,112},{56,120},{... | collective-permute-start | bytes 393224 | tf_op jit(solution)/shard_map/ppermute | solution.py:110
  194.0 6.8 %collective-permute-start.32 = (f32[2,128,128]{2,1,0:T(8,128)S(1)}, f32[2,128,128]{2,1,0:T(8,128)S(1)}, u32[]{:S(2)}, u32[]{:S(2)}) collective-permute-start(f32[2,128,128]{2,1,0:T(8,128)S(1)} %bitcast_add_fusion.14), channel_id=1, source_target_pairs={{0,48},{8,56},{16,0},{24,8},{32,16},{40,24},{48,32},{56,40},{64,11... | collective-permute-start | bytes 393224 | tf_op jit(solution)/shard_map/ppermute | solution.py:110
  196.7 6.9 %collective-permute-start.25 = (f32[2,128,128]{2,1,0:T(8,128)S(1)}, f32[2,128,128]{2,1,0:T(8,128)S(1)}, u32[]{:S(2)}, u32[]{:S(2)}) collective-permute-start(f32[2,128,128]{2,1,0:T(8,128)S(1)} %bitcast_add_fusion.17), channel_id=1, source_target_pairs={{0,16},{8,24},{16,32},{24,40},{32,48},{40,56},{48,0},{56,8},{64,80... | collective-permute-start | bytes 393224 | tf_op jit(solution)/shard_map/ppermute | solution.py:110
  196.9 6.8 %collective-permute-start.18 = (f32[2,128,128]{2,1,0:T(8,128)S(1)}, f32[2,128,128]{2,1,0:T(8,128)S(1)}, u32[]{:S(2)}, u32[]{:S(2)}) collective-permute-start(f32[2,128,128]{2,1,0:T(8,128)S(1)} %bitcast_add_fusion.20), channel_id=1, source_target_pairs={{0,192},{8,200},{16,208},{24,216},{32,224},{40,232},{48,240},{56,2... | collective-permute-start | bytes 393224 | tf_op jit(solution)/shard_map/ppermute | solution.py:110
  200.6 7.5 %collective-permute-start.11 = (f32[2,128,128]{2,1,0:T(8,128)S(1)}, f32[2,128,128]{2,1,0:T(8,128)S(1)}, u32[]{:S(2)}, u32[]{:S(2)}) collective-permute-start(f32[2,128,128]{2,1,0:T(8,128)S(1)} %bitcast_add_fusion.23), channel_id=1, source_target_pairs={{0,64},{8,72},{16,80},{24,88},{32,96},{40,104},{48,112},{56,120},{... | collective-permute-start | bytes 393224 | tf_op jit(solution)/shard_map/ppermute | solution.py:110
  200.8 7.5 %collective-permute-start.33 = (f32[2,128,128]{2,1,0:T(8,128)S(1)}, f32[2,128,128]{2,1,0:T(8,128)S(1)}, u32[]{:S(2)}, u32[]{:S(2)}) collective-permute-start(f32[2,128,128]{2,1,0:T(8,128)S(1)} %bitcast_add_fusion.13), channel_id=1, source_target_pairs={{0,48},{8,56},{16,0},{24,8},{32,16},{40,24},{48,32},{56,40},{64,11... | collective-permute-start | bytes 393224 | tf_op jit(solution)/shard_map/ppermute | solution.py:110
  203.6 10.9 %collective-permute-start.26 = (f32[2,128,128]{2,1,0:T(8,128)S(1)}, f32[2,128,128]{2,1,0:T(8,128)S(1)}, u32[]{:S(2)}, u32[]{:S(2)}) collective-permute-start(f32[2,128,128]{2,1,0:T(8,128)S(1)} %bitcast_add_fusion.16), channel_id=1, source_target_pairs={{0,16},{8,24},{16,32},{24,40},{32,48},{40,56},{48,0},{56,8},{64,80... | collective-permute-start | bytes 393224 | tf_op jit(solution)/shard_map/ppermute | solution.py:110
  203.7 12.5 %collective-permute-start.19 = (f32[2,128,128]{2,1,0:T(8,128)S(1)}, f32[2,128,128]{2,1,0:T(8,128)S(1)}, u32[]{:S(2)}, u32[]{:S(2)}) collective-permute-start(f32[2,128,128]{2,1,0:T(8,128)S(1)} %bitcast_add_fusion.19), channel_id=1, source_target_pairs={{0,192},{8,200},{16,208},{24,216},{32,224},{40,232},{48,240},{56,2... | collective-permute-start | bytes 393224 | tf_op jit(solution)/shard_map/ppermute | solution.py:110
  208.1 12.6 %collective-permute-start.12 = (f32[2,128,128]{2,1,0:T(8,128)S(1)}, f32[2,128,128]{2,1,0:T(8,128)S(1)}, u32[]{:S(2)}, u32[]{:S(2)}) collective-permute-start(f32[2,128,128]{2,1,0:T(8,128)S(1)} %bitcast_add_fusion.22), channel_id=1, source_target_pairs={{0,64},{8,72},{16,80},{24,88},{32,96},{40,104},{48,112},{56,120},{... | collective-permute-start | bytes 393224 | tf_op jit(solution)/shard_map/ppermute | solution.py:110
  208.3 14.1 %collective-permute-start.34 = (f32[128,128]{1,0:T(8,128)S(1)}, f32[128,128]{1,0:T(8,128)S(1)}, u32[]{:S(2)}, u32[]{:S(2)}) collective-permute-start(f32[128,128]{1,0:T(8,128)S(1)} %dynamic-slice_bitcast_fusion.8), channel_id=1, source_target_pairs={{0,8},{8,0},{16,24},{24,16},{32,40},{40,32},{48,56},{56,48},{64,72... | collective-permute-start | bytes 196616 | tf_op jit(solution)/shard_map/ppermute | solution.py:119
  214.5 8.5 %collective-permute-start.27 = (f32[128,128]{1,0:T(8,128)S(1)}, f32[128,128]{1,0:T(8,128)S(1)}, u32[]{:S(2)}, u32[]{:S(2)}) collective-permute-start(f32[128,128]{1,0:T(8,128)S(1)} %dynamic-slice_bitcast_fusion.9), channel_id=1, source_target_pairs={{0,8},{8,0},{16,24},{24,16},{32,40},{40,32},{48,56},{56,48},{64,72... | collective-permute-start | bytes 196616 | tf_op jit(solution)/shard_map/ppermute | solution.py:119
  216.2 8.7 %collective-permute-start.20 = (f32[128,128]{1,0:T(8,128)S(1)}, f32[128,128]{1,0:T(8,128)S(1)}, u32[]{:S(2)}, u32[]{:S(2)}) collective-permute-start(f32[128,128]{1,0:T(8,128)S(1)} %dynamic-slice_bitcast_fusion.10), channel_id=1, source_target_pairs={{0,8},{8,0},{16,24},{24,16},{32,40},{40,32},{48,56},{56,48},{64,72... | collective-permute-start | bytes 196616 | tf_op jit(solution)/shard_map/ppermute | solution.py:119
  220.7 8.3 %collective-permute-start.13 = (f32[128,128]{1,0:T(8,128)S(1)}, f32[128,128]{1,0:T(8,128)S(1)}, u32[]{:S(2)}, u32[]{:S(2)}) collective-permute-start(f32[128,128]{1,0:T(8,128)S(1)} %dynamic-slice_bitcast_fusion.11), channel_id=1, source_target_pairs={{0,8},{8,0},{16,24},{24,16},{32,40},{40,32},{48,56},{56,48},{64,72... | collective-permute-start | bytes 196616 | tf_op jit(solution)/shard_map/ppermute | solution.py:119

commit v5 on v4

--- a/solution.py
+++ b/solution.py
@@ -9,11 +9,10 @@
 OWNERS_PER_STEP = 4
 
 
-def _products_kernel(left_ref, right_ref, target_ref, x_ref, *out_refs):
+def _products_kernel(left_ref, right_ref, target_ref, x_ref, out_ref):
     step = pl.program_id(0)
     pair_count = left_ref.shape[0] // (pl.num_programs(0) * OWNERS_PER_STEP)
-    for out_ref in out_refs:
-        out_ref[...] = jnp.zeros_like(out_ref)
+    out_ref[...] = jnp.zeros_like(out_ref)
 
     def body(j, carry):
         k = j // pair_count
@@ -24,12 +23,7 @@
         prod = lax.dot_general(
             x_ref[l], x_ref[r], (((0,), (0,)), ((), ())), preferred_element_type=jnp.float32
         )
-        for c, out_ref in enumerate(out_refs):
-
-            @pl.when(t == c)
-            def _(out_ref=out_ref):
-                out_ref[k] += prod
-
+        out_ref[t, k] += prod
         return carry
 
     lax.fori_loop(0, OWNERS_PER_STEP * pair_count, body, 0, unroll=4)
@@ -42,7 +36,7 @@
     flops = 2 * owners * pair_count * block * block * block
     return pl.pallas_call(
         _products_kernel,
-        out_shape=[jax.ShapeDtypeStruct((owners, block, block), jnp.float32)] * CS,
+        out_shape=jax.ShapeDtypeStruct((CS, owners, block, block), jnp.float32),
         grid_spec=pltpu.PrefetchScalarGridSpec(
             num_scalar_prefetch=3,
             grid=(steps,),
@@ -53,10 +47,9 @@
                     pipeline_mode=pl.Buffered(1),
                 )
             ],
-            out_specs=[
-                pl.BlockSpec((OWNERS_PER_STEP, block, block), lambda i, *_: (i, 0, 0))
-            ]
-            * CS,
+            out_specs=pl.BlockSpec(
+                (CS, OWNERS_PER_STEP, block, block), lambda i, *_: (0, i, 0, 0)
+            ),
         ),
         compiler_params=pltpu.CompilerParams(
             dimension_semantics=("arbitrary",), vmem_limit_bytes=48 * 1024 * 1024
@@ -96,14 +89,27 @@
     return route
 
 
-def ring_reduce_scatter(data, axis, dim, direction, coord):
+def _take(data, lead, axis, index):
+    offset = len(lead)
+    starts = [0] * data.ndim
+    sizes = list(data.shape)
+    for i, v in enumerate(lead):
+        starts[i] = v
+        sizes[i] = 1
+    starts[offset + axis] = index
+    sizes[offset + axis] = 1
+    piece = lax.dynamic_slice(data, starts, sizes)
+    return piece.reshape(
+        [s for i, s in enumerate(sizes) if i >= offset and i != offset + axis]
+    )
+
+
+def ring_reduce_scatter(data, axis, dim, direction, coord, lead=()):
     size = BLK_DIMS[dim]
     route = _shift_route(dim, direction)
 
     def piece(k):
-        return lax.dynamic_index_in_dim(
-            data, (coord - direction * (1 + k)) % size, axis, keepdims=False
-        )
+        return _take(data, lead, axis, (coord - direction * (1 + k)) % size)
 
     send = piece(0)
     for k in range(size - 1):
@@ -170,15 +176,15 @@
     partials = owner_partials(gathered, left, right, target)
     block = x_blocks.shape[1]
     my_y, my_x, my_z = _blk_coords(me)
+    partials = partials.reshape((CS,) + BLK_DIMS + (block, block))
     results = []
     for c in range(CS):
-        data = partials[c].reshape(BLK_DIMS + (block, block))
         direction = 1 if c % 2 == 0 else -1
         if c < 2:
-            data = ring_reduce_scatter(data, 1, 1, direction, my_x)
+            data = ring_reduce_scatter(partials, 1, 1, direction, my_x, (c,))
             data = ring_reduce_scatter(data, 0, 0, direction, my_y)
         else:
-            data = ring_reduce_scatter(data, 0, 0, direction, my_y)
+            data = ring_reduce_scatter(partials, 0, 0, direction, my_y, (c,))
             data = ring_reduce_scatter(data, 0, 1, direction, my_x)
         results.append(pair_reduce_scatter(data, 2, my_z))
     summed = jnp.stack(results)

time: 231 us -> 184 us (0.80)
  Pallas kernels: 79.8 us -> 23.9 us
  waiting for transfers between devices: 58.9 us -> 70.1 us
  other arithmetic: 7.19 us -> 12.8 us
  local copies, waits for them, and re-layouts: 11.1 us -> 6.36 us
  starting transfers between devices: 72.1 us -> 68.6 us
    pallas_call x1, Pallas kernels: 79.8 us -> 23.9 us  [owner_partials(): pl.pallas_call(_products_kernel, out_shape=jax.ShapeDtypeStruct((CS, owne...]
    ppermute x24, waiting for transfers between devices: 21.2 us -> 33.4 us  [ring_reduce_scatter(): arrived = lax.ppermute(send, 'blk', route)]
    add x24 -> x15, other arithmetic: 2.01 us -> 7.6 us  [ring_reduce_scatter(): send = arrived + piece(k + 1)]
    squeeze x8 -> x0, local copies, waits for them, and re-layouts: 5.1 us -> none  [piece(): lax.dynamic_index_in_dim(data, (coord - direction * (1 + k)) % size, axis...]
    ppermute x24, starting transfers between devices: 40.6 us -> 35.9 us  [ring_reduce_scatter(): arrived = lax.ppermute(send, 'blk', route)]
    reshape x0 -> x6, local copies, waits for them, and re-layouts: none -> 3.41 us  [_take(): piece.reshape([s for i, s in enumerate(sizes) if i >= offset and i != off...]
  transfers between devices with their start and end apart: 35 -> 35, of which waited for: 17 -> 15; matrix products, arithmetic and copies ran while one was open for 3% -> 3% of each run, Pallas kernels for 0% -> 0%
where the time goes in v5:
time: 184 us; the launch traced here: 182 us
  waiting for transfers between devices  70.1 us (38%)
  starting transfers between devices  68.6 us (37%)
  Pallas kernels  23.9 us (13%)
  other arithmetic  12.8 us (7%)
  local copies, waits for them, and re-layouts  6.36 us (3%)
    ppermute x24, starting transfers between devices, ring_reduce_scatter(): arrived = lax.ppermute(send, 'blk', route)  35.9 us
    ppermute x24, waiting for transfers between devices, ring_reduce_scatter(): arrived = lax.ppermute(send, 'blk', route)  33.4 us
    ppermute x3, waiting for transfers between devices, line_all_gather(): send_down = lax.ppermute(send_down, 'grp', down)  27.2 us
    pallas_call x1, Pallas kernels, owner_partials(): pl.pallas_call(_products_kernel, out_shape=jax.ShapeDtypeStruct((CS, owne...  23.9 us
    ppermute x4, starting transfers between devices, pair_reduce_scatter(): return lax.ppermute(other, 'blk', route) + mine  15.1 us
    ppermute x3, starting transfers between devices, line_all_gather(): send_up = lax.ppermute(send_up, 'grp', up)  9.59 us
    ppermute x3, starting transfers between devices, line_all_gather(): send_down = lax.ppermute(send_down, 'grp', down)  7.91 us
    add x15, other arithmetic, ring_reduce_scatter(): send = arrived + piece(k + 1)  7.6 us
  transfers between devices with their start and end apart: 35, of which 15 were waited for; matrix products, arithmetic and copies ran while one was open for 3% of the time, Pallas kernels for 0%

profile of v5, /device:TPU:32, one launch (start us, length us, event | category | flops | bytes accessed | tf_op | source)
XLA Modules:
  0.0 182.2 jit_solution(895070402434272183)
XLA Ops:
  0.0 3.7 %collective-permute-start.3 = (bf16[16,128,128]{2,1,0:T(8,128)(2,1)}, bf16[16,128,128]{2,1,0:T(8,128)(2,1)S(1)}, u32[]{:S(2)}, u32[]{:S(2)}) collective-permute-start(bf16[16,128,128]{2,1,0:T(8,128)(2,1)} %param.6), channel_id=1, source_target_pairs={{2,0},{3,1},{4,2},{5,3},{6,4},{7,5},{10,8},{11,9},{12,10},{13,11},... | collective-permute-start | bytes 1572872 | tf_op jit(solution)/shard_map/ppermute | solution.py:141
  3.7 2.1 %collective-permute-start = (bf16[16,128,128]{2,1,0:T(8,128)(2,1)}, bf16[16,128,128]{2,1,0:T(8,128)(2,1)S(1)}, u32[]{:S(2)}, u32[]{:S(2)}) collective-permute-start(bf16[16,128,128]{2,1,0:T(8,128)(2,1)} %param.6), channel_id=1, source_target_pairs={{0,2},{1,3},{2,4},{3,5},{4,6},{5,7},{8,10},{9,11},{10,12},{11,13},... | collective-permute-start | bytes 1572872 | tf_op jit(solution)/shard_map/ppermute | solution.py:140
  5.9 10.1 %collective-permute-done.3 = bf16[16,128,128]{2,1,0:T(8,128)(2,1)S(1)} collective-permute-done((bf16[16,128,128]{2,1,0:T(8,128)(2,1)}, bf16[16,128,128]{2,1,0:T(8,128)(2,1)S(1)}, u32[]{:S(2)}, u32[]{:S(2)}) %collective-permute-start.3) | collective-permute-done | bytes 524320 | tf_op jit(solution)/shard_map/ppermute | solution.py:141
  15.9 2.0 %collective-permute-start.4 = (bf16[16,128,128]{2,1,0:T(8,128)(2,1)S(1)}, bf16[16,128,128]{2,1,0:T(8,128)(2,1)S(1)}, u32[]{:S(2)}, u32[]{:S(2)}) collective-permute-start(bf16[16,128,128]{2,1,0:T(8,128)(2,1)S(1)} %collective-permute-done.3), channel_id=1, source_target_pairs={{2,0},{3,1},{4,2},{5,3},{6,4},{7,5},{10,8},{11,9},{12,10},{13,11},... | collective-permute-start | bytes 1572872 | tf_op jit(solution)/shard_map/ppermute | solution.py:141
  18.0 3.8 %collective-permute-start.1 = (bf16[16,128,128]{2,1,0:T(8,128)(2,1)S(1)}, bf16[16,128,128]{2,1,0:T(8,128)(2,1)S(1)}, u32[]{:S(2)}, u32[]{:S(2)}) collective-permute-start(bf16[16,128,128]{2,1,0:T(8,128)(2,1)S(1)} %collective-permute-done), channel_id=1, source_target_pairs={{0,2},{1,3},{2,4},{3,5},{4,6},{5,7},{8,10},{9,11},{10,12},{11,13},... | collective-permute-start | bytes 1572872 | tf_op jit(solution)/shard_map/ppermute | solution.py:140
  21.8 9.0 %collective-permute-done.4 = bf16[16,128,128]{2,1,0:T(8,128)(2,1)S(1)} collective-permute-done((bf16[16,128,128]{2,1,0:T(8,128)(2,1)S(1)}, bf16[16,128,128]{2,1,0:T(8,128)(2,1)S(1)}, u32[]{:S(2)}, u32[]{:S(2)}) %collective-permute-start.4) | collective-permute-done | bytes 524320 | tf_op jit(solution)/shard_map/ppermute | solution.py:141
  30.8 2.2 %collective-permute-start.5 = (bf16[16,128,128]{2,1,0:T(8,128)(2,1)S(1)}, bf16[16,128,128]{2,1,0:T(8,128)(2,1)S(1)}, u32[]{:S(2)}, u32[]{:S(2)}) collective-permute-start(bf16[16,128,128]{2,1,0:T(8,128)(2,1)S(1)} %collective-permute-done.4), channel_id=1, source_target_pairs={{2,0},{3,1},{4,2},{5,3},{6,4},{7,5},{10,8},{11,9},{12,10},{13,11},... | collective-permute-start | bytes 1572872 | tf_op jit(solution)/shard_map/ppermute | solution.py:141
  33.0 3.6 %collective-permute-start.2 = (bf16[16,128,128]{2,1,0:T(8,128)(2,1)S(1)}, bf16[16,128,128]{2,1,0:T(8,128)(2,1)S(1)}, u32[]{:S(2)}, u32[]{:S(2)}) collective-permute-start(bf16[16,128,128]{2,1,0:T(8,128)(2,1)S(1)} %collective-permute-done.1), channel_id=1, source_target_pairs={{0,2},{1,3},{2,4},{3,5},{4,6},{5,7},{8,10},{9,11},{10,12},{11,13},... | collective-permute-start | bytes 1572872 | tf_op jit(solution)/shard_map/ppermute | solution.py:140
  36.7 8.1 %collective-permute-done.5 = bf16[16,128,128]{2,1,0:T(8,128)(2,1)S(1)} collective-permute-done((bf16[16,128,128]{2,1,0:T(8,128)(2,1)S(1)}, bf16[16,128,128]{2,1,0:T(8,128)(2,1)S(1)}, u32[]{:S(2)}, u32[]{:S(2)}) %collective-permute-start.5) | collective-permute-done | bytes 524320 | tf_op jit(solution)/shard_map/ppermute | solution.py:141
  45.0 1.9 %collective-permute-done.2 = bf16[16,128,128]{2,1,0:T(8,128)(2,1)S(1)} collective-permute-done((bf16[16,128,128]{2,1,0:T(8,128)(2,1)S(1)}, bf16[16,128,128]{2,1,0:T(8,128)(2,1)S(1)}, u32[]{:S(2)}, u32[]{:S(2)}) %collective-permute-start.2) | collective-permute-done | bytes 524320 | tf_op jit(solution)/shard_map/ppermute | solution.py:140
  47.4 1.6 pad_maximum_fusion.1
  51.5 2.0 %collective-permute-done.6 = bf16[4,16,128,128]{3,2,1,0:T(8,128)(2,1)} collective-permute-done((bf16[4,16,128,128]{3,2,1,0:T(8,128)(2,1)}, bf16[4,16,128,128]{3,2,1,0:T(8,128)(2,1)}, u32[]{:S(2)}, u32[]{:S(2)}) %collective-permute-start.6) | collective-permute-done | bytes 2097184 | tf_op jit(solution)/shard_map/ppermute | solution.py:159
  53.5 1.8 select_bitcast_fusion.1
  56.3 23.9 %shard_map.46 = f32[4,32,128,128]{3,2,1,0:T(8,128)} custom-call(s32[384]{0:T(512)S(1)} %reshape.188.left_ref, s32[384]{0:T(512)S(1)} %reshape.189.right_ref, s32[384]{0:T(512)S(1)} %reshape.190.target_ref, bf16[128,128,128]{2,1,0:T(8,128)(2,1)S(1)} %bitcast.143), custom_call_target="tpu_custom_call" | custom-call | flops 1610612736 | bytes 12582912 | tf_op jit(solution)/shard_map/pallas_call | solution.py:37
  80.2 1.3 dynamic-slice_bitcast_fusion.3
  81.5 1.6 collective-permute-start.7
  83.1 2.1 %dynamic-slice_bitcast_fusion.1 = (f32[4,2,128,128]{3,2,1,0:T(8,128)S(1)}, f32[4,2,128,128]{3,2,1,0:T(8,128)}) fusion(f32[4,4,4,2,128,128]{5,4,3,2,1,0:T(8,128)} %bitcast.145, s32[]{:T(128)S(6)} %select_n.337, s32[]{:T(128)S(6)} %select_n.356), kind=kLoop, calls=%fused_computation.30 | loop fusion | bytes 2097160 | tf_op jit(solution)/shard_map/reshape | solution.py:102
  85.2 3.0 %collective-permute-start.28 = (f32[4,2,128,128]{3,2,1,0:T(8,128)}, f32[4,2,128,128]{3,2,1,0:T(8,128)S(1)}, u32[]{:S(2)}, u32[]{:S(2)}) collective-permute-start(f32[4,2,128,128]{3,2,1,0:T(8,128)} %get-tuple-element.21), channel_id=1, source_target_pairs={{0,192},{8,200},{16,208},{24,216},{32,224},{40,232},{48,240},{56,2... | collective-permute-start | bytes 1572872 | tf_op jit(solution)/shard_map/ppermute | solution.py:116
  88.2 1.7 collective-permute-start.14
  89.9 6.8 %collective-permute-done.7 = f32[4,2,128,128]{3,2,1,0:T(8,128)S(1)} collective-permute-done((f32[4,2,128,128]{3,2,1,0:T(8,128)S(1)}, f32[4,2,128,128]{3,2,1,0:T(8,128)S(1)}, u32[]{:S(2)}, u32[]{:S(2)}) %collective-permute-start.7) | collective-permute-done | bytes 524320 | tf_op jit(solution)/shard_map/ppermute | solution.py:116
  96.8 2.9 %collective-permute-done.28 = f32[4,2,128,128]{3,2,1,0:T(8,128)S(1)} collective-permute-done((f32[4,2,128,128]{3,2,1,0:T(8,128)}, f32[4,2,128,128]{3,2,1,0:T(8,128)S(1)}, u32[]{:S(2)}, u32[]{:S(2)}) %collective-permute-start.28) | collective-permute-done | bytes 524320 | tf_op jit(solution)/shard_map/ppermute | solution.py:116
  99.7 3.1 %collective-permute-done.21 = f32[4,2,128,128]{3,2,1,0:T(8,128)S(1)} collective-permute-done((f32[4,2,128,128]{3,2,1,0:T(8,128)S(1)}, f32[4,2,128,128]{3,2,1,0:T(8,128)S(1)}, u32[]{:S(2)}, u32[]{:S(2)}) %collective-permute-start.21) | collective-permute-done | bytes 524320 | tf_op jit(solution)/shard_map/ppermute | solution.py:116
  102.8 2.7 %bitcast_add_fusion.11 = (f32[4,2,128,128]{3,2,1,0:T(8,128)}, f32[4,2,128,128]{3,2,1,0:T(8,128)S(1)}, f32[4,2,128,128]{3,2,1,0:T(8,128)S(1)}, f32[4,2,128,128]{3,2,1,0:T(8,128)S(1)}) fusion(f32[4,2,128,128]{3,2,1,0:T(8,128)S(1)} %collective-permute-done.7, f32[4,4,4,2,128,128]{5,4,3,2,1,0:T(8,128)} %bitcast.146, s32[]{:T(128)S(6)} %select_n.329, ...), kind=kLoop, calls=%fused_computation.20 | loop fusion | flops 524288 | bytes 6291472 | tf_op jit(solution)/shard_map/add | solution.py:117
  105.5 1.5 collective-permute-start.8
  107.0 1.8 %collective-permute-start.29 = (f32[4,2,128,128]{3,2,1,0:T(8,128)S(1)}, f32[4,2,128,128]{3,2,1,0:T(8,128)S(1)}, u32[]{:S(2)}, u32[]{:S(2)}) collective-permute-start(f32[4,2,128,128]{3,2,1,0:T(8,128)S(1)} %get-tuple-element.15), channel_id=1, source_target_pairs={{0,192},{8,200},{16,208},{24,216},{32,224},{40,232},{48,240},{56,2... | collective-permute-start | bytes 1572872 | tf_op jit(solution)/shard_map/ppermute | solution.py:116
  109.0 1.7 collective-permute-start.15
  110.8 8.7 %collective-permute-done.8 = f32[4,2,128,128]{3,2,1,0:T(8,128)S(1)} collective-permute-done((f32[4,2,128,128]{3,2,1,0:T(8,128)}, f32[4,2,128,128]{3,2,1,0:T(8,128)S(1)}, u32[]{:S(2)}, u32[]{:S(2)}) %collective-permute-start.8) | collective-permute-done | bytes 524320 | tf_op jit(solution)/shard_map/ppermute | solution.py:116
  119.5 2.3 %collective-permute-done.22 = f32[4,2,128,128]{3,2,1,0:T(8,128)S(1)} collective-permute-done((f32[4,2,128,128]{3,2,1,0:T(8,128)S(1)}, f32[4,2,128,128]{3,2,1,0:T(8,128)S(1)}, u32[]{:S(2)}, u32[]{:S(2)}) %collective-permute-start.22) | collective-permute-done | bytes 524320 | tf_op jit(solution)/shard_map/ppermute | solution.py:116
  121.8 2.7 %bitcast_add_fusion.10 = (f32[4,2,128,128]{3,2,1,0:T(8,128)}, f32[4,2,128,128]{3,2,1,0:T(8,128)S(1)}, f32[4,2,128,128]{3,2,1,0:T(8,128)S(1)}, f32[4,2,128,128]{3,2,1,0:T(8,128)S(1)}) fusion(f32[4,2,128,128]{3,2,1,0:T(8,128)S(1)} %collective-permute-done.8, f32[4,4,4,2,128,128]{5,4,3,2,1,0:T(8,128)} %bitcast.147, s32[]{:T(128)S(6)} %select_n.331, ...), kind=kLoop, calls=%fused_computation.19 | loop fusion | flops 524288 | bytes 6291472 | tf_op jit(solution)/shard_map/add | solution.py:117
  124.5 1.2 collective-permute-start.9
  125.7 1.8 %collective-permute-start.30 = (f32[4,2,128,128]{3,2,1,0:T(8,128)S(1)}, f32[4,2,128,128]{3,2,1,0:T(8,128)S(1)}, u32[]{:S(2)}, u32[]{:S(2)}) collective-permute-start(f32[4,2,128,128]{3,2,1,0:T(8,128)S(1)} %get-tuple-element.11), channel_id=1, source_target_pairs={{0,192},{8,200},{16,208},{24,216},{32,224},{40,232},{48,240},{56,2... | collective-permute-start | bytes 1572872 | tf_op jit(solution)/shard_map/ppermute | solution.py:116
  127.7 2.0 %collective-permute-start.16 = (f32[4,2,128,128]{3,2,1,0:T(8,128)S(1)}, f32[4,2,128,128]{3,2,1,0:T(8,128)}, u32[]{:S(2)}, u32[]{:S(2)}) collective-permute-start(f32[4,2,128,128]{3,2,1,0:T(8,128)S(1)} %get-tuple-element.13), channel_id=1, source_target_pairs={{0,48},{8,56},{16,0},{24,8},{32,16},{40,24},{48,32},{56,40},{64,11... | collective-permute-start | bytes 1572872 | tf_op jit(solution)/shard_map/ppermute | solution.py:116
  129.8 7.0 %collective-permute-done.9 = f32[4,2,128,128]{3,2,1,0:T(8,128)S(1)} collective-permute-done((f32[4,2,128,128]{3,2,1,0:T(8,128)}, f32[4,2,128,128]{3,2,1,0:T(8,128)S(1)}, u32[]{:S(2)}, u32[]{:S(2)}) %collective-permute-start.9) | collective-permute-done | bytes 524320 | tf_op jit(solution)/shard_map/ppermute | solution.py:116
  136.8 2.0 %collective-permute-done.23 = f32[4,2,128,128]{3,2,1,0:T(8,128)S(1)} collective-permute-done((f32[4,2,128,128]{3,2,1,0:T(8,128)S(1)}, f32[4,2,128,128]{3,2,1,0:T(8,128)S(1)}, u32[]{:S(2)}, u32[]{:S(2)}) %collective-permute-start.23) | collective-permute-done | bytes 524320 | tf_op jit(solution)/shard_map/ppermute | solution.py:116
  138.8 1.9 %bitcast_add_fusion.9 = (f32[4,2,128,128]{3,2,1,0:T(8,128)S(1)}, f32[4,2,128,128]{3,2,1,0:T(8,128)S(1)}, f32[4,2,128,128]{3,2,1,0:T(8,128)S(1)}, f32[4,2,128,128]{3,2,1,0:T(8,128)S(1)}) fusion(f32[4,2,128,128]{3,2,1,0:T(8,128)S(1)} %collective-permute-done.9, f32[4,4,4,2,128,128]{5,4,3,2,1,0:T(8,128)} %bitcast.148, s32[]{:T(128)S(6)} %select_n.333, ...), kind=kLoop, calls=%fused_computation.18 | loop fusion | flops 524288 | bytes 6291472 | tf_op jit(solution)/shard_map/add | solution.py:117
  140.7 2.4 %collective-permute-start.31 = (f32[2,128,128]{2,1,0:T(8,128)S(1)}, f32[2,128,128]{2,1,0:T(8,128)S(1)}, u32[]{:S(2)}, u32[]{:S(2)}) collective-permute-start(f32[2,128,128]{2,1,0:T(8,128)S(1)} %dynamic-slice_bitcast_fusion.4), channel_id=1, source_target_pairs={{0,48},{8,56},{16,0},{24,8},{32,16},{40,24},{48,32},{56,40},{64,11... | collective-permute-start | bytes 393224 | tf_op jit(solution)/shard_map/ppermute | solution.py:116
  143.2 2.9 %collective-permute-start.17 = (f32[2,128,128]{2,1,0:T(8,128)S(1)}, f32[2,128,128]{2,1,0:T(8,128)S(1)}, u32[]{:S(2)}, u32[]{:S(2)}) collective-permute-start(f32[2,128,128]{2,1,0:T(8,128)S(1)} %dynamic-slice_bitcast_fusion.6), channel_id=1, source_target_pairs={{0,192},{8,200},{16,208},{24,216},{32,224},{40,232},{48,240},{56,2... | collective-permute-start | bytes 393224 | tf_op jit(solution)/shard_map/ppermute | solution.py:116
  146.7 3.8 %collective-permute-start.32 = (f32[2,128,128]{2,1,0:T(8,128)S(1)}, f32[2,128,128]{2,1,0:T(8,128)S(1)}, u32[]{:S(2)}, u32[]{:S(2)}) collective-permute-start(f32[2,128,128]{2,1,0:T(8,128)S(1)} %bitcast_add_fusion.14), channel_id=1, source_target_pairs={{0,48},{8,56},{16,0},{24,8},{32,16},{40,24},{48,32},{56,40},{64,11... | collective-permute-start | bytes 393224 | tf_op jit(solution)/shard_map/ppermute | solution.py:116
  150.6 3.0 %collective-permute-start.18 = (f32[2,128,128]{2,1,0:T(8,128)S(1)}, f32[2,128,128]{2,1,0:T(8,128)S(1)}, u32[]{:S(2)}, u32[]{:S(2)}) collective-permute-start(f32[2,128,128]{2,1,0:T(8,128)S(1)} %bitcast_add_fusion.20), channel_id=1, source_target_pairs={{0,192},{8,200},{16,208},{24,216},{32,224},{40,232},{48,240},{56,2... | collective-permute-start | bytes 393224 | tf_op jit(solution)/shard_map/ppermute | solution.py:116
  153.8 3.3 %collective-permute-start.33 = (f32[2,128,128]{2,1,0:T(8,128)S(1)}, f32[2,128,128]{2,1,0:T(8,128)S(1)}, u32[]{:S(2)}, u32[]{:S(2)}) collective-permute-start(f32[2,128,128]{2,1,0:T(8,128)S(1)} %bitcast_add_fusion.13), channel_id=1, source_target_pairs={{0,48},{8,56},{16,0},{24,8},{32,16},{40,24},{48,32},{56,40},{64,11... | collective-permute-start | bytes 393224 | tf_op jit(solution)/shard_map/ppermute | solution.py:116
  157.2 3.3 %collective-permute-start.19 = (f32[2,128,128]{2,1,0:T(8,128)S(1)}, f32[2,128,128]{2,1,0:T(8,128)S(1)}, u32[]{:S(2)}, u32[]{:S(2)}) collective-permute-start(f32[2,128,128]{2,1,0:T(8,128)S(1)} %bitcast_add_fusion.19), channel_id=1, source_target_pairs={{0,192},{8,200},{16,208},{24,216},{32,224},{40,232},{48,240},{56,2... | collective-permute-start | bytes 393224 | tf_op jit(solution)/shard_map/ppermute | solution.py:116
  160.7 6.4 %collective-permute-start.34 = (f32[128,128]{1,0:T(8,128)S(1)}, f32[128,128]{1,0:T(8,128)S(1)}, u32[]{:S(2)}, u32[]{:S(2)}) collective-permute-start(f32[128,128]{1,0:T(8,128)S(1)} %dynamic-slice_bitcast_fusion.8), channel_id=1, source_target_pairs={{0,8},{8,0},{16,24},{24,16},{32,40},{40,32},{48,56},{56,48},{64,72... | collective-permute-start | bytes 196616 | tf_op jit(solution)/shard_map/ppermute | solution.py:125
  167.1 2.7 %collective-permute-start.27 = (f32[128,128]{1,0:T(8,128)S(1)}, f32[128,128]{1,0:T(8,128)S(1)}, u32[]{:S(2)}, u32[]{:S(2)}) collective-permute-start(f32[128,128]{1,0:T(8,128)S(1)} %dynamic-slice_bitcast_fusion.9), channel_id=1, source_target_pairs={{0,8},{8,0},{16,24},{24,16},{32,40},{40,32},{48,56},{56,48},{64,72... | collective-permute-start | bytes 196616 | tf_op jit(solution)/shard_map/ppermute | solution.py:125
  169.8 3.4 %collective-permute-start.20 = (f32[128,128]{1,0:T(8,128)S(1)}, f32[128,128]{1,0:T(8,128)S(1)}, u32[]{:S(2)}, u32[]{:S(2)}) collective-permute-start(f32[128,128]{1,0:T(8,128)S(1)} %dynamic-slice_bitcast_fusion.10), channel_id=1, source_target_pairs={{0,8},{8,0},{16,24},{24,16},{32,40},{40,32},{48,56},{56,48},{64,72... | collective-permute-start | bytes 196616 | tf_op jit(solution)/shard_map/ppermute | solution.py:125
  173.3 2.7 %collective-permute-start.13 = (f32[128,128]{1,0:T(8,128)S(1)}, f32[128,128]{1,0:T(8,128)S(1)}, u32[]{:S(2)}, u32[]{:S(2)}) collective-permute-start(f32[128,128]{1,0:T(8,128)S(1)} %dynamic-slice_bitcast_fusion.11), channel_id=1, source_target_pairs={{0,8},{8,0},{16,24},{24,16},{32,40},{40,32},{48,56},{56,48},{64,72... | collective-permute-start | bytes 196616 | tf_op jit(solution)/shard_map/ppermute | solution.py:125
  176.0 2.1 %collective-permute-done.20 = f32[128,128]{1,0:T(8,128)S(1)} collective-permute-done((f32[128,128]{1,0:T(8,128)S(1)}, f32[128,128]{1,0:T(8,128)S(1)}, u32[]{:S(2)}, u32[]{:S(2)}) %collective-permute-start.20) | collective-permute-done | bytes 65568 | tf_op jit(solution)/shard_map/ppermute | solution.py:125
  178.1 3.5 %collective-permute-done.13 = f32[128,128]{1,0:T(8,128)S(1)} collective-permute-done((f32[128,128]{1,0:T(8,128)S(1)}, f32[128,128]{1,0:T(8,128)S(1)}, u32[]{:S(2)}, u32[]{:S(2)}) %collective-permute-start.13) | collective-permute-done | bytes 65568 | tf_op jit(solution)/shard_map/ppermute | solution.py:125
  181.6 0.7 pad_maximum_fusion.4
  (81 shorter events, 5.7 us)
Async XLA Ops:
  0.0 15.9 %collective-permute-start.3 = (bf16[16,128,128]{2,1,0:T(8,128)(2,1)}, bf16[16,128,128]{2,1,0:T(8,128)(2,1)S(1)}, u32[]{:S(2)}, u32[]{:S(2)}) collective-permute-start(bf16[16,128,128]{2,1,0:T(8,128)(2,1)} %param.6), channel_id=1, source_target_pairs={{2,0},{3,1},{4,2},{5,3},{6,4},{7,5},{10,8},{11,9},{12,10},{13,11},... | collective-permute-start | bytes 1572872 | tf_op jit(solution)/shard_map/ppermute | solution.py:141
  3.7 14.2 %collective-permute-start = (bf16[16,128,128]{2,1,0:T(8,128)(2,1)}, bf16[16,128,128]{2,1,0:T(8,128)(2,1)S(1)}, u32[]{:S(2)}, u32[]{:S(2)}) collective-permute-start(bf16[16,128,128]{2,1,0:T(8,128)(2,1)} %param.6), channel_id=1, source_target_pairs={{0,2},{1,3},{2,4},{3,5},{4,6},{5,7},{8,10},{9,11},{10,12},{11,13},... | collective-permute-start | bytes 1572872 | tf_op jit(solution)/shard_map/ppermute | solution.py:140
  15.9 14.9 %collective-permute-start.4 = (bf16[16,128,128]{2,1,0:T(8,128)(2,1)S(1)}, bf16[16,128,128]{2,1,0:T(8,128)(2,1)S(1)}, u32[]{:S(2)}, u32[]{:S(2)}) collective-permute-start(bf16[16,128,128]{2,1,0:T(8,128)(2,1)S(1)} %collective-permute-done.3), channel_id=1, source_target_pairs={{2,0},{3,1},{4,2},{5,3},{6,4},{7,5},{10,8},{11,9},{12,10},{13,11},... | collective-permute-start | bytes 1572872 | tf_op jit(solution)/shard_map/ppermute | solution.py:141
  18.0 15.0 %collective-permute-start.1 = (bf16[16,128,128]{2,1,0:T(8,128)(2,1)S(1)}, bf16[16,128,128]{2,1,0:T(8,128)(2,1)S(1)}, u32[]{:S(2)}, u32[]{:S(2)}) collective-permute-start(bf16[16,128,128]{2,1,0:T(8,128)(2,1)S(1)} %collective-permute-done), channel_id=1, source_target_pairs={{0,2},{1,3},{2,4},{3,5},{4,6},{5,7},{8,10},{9,11},{10,12},{11,13},... | collective-permute-start | bytes 1572872 | tf_op jit(solution)/shard_map/ppermute | solution.py:140
  30.8 14.0 %collective-permute-start.5 = (bf16[16,128,128]{2,1,0:T(8,128)(2,1)S(1)}, bf16[16,128,128]{2,1,0:T(8,128)(2,1)S(1)}, u32[]{:S(2)}, u32[]{:S(2)}) collective-permute-start(bf16[16,128,128]{2,1,0:T(8,128)(2,1)S(1)} %collective-permute-done.4), channel_id=1, source_target_pairs={{2,0},{3,1},{4,2},{5,3},{6,4},{7,5},{10,8},{11,9},{12,10},{13,11},... | collective-permute-start | bytes 1572872 | tf_op jit(solution)/shard_map/ppermute | solution.py:141
  33.0 13.9 %collective-permute-start.2 = (bf16[16,128,128]{2,1,0:T(8,128)(2,1)S(1)}, bf16[16,128,128]{2,1,0:T(8,128)(2,1)S(1)}, u32[]{:S(2)}, u32[]{:S(2)}) collective-permute-start(bf16[16,128,128]{2,1,0:T(8,128)(2,1)S(1)} %collective-permute-done.1), channel_id=1, source_target_pairs={{0,2},{1,3},{2,4},{3,5},{4,6},{5,7},{8,10},{9,11},{10,12},{11,13},... | collective-permute-start | bytes 1572872 | tf_op jit(solution)/shard_map/ppermute | solution.py:140
  45.0 2.1 %copy-start = (bf16[16,128,128]{2,1,0:T(8,128)(2,1)S(1)}, bf16[16,128,128]{2,1,0:T(8,128)(2,1)}, u32[]{:S(2)}) copy-start(bf16[16,128,128]{2,1,0:T(8,128)(2,1)} %param.6) | copy-start | bytes 1572868
  47.4 1.7 copy-start.1
  47.4 1.7 copy-start.2
  47.4 3.0 %copy-start.3 = (s32[1,1,32,12]{2,1,3,0:T(1,128)S(1)}, s32[1,1,32,12]{2,1,3,0:T(1,128)}, u32[]{:S(2)}) copy-start(s32[1,1,32,12]{2,1,3,0:T(1,128)} %param.7) | copy-start | bytes 4612
  49.0 4.5 %collective-permute-start.6 = (bf16[4,16,128,128]{3,2,1,0:T(8,128)(2,1)}, bf16[4,16,128,128]{3,2,1,0:T(8,128)(2,1)}, u32[]{:S(2)}, u32[]{:S(2)}) collective-permute-start(bf16[4,16,128,128]{3,2,1,0:T(8,128)(2,1)} %pad_maximum_fusion.1), channel_id=1, source_target_pairs={{0,1},{1,0},{2,3},{3,2},{4,5},{5,4},{6,7},{7,6},{8,9},{9,8},{10,11... | collective-permute-start | bytes 6291464 | tf_op jit(solution)/shard_map/ppermute | solution.py:159
  81.5 15.3 %collective-permute-start.7 = (f32[4,2,128,128]{3,2,1,0:T(8,128)S(1)}, f32[4,2,128,128]{3,2,1,0:T(8,128)S(1)}, u32[]{:S(2)}, u32[]{:S(2)}) collective-permute-start(f32[4,2,128,128]{3,2,1,0:T(8,128)S(1)} %get-tuple-element.18), channel_id=1, source_target_pairs={{0,16},{8,24},{16,32},{24,40},{32,48},{40,56},{48,0},{56,8},{64,80... | collective-permute-start | bytes 1572872 | tf_op jit(solution)/shard_map/ppermute | solution.py:116
  85.2 14.5 %collective-permute-start.28 = (f32[4,2,128,128]{3,2,1,0:T(8,128)}, f32[4,2,128,128]{3,2,1,0:T(8,128)S(1)}, u32[]{:S(2)}, u32[]{:S(2)}) collective-permute-start(f32[4,2,128,128]{3,2,1,0:T(8,128)} %get-tuple-element.21), channel_id=1, source_target_pairs={{0,192},{8,200},{16,208},{24,216},{32,224},{40,232},{48,240},{56,2... | collective-permute-start | bytes 1572872 | tf_op jit(solution)/shard_map/ppermute | solution.py:116
  88.2 14.6 %collective-permute-start.21 = (f32[4,2,128,128]{3,2,1,0:T(8,128)S(1)}, f32[4,2,128,128]{3,2,1,0:T(8,128)S(1)}, u32[]{:S(2)}, u32[]{:S(2)}) collective-permute-start(f32[4,2,128,128]{3,2,1,0:T(8,128)S(1)} %get-tuple-element.20), channel_id=1, source_target_pairs={{0,64},{8,72},{16,80},{24,88},{32,96},{40,104},{48,112},{56,120},{... | collective-permute-start | bytes 1572872 | tf_op jit(solution)/shard_map/ppermute | solution.py:116
  88.2 14.6 %collective-permute-start.14 = (f32[4,2,128,128]{3,2,1,0:T(8,128)S(1)}, f32[4,2,128,128]{3,2,1,0:T(8,128)}, u32[]{:S(2)}, u32[]{:S(2)}) collective-permute-start(f32[4,2,128,128]{3,2,1,0:T(8,128)S(1)} %get-tuple-element.19), channel_id=1, source_target_pairs={{0,48},{8,56},{16,0},{24,8},{32,16},{40,24},{48,32},{56,40},{64,11... | collective-permute-start | bytes 1572872 | tf_op jit(solution)/shard_map/ppermute | solution.py:116
  105.5 14.0 %collective-permute-start.8 = (f32[4,2,128,128]{3,2,1,0:T(8,128)}, f32[4,2,128,128]{3,2,1,0:T(8,128)S(1)}, u32[]{:S(2)}, u32[]{:S(2)}) collective-permute-start(f32[4,2,128,128]{3,2,1,0:T(8,128)} %get-tuple-element.14), channel_id=1, source_target_pairs={{0,16},{8,24},{16,32},{24,40},{32,48},{40,56},{48,0},{56,8},{64,80... | collective-permute-start | bytes 1572872 | tf_op jit(solution)/shard_map/ppermute | solution.py:116
  107.0 12.5 %collective-permute-start.29 = (f32[4,2,128,128]{3,2,1,0:T(8,128)S(1)}, f32[4,2,128,128]{3,2,1,0:T(8,128)S(1)}, u32[]{:S(2)}, u32[]{:S(2)}) collective-permute-start(f32[4,2,128,128]{3,2,1,0:T(8,128)S(1)} %get-tuple-element.15), channel_id=1, source_target_pairs={{0,192},{8,200},{16,208},{24,216},{32,224},{40,232},{48,240},{56,2... | collective-permute-start | bytes 1572872 | tf_op jit(solution)/shard_map/ppermute | solution.py:116
  108.9 12.9 %collective-permute-start.22 = (f32[4,2,128,128]{3,2,1,0:T(8,128)S(1)}, f32[4,2,128,128]{3,2,1,0:T(8,128)S(1)}, u32[]{:S(2)}, u32[]{:S(2)}) collective-permute-start(f32[4,2,128,128]{3,2,1,0:T(8,128)S(1)} %get-tuple-element.16), channel_id=1, source_target_pairs={{0,64},{8,72},{16,80},{24,88},{32,96},{40,104},{48,112},{56,120},{... | collective-permute-start | bytes 1572872 | tf_op jit(solution)/shard_map/ppermute | solution.py:116
  109.0 12.7 %collective-permute-start.15 = (f32[4,2,128,128]{3,2,1,0:T(8,128)S(1)}, f32[4,2,128,128]{3,2,1,0:T(8,128)}, u32[]{:S(2)}, u32[]{:S(2)}) collective-permute-start(f32[4,2,128,128]{3,2,1,0:T(8,128)S(1)} %get-tuple-element.17), channel_id=1, source_target_pairs={{0,48},{8,56},{16,0},{24,8},{32,16},{40,24},{48,32},{56,40},{64,11... | collective-permute-start | bytes 1572872 | tf_op jit(solution)/shard_map/ppermute | solution.py:116
  124.5 12.3 %collective-permute-start.9 = (f32[4,2,128,128]{3,2,1,0:T(8,128)}, f32[4,2,128,128]{3,2,1,0:T(8,128)S(1)}, u32[]{:S(2)}, u32[]{:S(2)}) collective-permute-start(f32[4,2,128,128]{3,2,1,0:T(8,128)} %get-tuple-element.10), channel_id=1, source_target_pairs={{0,16},{8,24},{16,32},{24,40},{32,48},{40,56},{48,0},{56,8},{64,80... | collective-permute-start | bytes 1572872 | tf_op jit(solution)/shard_map/ppermute | solution.py:116
  125.7 11.1 %collective-permute-start.30 = (f32[4,2,128,128]{3,2,1,0:T(8,128)S(1)}, f32[4,2,128,128]{3,2,1,0:T(8,128)S(1)}, u32[]{:S(2)}, u32[]{:S(2)}) collective-permute-start(f32[4,2,128,128]{3,2,1,0:T(8,128)S(1)} %get-tuple-element.11), channel_id=1, source_target_pairs={{0,192},{8,200},{16,208},{24,216},{32,224},{40,232},{48,240},{56,2... | collective-permute-start | bytes 1572872 | tf_op jit(solution)/shard_map/ppermute | solution.py:116
  127.5 11.2 %collective-permute-start.23 = (f32[4,2,128,128]{3,2,1,0:T(8,128)S(1)}, f32[4,2,128,128]{3,2,1,0:T(8,128)S(1)}, u32[]{:S(2)}, u32[]{:S(2)}) collective-permute-start(f32[4,2,128,128]{3,2,1,0:T(8,128)S(1)} %get-tuple-element.12), channel_id=1, source_target_pairs={{0,64},{8,72},{16,80},{24,88},{32,96},{40,104},{48,112},{56,120},{... | collective-permute-start | bytes 1572872 | tf_op jit(solution)/shard_map/ppermute | solution.py:116
  127.7 11.1 %collective-permute-start.16 = (f32[4,2,128,128]{3,2,1,0:T(8,128)S(1)}, f32[4,2,128,128]{3,2,1,0:T(8,128)}, u32[]{:S(2)}, u32[]{:S(2)}) collective-permute-start(f32[4,2,128,128]{3,2,1,0:T(8,128)S(1)} %get-tuple-element.13), channel_id=1, source_target_pairs={{0,48},{8,56},{16,0},{24,8},{32,16},{40,24},{48,32},{56,40},{64,11... | collective-permute-start | bytes 1572872 | tf_op jit(solution)/shard_map/ppermute | solution.py:116
  140.7 5.9 %collective-permute-start.31 = (f32[2,128,128]{2,1,0:T(8,128)S(1)}, f32[2,128,128]{2,1,0:T(8,128)S(1)}, u32[]{:S(2)}, u32[]{:S(2)}) collective-permute-start(f32[2,128,128]{2,1,0:T(8,128)S(1)} %dynamic-slice_bitcast_fusion.4), channel_id=1, source_target_pairs={{0,48},{8,56},{16,0},{24,8},{32,16},{40,24},{48,32},{56,40},{64,11... | collective-permute-start | bytes 393224 | tf_op jit(solution)/shard_map/ppermute | solution.py:116
  143.1 7.3 %collective-permute-start.24 = (f32[2,128,128]{2,1,0:T(8,128)S(1)}, f32[2,128,128]{2,1,0:T(8,128)S(1)}, u32[]{:S(2)}, u32[]{:S(2)}) collective-permute-start(f32[2,128,128]{2,1,0:T(8,128)S(1)} %dynamic-slice_bitcast_fusion.5), channel_id=1, source_target_pairs={{0,16},{8,24},{16,32},{24,40},{32,48},{40,56},{48,0},{56,8},{64,80... | collective-permute-start | bytes 393224 | tf_op jit(solution)/shard_map/ppermute | solution.py:116
  143.2 7.3 %collective-permute-start.17 = (f32[2,128,128]{2,1,0:T(8,128)S(1)}, f32[2,128,128]{2,1,0:T(8,128)S(1)}, u32[]{:S(2)}, u32[]{:S(2)}) collective-permute-start(f32[2,128,128]{2,1,0:T(8,128)S(1)} %dynamic-slice_bitcast_fusion.6), channel_id=1, source_target_pairs={{0,192},{8,200},{16,208},{24,216},{32,224},{40,232},{48,240},{56,2... | collective-permute-start | bytes 393224 | tf_op jit(solution)/shard_map/ppermute | solution.py:116
  146.1 7.5 %collective-permute-start.10 = (f32[2,128,128]{2,1,0:T(8,128)S(1)}, f32[2,128,128]{2,1,0:T(8,128)S(1)}, u32[]{:S(2)}, u32[]{:S(2)}) collective-permute-start(f32[2,128,128]{2,1,0:T(8,128)S(1)} %dynamic-slice_bitcast_fusion.7), channel_id=1, source_target_pairs={{0,64},{8,72},{16,80},{24,88},{32,96},{40,104},{48,112},{56,120},{... | collective-permute-start | bytes 393224 | tf_op jit(solution)/shard_map/ppermute | solution.py:116
  146.7 7.0 %collective-permute-start.32 = (f32[2,128,128]{2,1,0:T(8,128)S(1)}, f32[2,128,128]{2,1,0:T(8,128)S(1)}, u32[]{:S(2)}, u32[]{:S(2)}) collective-permute-start(f32[2,128,128]{2,1,0:T(8,128)S(1)} %bitcast_add_fusion.14), channel_id=1, source_target_pairs={{0,48},{8,56},{16,0},{24,8},{32,16},{40,24},{48,32},{56,40},{64,11... | collective-permute-start | bytes 393224 | tf_op jit(solution)/shard_map/ppermute | solution.py:116
  150.5 6.6 %collective-permute-start.25 = (f32[2,128,128]{2,1,0:T(8,128)S(1)}, f32[2,128,128]{2,1,0:T(8,128)S(1)}, u32[]{:S(2)}, u32[]{:S(2)}) collective-permute-start(f32[2,128,128]{2,1,0:T(8,128)S(1)} %bitcast_add_fusion.17), channel_id=1, source_target_pairs={{0,16},{8,24},{16,32},{24,40},{32,48},{40,56},{48,0},{56,8},{64,80... | collective-permute-start | bytes 393224 | tf_op jit(solution)/shard_map/ppermute | solution.py:116
  150.6 6.6 %collective-permute-start.18 = (f32[2,128,128]{2,1,0:T(8,128)S(1)}, f32[2,128,128]{2,1,0:T(8,128)S(1)}, u32[]{:S(2)}, u32[]{:S(2)}) collective-permute-start(f32[2,128,128]{2,1,0:T(8,128)S(1)} %bitcast_add_fusion.20), channel_id=1, source_target_pairs={{0,192},{8,200},{16,208},{24,216},{32,224},{40,232},{48,240},{56,2... | collective-permute-start | bytes 393224 | tf_op jit(solution)/shard_map/ppermute | solution.py:116
  153.7 6.9 %collective-permute-start.11 = (f32[2,128,128]{2,1,0:T(8,128)S(1)}, f32[2,128,128]{2,1,0:T(8,128)S(1)}, u32[]{:S(2)}, u32[]{:S(2)}) collective-permute-start(f32[2,128,128]{2,1,0:T(8,128)S(1)} %bitcast_add_fusion.23), channel_id=1, source_target_pairs={{0,64},{8,72},{16,80},{24,88},{32,96},{40,104},{48,112},{56,120},{... | collective-permute-start | bytes 393224 | tf_op jit(solution)/shard_map/ppermute | solution.py:116
  153.8 6.8 %collective-permute-start.33 = (f32[2,128,128]{2,1,0:T(8,128)S(1)}, f32[2,128,128]{2,1,0:T(8,128)S(1)}, u32[]{:S(2)}, u32[]{:S(2)}) collective-permute-start(f32[2,128,128]{2,1,0:T(8,128)S(1)} %bitcast_add_fusion.13), channel_id=1, source_target_pairs={{0,48},{8,56},{16,0},{24,8},{32,16},{40,24},{48,32},{56,40},{64,11... | collective-permute-start | bytes 393224 | tf_op jit(solution)/shard_map/ppermute | solution.py:116
  157.1 10.0 %collective-permute-start.26 = (f32[2,128,128]{2,1,0:T(8,128)S(1)}, f32[2,128,128]{2,1,0:T(8,128)S(1)}, u32[]{:S(2)}, u32[]{:S(2)}) collective-permute-start(f32[2,128,128]{2,1,0:T(8,128)S(1)} %bitcast_add_fusion.16), channel_id=1, source_target_pairs={{0,16},{8,24},{16,32},{24,40},{32,48},{40,56},{48,0},{56,8},{64,80... | collective-permute-start | bytes 393224 | tf_op jit(solution)/shard_map/ppermute | solution.py:116
  157.2 12.5 %collective-permute-start.19 = (f32[2,128,128]{2,1,0:T(8,128)S(1)}, f32[2,128,128]{2,1,0:T(8,128)S(1)}, u32[]{:S(2)}, u32[]{:S(2)}) collective-permute-start(f32[2,128,128]{2,1,0:T(8,128)S(1)} %bitcast_add_fusion.19), channel_id=1, source_target_pairs={{0,192},{8,200},{16,208},{24,216},{32,224},{40,232},{48,240},{56,2... | collective-permute-start | bytes 393224 | tf_op jit(solution)/shard_map/ppermute | solution.py:116
  160.5 12.7 %collective-permute-start.12 = (f32[2,128,128]{2,1,0:T(8,128)S(1)}, f32[2,128,128]{2,1,0:T(8,128)S(1)}, u32[]{:S(2)}, u32[]{:S(2)}) collective-permute-start(f32[2,128,128]{2,1,0:T(8,128)S(1)} %bitcast_add_fusion.22), channel_id=1, source_target_pairs={{0,64},{8,72},{16,80},{24,88},{32,96},{40,104},{48,112},{56,120},{... | collective-permute-start | bytes 393224 | tf_op jit(solution)/shard_map/ppermute | solution.py:116
  160.7 15.3 %collective-permute-start.34 = (f32[128,128]{1,0:T(8,128)S(1)}, f32[128,128]{1,0:T(8,128)S(1)}, u32[]{:S(2)}, u32[]{:S(2)}) collective-permute-start(f32[128,128]{1,0:T(8,128)S(1)} %dynamic-slice_bitcast_fusion.8), channel_id=1, source_target_pairs={{0,8},{8,0},{16,24},{24,16},{32,40},{40,32},{48,56},{56,48},{64,72... | collective-permute-start | bytes 196616 | tf_op jit(solution)/shard_map/ppermute | solution.py:125
  167.1 8.9 %collective-permute-start.27 = (f32[128,128]{1,0:T(8,128)S(1)}, f32[128,128]{1,0:T(8,128)S(1)}, u32[]{:S(2)}, u32[]{:S(2)}) collective-permute-start(f32[128,128]{1,0:T(8,128)S(1)} %dynamic-slice_bitcast_fusion.9), channel_id=1, source_target_pairs={{0,8},{8,0},{16,24},{24,16},{32,40},{40,32},{48,56},{56,48},{64,72... | collective-permute-start | bytes 196616 | tf_op jit(solution)/shard_map/ppermute | solution.py:125
  169.8 8.3 %collective-permute-start.20 = (f32[128,128]{1,0:T(8,128)S(1)}, f32[128,128]{1,0:T(8,128)S(1)}, u32[]{:S(2)}, u32[]{:S(2)}) collective-permute-start(f32[128,128]{1,0:T(8,128)S(1)} %dynamic-slice_bitcast_fusion.10), channel_id=1, source_target_pairs={{0,8},{8,0},{16,24},{24,16},{32,40},{40,32},{48,56},{56,48},{64,72... | collective-permute-start | bytes 196616 | tf_op jit(solution)/shard_map/ppermute | solution.py:125
  173.3 8.3 %collective-permute-start.13 = (f32[128,128]{1,0:T(8,128)S(1)}, f32[128,128]{1,0:T(8,128)S(1)}, u32[]{:S(2)}, u32[]{:S(2)}) collective-permute-start(f32[128,128]{1,0:T(8,128)S(1)} %dynamic-slice_bitcast_fusion.11), channel_id=1, source_target_pairs={{0,8},{8,0},{16,24},{24,16},{32,40},{40,32},{48,56},{56,48},{64,72... | collective-permute-start | bytes 196616 | tf_op jit(solution)/shard_map/ppermute | solution.py:125

commit v6 on v5

--- a/solution.py
+++ b/solution.py
@@ -179,12 +179,13 @@
     partials = partials.reshape((CS,) + BLK_DIMS + (block, block))
     results = []
     for c in range(CS):
+        data = partials[c]
         direction = 1 if c % 2 == 0 else -1
         if c < 2:
-            data = ring_reduce_scatter(partials, 1, 1, direction, my_x, (c,))
+            data = ring_reduce_scatter(data, 1, 1, direction, my_x)
             data = ring_reduce_scatter(data, 0, 0, direction, my_y)
         else:
-            data = ring_reduce_scatter(partials, 0, 0, direction, my_y, (c,))
+            data = ring_reduce_scatter(data, 0, 0, direction, my_y)
             data = ring_reduce_scatter(data, 0, 1, direction, my_x)
         results.append(pair_reduce_scatter(data, 2, my_z))
     summed = jnp.stack(results)

time: 184 us -> 181 us (0.984)
  waiting for transfers between devices: 70.1 us -> 56.8 us
  local copies, waits for them, and re-layouts: 6.36 us -> 15.4 us
  starting transfers between devices: 68.6 us -> 72.6 us
  other arithmetic: 12.8 us -> 9.68 us
    ppermute x24, waiting for transfers between devices: 33.4 us -> 20.6 us  [ring_reduce_scatter(): arrived = lax.ppermute(send, 'blk', route)]
    slice x0 -> x1, local copies, waits for them, and re-layouts: none -> 6.5 us  [per_device(): data = partials[c]]
    add x15 -> x24, other arithmetic: 7.6 us -> 2.02 us  [ring_reduce_scatter(): send = arrived + piece(k + 1)]
    ppermute x24, starting transfers between devices: 35.9 us -> 40.9 us  [ring_reduce_scatter(): arrived = lax.ppermute(send, 'blk', route)]
    unnamed x11 -> x23, local copies, waits for them, and re-layouts: 0.28 us -> 2.46 us
    reshape x6 -> x8, local copies, waits for them, and re-layouts: 3.41 us -> 4.05 us  [_take(): piece.reshape([s for i, s in enumerate(sizes) if i >= offset and i != off...]
  transfers between devices with their start and end apart: 35 -> 35, of which waited for: 15 -> 16; matrix products, arithmetic and copies ran while one was open for 3% -> 5% of each run, Pallas kernels for 0% -> 0%
where the time goes in v6:
time: 181 us; the launch traced here: 179 us
  starting transfers between devices  72.6 us (40%)
  waiting for transfers between devices  56.8 us (31%)
  Pallas kernels  23.9 us (13%)
  local copies, waits for them, and re-layouts  15.4 us (9%)
  other arithmetic  9.68 us (5%)
    ppermute x24, starting transfers between devices, ring_reduce_scatter(): arrived = lax.ppermute(send, 'blk', route)  40.9 us
    ppermute x3, waiting for transfers between devices, line_all_gather(): send_down = lax.ppermute(send_down, 'grp', down)  27.3 us
    pallas_call x1, Pallas kernels, owner_partials(): pl.pallas_call(_products_kernel, out_shape=jax.ShapeDtypeStruct((CS, owne...  23.9 us
    ppermute x24, waiting for transfers between devices, ring_reduce_scatter(): arrived = lax.ppermute(send, 'blk', route)  20.6 us
    ppermute x4, starting transfers between devices, pair_reduce_scatter(): return lax.ppermute(other, 'blk', route) + mine  14.2 us
    ppermute x3, starting transfers between devices, line_all_gather(): send_up = lax.ppermute(send_up, 'grp', up)  9.59 us
    ppermute x3, starting transfers between devices, line_all_gather(): send_down = lax.ppermute(send_down, 'grp', down)  7.91 us
    slice x1, local copies, waits for them, and re-layouts, per_device(): data = partials[c]  6.5 us
  transfers between devices with their start and end apart: 35, of which 16 were waited for; matrix products, arithmetic and copies ran while one was open for 5% of the time, Pallas kernels for 0%

profile of v6, /device:TPU:32, one launch (start us, length us, event | category | flops | bytes accessed | tf_op | source)
XLA Modules:
  0.0 179.0 jit_solution(7632159793846860060)
XLA Ops:
  0.0 3.7 %collective-permute-start.3 = (bf16[16,128,128]{2,1,0:T(8,128)(2,1)}, bf16[16,128,128]{2,1,0:T(8,128)(2,1)S(1)}, u32[]{:S(2)}, u32[]{:S(2)}) collective-permute-start(bf16[16,128,128]{2,1,0:T(8,128)(2,1)} %param.6), channel_id=1, source_target_pairs={{2,0},{3,1},{4,2},{5,3},{6,4},{7,5},{10,8},{11,9},{12,10},{13,11},... | collective-permute-start | bytes 1572872 | tf_op jit(solution)/shard_map/ppermute | solution.py:141
  3.7 2.1 %collective-permute-start = (bf16[16,128,128]{2,1,0:T(8,128)(2,1)}, bf16[16,128,128]{2,1,0:T(8,128)(2,1)S(1)}, u32[]{:S(2)}, u32[]{:S(2)}) collective-permute-start(bf16[16,128,128]{2,1,0:T(8,128)(2,1)} %param.6), channel_id=1, source_target_pairs={{0,2},{1,3},{2,4},{3,5},{4,6},{5,7},{8,10},{9,11},{10,12},{11,13},... | collective-permute-start | bytes 1572872 | tf_op jit(solution)/shard_map/ppermute | solution.py:140
  5.9 10.1 %collective-permute-done.3 = bf16[16,128,128]{2,1,0:T(8,128)(2,1)S(1)} collective-permute-done((bf16[16,128,128]{2,1,0:T(8,128)(2,1)}, bf16[16,128,128]{2,1,0:T(8,128)(2,1)S(1)}, u32[]{:S(2)}, u32[]{:S(2)}) %collective-permute-start.3) | collective-permute-done | bytes 524320 | tf_op jit(solution)/shard_map/ppermute | solution.py:141
  15.9 2.0 %collective-permute-start.4 = (bf16[16,128,128]{2,1,0:T(8,128)(2,1)S(1)}, bf16[16,128,128]{2,1,0:T(8,128)(2,1)S(1)}, u32[]{:S(2)}, u32[]{:S(2)}) collective-permute-start(bf16[16,128,128]{2,1,0:T(8,128)(2,1)S(1)} %collective-permute-done.3), channel_id=1, source_target_pairs={{2,0},{3,1},{4,2},{5,3},{6,4},{7,5},{10,8},{11,9},{12,10},{13,11},... | collective-permute-start | bytes 1572872 | tf_op jit(solution)/shard_map/ppermute | solution.py:141
  18.0 3.8 %collective-permute-start.1 = (bf16[16,128,128]{2,1,0:T(8,128)(2,1)S(1)}, bf16[16,128,128]{2,1,0:T(8,128)(2,1)}, u32[]{:S(2)}, u32[]{:S(2)}) collective-permute-start(bf16[16,128,128]{2,1,0:T(8,128)(2,1)S(1)} %collective-permute-done), channel_id=1, source_target_pairs={{0,2},{1,3},{2,4},{3,5},{4,6},{5,7},{8,10},{9,11},{10,12},{11,13},... | collective-permute-start | bytes 1572872 | tf_op jit(solution)/shard_map/ppermute | solution.py:140
  21.8 9.0 %collective-permute-done.4 = bf16[16,128,128]{2,1,0:T(8,128)(2,1)S(1)} collective-permute-done((bf16[16,128,128]{2,1,0:T(8,128)(2,1)S(1)}, bf16[16,128,128]{2,1,0:T(8,128)(2,1)S(1)}, u32[]{:S(2)}, u32[]{:S(2)}) %collective-permute-start.4) | collective-permute-done | bytes 524320 | tf_op jit(solution)/shard_map/ppermute | solution.py:141
  30.8 2.2 %collective-permute-start.5 = (bf16[16,128,128]{2,1,0:T(8,128)(2,1)S(1)}, bf16[16,128,128]{2,1,0:T(8,128)(2,1)S(1)}, u32[]{:S(2)}, u32[]{:S(2)}) collective-permute-start(bf16[16,128,128]{2,1,0:T(8,128)(2,1)S(1)} %collective-permute-done.4), channel_id=1, source_target_pairs={{2,0},{3,1},{4,2},{5,3},{6,4},{7,5},{10,8},{11,9},{12,10},{13,11},... | collective-permute-start | bytes 1572872 | tf_op jit(solution)/shard_map/ppermute | solution.py:141
  33.0 3.6 %collective-permute-start.2 = (bf16[16,128,128]{2,1,0:T(8,128)(2,1)}, bf16[16,128,128]{2,1,0:T(8,128)(2,1)}, u32[]{:S(2)}, u32[]{:S(2)}) collective-permute-start(bf16[16,128,128]{2,1,0:T(8,128)(2,1)} %collective-permute-done.1), channel_id=1, source_target_pairs={{0,2},{1,3},{2,4},{3,5},{4,6},{5,7},{8,10},{9,11},{10,12},{11,13},... | collective-permute-start | bytes 1572872 | tf_op jit(solution)/shard_map/ppermute | solution.py:140
  36.7 8.2 %collective-permute-done.5 = bf16[16,128,128]{2,1,0:T(8,128)(2,1)S(1)} collective-permute-done((bf16[16,128,128]{2,1,0:T(8,128)(2,1)S(1)}, bf16[16,128,128]{2,1,0:T(8,128)(2,1)S(1)}, u32[]{:S(2)}, u32[]{:S(2)}) %collective-permute-start.5) | collective-permute-done | bytes 524320 | tf_op jit(solution)/shard_map/ppermute | solution.py:141
  44.9 0.8 copy-done.5
  45.8 1.2 pad_maximum_fusion.3
  47.3 1.4 pad_maximum_fusion.2
  49.1 1.6 pad_maximum_fusion.1
  53.1 2.0 %collective-permute-done.6 = bf16[4,16,128,128]{3,2,1,0:T(8,128)(2,1)} collective-permute-done((bf16[4,16,128,128]{3,2,1,0:T(8,128)(2,1)}, bf16[4,16,128,128]{3,2,1,0:T(8,128)(2,1)}, u32[]{:S(2)}, u32[]{:S(2)}) %collective-permute-start.6) | collective-permute-done | bytes 2097184 | tf_op jit(solution)/shard_map/ppermute | solution.py:159
  55.2 1.9 %select_bitcast_fusion.1 = (bf16[4,1,16,128,128]{4,3,2,0,1:T(8,128)(2,1)S(1)}, bf16[4,1,16,128,128]{4,3,2,0,1:T(8,128)(2,1)S(1)}) fusion(bf16[4,16,128,128]{3,2,1,0:T(8,128)(2,1)} %collective-permute-done.6, pred[]{:T(512)S(6)} %eq.55, bf16[1,16,128,128]{3,2,1,0:T(8,128)(2,1)S(1)} %get-tuple-element.14, bf16[1,16,128,128]{3,2,1,0:T(8,128)(2,1)} %copy-done.4, ...), kind=kLoop, calls=%fused_computation.6 | loop fusion | flops 5242880 | bytes 8388609 | tf_op jit(solution)/shard_map/stack | solution.py:162
  57.8 23.9 %shard_map.46 = f32[4,32,128,128]{3,2,1,0:T(8,128)} custom-call(s32[384]{0:T(512)S(1)} %reshape.194.left_ref, s32[384]{0:T(512)S(1)} %reshape.195.right_ref, s32[384]{0:T(512)S(1)} %reshape.196.target_ref, bf16[128,128,128]{2,1,0:T(8,128)(2,1)S(1)} %bitcast.146), custom_call_target="tpu_custom_call" | custom-call | flops 1610612736 | bytes 12582912 | tf_op jit(solution)/shard_map/pallas_call | solution.py:37
  81.7 6.5 %fusion.13 = (f32[1,32,128,128]{3,2,1,0:T(8,128)S(1)}, f32[1,32,128,128]{3,2,1,0:T(8,128)S(1)}, f32[1,32,128,128]{3,2,1,0:T(8,128)}, f32[1,32,128,128]{3,2,1,0:T(8,128)}) fusion(f32[4,32,128,128]{3,2,1,0:T(8,128)} %shard_map.46), kind=kLoop, calls=%fused_computation.76 | loop fusion | bytes 16777216 | tf_op jit(solution)/shard_map/slice | solution.py:182
  88.2 1.3 copy-done.2
  89.5 0.8 dynamic-slice_bitcast_fusion
  90.4 3.0 %collective-permute-start.28 = (f32[4,2,128,128]{3,2,1,0:T(8,128)}, f32[4,2,128,128]{3,2,1,0:T(8,128)S(1)}, u32[]{:S(2)}, u32[]{:S(2)}) collective-permute-start(f32[4,2,128,128]{3,2,1,0:T(8,128)} %dynamic-slice_bitcast_fusion), channel_id=1, source_target_pairs={{0,192},{8,200},{16,208},{24,216},{32,224},{40,232},{48,240},{56,2... | collective-permute-start | bytes 1572872 | tf_op jit(solution)/shard_map/ppermute | solution.py:116
  93.4 1.9 %dynamic-slice_bitcast_fusion.1 = f32[4,2,128,128]{3,2,1,0:T(8,128)} fusion(f32[4,4,2,128,128]{4,3,2,1,0:T(8,128)} %bitcast.155, s32[]{:T(128)S(6)} %select_n.337), kind=kLoop, calls=%fused_computation.30 | loop fusion | bytes 1048580 | tf_op jit(solution)/shard_map/reshape | solution.py:102
  95.3 1.2 dynamic-slice_bitcast_fusion.2
  96.5 2.8 %collective-permute-start.14 = (f32[4,2,128,128]{3,2,1,0:T(8,128)S(1)}, f32[4,2,128,128]{3,2,1,0:T(8,128)S(1)}, u32[]{:S(2)}, u32[]{:S(2)}) collective-permute-start(f32[4,2,128,128]{3,2,1,0:T(8,128)S(1)} %dynamic-slice_bitcast_fusion.2), channel_id=1, source_target_pairs={{0,48},{8,56},{16,0},{24,8},{32,16},{40,24},{48,32},{56,40},{64,11... | collective-permute-start | bytes 1572872 | tf_op jit(solution)/shard_map/ppermute | solution.py:116
  99.5 5.7 %collective-permute-done.28 = f32[4,2,128,128]{3,2,1,0:T(8,128)S(1)} collective-permute-done((f32[4,2,128,128]{3,2,1,0:T(8,128)}, f32[4,2,128,128]{3,2,1,0:T(8,128)S(1)}, u32[]{:S(2)}, u32[]{:S(2)}) %collective-permute-start.28) | collective-permute-done | bytes 524320 | tf_op jit(solution)/shard_map/ppermute | solution.py:116
  105.2 1.1 bitcast_add_fusion.2
  106.3 3.7 %collective-permute-start.29 = (f32[4,2,128,128]{3,2,1,0:T(8,128)S(1)}, f32[4,2,128,128]{3,2,1,0:T(8,128)S(1)}, u32[]{:S(2)}, u32[]{:S(2)}) collective-permute-start(f32[4,2,128,128]{3,2,1,0:T(8,128)S(1)} %bitcast_add_fusion.2), channel_id=1, source_target_pairs={{0,192},{8,200},{16,208},{24,216},{32,224},{40,232},{48,240},{56,2... | collective-permute-start | bytes 1572872 | tf_op jit(solution)/shard_map/ppermute | solution.py:116
  110.6 3.7 %collective-permute-start.15 = (f32[4,2,128,128]{3,2,1,0:T(8,128)S(1)}, f32[4,2,128,128]{3,2,1,0:T(8,128)S(1)}, u32[]{:S(2)}, u32[]{:S(2)}) collective-permute-start(f32[4,2,128,128]{3,2,1,0:T(8,128)S(1)} %bitcast_add_fusion.8), channel_id=1, source_target_pairs={{0,48},{8,56},{16,0},{24,8},{32,16},{40,24},{48,32},{56,40},{64,11... | collective-permute-start | bytes 1572872 | tf_op jit(solution)/shard_map/ppermute | solution.py:116
  114.6 6.0 %collective-permute-done.29 = f32[4,2,128,128]{3,2,1,0:T(8,128)S(1)} collective-permute-done((f32[4,2,128,128]{3,2,1,0:T(8,128)S(1)}, f32[4,2,128,128]{3,2,1,0:T(8,128)S(1)}, u32[]{:S(2)}, u32[]{:S(2)}) %collective-permute-start.29) | collective-permute-done | bytes 524320 | tf_op jit(solution)/shard_map/ppermute | solution.py:116
  120.7 3.9 %collective-permute-start.30 = (f32[4,2,128,128]{3,2,1,0:T(8,128)S(1)}, f32[4,2,128,128]{3,2,1,0:T(8,128)S(1)}, u32[]{:S(2)}, u32[]{:S(2)}) collective-permute-start(f32[4,2,128,128]{3,2,1,0:T(8,128)S(1)} %bitcast_add_fusion.1), channel_id=1, source_target_pairs={{0,192},{8,200},{16,208},{24,216},{32,224},{40,232},{48,240},{56,2... | collective-permute-start | bytes 1572872 | tf_op jit(solution)/shard_map/ppermute | solution.py:116
  124.9 3.7 %collective-permute-start.16 = (f32[4,2,128,128]{3,2,1,0:T(8,128)S(1)}, f32[4,2,128,128]{3,2,1,0:T(8,128)S(1)}, u32[]{:S(2)}, u32[]{:S(2)}) collective-permute-start(f32[4,2,128,128]{3,2,1,0:T(8,128)S(1)} %bitcast_add_fusion.7), channel_id=1, source_target_pairs={{0,48},{8,56},{16,0},{24,8},{32,16},{40,24},{48,32},{56,40},{64,11... | collective-permute-start | bytes 1572872 | tf_op jit(solution)/shard_map/ppermute | solution.py:116
  128.7 5.7 %collective-permute-done.30 = f32[4,2,128,128]{3,2,1,0:T(8,128)S(1)} collective-permute-done((f32[4,2,128,128]{3,2,1,0:T(8,128)S(1)}, f32[4,2,128,128]{3,2,1,0:T(8,128)S(1)}, u32[]{:S(2)}, u32[]{:S(2)}) %collective-permute-start.30) | collective-permute-done | bytes 524320 | tf_op jit(solution)/shard_map/ppermute | solution.py:116
  134.5 2.8 %collective-permute-start.31 = (f32[2,128,128]{2,1,0:T(8,128)S(1)}, f32[2,128,128]{2,1,0:T(8,128)S(1)}, u32[]{:S(2)}, u32[]{:S(2)}) collective-permute-start(f32[2,128,128]{2,1,0:T(8,128)S(1)} %dynamic-slice_bitcast_fusion.4), channel_id=1, source_target_pairs={{0,48},{8,56},{16,0},{24,8},{32,16},{40,24},{48,32},{56,40},{64,11... | collective-permute-start | bytes 393224 | tf_op jit(solution)/shard_map/ppermute | solution.py:116
  138.0 1.6 collective-permute-start.24
  139.7 2.3 %collective-permute-start.17 = (f32[2,128,128]{2,1,0:T(8,128)S(1)}, f32[2,128,128]{2,1,0:T(8,128)S(1)}, u32[]{:S(2)}, u32[]{:S(2)}) collective-permute-start(f32[2,128,128]{2,1,0:T(8,128)S(1)} %dynamic-slice_bitcast_fusion.6), channel_id=1, source_target_pairs={{0,192},{8,200},{16,208},{24,216},{32,224},{40,232},{48,240},{56,2... | collective-permute-start | bytes 393224 | tf_op jit(solution)/shard_map/ppermute | solution.py:116
  142.0 1.0 collective-permute-done.9
  143.3 2.8 %collective-permute-start.32 = (f32[2,128,128]{2,1,0:T(8,128)S(1)}, f32[2,128,128]{2,1,0:T(8,128)S(1)}, u32[]{:S(2)}, u32[]{:S(2)}) collective-permute-start(f32[2,128,128]{2,1,0:T(8,128)S(1)} %bitcast_add_fusion.14), channel_id=1, source_target_pairs={{0,48},{8,56},{16,0},{24,8},{32,16},{40,24},{48,32},{56,40},{64,11... | collective-permute-start | bytes 393224 | tf_op jit(solution)/shard_map/ppermute | solution.py:116
  146.2 3.3 %collective-permute-start.18 = (f32[2,128,128]{2,1,0:T(8,128)S(1)}, f32[2,128,128]{2,1,0:T(8,128)S(1)}, u32[]{:S(2)}, u32[]{:S(2)}) collective-permute-start(f32[2,128,128]{2,1,0:T(8,128)S(1)} %bitcast_add_fusion.20), channel_id=1, source_target_pairs={{0,192},{8,200},{16,208},{24,216},{32,224},{40,232},{48,240},{56,2... | collective-permute-start | bytes 393224 | tf_op jit(solution)/shard_map/ppermute | solution.py:116
  149.9 3.0 %collective-permute-start.33 = (f32[2,128,128]{2,1,0:T(8,128)S(1)}, f32[2,128,128]{2,1,0:T(8,128)S(1)}, u32[]{:S(2)}, u32[]{:S(2)}) collective-permute-start(f32[2,128,128]{2,1,0:T(8,128)S(1)} %bitcast_add_fusion.13), channel_id=1, source_target_pairs={{0,48},{8,56},{16,0},{24,8},{32,16},{40,24},{48,32},{56,40},{64,11... | collective-permute-start | bytes 393224 | tf_op jit(solution)/shard_map/ppermute | solution.py:116
  153.1 3.3 %collective-permute-start.19 = (f32[2,128,128]{2,1,0:T(8,128)S(1)}, f32[2,128,128]{2,1,0:T(8,128)S(1)}, u32[]{:S(2)}, u32[]{:S(2)}) collective-permute-start(f32[2,128,128]{2,1,0:T(8,128)S(1)} %bitcast_add_fusion.19), channel_id=1, source_target_pairs={{0,192},{8,200},{16,208},{24,216},{32,224},{40,232},{48,240},{56,2... | collective-permute-start | bytes 393224 | tf_op jit(solution)/shard_map/ppermute | solution.py:116
  156.4 0.8 collective-permute-done.11
  157.4 6.4 %collective-permute-start.34 = (f32[128,128]{1,0:T(8,128)S(1)}, f32[128,128]{1,0:T(8,128)S(1)}, u32[]{:S(2)}, u32[]{:S(2)}) collective-permute-start(f32[128,128]{1,0:T(8,128)S(1)} %dynamic-slice_bitcast_fusion.8), channel_id=1, source_target_pairs={{0,8},{8,0},{16,24},{24,16},{32,40},{40,32},{48,56},{56,48},{64,72... | collective-permute-start | bytes 196616 | tf_op jit(solution)/shard_map/ppermute | solution.py:125
  163.9 1.7 collective-permute-start.27
  165.6 4.4 %collective-permute-start.20 = (f32[128,128]{1,0:T(8,128)S(1)}, f32[128,128]{1,0:T(8,128)S(1)}, u32[]{:S(2)}, u32[]{:S(2)}) collective-permute-start(f32[128,128]{1,0:T(8,128)S(1)} %dynamic-slice_bitcast_fusion.10), channel_id=1, source_target_pairs={{0,8},{8,0},{16,24},{24,16},{32,40},{40,32},{48,56},{56,48},{64,72... | collective-permute-start | bytes 196616 | tf_op jit(solution)/shard_map/ppermute | solution.py:125
  170.1 1.7 collective-permute-start.13
  171.8 0.6 collective-permute-done.27
  172.5 1.5 collective-permute-done.20
  174.0 4.3 %collective-permute-done.13 = f32[128,128]{1,0:T(8,128)S(1)} collective-permute-done((f32[128,128]{1,0:T(8,128)S(1)}, f32[128,128]{1,0:T(8,128)S(1)}, u32[]{:S(2)}, u32[]{:S(2)}) %collective-permute-start.13) | collective-permute-done | bytes 65568 | tf_op jit(solution)/shard_map/ppermute | solution.py:125
  178.3 0.7 pad_maximum_fusion.4
  (105 shorter events, 7.1 us)
Async XLA Ops:
  0.0 15.9 %collective-permute-start.3 = (bf16[16,128,128]{2,1,0:T(8,128)(2,1)}, bf16[16,128,128]{2,1,0:T(8,128)(2,1)S(1)}, u32[]{:S(2)}, u32[]{:S(2)}) collective-permute-start(bf16[16,128,128]{2,1,0:T(8,128)(2,1)} %param.6), channel_id=1, source_target_pairs={{2,0},{3,1},{4,2},{5,3},{6,4},{7,5},{10,8},{11,9},{12,10},{13,11},... | collective-permute-start | bytes 1572872 | tf_op jit(solution)/shard_map/ppermute | solution.py:141
  3.7 14.2 %collective-permute-start = (bf16[16,128,128]{2,1,0:T(8,128)(2,1)}, bf16[16,128,128]{2,1,0:T(8,128)(2,1)S(1)}, u32[]{:S(2)}, u32[]{:S(2)}) collective-permute-start(bf16[16,128,128]{2,1,0:T(8,128)(2,1)} %param.6), channel_id=1, source_target_pairs={{0,2},{1,3},{2,4},{3,5},{4,6},{5,7},{8,10},{9,11},{10,12},{11,13},... | collective-permute-start | bytes 1572872 | tf_op jit(solution)/shard_map/ppermute | solution.py:140
  15.9 14.9 %collective-permute-start.4 = (bf16[16,128,128]{2,1,0:T(8,128)(2,1)S(1)}, bf16[16,128,128]{2,1,0:T(8,128)(2,1)S(1)}, u32[]{:S(2)}, u32[]{:S(2)}) collective-permute-start(bf16[16,128,128]{2,1,0:T(8,128)(2,1)S(1)} %collective-permute-done.3), channel_id=1, source_target_pairs={{2,0},{3,1},{4,2},{5,3},{6,4},{7,5},{10,8},{11,9},{12,10},{13,11},... | collective-permute-start | bytes 1572872 | tf_op jit(solution)/shard_map/ppermute | solution.py:141
  18.0 15.0 %collective-permute-start.1 = (bf16[16,128,128]{2,1,0:T(8,128)(2,1)S(1)}, bf16[16,128,128]{2,1,0:T(8,128)(2,1)}, u32[]{:S(2)}, u32[]{:S(2)}) collective-permute-start(bf16[16,128,128]{2,1,0:T(8,128)(2,1)S(1)} %collective-permute-done), channel_id=1, source_target_pairs={{0,2},{1,3},{2,4},{3,5},{4,6},{5,7},{8,10},{9,11},{10,12},{11,13},... | collective-permute-start | bytes 1572872 | tf_op jit(solution)/shard_map/ppermute | solution.py:140
  30.8 14.1 %collective-permute-start.5 = (bf16[16,128,128]{2,1,0:T(8,128)(2,1)S(1)}, bf16[16,128,128]{2,1,0:T(8,128)(2,1)S(1)}, u32[]{:S(2)}, u32[]{:S(2)}) collective-permute-start(bf16[16,128,128]{2,1,0:T(8,128)(2,1)S(1)} %collective-permute-done.4), channel_id=1, source_target_pairs={{2,0},{3,1},{4,2},{5,3},{6,4},{7,5},{10,8},{11,9},{12,10},{13,11},... | collective-permute-start | bytes 1572872 | tf_op jit(solution)/shard_map/ppermute | solution.py:141
  33.0 14.2 %collective-permute-start.2 = (bf16[16,128,128]{2,1,0:T(8,128)(2,1)}, bf16[16,128,128]{2,1,0:T(8,128)(2,1)}, u32[]{:S(2)}, u32[]{:S(2)}) collective-permute-start(bf16[16,128,128]{2,1,0:T(8,128)(2,1)} %collective-permute-done.1), channel_id=1, source_target_pairs={{0,2},{1,3},{2,4},{3,5},{4,6},{5,7},{8,10},{9,11},{10,12},{11,13},... | collective-permute-start | bytes 1572872 | tf_op jit(solution)/shard_map/ppermute | solution.py:140
  44.9 0.8 copy-start.5
  47.0 1.7 copy-start.6
  49.0 1.6 copy-start.4
  49.0 1.6 copy-start.7
  49.1 1.7 copy-start.8
  49.1 3.0 %copy-start.9 = (s32[1,1,32,12]{2,1,3,0:T(1,128)S(1)}, s32[1,1,32,12]{2,1,3,0:T(1,128)}, u32[]{:S(2)}) copy-start(s32[1,1,32,12]{2,1,3,0:T(1,128)} %param.7) | copy-start | bytes 4612
  50.7 4.5 %collective-permute-start.6 = (bf16[4,16,128,128]{3,2,1,0:T(8,128)(2,1)}, bf16[4,16,128,128]{3,2,1,0:T(8,128)(2,1)}, u32[]{:S(2)}, u32[]{:S(2)}) collective-permute-start(bf16[4,16,128,128]{3,2,1,0:T(8,128)(2,1)} %pad_maximum_fusion.1), channel_id=1, source_target_pairs={{0,1},{1,0},{2,3},{3,2},{4,5},{5,4},{6,7},{7,6},{8,9},{9,8},{10,11... | collective-permute-start | bytes 6291464 | tf_op jit(solution)/shard_map/ppermute | solution.py:159
  88.2 1.3 copy-start.2
  90.4 14.8 %collective-permute-start.28 = (f32[4,2,128,128]{3,2,1,0:T(8,128)}, f32[4,2,128,128]{3,2,1,0:T(8,128)S(1)}, u32[]{:S(2)}, u32[]{:S(2)}) collective-permute-start(f32[4,2,128,128]{3,2,1,0:T(8,128)} %dynamic-slice_bitcast_fusion), channel_id=1, source_target_pairs={{0,192},{8,200},{16,208},{24,216},{32,224},{40,232},{48,240},{56,2... | collective-permute-start | bytes 1572872 | tf_op jit(solution)/shard_map/ppermute | solution.py:116
  95.3 15.1 %collective-permute-start.21 = (f32[4,2,128,128]{3,2,1,0:T(8,128)}, f32[4,2,128,128]{3,2,1,0:T(8,128)S(1)}, u32[]{:S(2)}, u32[]{:S(2)}) collective-permute-start(f32[4,2,128,128]{3,2,1,0:T(8,128)} %dynamic-slice_bitcast_fusion.1), channel_id=1, source_target_pairs={{0,64},{8,72},{16,80},{24,88},{32,96},{40,104},{48,112},{56,120},{... | collective-permute-start | bytes 1572872 | tf_op jit(solution)/shard_map/ppermute | solution.py:116
  95.3 15.1 %copy-start.1 = (f32[1,32,128,128]{3,2,1,0:T(8,128)S(1)}, f32[1,32,128,128]{3,2,1,0:T(8,128)}, u32[]{:S(2)}) copy-start(f32[1,32,128,128]{3,2,1,0:T(8,128)} %get-tuple-element.8) | copy-start | bytes 6291460
  96.5 14.0 %collective-permute-start.14 = (f32[4,2,128,128]{3,2,1,0:T(8,128)S(1)}, f32[4,2,128,128]{3,2,1,0:T(8,128)S(1)}, u32[]{:S(2)}, u32[]{:S(2)}) collective-permute-start(f32[4,2,128,128]{3,2,1,0:T(8,128)S(1)} %dynamic-slice_bitcast_fusion.2), channel_id=1, source_target_pairs={{0,48},{8,56},{16,0},{24,8},{32,16},{40,24},{48,32},{56,40},{64,11... | collective-permute-start | bytes 1572872 | tf_op jit(solution)/shard_map/ppermute | solution.py:116
  99.4 11.2 %copy-start = (f32[1,32,128,128]{3,2,1,0:T(8,128)S(1)}, f32[1,32,128,128]{3,2,1,0:T(8,128)}, u32[]{:S(2)}) copy-start(f32[1,32,128,128]{3,2,1,0:T(8,128)} %get-tuple-element.9) | copy-start | bytes 6291460
  99.4 15.0 %collective-permute-start.7 = (f32[4,2,128,128]{3,2,1,0:T(8,128)S(1)}, f32[4,2,128,128]{3,2,1,0:T(8,128)S(1)}, u32[]{:S(2)}, u32[]{:S(2)}) collective-permute-start(f32[4,2,128,128]{3,2,1,0:T(8,128)S(1)} %dynamic-slice_bitcast_fusion.3), channel_id=1, source_target_pairs={{0,16},{8,24},{16,32},{24,40},{32,48},{40,56},{48,0},{56,8},{64,80... | collective-permute-start | bytes 1572872 | tf_op jit(solution)/shard_map/ppermute | solution.py:116
  106.3 14.3 %copy-start.3 = (f32[1,32,128,128]{3,2,1,0:T(8,128)S(1)}, f32[1,32,128,128]{3,2,1,0:T(8,128)}, u32[]{:S(2)}) copy-start(f32[1,32,128,128]{3,2,1,0:T(8,128)} %copy-done.2) | copy-start | bytes 6291460
  106.3 14.3 %collective-permute-start.29 = (f32[4,2,128,128]{3,2,1,0:T(8,128)S(1)}, f32[4,2,128,128]{3,2,1,0:T(8,128)S(1)}, u32[]{:S(2)}, u32[]{:S(2)}) collective-permute-start(f32[4,2,128,128]{3,2,1,0:T(8,128)S(1)} %bitcast_add_fusion.2), channel_id=1, source_target_pairs={{0,192},{8,200},{16,208},{24,216},{32,224},{40,232},{48,240},{56,2... | collective-permute-start | bytes 1572872 | tf_op jit(solution)/shard_map/ppermute | solution.py:116
  110.5 14.2 %collective-permute-start.22 = (f32[4,2,128,128]{3,2,1,0:T(8,128)S(1)}, f32[4,2,128,128]{3,2,1,0:T(8,128)S(1)}, u32[]{:S(2)}, u32[]{:S(2)}) collective-permute-start(f32[4,2,128,128]{3,2,1,0:T(8,128)S(1)} %bitcast_add_fusion.5), channel_id=1, source_target_pairs={{0,64},{8,72},{16,80},{24,88},{32,96},{40,104},{48,112},{56,120},{... | collective-permute-start | bytes 1572872 | tf_op jit(solution)/shard_map/ppermute | solution.py:116
  110.6 14.1 %collective-permute-start.15 = (f32[4,2,128,128]{3,2,1,0:T(8,128)S(1)}, f32[4,2,128,128]{3,2,1,0:T(8,128)S(1)}, u32[]{:S(2)}, u32[]{:S(2)}) collective-permute-start(f32[4,2,128,128]{3,2,1,0:T(8,128)S(1)} %bitcast_add_fusion.8), channel_id=1, source_target_pairs={{0,48},{8,56},{16,0},{24,8},{32,16},{40,24},{48,32},{56,40},{64,11... | collective-permute-start | bytes 1572872 | tf_op jit(solution)/shard_map/ppermute | solution.py:116
  114.5 14.1 %collective-permute-start.8 = (f32[4,2,128,128]{3,2,1,0:T(8,128)S(1)}, f32[4,2,128,128]{3,2,1,0:T(8,128)S(1)}, u32[]{:S(2)}, u32[]{:S(2)}) collective-permute-start(f32[4,2,128,128]{3,2,1,0:T(8,128)S(1)} %bitcast_add_fusion.11), channel_id=1, source_target_pairs={{0,16},{8,24},{16,32},{24,40},{32,48},{40,56},{48,0},{56,8},{64,80... | collective-permute-start | bytes 1572872 | tf_op jit(solution)/shard_map/ppermute | solution.py:116
  120.7 13.7 %collective-permute-start.30 = (f32[4,2,128,128]{3,2,1,0:T(8,128)S(1)}, f32[4,2,128,128]{3,2,1,0:T(8,128)S(1)}, u32[]{:S(2)}, u32[]{:S(2)}) collective-permute-start(f32[4,2,128,128]{3,2,1,0:T(8,128)S(1)} %bitcast_add_fusion.1), channel_id=1, source_target_pairs={{0,192},{8,200},{16,208},{24,216},{32,224},{40,232},{48,240},{56,2... | collective-permute-start | bytes 1572872 | tf_op jit(solution)/shard_map/ppermute | solution.py:116
  124.7 13.3 %collective-permute-start.23 = (f32[4,2,128,128]{3,2,1,0:T(8,128)S(1)}, f32[4,2,128,128]{3,2,1,0:T(8,128)S(1)}, u32[]{:S(2)}, u32[]{:S(2)}) collective-permute-start(f32[4,2,128,128]{3,2,1,0:T(8,128)S(1)} %bitcast_add_fusion.4), channel_id=1, source_target_pairs={{0,64},{8,72},{16,80},{24,88},{32,96},{40,104},{48,112},{56,120},{... | collective-permute-start | bytes 1572872 | tf_op jit(solution)/shard_map/ppermute | solution.py:116
  124.9 14.7 %collective-permute-start.16 = (f32[4,2,128,128]{3,2,1,0:T(8,128)S(1)}, f32[4,2,128,128]{3,2,1,0:T(8,128)S(1)}, u32[]{:S(2)}, u32[]{:S(2)}) collective-permute-start(f32[4,2,128,128]{3,2,1,0:T(8,128)S(1)} %bitcast_add_fusion.7), channel_id=1, source_target_pairs={{0,48},{8,56},{16,0},{24,8},{32,16},{40,24},{48,32},{56,40},{64,11... | collective-permute-start | bytes 1572872 | tf_op jit(solution)/shard_map/ppermute | solution.py:116
  128.7 14.4 %collective-permute-start.9 = (f32[4,2,128,128]{3,2,1,0:T(8,128)S(1)}, f32[4,2,128,128]{3,2,1,0:T(8,128)S(1)}, u32[]{:S(2)}, u32[]{:S(2)}) collective-permute-start(f32[4,2,128,128]{3,2,1,0:T(8,128)S(1)} %bitcast_add_fusion.10), channel_id=1, source_target_pairs={{0,16},{8,24},{16,32},{24,40},{32,48},{40,56},{48,0},{56,8},{64,80... | collective-permute-start | bytes 1572872 | tf_op jit(solution)/shard_map/ppermute | solution.py:116
  134.5 8.8 %collective-permute-start.31 = (f32[2,128,128]{2,1,0:T(8,128)S(1)}, f32[2,128,128]{2,1,0:T(8,128)S(1)}, u32[]{:S(2)}, u32[]{:S(2)}) collective-permute-start(f32[2,128,128]{2,1,0:T(8,128)S(1)} %dynamic-slice_bitcast_fusion.4), channel_id=1, source_target_pairs={{0,48},{8,56},{16,0},{24,8},{32,16},{40,24},{48,32},{56,40},{64,11... | collective-permute-start | bytes 393224 | tf_op jit(solution)/shard_map/ppermute | solution.py:116
  138.0 8.0 %collective-permute-start.24 = (f32[2,128,128]{2,1,0:T(8,128)S(1)}, f32[2,128,128]{2,1,0:T(8,128)S(1)}, u32[]{:S(2)}, u32[]{:S(2)}) collective-permute-start(f32[2,128,128]{2,1,0:T(8,128)S(1)} %dynamic-slice_bitcast_fusion.5), channel_id=1, source_target_pairs={{0,16},{8,24},{16,32},{24,40},{32,48},{40,56},{48,0},{56,8},{64,80... | collective-permute-start | bytes 393224 | tf_op jit(solution)/shard_map/ppermute | solution.py:116
  139.7 6.4 %collective-permute-start.17 = (f32[2,128,128]{2,1,0:T(8,128)S(1)}, f32[2,128,128]{2,1,0:T(8,128)S(1)}, u32[]{:S(2)}, u32[]{:S(2)}) collective-permute-start(f32[2,128,128]{2,1,0:T(8,128)S(1)} %dynamic-slice_bitcast_fusion.6), channel_id=1, source_target_pairs={{0,192},{8,200},{16,208},{24,216},{32,224},{40,232},{48,240},{56,2... | collective-permute-start | bytes 393224 | tf_op jit(solution)/shard_map/ppermute | solution.py:116
  143.1 6.6 %collective-permute-start.10 = (f32[2,128,128]{2,1,0:T(8,128)S(1)}, f32[2,128,128]{2,1,0:T(8,128)S(1)}, u32[]{:S(2)}, u32[]{:S(2)}) collective-permute-start(f32[2,128,128]{2,1,0:T(8,128)S(1)} %dynamic-slice_bitcast_fusion.7), channel_id=1, source_target_pairs={{0,64},{8,72},{16,80},{24,88},{32,96},{40,104},{48,112},{56,120},{... | collective-permute-start | bytes 393224 | tf_op jit(solution)/shard_map/ppermute | solution.py:116
  143.3 6.6 %collective-permute-start.32 = (f32[2,128,128]{2,1,0:T(8,128)S(1)}, f32[2,128,128]{2,1,0:T(8,128)S(1)}, u32[]{:S(2)}, u32[]{:S(2)}) collective-permute-start(f32[2,128,128]{2,1,0:T(8,128)S(1)} %bitcast_add_fusion.14), channel_id=1, source_target_pairs={{0,48},{8,56},{16,0},{24,8},{32,16},{40,24},{48,32},{56,40},{64,11... | collective-permute-start | bytes 393224 | tf_op jit(solution)/shard_map/ppermute | solution.py:116
  146.0 6.9 %collective-permute-start.25 = (f32[2,128,128]{2,1,0:T(8,128)S(1)}, f32[2,128,128]{2,1,0:T(8,128)S(1)}, u32[]{:S(2)}, u32[]{:S(2)}) collective-permute-start(f32[2,128,128]{2,1,0:T(8,128)S(1)} %bitcast_add_fusion.17), channel_id=1, source_target_pairs={{0,16},{8,24},{16,32},{24,40},{32,48},{40,56},{48,0},{56,8},{64,80... | collective-permute-start | bytes 393224 | tf_op jit(solution)/shard_map/ppermute | solution.py:116
  146.2 6.8 %collective-permute-start.18 = (f32[2,128,128]{2,1,0:T(8,128)S(1)}, f32[2,128,128]{2,1,0:T(8,128)S(1)}, u32[]{:S(2)}, u32[]{:S(2)}) collective-permute-start(f32[2,128,128]{2,1,0:T(8,128)S(1)} %bitcast_add_fusion.20), channel_id=1, source_target_pairs={{0,192},{8,200},{16,208},{24,216},{32,224},{40,232},{48,240},{56,2... | collective-permute-start | bytes 393224 | tf_op jit(solution)/shard_map/ppermute | solution.py:116
  149.8 7.5 %collective-permute-start.11 = (f32[2,128,128]{2,1,0:T(8,128)S(1)}, f32[2,128,128]{2,1,0:T(8,128)S(1)}, u32[]{:S(2)}, u32[]{:S(2)}) collective-permute-start(f32[2,128,128]{2,1,0:T(8,128)S(1)} %bitcast_add_fusion.23), channel_id=1, source_target_pairs={{0,64},{8,72},{16,80},{24,88},{32,96},{40,104},{48,112},{56,120},{... | collective-permute-start | bytes 393224 | tf_op jit(solution)/shard_map/ppermute | solution.py:116
  149.9 7.5 %collective-permute-start.33 = (f32[2,128,128]{2,1,0:T(8,128)S(1)}, f32[2,128,128]{2,1,0:T(8,128)S(1)}, u32[]{:S(2)}, u32[]{:S(2)}) collective-permute-start(f32[2,128,128]{2,1,0:T(8,128)S(1)} %bitcast_add_fusion.13), channel_id=1, source_target_pairs={{0,48},{8,56},{16,0},{24,8},{32,16},{40,24},{48,32},{56,40},{64,11... | collective-permute-start | bytes 393224 | tf_op jit(solution)/shard_map/ppermute | solution.py:116
  152.9 10.9 %collective-permute-start.26 = (f32[2,128,128]{2,1,0:T(8,128)S(1)}, f32[2,128,128]{2,1,0:T(8,128)S(1)}, u32[]{:S(2)}, u32[]{:S(2)}) collective-permute-start(f32[2,128,128]{2,1,0:T(8,128)S(1)} %bitcast_add_fusion.16), channel_id=1, source_target_pairs={{0,16},{8,24},{16,32},{24,40},{32,48},{40,56},{48,0},{56,8},{64,80... | collective-permute-start | bytes 393224 | tf_op jit(solution)/shard_map/ppermute | solution.py:116
  153.1 12.5 %collective-permute-start.19 = (f32[2,128,128]{2,1,0:T(8,128)S(1)}, f32[2,128,128]{2,1,0:T(8,128)S(1)}, u32[]{:S(2)}, u32[]{:S(2)}) collective-permute-start(f32[2,128,128]{2,1,0:T(8,128)S(1)} %bitcast_add_fusion.19), channel_id=1, source_target_pairs={{0,192},{8,200},{16,208},{24,216},{32,224},{40,232},{48,240},{56,2... | collective-permute-start | bytes 393224 | tf_op jit(solution)/shard_map/ppermute | solution.py:116
  157.3 12.7 %collective-permute-start.12 = (f32[2,128,128]{2,1,0:T(8,128)S(1)}, f32[2,128,128]{2,1,0:T(8,128)S(1)}, u32[]{:S(2)}, u32[]{:S(2)}) collective-permute-start(f32[2,128,128]{2,1,0:T(8,128)S(1)} %bitcast_add_fusion.22), channel_id=1, source_target_pairs={{0,64},{8,72},{16,80},{24,88},{32,96},{40,104},{48,112},{56,120},{... | collective-permute-start | bytes 393224 | tf_op jit(solution)/shard_map/ppermute | solution.py:116
  157.4 14.4 %collective-permute-start.34 = (f32[128,128]{1,0:T(8,128)S(1)}, f32[128,128]{1,0:T(8,128)S(1)}, u32[]{:S(2)}, u32[]{:S(2)}) collective-permute-start(f32[128,128]{1,0:T(8,128)S(1)} %dynamic-slice_bitcast_fusion.8), channel_id=1, source_target_pairs={{0,8},{8,0},{16,24},{24,16},{32,40},{40,32},{48,56},{56,48},{64,72... | collective-permute-start | bytes 196616 | tf_op jit(solution)/shard_map/ppermute | solution.py:125
  163.9 8.6 %collective-permute-start.27 = (f32[128,128]{1,0:T(8,128)S(1)}, f32[128,128]{1,0:T(8,128)S(1)}, u32[]{:S(2)}, u32[]{:S(2)}) collective-permute-start(f32[128,128]{1,0:T(8,128)S(1)} %dynamic-slice_bitcast_fusion.9), channel_id=1, source_target_pairs={{0,8},{8,0},{16,24},{24,16},{32,40},{40,32},{48,56},{56,48},{64,72... | collective-permute-start | bytes 196616 | tf_op jit(solution)/shard_map/ppermute | solution.py:125
  165.6 8.4 %collective-permute-start.20 = (f32[128,128]{1,0:T(8,128)S(1)}, f32[128,128]{1,0:T(8,128)S(1)}, u32[]{:S(2)}, u32[]{:S(2)}) collective-permute-start(f32[128,128]{1,0:T(8,128)S(1)} %dynamic-slice_bitcast_fusion.10), channel_id=1, source_target_pairs={{0,8},{8,0},{16,24},{24,16},{32,40},{40,32},{48,56},{56,48},{64,72... | collective-permute-start | bytes 196616 | tf_op jit(solution)/shard_map/ppermute | solution.py:125
  170.1 8.3 %collective-permute-start.13 = (f32[128,128]{1,0:T(8,128)S(1)}, f32[128,128]{1,0:T(8,128)S(1)}, u32[]{:S(2)}, u32[]{:S(2)}) collective-permute-start(f32[128,128]{1,0:T(8,128)S(1)} %dynamic-slice_bitcast_fusion.11), channel_id=1, source_target_pairs={{0,8},{8,0},{16,24},{24,16},{32,40},{40,32},{48,56},{56,48},{64,72... | collective-permute-start | bytes 196616 | tf_op jit(solution)/shard_map/ppermute | solution.py:125

commit v7 on v6

--- a/solution.py
+++ b/solution.py
@@ -9,10 +9,11 @@
 OWNERS_PER_STEP = 4
 
 
-def _products_kernel(left_ref, right_ref, target_ref, x_ref, out_ref):
+def _products_kernel(left_ref, right_ref, target_ref, x_ref, *refs):
+    out_refs, acc_ref = refs[:CS], refs[CS]
     step = pl.program_id(0)
     pair_count = left_ref.shape[0] // (pl.num_programs(0) * OWNERS_PER_STEP)
-    out_ref[...] = jnp.zeros_like(out_ref)
+    acc_ref[...] = jnp.zeros_like(acc_ref)
 
     def body(j, carry):
         k = j // pair_count
@@ -23,10 +24,12 @@
         prod = lax.dot_general(
             x_ref[l], x_ref[r], (((0,), (0,)), ((), ())), preferred_element_type=jnp.float32
         )
-        out_ref[t, k] += prod
+        acc_ref[t, k] += prod
         return carry
 
     lax.fori_loop(0, OWNERS_PER_STEP * pair_count, body, 0, unroll=4)
+    for c, out_ref in enumerate(out_refs):
+        out_ref[...] = acc_ref[c]
 
 
 def owner_partials(gathered, left, right, target):
@@ -36,7 +39,7 @@
     flops = 2 * owners * pair_count * block * block * block
     return pl.pallas_call(
         _products_kernel,
-        out_shape=jax.ShapeDtypeStruct((CS, owners, block, block), jnp.float32),
+        out_shape=[jax.ShapeDtypeStruct((owners, block, block), jnp.float32)] * CS,
         grid_spec=pltpu.PrefetchScalarGridSpec(
             num_scalar_prefetch=3,
             grid=(steps,),
@@ -47,9 +50,11 @@
                     pipeline_mode=pl.Buffered(1),
                 )
             ],
-            out_specs=pl.BlockSpec(
-                (CS, OWNERS_PER_STEP, block, block), lambda i, *_: (0, i, 0, 0)
-            ),
+            out_specs=[
+                pl.BlockSpec((OWNERS_PER_STEP, block, block), lambda i, *_: (i, 0, 0))
+            ]
+            * CS,
+            scratch_shapes=[pltpu.VMEM((CS, OWNERS_PER_STEP, block, block), jnp.float32)],
         ),
         compiler_params=pltpu.CompilerParams(
             dimension_semantics=("arbitrary",), vmem_limit_bytes=48 * 1024 * 1024
@@ -118,10 +123,10 @@
     return send
 
 
-def pair_reduce_scatter(data, dim, coord):
-    route = _shift_route(dim, 1)
-    other = lax.dynamic_index_in_dim(data, 1 - coord, 0, keepdims=False)
-    mine = lax.dynamic_index_in_dim(data, coord, 0, keepdims=False)
+def pair_reduce_scatter(data, axis, coord):
+    route = _shift_route(2, 1)
+    other = lax.dynamic_index_in_dim(data, 1 - coord, axis, keepdims=False)
+    mine = lax.dynamic_index_in_dim(data, coord, axis, keepdims=False)
     return lax.ppermute(other, "blk", route) + mine
 
 
@@ -176,10 +181,9 @@
     partials = owner_partials(gathered, left, right, target)
     block = x_blocks.shape[1]
     my_y, my_x, my_z = _blk_coords(me)
-    partials = partials.reshape((CS,) + BLK_DIMS + (block, block))
     results = []
     for c in range(CS):
-        data = partials[c]
+        data = partials[c].reshape(BLK_DIMS + (block, block))
         direction = 1 if c % 2 == 0 else -1
         if c < 2:
             data = ring_reduce_scatter(data, 1, 1, direction, my_x)
@@ -187,8 +191,8 @@
         else:
             data = ring_reduce_scatter(data, 0, 0, direction, my_y)
             data = ring_reduce_scatter(data, 0, 1, direction, my_x)
-        results.append(pair_reduce_scatter(data, 2, my_z))
-    summed = jnp.stack(results)
+        results.append(data)
+    summed = pair_reduce_scatter(jnp.stack(results), 1, my_z)
     return summed.astype(jnp.bfloat16).reshape(1, 1, CS, block, block)
 
 

time: 181 us -> 176 us (0.972)
  waiting for transfers between devices: 56.8 us -> 65.1 us
  starting transfers between devices: 72.6 us -> 64.4 us
  local copies, waits for them, and re-layouts: 15.4 us -> 11.1 us
  Pallas kernels: 23.9 us -> 26.4 us
  other arithmetic: 9.68 us -> 7.21 us
    ppermute x4 -> x1, starting transfers between devices: 14.2 us -> 6.37 us  [pair_reduce_scatter(): return lax.ppermute(other, 'blk', route) + mine]
    ppermute x24, waiting for transfers between devices: 20.6 us -> 27.2 us  [ring_reduce_scatter(): arrived = lax.ppermute(send, 'blk', route)]
    slice x1 -> x0, local copies, waits for them, and re-layouts: 6.5 us -> none  [per_device(): data = partials[c]]
    pallas_call x1, Pallas kernels: 23.9 us -> 26.4 us  [owner_partials(): pl.pallas_call(_products_kernel, out_shape=[jax.ShapeDtypeStruct((owners,...]
    another operation x1, local copies, waits for them, and re-layouts: 0.31 us -> 2.29 us  [line_all_gather(): gathered = jnp.stack([first, second], axis=1)]
    ppermute x4 -> x1, waiting for transfers between devices: 6.49 us -> 6.73 us  [pair_reduce_scatter(): return lax.ppermute(other, 'blk', route) + mine]
  transfers between devices with their start and end apart: 35 -> 32, of which waited for: 16 -> 17; matrix products, arithmetic and copies ran while one was open for 5% -> 4% of each run, Pallas kernels for 0% -> 0%
where the time goes in v7:
time: 176 us; the launch traced here: 175 us
  waiting for transfers between devices  65.1 us (37%)
  starting transfers between devices  64.4 us (37%)
  Pallas kernels  26.4 us (15%)
  local copies, waits for them, and re-layouts  11.1 us (6%)
  other arithmetic  7.21 us (4%)
    ppermute x24, starting transfers between devices, ring_reduce_scatter(): arrived = lax.ppermute(send, 'blk', route)  40.6 us
    ppermute x3, waiting for transfers between devices, line_all_gather(): send_down = lax.ppermute(send_down, 'grp', down)  27.2 us
    ppermute x24, waiting for transfers between devices, ring_reduce_scatter(): arrived = lax.ppermute(send, 'blk', route)  27.2 us
    pallas_call x1, Pallas kernels, owner_partials(): pl.pallas_call(_products_kernel, out_shape=[jax.ShapeDtypeStruct((owners,...  26.4 us
    ppermute x3, starting transfers between devices, line_all_gather(): send_up = lax.ppermute(send_up, 'grp', up)  9.59 us
    ppermute x3, starting transfers between devices, line_all_gather(): send_down = lax.ppermute(send_down, 'grp', down)  7.91 us
    ppermute x1, waiting for transfers between devices, pair_reduce_scatter(): return lax.ppermute(other, 'blk', route) + mine  6.73 us
    ppermute x1, starting transfers between devices, pair_reduce_scatter(): return lax.ppermute(other, 'blk', route) + mine  6.37 us
  transfers between devices with their start and end apart: 32, of which 17 were waited for; matrix products, arithmetic and copies ran while one was open for 4% of the time, Pallas kernels for 0%

profile of v7, /device:TPU:32, one launch (start us, length us, event | category | flops | bytes accessed | tf_op | source)
XLA Modules:
  0.0 174.9 jit_solution(9439812850156245177)
XLA Ops:
  0.0 3.7 %collective-permute-start.3 = (bf16[16,128,128]{2,1,0:T(8,128)(2,1)}, bf16[16,128,128]{2,1,0:T(8,128)(2,1)S(1)}, u32[]{:S(2)}, u32[]{:S(2)}) collective-permute-start(bf16[16,128,128]{2,1,0:T(8,128)(2,1)} %param.6), channel_id=1, source_target_pairs={{2,0},{3,1},{4,2},{5,3},{6,4},{7,5},{10,8},{11,9},{12,10},{13,11},... | collective-permute-start | bytes 1572872 | tf_op jit(solution)/shard_map/ppermute | solution.py:146
  3.7 2.1 %collective-permute-start = (bf16[16,128,128]{2,1,0:T(8,128)(2,1)}, bf16[16,128,128]{2,1,0:T(8,128)(2,1)S(1)}, u32[]{:S(2)}, u32[]{:S(2)}) collective-permute-start(bf16[16,128,128]{2,1,0:T(8,128)(2,1)} %param.6), channel_id=1, source_target_pairs={{0,2},{1,3},{2,4},{3,5},{4,6},{5,7},{8,10},{9,11},{10,12},{11,13},... | collective-permute-start | bytes 1572872 | tf_op jit(solution)/shard_map/ppermute | solution.py:145
  5.9 10.1 %collective-permute-done.3 = bf16[16,128,128]{2,1,0:T(8,128)(2,1)S(1)} collective-permute-done((bf16[16,128,128]{2,1,0:T(8,128)(2,1)}, bf16[16,128,128]{2,1,0:T(8,128)(2,1)S(1)}, u32[]{:S(2)}, u32[]{:S(2)}) %collective-permute-start.3) | collective-permute-done | bytes 524320 | tf_op jit(solution)/shard_map/ppermute | solution.py:146
  15.9 2.0 %collective-permute-start.4 = (bf16[16,128,128]{2,1,0:T(8,128)(2,1)S(1)}, bf16[16,128,128]{2,1,0:T(8,128)(2,1)S(1)}, u32[]{:S(2)}, u32[]{:S(2)}) collective-permute-start(bf16[16,128,128]{2,1,0:T(8,128)(2,1)S(1)} %collective-permute-done.3), channel_id=1, source_target_pairs={{2,0},{3,1},{4,2},{5,3},{6,4},{7,5},{10,8},{11,9},{12,10},{13,11},... | collective-permute-start | bytes 1572872 | tf_op jit(solution)/shard_map/ppermute | solution.py:146
  18.0 3.8 %collective-permute-start.1 = (bf16[16,128,128]{2,1,0:T(8,128)(2,1)S(1)}, bf16[16,128,128]{2,1,0:T(8,128)(2,1)S(1)}, u32[]{:S(2)}, u32[]{:S(2)}) collective-permute-start(bf16[16,128,128]{2,1,0:T(8,128)(2,1)S(1)} %collective-permute-done), channel_id=1, source_target_pairs={{0,2},{1,3},{2,4},{3,5},{4,6},{5,7},{8,10},{9,11},{10,12},{11,13},... | collective-permute-start | bytes 1572872 | tf_op jit(solution)/shard_map/ppermute | solution.py:145
  21.8 9.0 %collective-permute-done.4 = bf16[16,128,128]{2,1,0:T(8,128)(2,1)S(1)} collective-permute-done((bf16[16,128,128]{2,1,0:T(8,128)(2,1)S(1)}, bf16[16,128,128]{2,1,0:T(8,128)(2,1)S(1)}, u32[]{:S(2)}, u32[]{:S(2)}) %collective-permute-start.4) | collective-permute-done | bytes 524320 | tf_op jit(solution)/shard_map/ppermute | solution.py:146
  30.8 2.2 %collective-permute-start.5 = (bf16[16,128,128]{2,1,0:T(8,128)(2,1)S(1)}, bf16[16,128,128]{2,1,0:T(8,128)(2,1)S(1)}, u32[]{:S(2)}, u32[]{:S(2)}) collective-permute-start(bf16[16,128,128]{2,1,0:T(8,128)(2,1)S(1)} %collective-permute-done.4), channel_id=1, source_target_pairs={{2,0},{3,1},{4,2},{5,3},{6,4},{7,5},{10,8},{11,9},{12,10},{13,11},... | collective-permute-start | bytes 1572872 | tf_op jit(solution)/shard_map/ppermute | solution.py:146
  33.0 3.6 %collective-permute-start.2 = (bf16[16,128,128]{2,1,0:T(8,128)(2,1)S(1)}, bf16[16,128,128]{2,1,0:T(8,128)(2,1)S(1)}, u32[]{:S(2)}, u32[]{:S(2)}) collective-permute-start(bf16[16,128,128]{2,1,0:T(8,128)(2,1)S(1)} %collective-permute-done.1), channel_id=1, source_target_pairs={{0,2},{1,3},{2,4},{3,5},{4,6},{5,7},{8,10},{9,11},{10,12},{11,13},... | collective-permute-start | bytes 1572872 | tf_op jit(solution)/shard_map/ppermute | solution.py:145
  36.7 8.1 %collective-permute-done.5 = bf16[16,128,128]{2,1,0:T(8,128)(2,1)S(1)} collective-permute-done((bf16[16,128,128]{2,1,0:T(8,128)(2,1)S(1)}, bf16[16,128,128]{2,1,0:T(8,128)(2,1)S(1)}, u32[]{:S(2)}, u32[]{:S(2)}) %collective-permute-start.5) | collective-permute-done | bytes 524320 | tf_op jit(solution)/shard_map/ppermute | solution.py:146
  45.0 1.9 %collective-permute-done.2 = bf16[16,128,128]{2,1,0:T(8,128)(2,1)S(1)} collective-permute-done((bf16[16,128,128]{2,1,0:T(8,128)(2,1)S(1)}, bf16[16,128,128]{2,1,0:T(8,128)(2,1)S(1)}, u32[]{:S(2)}, u32[]{:S(2)}) %collective-permute-start.2) | collective-permute-done | bytes 524320 | tf_op jit(solution)/shard_map/ppermute | solution.py:145
  47.4 1.6 pad_maximum_fusion.1
  49.3 0.6 gather_fusion.2
  49.8 0.6 gather_fusion.1
  50.5 0.6 gather_fusion
  51.5 2.0 %collective-permute-done.6 = bf16[4,16,128,128]{3,2,1,0:T(8,128)(2,1)} collective-permute-done((bf16[4,16,128,128]{3,2,1,0:T(8,128)(2,1)}, bf16[4,16,128,128]{3,2,1,0:T(8,128)(2,1)}, u32[]{:S(2)}, u32[]{:S(2)}) %collective-permute-start.6) | collective-permute-done | bytes 2097184 | tf_op jit(solution)/shard_map/ppermute | solution.py:164
  53.6 1.8 %select_bitcast_fusion.1 = (bf16[4,1,16,128,128]{4,3,2,0,1:T(8,128)(2,1)S(1)}, bf16[4,1,16,128,128]{4,3,2,0,1:T(8,128)(2,1)S(1)}) fusion(bf16[4,16,128,128]{3,2,1,0:T(8,128)(2,1)} %collective-permute-done.6, pred[]{:T(512)S(6)} %eq.55, bf16[1,16,128,128]{3,2,1,0:T(8,128)(2,1)S(1)} %get-tuple-element.18, bf16[1,16,128,128]{3,2,1,0:T(8,128)(2,1)S(1)} %get-tuple-element.19, ...), kind=kLoop, calls=%fused_computation.6 | loop fusion | flops 5242880 | bytes 8388609 | tf_op jit(solution)/shard_map/stack | solution.py:167
  55.7 2.3 %copy.12 = bf16[4,2,16,128,128]{4,3,2,1,0:T(8,128)(2,1)} copy(bf16[4,2,16,128,128]{4,3,2,0,1:T(8,128)(2,1)S(1)} %pad_maximum_fusion) | data formatting | bytes 8388608 | tf_op jit(solution)/shard_map/stack | solution.py:167
  58.0 26.4 %shard_map.46 = (f32[32,128,128]{2,1,0:T(8,128)S(1)}, f32[32,128,128]{2,1,0:T(8,128)S(1)}, f32[32,128,128]{2,1,0:T(8,128)}, f32[32,128,128]{2,1,0:T(8,128)}) custom-call(s32[384]{0:T(512)S(1)} %reshape.136.left_ref, s32[384]{0:T(512)S(1)} %reshape.137.right_ref, s32[384]{0:T(512)S(1)} %reshape.138.target_ref, bf16[128,128,128]{2,1,0:T(8,128)(2,1)} %bitcast.140), custom_call_target="tpu_custom_call" | custom-call | flops 1610612736 | bytes 12582912 | tf_op jit(solution)/shard_map/pallas_call | solution.py:40
  84.4 1.4 copy-done
  85.8 1.9 %dynamic-slice_bitcast_fusion = f32[4,2,128,128]{3,2,1,0:T(8,128)} fusion(f32[4,4,2,128,128]{4,3,2,1,0:T(8,128)} %bitcast.145, s32[]{:T(128)S(6)} %select_n.347), kind=kLoop, calls=%fused_computation.30 | loop fusion | bytes 1048580 | tf_op jit(solution)/shard_map/reshape | solution.py:107
  87.7 3.0 %collective-permute-start.25 = (f32[4,2,128,128]{3,2,1,0:T(8,128)}, f32[4,2,128,128]{3,2,1,0:T(8,128)S(1)}, u32[]{:S(2)}, u32[]{:S(2)}) collective-permute-start(f32[4,2,128,128]{3,2,1,0:T(8,128)} %dynamic-slice_bitcast_fusion), channel_id=1, source_target_pairs={{0,192},{8,200},{16,208},{24,216},{32,224},{40,232},{48,240},{56,2... | collective-permute-start | bytes 1572872 | tf_op jit(solution)/shard_map/ppermute | solution.py:121
  90.7 1.9 %dynamic-slice_bitcast_fusion.1 = f32[4,2,128,128]{3,2,1,0:T(8,128)} fusion(f32[4,4,2,128,128]{4,3,2,1,0:T(8,128)} %bitcast.141, s32[]{:T(128)S(6)} %select_n.331), kind=kLoop, calls=%fused_computation.31 | loop fusion | bytes 1048580 | tf_op jit(solution)/shard_map/reshape | solution.py:107
  92.6 1.2 dynamic-slice_bitcast_fusion.2
  93.8 2.8 %collective-permute-start.13 = (f32[4,2,128,128]{3,2,1,0:T(8,128)S(1)}, f32[4,2,128,128]{3,2,1,0:T(8,128)S(1)}, u32[]{:S(2)}, u32[]{:S(2)}) collective-permute-start(f32[4,2,128,128]{3,2,1,0:T(8,128)S(1)} %dynamic-slice_bitcast_fusion.2), channel_id=1, source_target_pairs={{0,48},{8,56},{16,0},{24,8},{32,16},{40,24},{48,32},{56,40},{64,11... | collective-permute-start | bytes 1572872 | tf_op jit(solution)/shard_map/ppermute | solution.py:121
  96.8 5.7 %collective-permute-done.25 = f32[4,2,128,128]{3,2,1,0:T(8,128)S(1)} collective-permute-done((f32[4,2,128,128]{3,2,1,0:T(8,128)}, f32[4,2,128,128]{3,2,1,0:T(8,128)S(1)}, u32[]{:S(2)}, u32[]{:S(2)}) %collective-permute-start.25) | collective-permute-done | bytes 524320 | tf_op jit(solution)/shard_map/ppermute | solution.py:121
  102.5 1.1 bitcast_add_fusion.2
  103.6 3.7 %collective-permute-start.26 = (f32[4,2,128,128]{3,2,1,0:T(8,128)S(1)}, f32[4,2,128,128]{3,2,1,0:T(8,128)S(1)}, u32[]{:S(2)}, u32[]{:S(2)}) collective-permute-start(f32[4,2,128,128]{3,2,1,0:T(8,128)S(1)} %bitcast_add_fusion.2), channel_id=1, source_target_pairs={{0,192},{8,200},{16,208},{24,216},{32,224},{40,232},{48,240},{56,2... | collective-permute-start | bytes 1572872 | tf_op jit(solution)/shard_map/ppermute | solution.py:121
  108.0 3.7 %collective-permute-start.14 = (f32[4,2,128,128]{3,2,1,0:T(8,128)S(1)}, f32[4,2,128,128]{3,2,1,0:T(8,128)S(1)}, u32[]{:S(2)}, u32[]{:S(2)}) collective-permute-start(f32[4,2,128,128]{3,2,1,0:T(8,128)S(1)} %bitcast_add_fusion.8), channel_id=1, source_target_pairs={{0,48},{8,56},{16,0},{24,8},{32,16},{40,24},{48,32},{56,40},{64,11... | collective-permute-start | bytes 1572872 | tf_op jit(solution)/shard_map/ppermute | solution.py:121
  111.9 6.0 %collective-permute-done.26 = f32[4,2,128,128]{3,2,1,0:T(8,128)S(1)} collective-permute-done((f32[4,2,128,128]{3,2,1,0:T(8,128)S(1)}, f32[4,2,128,128]{3,2,1,0:T(8,128)S(1)}, u32[]{:S(2)}, u32[]{:S(2)}) %collective-permute-start.26) | collective-permute-done | bytes 524320 | tf_op jit(solution)/shard_map/ppermute | solution.py:121
  118.0 3.8 %collective-permute-start.27 = (f32[4,2,128,128]{3,2,1,0:T(8,128)S(1)}, f32[4,2,128,128]{3,2,1,0:T(8,128)S(1)}, u32[]{:S(2)}, u32[]{:S(2)}) collective-permute-start(f32[4,2,128,128]{3,2,1,0:T(8,128)S(1)} %bitcast_add_fusion.1), channel_id=1, source_target_pairs={{0,192},{8,200},{16,208},{24,216},{32,224},{40,232},{48,240},{56,2... | collective-permute-start | bytes 1572872 | tf_op jit(solution)/shard_map/ppermute | solution.py:121
  122.3 3.6 %collective-permute-start.15 = (f32[4,2,128,128]{3,2,1,0:T(8,128)S(1)}, f32[4,2,128,128]{3,2,1,0:T(8,128)S(1)}, u32[]{:S(2)}, u32[]{:S(2)}) collective-permute-start(f32[4,2,128,128]{3,2,1,0:T(8,128)S(1)} %bitcast_add_fusion.7), channel_id=1, source_target_pairs={{0,48},{8,56},{16,0},{24,8},{32,16},{40,24},{48,32},{56,40},{64,11... | collective-permute-start | bytes 1572872 | tf_op jit(solution)/shard_map/ppermute | solution.py:121
  126.0 5.5 %collective-permute-done.27 = f32[4,2,128,128]{3,2,1,0:T(8,128)S(1)} collective-permute-done((f32[4,2,128,128]{3,2,1,0:T(8,128)S(1)}, f32[4,2,128,128]{3,2,1,0:T(8,128)S(1)}, u32[]{:S(2)}, u32[]{:S(2)}) %collective-permute-start.27) | collective-permute-done | bytes 524320 | tf_op jit(solution)/shard_map/ppermute | solution.py:121
  131.6 2.8 %collective-permute-start.28 = (f32[2,128,128]{2,1,0:T(8,128)S(1)}, f32[2,128,128]{2,1,0:T(8,128)S(1)}, u32[]{:S(2)}, u32[]{:S(2)}) collective-permute-start(f32[2,128,128]{2,1,0:T(8,128)S(1)} %dynamic-slice_bitcast_fusion.5), channel_id=1, source_target_pairs={{0,48},{8,56},{16,0},{24,8},{32,16},{40,24},{48,32},{56,40},{64,11... | collective-permute-start | bytes 393224 | tf_op jit(solution)/shard_map/ppermute | solution.py:121
  134.4 1.0 collective-permute-done.21
  135.5 1.6 collective-permute-start.22
  137.1 2.2 %collective-permute-start.16 = (f32[2,128,128]{2,1,0:T(8,128)S(1)}, f32[2,128,128]{2,1,0:T(8,128)S(1)}, u32[]{:S(2)}, u32[]{:S(2)}) collective-permute-start(f32[2,128,128]{2,1,0:T(8,128)S(1)} %dynamic-slice_bitcast_fusion.7), channel_id=1, source_target_pairs={{0,192},{8,200},{16,208},{24,216},{32,224},{40,232},{48,240},{56,2... | collective-permute-start | bytes 393224 | tf_op jit(solution)/shard_map/ppermute | solution.py:121
  139.3 1.0 collective-permute-done.9
  140.6 2.8 %collective-permute-start.29 = (f32[2,128,128]{2,1,0:T(8,128)S(1)}, f32[2,128,128]{2,1,0:T(8,128)S(1)}, u32[]{:S(2)}, u32[]{:S(2)}) collective-permute-start(f32[2,128,128]{2,1,0:T(8,128)S(1)} %bitcast_add_fusion.15), channel_id=1, source_target_pairs={{0,48},{8,56},{16,0},{24,8},{32,16},{40,24},{48,32},{56,40},{64,11... | collective-permute-start | bytes 393224 | tf_op jit(solution)/shard_map/ppermute | solution.py:121
  143.5 3.3 %collective-permute-start.17 = (f32[2,128,128]{2,1,0:T(8,128)S(1)}, f32[2,128,128]{2,1,0:T(8,128)S(1)}, u32[]{:S(2)}, u32[]{:S(2)}) collective-permute-start(f32[2,128,128]{2,1,0:T(8,128)S(1)} %bitcast_add_fusion.21), channel_id=1, source_target_pairs={{0,192},{8,200},{16,208},{24,216},{32,224},{40,232},{48,240},{56,2... | collective-permute-start | bytes 393224 | tf_op jit(solution)/shard_map/ppermute | solution.py:121
  146.8 0.5 collective-permute-done.10
  147.4 2.8 %collective-permute-start.30 = (f32[2,128,128]{2,1,0:T(8,128)S(1)}, f32[2,128,128]{2,1,0:T(8,128)S(1)}, u32[]{:S(2)}, u32[]{:S(2)}) collective-permute-start(f32[2,128,128]{2,1,0:T(8,128)S(1)} %bitcast_add_fusion.14), channel_id=1, source_target_pairs={{0,48},{8,56},{16,0},{24,8},{32,16},{40,24},{48,32},{56,40},{64,11... | collective-permute-start | bytes 393224 | tf_op jit(solution)/shard_map/ppermute | solution.py:121
  150.4 3.6 %collective-permute-start.18 = (f32[2,128,128]{2,1,0:T(8,128)S(1)}, f32[2,128,128]{2,1,0:T(8,128)S(1)}, u32[]{:S(2)}, u32[]{:S(2)}) collective-permute-start(f32[2,128,128]{2,1,0:T(8,128)S(1)} %bitcast_add_fusion.20), channel_id=1, source_target_pairs={{0,192},{8,200},{16,208},{24,216},{32,224},{40,232},{48,240},{56,2... | collective-permute-start | bytes 393224 | tf_op jit(solution)/shard_map/ppermute | solution.py:121
  153.9 0.8 collective-permute-done.11
  154.8 1.6 collective-permute-done.24
  156.5 4.4 %collective-permute-done.12 = f32[2,128,128]{2,1,0:T(8,128)S(1)} collective-permute-done((f32[2,128,128]{2,1,0:T(8,128)S(1)}, f32[2,128,128]{2,1,0:T(8,128)S(1)}, u32[]{:S(2)}, u32[]{:S(2)}) %collective-permute-start.12) | collective-permute-done | bytes 131104 | tf_op jit(solution)/shard_map/ppermute | solution.py:121
  161.1 6.4 %collective-permute-start.31 = (f32[4,128,128]{2,1,0:T(8,128)S(1)}, f32[4,128,128]{2,1,0:T(8,128)S(1)}, u32[]{:S(2)}, u32[]{:S(2)}) collective-permute-start(f32[4,128,128]{2,1,0:T(8,128)S(1)} %dynamic-slice_bitcast_fusion.4), channel_id=1, source_target_pairs={{0,8},{8,0},{16,24},{24,16},{32,40},{40,32},{48,56},{56,48},{64,72... | collective-permute-start | bytes 786440 | tf_op jit(solution)/shard_map/ppermute | solution.py:130
  167.4 6.7 %collective-permute-done.31 = f32[4,128,128]{2,1,0:T(8,128)S(1)} collective-permute-done((f32[4,128,128]{2,1,0:T(8,128)S(1)}, f32[4,128,128]{2,1,0:T(8,128)S(1)}, u32[]{:S(2)}, u32[]{:S(2)}) %collective-permute-start.31) | collective-permute-done | bytes 262176 | tf_op jit(solution)/shard_map/ppermute | solution.py:130
  174.2 0.7 fusion.5
  (88 shorter events, 4.5 us)
Async XLA Ops:
  0.0 15.9 %collective-permute-start.3 = (bf16[16,128,128]{2,1,0:T(8,128)(2,1)}, bf16[16,128,128]{2,1,0:T(8,128)(2,1)S(1)}, u32[]{:S(2)}, u32[]{:S(2)}) collective-permute-start(bf16[16,128,128]{2,1,0:T(8,128)(2,1)} %param.6), channel_id=1, source_target_pairs={{2,0},{3,1},{4,2},{5,3},{6,4},{7,5},{10,8},{11,9},{12,10},{13,11},... | collective-permute-start | bytes 1572872 | tf_op jit(solution)/shard_map/ppermute | solution.py:146
  3.7 14.2 %collective-permute-start = (bf16[16,128,128]{2,1,0:T(8,128)(2,1)}, bf16[16,128,128]{2,1,0:T(8,128)(2,1)S(1)}, u32[]{:S(2)}, u32[]{:S(2)}) collective-permute-start(bf16[16,128,128]{2,1,0:T(8,128)(2,1)} %param.6), channel_id=1, source_target_pairs={{0,2},{1,3},{2,4},{3,5},{4,6},{5,7},{8,10},{9,11},{10,12},{11,13},... | collective-permute-start | bytes 1572872 | tf_op jit(solution)/shard_map/ppermute | solution.py:145
  15.9 14.9 %collective-permute-start.4 = (bf16[16,128,128]{2,1,0:T(8,128)(2,1)S(1)}, bf16[16,128,128]{2,1,0:T(8,128)(2,1)S(1)}, u32[]{:S(2)}, u32[]{:S(2)}) collective-permute-start(bf16[16,128,128]{2,1,0:T(8,128)(2,1)S(1)} %collective-permute-done.3), channel_id=1, source_target_pairs={{2,0},{3,1},{4,2},{5,3},{6,4},{7,5},{10,8},{11,9},{12,10},{13,11},... | collective-permute-start | bytes 1572872 | tf_op jit(solution)/shard_map/ppermute | solution.py:146
  18.0 15.0 %collective-permute-start.1 = (bf16[16,128,128]{2,1,0:T(8,128)(2,1)S(1)}, bf16[16,128,128]{2,1,0:T(8,128)(2,1)S(1)}, u32[]{:S(2)}, u32[]{:S(2)}) collective-permute-start(bf16[16,128,128]{2,1,0:T(8,128)(2,1)S(1)} %collective-permute-done), channel_id=1, source_target_pairs={{0,2},{1,3},{2,4},{3,5},{4,6},{5,7},{8,10},{9,11},{10,12},{11,13},... | collective-permute-start | bytes 1572872 | tf_op jit(solution)/shard_map/ppermute | solution.py:145
  30.8 14.0 %collective-permute-start.5 = (bf16[16,128,128]{2,1,0:T(8,128)(2,1)S(1)}, bf16[16,128,128]{2,1,0:T(8,128)(2,1)S(1)}, u32[]{:S(2)}, u32[]{:S(2)}) collective-permute-start(bf16[16,128,128]{2,1,0:T(8,128)(2,1)S(1)} %collective-permute-done.4), channel_id=1, source_target_pairs={{2,0},{3,1},{4,2},{5,3},{6,4},{7,5},{10,8},{11,9},{12,10},{13,11},... | collective-permute-start | bytes 1572872 | tf_op jit(solution)/shard_map/ppermute | solution.py:146
  33.0 13.9 %collective-permute-start.2 = (bf16[16,128,128]{2,1,0:T(8,128)(2,1)S(1)}, bf16[16,128,128]{2,1,0:T(8,128)(2,1)S(1)}, u32[]{:S(2)}, u32[]{:S(2)}) collective-permute-start(bf16[16,128,128]{2,1,0:T(8,128)(2,1)S(1)} %collective-permute-done.1), channel_id=1, source_target_pairs={{0,2},{1,3},{2,4},{3,5},{4,6},{5,7},{8,10},{9,11},{10,12},{11,13},... | collective-permute-start | bytes 1572872 | tf_op jit(solution)/shard_map/ppermute | solution.py:145
  45.0 2.1 %copy-start.4 = (bf16[16,128,128]{2,1,0:T(8,128)(2,1)S(1)}, bf16[16,128,128]{2,1,0:T(8,128)(2,1)}, u32[]{:S(2)}) copy-start(bf16[16,128,128]{2,1,0:T(8,128)(2,1)} %param.6) | copy-start | bytes 1572868
  47.4 1.7 copy-start.5
  47.4 1.7 copy-start.6
  47.4 3.0 %copy-start.7 = (s32[1,1,32,12]{2,1,3,0:T(1,128)S(1)}, s32[1,1,32,12]{2,1,3,0:T(1,128)}, u32[]{:S(2)}) copy-start(s32[1,1,32,12]{2,1,3,0:T(1,128)} %param.7) | copy-start | bytes 4612
  49.1 4.5 %collective-permute-start.6 = (bf16[4,16,128,128]{3,2,1,0:T(8,128)(2,1)}, bf16[4,16,128,128]{3,2,1,0:T(8,128)(2,1)}, u32[]{:S(2)}, u32[]{:S(2)}) collective-permute-start(bf16[4,16,128,128]{3,2,1,0:T(8,128)(2,1)} %pad_maximum_fusion.1), channel_id=1, source_target_pairs={{0,1},{1,0},{2,3},{3,2},{4,5},{5,4},{6,7},{7,6},{8,9},{9,8},{10,11... | collective-permute-start | bytes 6291464 | tf_op jit(solution)/shard_map/ppermute | solution.py:164
  84.4 1.4 copy-start
  87.7 14.8 %collective-permute-start.25 = (f32[4,2,128,128]{3,2,1,0:T(8,128)}, f32[4,2,128,128]{3,2,1,0:T(8,128)S(1)}, u32[]{:S(2)}, u32[]{:S(2)}) collective-permute-start(f32[4,2,128,128]{3,2,1,0:T(8,128)} %dynamic-slice_bitcast_fusion), channel_id=1, source_target_pairs={{0,192},{8,200},{16,208},{24,216},{32,224},{40,232},{48,240},{56,2... | collective-permute-start | bytes 1572872 | tf_op jit(solution)/shard_map/ppermute | solution.py:121
  92.6 15.1 %collective-permute-start.19 = (f32[4,2,128,128]{3,2,1,0:T(8,128)}, f32[4,2,128,128]{3,2,1,0:T(8,128)S(1)}, u32[]{:S(2)}, u32[]{:S(2)}) collective-permute-start(f32[4,2,128,128]{3,2,1,0:T(8,128)} %dynamic-slice_bitcast_fusion.1), channel_id=1, source_target_pairs={{0,64},{8,72},{16,80},{24,88},{32,96},{40,104},{48,112},{56,120},{... | collective-permute-start | bytes 1572872 | tf_op jit(solution)/shard_map/ppermute | solution.py:121
  92.6 15.1 %copy-start.2 = (f32[32,128,128]{2,1,0:T(8,128)S(1)}, f32[32,128,128]{2,1,0:T(8,128)}, u32[]{:S(2)}) copy-start(f32[32,128,128]{2,1,0:T(8,128)} %get-tuple-element.12) | copy-start | bytes 6291460
  93.8 14.0 %collective-permute-start.13 = (f32[4,2,128,128]{3,2,1,0:T(8,128)S(1)}, f32[4,2,128,128]{3,2,1,0:T(8,128)S(1)}, u32[]{:S(2)}, u32[]{:S(2)}) collective-permute-start(f32[4,2,128,128]{3,2,1,0:T(8,128)S(1)} %dynamic-slice_bitcast_fusion.2), channel_id=1, source_target_pairs={{0,48},{8,56},{16,0},{24,8},{32,16},{40,24},{48,32},{56,40},{64,11... | collective-permute-start | bytes 1572872 | tf_op jit(solution)/shard_map/ppermute | solution.py:121
  96.7 11.2 %copy-start.1 = (f32[32,128,128]{2,1,0:T(8,128)S(1)}, f32[32,128,128]{2,1,0:T(8,128)}, u32[]{:S(2)}) copy-start(f32[32,128,128]{2,1,0:T(8,128)} %copy-done) | copy-start | bytes 6291460
  96.7 15.0 %collective-permute-start.7 = (f32[4,2,128,128]{3,2,1,0:T(8,128)S(1)}, f32[4,2,128,128]{3,2,1,0:T(8,128)S(1)}, u32[]{:S(2)}, u32[]{:S(2)}) collective-permute-start(f32[4,2,128,128]{3,2,1,0:T(8,128)S(1)} %dynamic-slice_bitcast_fusion.3), channel_id=1, source_target_pairs={{0,16},{8,24},{16,32},{24,40},{32,48},{40,56},{48,0},{56,8},{64,80... | collective-permute-start | bytes 1572872 | tf_op jit(solution)/shard_map/ppermute | solution.py:121
  103.6 14.3 %copy-start.3 = (f32[32,128,128]{2,1,0:T(8,128)S(1)}, f32[32,128,128]{2,1,0:T(8,128)}, u32[]{:S(2)}) copy-start(f32[32,128,128]{2,1,0:T(8,128)} %get-tuple-element.13) | copy-start | bytes 6291460
  103.6 14.3 %collective-permute-start.26 = (f32[4,2,128,128]{3,2,1,0:T(8,128)S(1)}, f32[4,2,128,128]{3,2,1,0:T(8,128)S(1)}, u32[]{:S(2)}, u32[]{:S(2)}) collective-permute-start(f32[4,2,128,128]{3,2,1,0:T(8,128)S(1)} %bitcast_add_fusion.2), channel_id=1, source_target_pairs={{0,192},{8,200},{16,208},{24,216},{32,224},{40,232},{48,240},{56,2... | collective-permute-start | bytes 1572872 | tf_op jit(solution)/shard_map/ppermute | solution.py:121
  107.8 14.1 %collective-permute-start.20 = (f32[4,2,128,128]{3,2,1,0:T(8,128)S(1)}, f32[4,2,128,128]{3,2,1,0:T(8,128)S(1)}, u32[]{:S(2)}, u32[]{:S(2)}) collective-permute-start(f32[4,2,128,128]{3,2,1,0:T(8,128)S(1)} %bitcast_add_fusion.5), channel_id=1, source_target_pairs={{0,64},{8,72},{16,80},{24,88},{32,96},{40,104},{48,112},{56,120},{... | collective-permute-start | bytes 1572872 | tf_op jit(solution)/shard_map/ppermute | solution.py:121
  108.0 14.3 %collective-permute-start.14 = (f32[4,2,128,128]{3,2,1,0:T(8,128)S(1)}, f32[4,2,128,128]{3,2,1,0:T(8,128)S(1)}, u32[]{:S(2)}, u32[]{:S(2)}) collective-permute-start(f32[4,2,128,128]{3,2,1,0:T(8,128)S(1)} %bitcast_add_fusion.8), channel_id=1, source_target_pairs={{0,48},{8,56},{16,0},{24,8},{32,16},{40,24},{48,32},{56,40},{64,11... | collective-permute-start | bytes 1572872 | tf_op jit(solution)/shard_map/ppermute | solution.py:121
  111.8 14.1 %collective-permute-start.8 = (f32[4,2,128,128]{3,2,1,0:T(8,128)S(1)}, f32[4,2,128,128]{3,2,1,0:T(8,128)S(1)}, u32[]{:S(2)}, u32[]{:S(2)}) collective-permute-start(f32[4,2,128,128]{3,2,1,0:T(8,128)S(1)} %bitcast_add_fusion.11), channel_id=1, source_target_pairs={{0,16},{8,24},{16,32},{24,40},{32,48},{40,56},{48,0},{56,8},{64,80... | collective-permute-start | bytes 1572872 | tf_op jit(solution)/shard_map/ppermute | solution.py:121
  118.0 13.5 %collective-permute-start.27 = (f32[4,2,128,128]{3,2,1,0:T(8,128)S(1)}, f32[4,2,128,128]{3,2,1,0:T(8,128)S(1)}, u32[]{:S(2)}, u32[]{:S(2)}) collective-permute-start(f32[4,2,128,128]{3,2,1,0:T(8,128)S(1)} %bitcast_add_fusion.1), channel_id=1, source_target_pairs={{0,192},{8,200},{16,208},{24,216},{32,224},{40,232},{48,240},{56,2... | collective-permute-start | bytes 1572872 | tf_op jit(solution)/shard_map/ppermute | solution.py:121
  122.0 13.4 %collective-permute-start.21 = (f32[4,2,128,128]{3,2,1,0:T(8,128)S(1)}, f32[4,2,128,128]{3,2,1,0:T(8,128)S(1)}, u32[]{:S(2)}, u32[]{:S(2)}) collective-permute-start(f32[4,2,128,128]{3,2,1,0:T(8,128)S(1)} %bitcast_add_fusion.4), channel_id=1, source_target_pairs={{0,64},{8,72},{16,80},{24,88},{32,96},{40,104},{48,112},{56,120},{... | collective-permute-start | bytes 1572872 | tf_op jit(solution)/shard_map/ppermute | solution.py:121
  122.3 14.8 %collective-permute-start.15 = (f32[4,2,128,128]{3,2,1,0:T(8,128)S(1)}, f32[4,2,128,128]{3,2,1,0:T(8,128)S(1)}, u32[]{:S(2)}, u32[]{:S(2)}) collective-permute-start(f32[4,2,128,128]{3,2,1,0:T(8,128)S(1)} %bitcast_add_fusion.7), channel_id=1, source_target_pairs={{0,48},{8,56},{16,0},{24,8},{32,16},{40,24},{48,32},{56,40},{64,11... | collective-permute-start | bytes 1572872 | tf_op jit(solution)/shard_map/ppermute | solution.py:121
  126.0 14.4 %collective-permute-start.9 = (f32[4,2,128,128]{3,2,1,0:T(8,128)S(1)}, f32[4,2,128,128]{3,2,1,0:T(8,128)S(1)}, u32[]{:S(2)}, u32[]{:S(2)}) collective-permute-start(f32[4,2,128,128]{3,2,1,0:T(8,128)S(1)} %bitcast_add_fusion.10), channel_id=1, source_target_pairs={{0,16},{8,24},{16,32},{24,40},{32,48},{40,56},{48,0},{56,8},{64,80... | collective-permute-start | bytes 1572872 | tf_op jit(solution)/shard_map/ppermute | solution.py:121
  131.6 9.0 %collective-permute-start.28 = (f32[2,128,128]{2,1,0:T(8,128)S(1)}, f32[2,128,128]{2,1,0:T(8,128)S(1)}, u32[]{:S(2)}, u32[]{:S(2)}) collective-permute-start(f32[2,128,128]{2,1,0:T(8,128)S(1)} %dynamic-slice_bitcast_fusion.5), channel_id=1, source_target_pairs={{0,48},{8,56},{16,0},{24,8},{32,16},{40,24},{48,32},{56,40},{64,11... | collective-permute-start | bytes 393224 | tf_op jit(solution)/shard_map/ppermute | solution.py:121
  135.5 7.8 %collective-permute-start.22 = (f32[2,128,128]{2,1,0:T(8,128)S(1)}, f32[2,128,128]{2,1,0:T(8,128)S(1)}, u32[]{:S(2)}, u32[]{:S(2)}) collective-permute-start(f32[2,128,128]{2,1,0:T(8,128)S(1)} %dynamic-slice_bitcast_fusion.6), channel_id=1, source_target_pairs={{0,16},{8,24},{16,32},{24,40},{32,48},{40,56},{48,0},{56,8},{64,80... | collective-permute-start | bytes 393224 | tf_op jit(solution)/shard_map/ppermute | solution.py:121
  137.1 6.3 %collective-permute-start.16 = (f32[2,128,128]{2,1,0:T(8,128)S(1)}, f32[2,128,128]{2,1,0:T(8,128)S(1)}, u32[]{:S(2)}, u32[]{:S(2)}) collective-permute-start(f32[2,128,128]{2,1,0:T(8,128)S(1)} %dynamic-slice_bitcast_fusion.7), channel_id=1, source_target_pairs={{0,192},{8,200},{16,208},{24,216},{32,224},{40,232},{48,240},{56,2... | collective-permute-start | bytes 393224 | tf_op jit(solution)/shard_map/ppermute | solution.py:121
  140.4 6.8 %collective-permute-start.10 = (f32[2,128,128]{2,1,0:T(8,128)S(1)}, f32[2,128,128]{2,1,0:T(8,128)S(1)}, u32[]{:S(2)}, u32[]{:S(2)}) collective-permute-start(f32[2,128,128]{2,1,0:T(8,128)S(1)} %dynamic-slice_bitcast_fusion.8), channel_id=1, source_target_pairs={{0,64},{8,72},{16,80},{24,88},{32,96},{40,104},{48,112},{56,120},{... | collective-permute-start | bytes 393224 | tf_op jit(solution)/shard_map/ppermute | solution.py:121
  140.6 6.8 %collective-permute-start.29 = (f32[2,128,128]{2,1,0:T(8,128)S(1)}, f32[2,128,128]{2,1,0:T(8,128)S(1)}, u32[]{:S(2)}, u32[]{:S(2)}) collective-permute-start(f32[2,128,128]{2,1,0:T(8,128)S(1)} %bitcast_add_fusion.15), channel_id=1, source_target_pairs={{0,48},{8,56},{16,0},{24,8},{32,16},{40,24},{48,32},{56,40},{64,11... | collective-permute-start | bytes 393224 | tf_op jit(solution)/shard_map/ppermute | solution.py:121
  143.3 6.9 %collective-permute-start.23 = (f32[2,128,128]{2,1,0:T(8,128)S(1)}, f32[2,128,128]{2,1,0:T(8,128)S(1)}, u32[]{:S(2)}, u32[]{:S(2)}) collective-permute-start(f32[2,128,128]{2,1,0:T(8,128)S(1)} %bitcast_add_fusion.18), channel_id=1, source_target_pairs={{0,16},{8,24},{16,32},{24,40},{32,48},{40,56},{48,0},{56,8},{64,80... | collective-permute-start | bytes 393224 | tf_op jit(solution)/shard_map/ppermute | solution.py:121
  143.5 6.8 %collective-permute-start.17 = (f32[2,128,128]{2,1,0:T(8,128)S(1)}, f32[2,128,128]{2,1,0:T(8,128)S(1)}, u32[]{:S(2)}, u32[]{:S(2)}) collective-permute-start(f32[2,128,128]{2,1,0:T(8,128)S(1)} %bitcast_add_fusion.21), channel_id=1, source_target_pairs={{0,192},{8,200},{16,208},{24,216},{32,224},{40,232},{48,240},{56,2... | collective-permute-start | bytes 393224 | tf_op jit(solution)/shard_map/ppermute | solution.py:121
  147.3 7.4 %collective-permute-start.11 = (f32[2,128,128]{2,1,0:T(8,128)S(1)}, f32[2,128,128]{2,1,0:T(8,128)S(1)}, u32[]{:S(2)}, u32[]{:S(2)}) collective-permute-start(f32[2,128,128]{2,1,0:T(8,128)S(1)} %bitcast_add_fusion.24), channel_id=1, source_target_pairs={{0,64},{8,72},{16,80},{24,88},{32,96},{40,104},{48,112},{56,120},{... | collective-permute-start | bytes 393224 | tf_op jit(solution)/shard_map/ppermute | solution.py:121
  147.4 7.4 %collective-permute-start.30 = (f32[2,128,128]{2,1,0:T(8,128)S(1)}, f32[2,128,128]{2,1,0:T(8,128)S(1)}, u32[]{:S(2)}, u32[]{:S(2)}) collective-permute-start(f32[2,128,128]{2,1,0:T(8,128)S(1)} %bitcast_add_fusion.14), channel_id=1, source_target_pairs={{0,48},{8,56},{16,0},{24,8},{32,16},{40,24},{48,32},{56,40},{64,11... | collective-permute-start | bytes 393224 | tf_op jit(solution)/shard_map/ppermute | solution.py:121
  150.2 6.3 %collective-permute-start.24 = (f32[2,128,128]{2,1,0:T(8,128)S(1)}, f32[2,128,128]{2,1,0:T(8,128)S(1)}, u32[]{:S(2)}, u32[]{:S(2)}) collective-permute-start(f32[2,128,128]{2,1,0:T(8,128)S(1)} %bitcast_add_fusion.17), channel_id=1, source_target_pairs={{0,16},{8,24},{16,32},{24,40},{32,48},{40,56},{48,0},{56,8},{64,80... | collective-permute-start | bytes 393224 | tf_op jit(solution)/shard_map/ppermute | solution.py:121
  150.4 6.1 %collective-permute-start.18 = (f32[2,128,128]{2,1,0:T(8,128)S(1)}, f32[2,128,128]{2,1,0:T(8,128)S(1)}, u32[]{:S(2)}, u32[]{:S(2)}) collective-permute-start(f32[2,128,128]{2,1,0:T(8,128)S(1)} %bitcast_add_fusion.20), channel_id=1, source_target_pairs={{0,192},{8,200},{16,208},{24,216},{32,224},{40,232},{48,240},{56,2... | collective-permute-start | bytes 393224 | tf_op jit(solution)/shard_map/ppermute | solution.py:121
  154.7 6.3 %collective-permute-start.12 = (f32[2,128,128]{2,1,0:T(8,128)S(1)}, f32[2,128,128]{2,1,0:T(8,128)S(1)}, u32[]{:S(2)}, u32[]{:S(2)}) collective-permute-start(f32[2,128,128]{2,1,0:T(8,128)S(1)} %bitcast_add_fusion.23), channel_id=1, source_target_pairs={{0,64},{8,72},{16,80},{24,88},{32,96},{40,104},{48,112},{56,120},{... | collective-permute-start | bytes 393224 | tf_op jit(solution)/shard_map/ppermute | solution.py:121
  161.1 13.1 %collective-permute-start.31 = (f32[4,128,128]{2,1,0:T(8,128)S(1)}, f32[4,128,128]{2,1,0:T(8,128)S(1)}, u32[]{:S(2)}, u32[]{:S(2)}) collective-permute-start(f32[4,128,128]{2,1,0:T(8,128)S(1)} %dynamic-slice_bitcast_fusion.4), channel_id=1, source_target_pairs={{0,8},{8,0},{16,24},{24,16},{32,40},{40,32},{48,56},{56,48},{64,72... | collective-permute-start | bytes 786440 | tf_op jit(solution)/shard_map/ppermute | solution.py:130

commit v8 on v7

--- a/solution.py
+++ b/solution.py
@@ -181,18 +181,19 @@
     partials = owner_partials(gathered, left, right, target)
     block = x_blocks.shape[1]
     my_y, my_x, my_z = _blk_coords(me)
-    results = []
+    firsts = []
     for c in range(CS):
         data = partials[c].reshape(BLK_DIMS + (block, block))
         direction = 1 if c % 2 == 0 else -1
         if c < 2:
-            data = ring_reduce_scatter(data, 1, 1, direction, my_x)
-            data = ring_reduce_scatter(data, 0, 0, direction, my_y)
+            firsts.append(ring_reduce_scatter(data, 1, 1, direction, my_x))
         else:
-            data = ring_reduce_scatter(data, 0, 0, direction, my_y)
-            data = ring_reduce_scatter(data, 0, 1, direction, my_x)
-        results.append(data)
-    summed = pair_reduce_scatter(jnp.stack(results), 1, my_z)
+            firsts.append(ring_reduce_scatter(data, 0, 0, direction, my_y))
+    half = CS // 2
+    along_y = ring_reduce_scatter(jnp.stack(firsts[:half]), 1, 0, 1, my_y)
+    along_x = ring_reduce_scatter(jnp.stack(firsts[half:]), 1, 1, 1, my_x)
+    results = jnp.concatenate([along_y, along_x])
+    summed = pair_reduce_scatter(results, 1, my_z)
     return summed.astype(jnp.bfloat16).reshape(1, 1, CS, block, block)
 
 

time: 176 us -> 184 us (1.045)
  waiting for transfers between devices: 65.1 us -> 93.5 us
  starting transfers between devices: 64.4 us -> 45.1 us
    ppermute x24 -> x18, waiting for transfers between devices: 27.2 us -> 53.4 us  [ring_reduce_scatter(): arrived = lax.ppermute(send, 'blk', route)]
    ppermute x3, waiting for transfers between devices: 1.94 us -> 26.6 us  [line_all_gather(): send_up = lax.ppermute(send_up, 'grp', up)]
    ppermute x3, waiting for transfers between devices: 27.2 us -> 3.56 us  [line_all_gather(): send_down = lax.ppermute(send_down, 'grp', down)]
    ppermute x24 -> x18, starting transfers between devices: 40.6 us -> 22.3 us  [ring_reduce_scatter(): arrived = lax.ppermute(send, 'blk', route)]
    ppermute x3, starting transfers between devices: 9.59 us -> 11.4 us  [line_all_gather(): send_up = lax.ppermute(send_up, 'grp', up)]
    reshape x8 -> x4, local copies, waits for them, and re-layouts: 5.11 us -> 4.86 us  [_take(): piece.reshape([s for i, s in enumerate(sizes) if i >= offset and i != off...]
  transfers between devices with their start and end apart: 32 -> 26, of which waited for: 17 -> 19; matrix products, arithmetic and copies ran while one was open for 4% -> 4% of each run, Pallas kernels for 0% -> 0%
where the time goes in v8:
time: 184 us
  waiting for transfers between devices  93.5 us (51%)
  starting transfers between devices  45.1 us (25%)
  Pallas kernels  26.4 us (14%)
  local copies, waits for them, and re-layouts  10.9 us (6%)
  other arithmetic  7.34 us (4%)
    ppermute x18, waiting for transfers between devices, ring_reduce_scatter(): arrived = lax.ppermute(send, 'blk', route)  53.4 us
    ppermute x3, waiting for transfers between devices, line_all_gather(): send_up = lax.ppermute(send_up, 'grp', up)  26.6 us
    pallas_call x1, Pallas kernels, owner_partials(): pl.pallas_call(_products_kernel, out_shape=[jax.ShapeDtypeStruct((owners,...  26.4 us
    ppermute x18, starting transfers between devices, ring_reduce_scatter(): arrived = lax.ppermute(send, 'blk', route)  22.3 us
    ppermute x3, starting transfers between devices, line_all_gather(): send_up = lax.ppermute(send_up, 'grp', up)  11.4 us
    ppermute x1, waiting for transfers between devices, pair_reduce_scatter(): return lax.ppermute(other, 'blk', route) + mine  7.9 us
    ppermute x3, starting transfers between devices, line_all_gather(): send_down = lax.ppermute(send_down, 'grp', down)  6.14 us
    ppermute x1, starting transfers between devices, pair_reduce_scatter(): return lax.ppermute(other, 'blk', route) + mine  5.28 us
  transfers between devices with their start and end apart: 26, of which 19 were waited for; matrix products, arithmetic and copies ran while one was open for 4% of the time, Pallas kernels for 0%

profile of v8, /device:TPU:32, one launch (start us, length us, event | category | flops | bytes accessed | tf_op | source)
XLA Modules:
  0.0 183.7 jit_solution(1915412404864012277)
XLA Ops:
  0.0 3.8 %collective-permute-start = (bf16[16,128,128]{2,1,0:T(8,128)(2,1)}, bf16[16,128,128]{2,1,0:T(8,128)(2,1)S(1)}, u32[]{:S(2)}, u32[]{:S(2)}) collective-permute-start(bf16[16,128,128]{2,1,0:T(8,128)(2,1)} %param.6), channel_id=1, source_target_pairs={{0,2},{1,3},{2,4},{3,5},{4,6},{5,7},{8,10},{9,11},{10,12},{11,13},... | collective-permute-start | bytes 1572872 | tf_op jit(solution)/shard_map/ppermute | solution.py:145
  3.8 2.0 %collective-permute-start.3 = (bf16[16,128,128]{2,1,0:T(8,128)(2,1)}, bf16[16,128,128]{2,1,0:T(8,128)(2,1)S(1)}, u32[]{:S(2)}, u32[]{:S(2)}) collective-permute-start(bf16[16,128,128]{2,1,0:T(8,128)(2,1)} %param.6), channel_id=1, source_target_pairs={{2,0},{3,1},{4,2},{5,3},{6,4},{7,5},{10,8},{11,9},{12,10},{13,11},... | collective-permute-start | bytes 1572872 | tf_op jit(solution)/shard_map/ppermute | solution.py:146
  5.9 9.9 %collective-permute-done = bf16[16,128,128]{2,1,0:T(8,128)(2,1)S(1)} collective-permute-done((bf16[16,128,128]{2,1,0:T(8,128)(2,1)}, bf16[16,128,128]{2,1,0:T(8,128)(2,1)S(1)}, u32[]{:S(2)}, u32[]{:S(2)}) %collective-permute-start) | collective-permute-done | bytes 524320 | tf_op jit(solution)/shard_map/ppermute | solution.py:145
  15.8 3.8 %collective-permute-start.1 = (bf16[16,128,128]{2,1,0:T(8,128)(2,1)S(1)}, bf16[16,128,128]{2,1,0:T(8,128)(2,1)S(1)}, u32[]{:S(2)}, u32[]{:S(2)}) collective-permute-start(bf16[16,128,128]{2,1,0:T(8,128)(2,1)S(1)} %collective-permute-done), channel_id=1, source_target_pairs={{0,2},{1,3},{2,4},{3,5},{4,6},{5,7},{8,10},{9,11},{10,12},{11,13},... | collective-permute-start | bytes 1572872 | tf_op jit(solution)/shard_map/ppermute | solution.py:145
  19.6 2.0 %collective-permute-start.4 = (bf16[16,128,128]{2,1,0:T(8,128)(2,1)S(1)}, bf16[16,128,128]{2,1,0:T(8,128)(2,1)S(1)}, u32[]{:S(2)}, u32[]{:S(2)}) collective-permute-start(bf16[16,128,128]{2,1,0:T(8,128)(2,1)S(1)} %collective-permute-done.3), channel_id=1, source_target_pairs={{2,0},{3,1},{4,2},{5,3},{6,4},{7,5},{10,8},{11,9},{12,10},{13,11},... | collective-permute-start | bytes 1572872 | tf_op jit(solution)/shard_map/ppermute | solution.py:146
  21.6 8.8 %collective-permute-done.1 = bf16[16,128,128]{2,1,0:T(8,128)(2,1)S(1)} collective-permute-done((bf16[16,128,128]{2,1,0:T(8,128)(2,1)S(1)}, bf16[16,128,128]{2,1,0:T(8,128)(2,1)S(1)}, u32[]{:S(2)}, u32[]{:S(2)}) %collective-permute-start.1) | collective-permute-done | bytes 524320 | tf_op jit(solution)/shard_map/ppermute | solution.py:145
  30.4 3.8 %collective-permute-start.2 = (bf16[16,128,128]{2,1,0:T(8,128)(2,1)S(1)}, bf16[16,128,128]{2,1,0:T(8,128)(2,1)S(1)}, u32[]{:S(2)}, u32[]{:S(2)}) collective-permute-start(bf16[16,128,128]{2,1,0:T(8,128)(2,1)S(1)} %collective-permute-done.1), channel_id=1, source_target_pairs={{0,2},{1,3},{2,4},{3,5},{4,6},{5,7},{8,10},{9,11},{10,12},{11,13},... | collective-permute-start | bytes 1572872 | tf_op jit(solution)/shard_map/ppermute | solution.py:145
  34.3 2.0 %collective-permute-start.5 = (bf16[16,128,128]{2,1,0:T(8,128)(2,1)S(1)}, bf16[16,128,128]{2,1,0:T(8,128)(2,1)S(1)}, u32[]{:S(2)}, u32[]{:S(2)}) collective-permute-start(bf16[16,128,128]{2,1,0:T(8,128)(2,1)S(1)} %collective-permute-done.4), channel_id=1, source_target_pairs={{2,0},{3,1},{4,2},{5,3},{6,4},{7,5},{10,8},{11,9},{12,10},{13,11},... | collective-permute-start | bytes 1572872 | tf_op jit(solution)/shard_map/ppermute | solution.py:146
  36.4 7.9 %collective-permute-done.2 = bf16[16,128,128]{2,1,0:T(8,128)(2,1)S(1)} collective-permute-done((bf16[16,128,128]{2,1,0:T(8,128)(2,1)S(1)}, bf16[16,128,128]{2,1,0:T(8,128)(2,1)S(1)}, u32[]{:S(2)}, u32[]{:S(2)}) %collective-permute-start.2) | collective-permute-done | bytes 524320 | tf_op jit(solution)/shard_map/ppermute | solution.py:145
  44.5 3.6 %collective-permute-done.5 = bf16[16,128,128]{2,1,0:T(8,128)(2,1)S(1)} collective-permute-done((bf16[16,128,128]{2,1,0:T(8,128)(2,1)S(1)}, bf16[16,128,128]{2,1,0:T(8,128)(2,1)S(1)}, u32[]{:S(2)}, u32[]{:S(2)}) %collective-permute-start.5) | collective-permute-done | bytes 524320 | tf_op jit(solution)/shard_map/ppermute | solution.py:146
  48.5 1.6 pad_maximum_fusion.1
  50.3 0.6 gather_fusion
  50.9 0.6 gather_fusion.1
  51.6 0.6 gather_fusion.2
  52.6 2.1 %collective-permute-done.6 = bf16[4,16,128,128]{3,2,1,0:T(8,128)(2,1)} collective-permute-done((bf16[4,16,128,128]{3,2,1,0:T(8,128)(2,1)}, bf16[4,16,128,128]{3,2,1,0:T(8,128)(2,1)}, u32[]{:S(2)}, u32[]{:S(2)}) %collective-permute-start.6) | collective-permute-done | bytes 2097184 | tf_op jit(solution)/shard_map/ppermute | solution.py:164
  54.6 1.8 select_bitcast_fusion.1
  56.4 0.4 pad_maximum_fusion
  56.8 2.3 %copy.20 = bf16[4,2,16,128,128]{4,3,2,1,0:T(8,128)(2,1)} copy(bf16[4,2,16,128,128]{4,3,2,0,1:T(8,128)(2,1)S(1)} %pad_maximum_fusion) | data formatting | bytes 8388608 | tf_op jit(solution)/shard_map/stack | solution.py:167
  59.1 26.4 %shard_map.46 = (f32[32,128,128]{2,1,0:T(8,128)S(1)}, f32[32,128,128]{2,1,0:T(8,128)S(1)}, f32[32,128,128]{2,1,0:T(8,128)}, f32[32,128,128]{2,1,0:T(8,128)}) custom-call(s32[384]{0:T(512)S(1)} %reshape.112.left_ref, s32[384]{0:T(512)S(1)} %reshape.113.right_ref, s32[384]{0:T(512)S(1)} %reshape.114.target_ref, bf16[128,128,128]{2,1,0:T(8,128)(2,1)} %bitcast.128), custom_call_target="tpu_custom_call" | custom-call | flops 1610612736 | bytes 12582912 | tf_op jit(solution)/shard_map/pallas_call | solution.py:40
  85.5 1.4 copy-done
  86.9 1.9 %dynamic-slice_bitcast_fusion = f32[4,2,128,128]{3,2,1,0:T(8,128)} fusion(f32[4,4,2,128,128]{4,3,2,1,0:T(8,128)} %bitcast.133, s32[]{:T(128)S(6)} %select_n.323), kind=kLoop, calls=%fused_computation.53 | loop fusion | bytes 1048580 | tf_op jit(solution)/shard_map/reshape | solution.py:107
  88.7 3.0 %collective-permute-start.19 = (f32[4,2,128,128]{3,2,1,0:T(8,128)}, f32[4,2,128,128]{3,2,1,0:T(8,128)S(1)}, u32[]{:S(2)}, u32[]{:S(2)}) collective-permute-start(f32[4,2,128,128]{3,2,1,0:T(8,128)} %dynamic-slice_bitcast_fusion), channel_id=1, source_target_pairs={{0,192},{8,200},{16,208},{24,216},{32,224},{40,232},{48,240},{56,2... | collective-permute-start | bytes 1572872 | tf_op jit(solution)/shard_map/ppermute | solution.py:121
  91.7 1.9 %dynamic-slice_bitcast_fusion.1 = f32[4,2,128,128]{3,2,1,0:T(8,128)} fusion(f32[4,4,2,128,128]{4,3,2,1,0:T(8,128)} %bitcast.129, s32[]{:T(128)S(6)} %select_n.315), kind=kLoop, calls=%fused_computation.54 | loop fusion | bytes 1048580 | tf_op jit(solution)/shard_map/reshape | solution.py:107
  93.7 2.8 %collective-permute-start.10 = (f32[4,2,128,128]{3,2,1,0:T(8,128)S(1)}, f32[4,2,128,128]{3,2,1,0:T(8,128)S(1)}, u32[]{:S(2)}, u32[]{:S(2)}) collective-permute-start(f32[4,2,128,128]{3,2,1,0:T(8,128)S(1)} %dynamic-slice_bitcast_fusion.2), channel_id=1, source_target_pairs={{0,48},{8,56},{16,0},{24,8},{32,16},{40,24},{48,32},{56,40},{64,11... | collective-permute-start | bytes 1572872 | tf_op jit(solution)/shard_map/ppermute | solution.py:121
  96.5 1.1 dynamic-slice_bitcast_fusion.3
  97.7 5.9 %collective-permute-done.19 = f32[4,2,128,128]{3,2,1,0:T(8,128)S(1)} collective-permute-done((f32[4,2,128,128]{3,2,1,0:T(8,128)}, f32[4,2,128,128]{3,2,1,0:T(8,128)S(1)}, u32[]{:S(2)}, u32[]{:S(2)}) %collective-permute-start.19) | collective-permute-done | bytes 524320 | tf_op jit(solution)/shard_map/ppermute | solution.py:121
  103.5 1.1 bitcast_add_fusion.2
  104.7 3.7 %collective-permute-start.20 = (f32[4,2,128,128]{3,2,1,0:T(8,128)S(1)}, f32[4,2,128,128]{3,2,1,0:T(8,128)S(1)}, u32[]{:S(2)}, u32[]{:S(2)}) collective-permute-start(f32[4,2,128,128]{3,2,1,0:T(8,128)S(1)} %bitcast_add_fusion.2), channel_id=1, source_target_pairs={{0,192},{8,200},{16,208},{24,216},{32,224},{40,232},{48,240},{56,2... | collective-permute-start | bytes 1572872 | tf_op jit(solution)/shard_map/ppermute | solution.py:121
  108.3 0.4 collective-permute-done.16
  109.0 2.8 %collective-permute-start.11 = (f32[4,2,128,128]{3,2,1,0:T(8,128)S(1)}, f32[4,2,128,128]{3,2,1,0:T(8,128)S(1)}, u32[]{:S(2)}, u32[]{:S(2)}) collective-permute-start(f32[4,2,128,128]{3,2,1,0:T(8,128)S(1)} %bitcast_add_fusion.8), channel_id=1, source_target_pairs={{0,48},{8,56},{16,0},{24,8},{32,16},{40,24},{48,32},{56,40},{64,11... | collective-permute-start | bytes 1572872 | tf_op jit(solution)/shard_map/ppermute | solution.py:121
  111.8 0.5 collective-permute-done.7
  112.4 6.5 %collective-permute-done.20 = f32[4,2,128,128]{3,2,1,0:T(8,128)S(1)} collective-permute-done((f32[4,2,128,128]{3,2,1,0:T(8,128)S(1)}, f32[4,2,128,128]{3,2,1,0:T(8,128)S(1)}, u32[]{:S(2)}, u32[]{:S(2)}) %collective-permute-start.20) | collective-permute-done | bytes 524320 | tf_op jit(solution)/shard_map/ppermute | solution.py:121
  119.0 3.8 %collective-permute-start.21 = (f32[4,2,128,128]{3,2,1,0:T(8,128)S(1)}, f32[4,2,128,128]{3,2,1,0:T(8,128)S(1)}, u32[]{:S(2)}, u32[]{:S(2)}) collective-permute-start(f32[4,2,128,128]{3,2,1,0:T(8,128)S(1)} %bitcast_add_fusion.1), channel_id=1, source_target_pairs={{0,192},{8,200},{16,208},{24,216},{32,224},{40,232},{48,240},{56,2... | collective-permute-start | bytes 1572872 | tf_op jit(solution)/shard_map/ppermute | solution.py:121
  123.0 0.3 collective-permute-start.18
  123.4 2.8 %collective-permute-start.12 = (f32[4,2,128,128]{3,2,1,0:T(8,128)S(1)}, f32[4,2,128,128]{3,2,1,0:T(8,128)S(1)}, u32[]{:S(2)}, u32[]{:S(2)}) collective-permute-start(f32[4,2,128,128]{3,2,1,0:T(8,128)S(1)} %bitcast_add_fusion.7), channel_id=1, source_target_pairs={{0,48},{8,56},{16,0},{24,8},{32,16},{40,24},{48,32},{56,40},{64,11... | collective-permute-start | bytes 1572872 | tf_op jit(solution)/shard_map/ppermute | solution.py:121
  126.3 6.2 %collective-permute-done.21 = f32[4,2,128,128]{3,2,1,0:T(8,128)S(1)} collective-permute-done((f32[4,2,128,128]{3,2,1,0:T(8,128)S(1)}, f32[4,2,128,128]{3,2,1,0:T(8,128)S(1)}, u32[]{:S(2)}, u32[]{:S(2)}) %collective-permute-start.21) | collective-permute-done | bytes 524320 | tf_op jit(solution)/shard_map/ppermute | solution.py:121
  132.6 3.8 %collective-permute-done.18 = f32[4,2,128,128]{3,2,1,0:T(8,128)S(1)} collective-permute-done((f32[4,2,128,128]{3,2,1,0:T(8,128)S(1)}, f32[4,2,128,128]{3,2,1,0:T(8,128)S(1)}, u32[]{:S(2)}, u32[]{:S(2)}) %collective-permute-start.18) | collective-permute-done | bytes 524320 | tf_op jit(solution)/shard_map/ppermute | solution.py:121
  136.7 1.5 collective-permute-start.22
  138.2 2.4 %collective-permute-done.9 = f32[4,2,128,128]{3,2,1,0:T(8,128)S(1)} collective-permute-done((f32[4,2,128,128]{3,2,1,0:T(8,128)S(1)}, f32[4,2,128,128]{3,2,1,0:T(8,128)S(1)}, u32[]{:S(2)}, u32[]{:S(2)}) %collective-permute-start.9) | collective-permute-done | bytes 524320 | tf_op jit(solution)/shard_map/ppermute | solution.py:121
  141.1 3.8 %collective-permute-done.22 = f32[2,2,128,128]{3,2,0,1:T(8,128)S(1)} collective-permute-done((f32[2,2,128,128]{3,2,0,1:T(8,128)S(1)}, f32[2,2,128,128]{3,2,0,1:T(8,128)S(1)}, u32[]{:S(2)}, u32[]{:S(2)}) %collective-permute-start.22) | collective-permute-done | bytes 262176 | tf_op jit(solution)/shard_map/ppermute | solution.py:121
  145.0 7.1 %collective-permute-done.13 = f32[2,2,128,128]{3,2,0,1:T(8,128)S(1)} collective-permute-done((f32[2,2,128,128]{3,2,0,1:T(8,128)S(1)}, f32[2,2,128,128]{3,2,0,1:T(8,128)S(1)}, u32[]{:S(2)}, u32[]{:S(2)}) %collective-permute-start.13) | collective-permute-done | bytes 262176 | tf_op jit(solution)/shard_map/ppermute | solution.py:121
  152.2 0.3 collective-permute-done.23
  152.6 0.8 collective-permute-start.24
  153.3 8.8 %collective-permute-done.14 = f32[2,2,128,128]{3,2,0,1:T(8,128)S(1)} collective-permute-done((f32[2,2,128,128]{3,2,0,1:T(8,128)S(1)}, f32[2,2,128,128]{3,2,0,1:T(8,128)S(1)}, u32[]{:S(2)}, u32[]{:S(2)}) %collective-permute-start.14) | collective-permute-done | bytes 262176 | tf_op jit(solution)/shard_map/ppermute | solution.py:121
  162.3 7.5 %collective-permute-done.15 = f32[2,2,128,128]{3,2,0,1:T(8,128)S(1)} collective-permute-done((f32[2,2,128,128]{3,2,0,1:T(8,128)S(1)}, f32[2,2,128,128]{3,2,0,1:T(8,128)S(1)}, u32[]{:S(2)}, u32[]{:S(2)}) %collective-permute-start.15) | collective-permute-done | bytes 262176 | tf_op jit(solution)/shard_map/ppermute | solution.py:121
  169.9 5.3 %collective-permute-start.25 = (f32[4,128,128]{2,1,0:T(8,128)S(1)}, f32[4,128,128]{2,1,0:T(8,128)S(1)}, u32[]{:S(2)}, u32[]{:S(2)}) collective-permute-start(f32[4,128,128]{2,1,0:T(8,128)S(1)} %fusion.13), channel_id=1, source_target_pairs={{0,8},{8,0},{16,24},{24,16},{32,40},{40,32},{48,56},{56,48},{64,72... | collective-permute-start | bytes 786440 | tf_op jit(solution)/shard_map/ppermute | solution.py:130
  175.2 7.9 %collective-permute-done.25 = f32[4,128,128]{2,1,0:T(8,128)S(1)} collective-permute-done((f32[4,128,128]{2,1,0:T(8,128)S(1)}, f32[4,128,128]{2,1,0:T(8,128)S(1)}, u32[]{:S(2)}, u32[]{:S(2)}) %collective-permute-start.25) | collective-permute-done | bytes 262176 | tf_op jit(solution)/shard_map/ppermute | solution.py:130
  183.1 0.7 fusion.22
  (69 shorter events, 3.4 us)
Async XLA Ops:
  0.0 15.8 %collective-permute-start = (bf16[16,128,128]{2,1,0:T(8,128)(2,1)}, bf16[16,128,128]{2,1,0:T(8,128)(2,1)S(1)}, u32[]{:S(2)}, u32[]{:S(2)}) collective-permute-start(bf16[16,128,128]{2,1,0:T(8,128)(2,1)} %param.6), channel_id=1, source_target_pairs={{0,2},{1,3},{2,4},{3,5},{4,6},{5,7},{8,10},{9,11},{10,12},{11,13},... | collective-permute-start | bytes 1572872 | tf_op jit(solution)/shard_map/ppermute | solution.py:145
  3.8 15.8 %collective-permute-start.3 = (bf16[16,128,128]{2,1,0:T(8,128)(2,1)}, bf16[16,128,128]{2,1,0:T(8,128)(2,1)S(1)}, u32[]{:S(2)}, u32[]{:S(2)}) collective-permute-start(bf16[16,128,128]{2,1,0:T(8,128)(2,1)} %param.6), channel_id=1, source_target_pairs={{2,0},{3,1},{4,2},{5,3},{6,4},{7,5},{10,8},{11,9},{12,10},{13,11},... | collective-permute-start | bytes 1572872 | tf_op jit(solution)/shard_map/ppermute | solution.py:146
  15.8 14.7 %collective-permute-start.1 = (bf16[16,128,128]{2,1,0:T(8,128)(2,1)S(1)}, bf16[16,128,128]{2,1,0:T(8,128)(2,1)S(1)}, u32[]{:S(2)}, u32[]{:S(2)}) collective-permute-start(bf16[16,128,128]{2,1,0:T(8,128)(2,1)S(1)} %collective-permute-done), channel_id=1, source_target_pairs={{0,2},{1,3},{2,4},{3,5},{4,6},{5,7},{8,10},{9,11},{10,12},{11,13},... | collective-permute-start | bytes 1572872 | tf_op jit(solution)/shard_map/ppermute | solution.py:145
  19.6 14.7 %collective-permute-start.4 = (bf16[16,128,128]{2,1,0:T(8,128)(2,1)S(1)}, bf16[16,128,128]{2,1,0:T(8,128)(2,1)S(1)}, u32[]{:S(2)}, u32[]{:S(2)}) collective-permute-start(bf16[16,128,128]{2,1,0:T(8,128)(2,1)S(1)} %collective-permute-done.3), channel_id=1, source_target_pairs={{2,0},{3,1},{4,2},{5,3},{6,4},{7,5},{10,8},{11,9},{12,10},{13,11},... | collective-permute-start | bytes 1572872 | tf_op jit(solution)/shard_map/ppermute | solution.py:146
  30.4 13.8 %collective-permute-start.2 = (bf16[16,128,128]{2,1,0:T(8,128)(2,1)S(1)}, bf16[16,128,128]{2,1,0:T(8,128)(2,1)S(1)}, u32[]{:S(2)}, u32[]{:S(2)}) collective-permute-start(bf16[16,128,128]{2,1,0:T(8,128)(2,1)S(1)} %collective-permute-done.1), channel_id=1, source_target_pairs={{0,2},{1,3},{2,4},{3,5},{4,6},{5,7},{8,10},{9,11},{10,12},{11,13},... | collective-permute-start | bytes 1572872 | tf_op jit(solution)/shard_map/ppermute | solution.py:145
  34.3 13.8 %collective-permute-start.5 = (bf16[16,128,128]{2,1,0:T(8,128)(2,1)S(1)}, bf16[16,128,128]{2,1,0:T(8,128)(2,1)S(1)}, u32[]{:S(2)}, u32[]{:S(2)}) collective-permute-start(bf16[16,128,128]{2,1,0:T(8,128)(2,1)S(1)} %collective-permute-done.4), channel_id=1, source_target_pairs={{2,0},{3,1},{4,2},{5,3},{6,4},{7,5},{10,8},{11,9},{12,10},{13,11},... | collective-permute-start | bytes 1572872 | tf_op jit(solution)/shard_map/ppermute | solution.py:146
  44.5 3.8 %copy-start.4 = (bf16[16,128,128]{2,1,0:T(8,128)(2,1)S(1)}, bf16[16,128,128]{2,1,0:T(8,128)(2,1)}, u32[]{:S(2)}) copy-start(bf16[16,128,128]{2,1,0:T(8,128)(2,1)} %param.6) | copy-start | bytes 1572868
  48.5 1.7 copy-start.5
  48.5 1.7 copy-start.6
  48.5 3.0 %copy-start.7 = (s32[1,1,32,12]{2,1,3,0:T(1,128)S(1)}, s32[1,1,32,12]{2,1,3,0:T(1,128)}, u32[]{:S(2)}) copy-start(s32[1,1,32,12]{2,1,3,0:T(1,128)} %param.9) | copy-start | bytes 4612
  50.1 4.5 %collective-permute-start.6 = (bf16[4,16,128,128]{3,2,1,0:T(8,128)(2,1)}, bf16[4,16,128,128]{3,2,1,0:T(8,128)(2,1)}, u32[]{:S(2)}, u32[]{:S(2)}) collective-permute-start(bf16[4,16,128,128]{3,2,1,0:T(8,128)(2,1)} %pad_maximum_fusion.1), channel_id=1, source_target_pairs={{0,1},{1,0},{2,3},{3,2},{4,5},{5,4},{6,7},{7,6},{8,9},{9,8},{10,11... | collective-permute-start | bytes 6291464 | tf_op jit(solution)/shard_map/ppermute | solution.py:164
  85.5 1.4 copy-start
  88.7 14.8 %collective-permute-start.19 = (f32[4,2,128,128]{3,2,1,0:T(8,128)}, f32[4,2,128,128]{3,2,1,0:T(8,128)S(1)}, u32[]{:S(2)}, u32[]{:S(2)}) collective-permute-start(f32[4,2,128,128]{3,2,1,0:T(8,128)} %dynamic-slice_bitcast_fusion), channel_id=1, source_target_pairs={{0,192},{8,200},{16,208},{24,216},{32,224},{40,232},{48,240},{56,2... | collective-permute-start | bytes 1572872 | tf_op jit(solution)/shard_map/ppermute | solution.py:121
  93.6 15.1 %collective-permute-start.16 = (f32[4,2,128,128]{3,2,1,0:T(8,128)}, f32[4,2,128,128]{3,2,1,0:T(8,128)S(1)}, u32[]{:S(2)}, u32[]{:S(2)}) collective-permute-start(f32[4,2,128,128]{3,2,1,0:T(8,128)} %dynamic-slice_bitcast_fusion.1), channel_id=1, source_target_pairs={{0,64},{8,72},{16,80},{24,88},{32,96},{40,104},{48,112},{56,120},{... | collective-permute-start | bytes 1572872 | tf_op jit(solution)/shard_map/ppermute | solution.py:121
  93.6 15.1 %copy-start.2 = (f32[32,128,128]{2,1,0:T(8,128)S(1)}, f32[32,128,128]{2,1,0:T(8,128)}, u32[]{:S(2)}) copy-start(f32[32,128,128]{2,1,0:T(8,128)} %get-tuple-element.12) | copy-start | bytes 6291460
  93.7 15.2 %collective-permute-start.10 = (f32[4,2,128,128]{3,2,1,0:T(8,128)S(1)}, f32[4,2,128,128]{3,2,1,0:T(8,128)S(1)}, u32[]{:S(2)}, u32[]{:S(2)}) collective-permute-start(f32[4,2,128,128]{3,2,1,0:T(8,128)S(1)} %dynamic-slice_bitcast_fusion.2), channel_id=1, source_target_pairs={{0,48},{8,56},{16,0},{24,8},{32,16},{40,24},{48,32},{56,40},{64,11... | collective-permute-start | bytes 1572872 | tf_op jit(solution)/shard_map/ppermute | solution.py:121
  97.6 14.7 %copy-start.1 = (f32[32,128,128]{2,1,0:T(8,128)S(1)}, f32[32,128,128]{2,1,0:T(8,128)}, u32[]{:S(2)}) copy-start(f32[32,128,128]{2,1,0:T(8,128)} %copy-done) | copy-start | bytes 6291460
  97.6 14.7 %collective-permute-start.7 = (f32[4,2,128,128]{3,2,1,0:T(8,128)S(1)}, f32[4,2,128,128]{3,2,1,0:T(8,128)S(1)}, u32[]{:S(2)}, u32[]{:S(2)}) collective-permute-start(f32[4,2,128,128]{3,2,1,0:T(8,128)S(1)} %dynamic-slice_bitcast_fusion.3), channel_id=1, source_target_pairs={{0,16},{8,24},{16,32},{24,40},{32,48},{40,56},{48,0},{56,8},{64,80... | collective-permute-start | bytes 1572872 | tf_op jit(solution)/shard_map/ppermute | solution.py:121
  104.6 14.3 %copy-start.3 = (f32[32,128,128]{2,1,0:T(8,128)S(1)}, f32[32,128,128]{2,1,0:T(8,128)}, u32[]{:S(2)}) copy-start(f32[32,128,128]{2,1,0:T(8,128)} %get-tuple-element.13) | copy-start | bytes 6291460
  104.7 14.3 %collective-permute-start.20 = (f32[4,2,128,128]{3,2,1,0:T(8,128)S(1)}, f32[4,2,128,128]{3,2,1,0:T(8,128)S(1)}, u32[]{:S(2)}, u32[]{:S(2)}) collective-permute-start(f32[4,2,128,128]{3,2,1,0:T(8,128)S(1)} %bitcast_add_fusion.2), channel_id=1, source_target_pairs={{0,192},{8,200},{16,208},{24,216},{32,224},{40,232},{48,240},{56,2... | collective-permute-start | bytes 1572872 | tf_op jit(solution)/shard_map/ppermute | solution.py:121
  108.8 14.1 %collective-permute-start.17 = (f32[4,2,128,128]{3,2,1,0:T(8,128)S(1)}, f32[4,2,128,128]{3,2,1,0:T(8,128)S(1)}, u32[]{:S(2)}, u32[]{:S(2)}) collective-permute-start(f32[4,2,128,128]{3,2,1,0:T(8,128)S(1)} %bitcast_add_fusion.5), channel_id=1, source_target_pairs={{0,64},{8,72},{16,80},{24,88},{32,96},{40,104},{48,112},{56,120},{... | collective-permute-start | bytes 1572872 | tf_op jit(solution)/shard_map/ppermute | solution.py:121
  109.0 14.3 %collective-permute-start.11 = (f32[4,2,128,128]{3,2,1,0:T(8,128)S(1)}, f32[4,2,128,128]{3,2,1,0:T(8,128)S(1)}, u32[]{:S(2)}, u32[]{:S(2)}) collective-permute-start(f32[4,2,128,128]{3,2,1,0:T(8,128)S(1)} %bitcast_add_fusion.8), channel_id=1, source_target_pairs={{0,48},{8,56},{16,0},{24,8},{32,16},{40,24},{48,32},{56,40},{64,11... | collective-permute-start | bytes 1572872 | tf_op jit(solution)/shard_map/ppermute | solution.py:121
  112.4 13.8 %collective-permute-start.8 = (f32[4,2,128,128]{3,2,1,0:T(8,128)S(1)}, f32[4,2,128,128]{3,2,1,0:T(8,128)S(1)}, u32[]{:S(2)}, u32[]{:S(2)}) collective-permute-start(f32[4,2,128,128]{3,2,1,0:T(8,128)S(1)} %bitcast_add_fusion.11), channel_id=1, source_target_pairs={{0,16},{8,24},{16,32},{24,40},{32,48},{40,56},{48,0},{56,8},{64,80... | collective-permute-start | bytes 1572872 | tf_op jit(solution)/shard_map/ppermute | solution.py:121
  119.0 13.5 %collective-permute-start.21 = (f32[4,2,128,128]{3,2,1,0:T(8,128)S(1)}, f32[4,2,128,128]{3,2,1,0:T(8,128)S(1)}, u32[]{:S(2)}, u32[]{:S(2)}) collective-permute-start(f32[4,2,128,128]{3,2,1,0:T(8,128)S(1)} %bitcast_add_fusion.1), channel_id=1, source_target_pairs={{0,192},{8,200},{16,208},{24,216},{32,224},{40,232},{48,240},{56,2... | collective-permute-start | bytes 1572872 | tf_op jit(solution)/shard_map/ppermute | solution.py:121
  123.0 13.4 %collective-permute-start.18 = (f32[4,2,128,128]{3,2,1,0:T(8,128)S(1)}, f32[4,2,128,128]{3,2,1,0:T(8,128)S(1)}, u32[]{:S(2)}, u32[]{:S(2)}) collective-permute-start(f32[4,2,128,128]{3,2,1,0:T(8,128)S(1)} %bitcast_add_fusion.4), channel_id=1, source_target_pairs={{0,64},{8,72},{16,80},{24,88},{32,96},{40,104},{48,112},{56,120},{... | collective-permute-start | bytes 1572872 | tf_op jit(solution)/shard_map/ppermute | solution.py:121
  123.4 17.3 %collective-permute-start.12 = (f32[4,2,128,128]{3,2,1,0:T(8,128)S(1)}, f32[4,2,128,128]{3,2,1,0:T(8,128)S(1)}, u32[]{:S(2)}, u32[]{:S(2)}) collective-permute-start(f32[4,2,128,128]{3,2,1,0:T(8,128)S(1)} %bitcast_add_fusion.7), channel_id=1, source_target_pairs={{0,48},{8,56},{16,0},{24,8},{32,16},{40,24},{48,32},{56,40},{64,11... | collective-permute-start | bytes 1572872 | tf_op jit(solution)/shard_map/ppermute | solution.py:121
  126.3 14.4 %collective-permute-start.9 = (f32[4,2,128,128]{3,2,1,0:T(8,128)S(1)}, f32[4,2,128,128]{3,2,1,0:T(8,128)S(1)}, u32[]{:S(2)}, u32[]{:S(2)}) collective-permute-start(f32[4,2,128,128]{3,2,1,0:T(8,128)S(1)} %bitcast_add_fusion.10), channel_id=1, source_target_pairs={{0,16},{8,24},{16,32},{24,40},{32,48},{40,56},{48,0},{56,8},{64,80... | collective-permute-start | bytes 1572872 | tf_op jit(solution)/shard_map/ppermute | solution.py:121
  136.7 8.2 %collective-permute-start.22 = (f32[2,2,128,128]{3,2,0,1:T(8,128)S(1)}, f32[2,2,128,128]{3,2,0,1:T(8,128)S(1)}, u32[]{:S(2)}, u32[]{:S(2)}) collective-permute-start(f32[2,2,128,128]{3,2,0,1:T(8,128)S(1)} %bitcast.146), channel_id=1, source_target_pairs={{0,16},{8,24},{16,32},{24,40},{32,48},{40,56},{48,0},{56,8},{64,80... | collective-permute-start | bytes 786440 | tf_op jit(solution)/shard_map/ppermute | solution.py:121
  140.9 11.2 %collective-permute-start.13 = (f32[2,2,128,128]{3,2,0,1:T(8,128)S(1)}, f32[2,2,128,128]{3,2,0,1:T(8,128)S(1)}, u32[]{:S(2)}, u32[]{:S(2)}) collective-permute-start(f32[2,2,128,128]{3,2,0,1:T(8,128)S(1)} %bitcast.147), channel_id=1, source_target_pairs={{0,64},{8,72},{16,80},{24,88},{32,96},{40,104},{48,112},{56,120},{... | collective-permute-start | bytes 786440 | tf_op jit(solution)/shard_map/ppermute | solution.py:121
  144.9 7.7 %collective-permute-start.23 = (f32[2,2,128,128]{3,2,0,1:T(8,128)S(1)}, f32[2,2,128,128]{3,2,0,1:T(8,128)S(1)}, u32[]{:S(2)}, u32[]{:S(2)}) collective-permute-start(f32[2,2,128,128]{3,2,0,1:T(8,128)S(1)} %bitcast_add_fusion.14), channel_id=1, source_target_pairs={{0,16},{8,24},{16,32},{24,40},{32,48},{40,56},{48,0},{56,8},{64,80... | collective-permute-start | bytes 786440 | tf_op jit(solution)/shard_map/ppermute | solution.py:121
  152.1 10.0 %collective-permute-start.14 = (f32[2,2,128,128]{3,2,0,1:T(8,128)S(1)}, f32[2,2,128,128]{3,2,0,1:T(8,128)S(1)}, u32[]{:S(2)}, u32[]{:S(2)}) collective-permute-start(f32[2,2,128,128]{3,2,0,1:T(8,128)S(1)} %bitcast_add_fusion.17), channel_id=1, source_target_pairs={{0,64},{8,72},{16,80},{24,88},{32,96},{40,104},{48,112},{56,120},{... | collective-permute-start | bytes 786440 | tf_op jit(solution)/shard_map/ppermute | solution.py:121
  152.6 9.7 %collective-permute-start.24 = (f32[2,2,128,128]{3,2,0,1:T(8,128)S(1)}, f32[2,2,128,128]{3,2,0,1:T(8,128)S(1)}, u32[]{:S(2)}, u32[]{:S(2)}) collective-permute-start(f32[2,2,128,128]{3,2,0,1:T(8,128)S(1)} %bitcast_add_fusion.13), channel_id=1, source_target_pairs={{0,16},{8,24},{16,32},{24,40},{32,48},{40,56},{48,0},{56,8},{64,80... | collective-permute-start | bytes 786440 | tf_op jit(solution)/shard_map/ppermute | solution.py:121
  162.2 7.7 %collective-permute-start.15 = (f32[2,2,128,128]{3,2,0,1:T(8,128)S(1)}, f32[2,2,128,128]{3,2,0,1:T(8,128)S(1)}, u32[]{:S(2)}, u32[]{:S(2)}) collective-permute-start(f32[2,2,128,128]{3,2,0,1:T(8,128)S(1)} %bitcast_add_fusion.16), channel_id=1, source_target_pairs={{0,64},{8,72},{16,80},{24,88},{32,96},{40,104},{48,112},{56,120},{... | collective-permute-start | bytes 786440 | tf_op jit(solution)/shard_map/ppermute | solution.py:121
  169.9 13.2 %collective-permute-start.25 = (f32[4,128,128]{2,1,0:T(8,128)S(1)}, f32[4,128,128]{2,1,0:T(8,128)S(1)}, u32[]{:S(2)}, u32[]{:S(2)}) collective-permute-start(f32[4,128,128]{2,1,0:T(8,128)S(1)} %fusion.13), channel_id=1, source_target_pairs={{0,8},{8,0},{16,24},{24,16},{32,40},{40,32},{48,56},{56,48},{64,72... | collective-permute-start | bytes 786440 | tf_op jit(solution)/shard_map/ppermute | solution.py:130

commit v9 on v8

--- a/solution.py
+++ b/solution.py
@@ -123,6 +123,15 @@
     return send
 
 
+def direct_reduce_scatter(data, axis, dim, coord):
+    size = BLK_DIMS[dim]
+    total = lax.dynamic_index_in_dim(data, coord, axis, keepdims=False)
+    for shift in range(1, size):
+        piece = lax.dynamic_index_in_dim(data, (coord + shift) % size, axis, keepdims=False)
+        total = total + lax.ppermute(piece, "blk", _shift_route(dim, shift))
+    return total
+
+
 def pair_reduce_scatter(data, axis, coord):
     route = _shift_route(2, 1)
     other = lax.dynamic_index_in_dim(data, 1 - coord, axis, keepdims=False)
@@ -190,8 +199,8 @@
         else:
             firsts.append(ring_reduce_scatter(data, 0, 0, direction, my_y))
     half = CS // 2
-    along_y = ring_reduce_scatter(jnp.stack(firsts[:half]), 1, 0, 1, my_y)
-    along_x = ring_reduce_scatter(jnp.stack(firsts[half:]), 1, 1, 1, my_x)
+    along_y = direct_reduce_scatter(jnp.stack(firsts[:half]), 1, 0, my_y)
+    along_x = direct_reduce_scatter(jnp.stack(firsts[half:]), 1, 1, my_x)
     results = jnp.concatenate([along_y, along_x])
     summed = pair_reduce_scatter(results, 1, my_z)
     return summed.astype(jnp.bfloat16).reshape(1, 1, CS, block, block)

time: 184 us -> 174 us (0.946)
  waiting for transfers between devices: 93.5 us -> 70.6 us
  starting transfers between devices: 45.1 us -> 56.2 us
    ppermute x18 -> x12, waiting for transfers between devices: 53.4 us -> 21.8 us  [ring_reduce_scatter(): arrived = lax.ppermute(send, 'blk', route)]
    ppermute x0 -> x6, starting transfers between devices: none -> 12.1 us  [direct_reduce_scatter(): total = total + lax.ppermute(piece, 'blk', _shift_route(dim, shift))]
    ppermute x0 -> x6, waiting for transfers between devices: none -> 7.53 us  [direct_reduce_scatter(): total = total + lax.ppermute(piece, 'blk', _shift_route(dim, shift))]
    ppermute x18 -> x12, starting transfers between devices: 22.3 us -> 21.2 us  [ring_reduce_scatter(): arrived = lax.ppermute(send, 'blk', route)]
  transfers between devices with their start and end apart: 26 -> 26, of which waited for: 19 -> 16; matrix products, arithmetic and copies ran while one was open for 4% -> 5% of each run, Pallas kernels for 0% -> 0%
where the time goes in v9:
time: 174 us; the launch traced here: 173 us
  waiting for transfers between devices  70.6 us (41%)
  starting transfers between devices  56.2 us (32%)
  Pallas kernels  26.4 us (15%)
  local copies, waits for them, and re-layouts  11.8 us (7%)
  other arithmetic  7.27 us (4%)
    ppermute x3, waiting for transfers between devices, line_all_gather(): send_up = lax.ppermute(send_up, 'grp', up)  26.6 us
    pallas_call x1, Pallas kernels, owner_partials(): pl.pallas_call(_products_kernel, out_shape=[jax.ShapeDtypeStruct((owners,...  26.4 us
    ppermute x12, waiting for transfers between devices, ring_reduce_scatter(): arrived = lax.ppermute(send, 'blk', route)  21.8 us
    ppermute x12, starting transfers between devices, ring_reduce_scatter(): arrived = lax.ppermute(send, 'blk', route)  21.2 us
    ppermute x6, starting transfers between devices, direct_reduce_scatter(): total = total + lax.ppermute(piece, 'blk', _shift_route(dim, shift))  12.1 us
    ppermute x3, starting transfers between devices, line_all_gather(): send_up = lax.ppermute(send_up, 'grp', up)  11.4 us
    ppermute x1, waiting for transfers between devices, pair_reduce_scatter(): return lax.ppermute(other, 'blk', route) + mine  9 us
    ppermute x6, waiting for transfers between devices, direct_reduce_scatter(): total = total + lax.ppermute(piece, 'blk', _shift_route(dim, shift))  7.53 us
  transfers between devices with their start and end apart: 26, of which 16 were waited for; matrix products, arithmetic and copies ran while one was open for 5% of the time, Pallas kernels for 0%

profile of v9, /device:TPU:32, one launch (start us, length us, event | category | flops | bytes accessed | tf_op | source)
XLA Modules:
  0.0 172.6 jit_solution(15809120901054734273)
XLA Ops:
  0.0 3.8 %collective-permute-start = (bf16[16,128,128]{2,1,0:T(8,128)(2,1)}, bf16[16,128,128]{2,1,0:T(8,128)(2,1)S(1)}, u32[]{:S(2)}, u32[]{:S(2)}) collective-permute-start(bf16[16,128,128]{2,1,0:T(8,128)(2,1)} %param.6), channel_id=1, source_target_pairs={{0,2},{1,3},{2,4},{3,5},{4,6},{5,7},{8,10},{9,11},{10,12},{11,13},... | collective-permute-start | bytes 1572872 | tf_op jit(solution)/shard_map/ppermute | solution.py:154
  3.8 2.0 %collective-permute-start.3 = (bf16[16,128,128]{2,1,0:T(8,128)(2,1)}, bf16[16,128,128]{2,1,0:T(8,128)(2,1)S(1)}, u32[]{:S(2)}, u32[]{:S(2)}) collective-permute-start(bf16[16,128,128]{2,1,0:T(8,128)(2,1)} %param.6), channel_id=1, source_target_pairs={{2,0},{3,1},{4,2},{5,3},{6,4},{7,5},{10,8},{11,9},{12,10},{13,11},... | collective-permute-start | bytes 1572872 | tf_op jit(solution)/shard_map/ppermute | solution.py:155
  5.9 9.9 %collective-permute-done = bf16[16,128,128]{2,1,0:T(8,128)(2,1)S(1)} collective-permute-done((bf16[16,128,128]{2,1,0:T(8,128)(2,1)}, bf16[16,128,128]{2,1,0:T(8,128)(2,1)S(1)}, u32[]{:S(2)}, u32[]{:S(2)}) %collective-permute-start) | collective-permute-done | bytes 524320 | tf_op jit(solution)/shard_map/ppermute | solution.py:154
  15.8 3.8 %collective-permute-start.1 = (bf16[16,128,128]{2,1,0:T(8,128)(2,1)S(1)}, bf16[16,128,128]{2,1,0:T(8,128)(2,1)S(1)}, u32[]{:S(2)}, u32[]{:S(2)}) collective-permute-start(bf16[16,128,128]{2,1,0:T(8,128)(2,1)S(1)} %collective-permute-done), channel_id=1, source_target_pairs={{0,2},{1,3},{2,4},{3,5},{4,6},{5,7},{8,10},{9,11},{10,12},{11,13},... | collective-permute-start | bytes 1572872 | tf_op jit(solution)/shard_map/ppermute | solution.py:154
  19.6 2.0 %collective-permute-start.4 = (bf16[16,128,128]{2,1,0:T(8,128)(2,1)S(1)}, bf16[16,128,128]{2,1,0:T(8,128)(2,1)S(1)}, u32[]{:S(2)}, u32[]{:S(2)}) collective-permute-start(bf16[16,128,128]{2,1,0:T(8,128)(2,1)S(1)} %collective-permute-done.3), channel_id=1, source_target_pairs={{2,0},{3,1},{4,2},{5,3},{6,4},{7,5},{10,8},{11,9},{12,10},{13,11},... | collective-permute-start | bytes 1572872 | tf_op jit(solution)/shard_map/ppermute | solution.py:155
  21.6 8.8 %collective-permute-done.1 = bf16[16,128,128]{2,1,0:T(8,128)(2,1)S(1)} collective-permute-done((bf16[16,128,128]{2,1,0:T(8,128)(2,1)S(1)}, bf16[16,128,128]{2,1,0:T(8,128)(2,1)S(1)}, u32[]{:S(2)}, u32[]{:S(2)}) %collective-permute-start.1) | collective-permute-done | bytes 524320 | tf_op jit(solution)/shard_map/ppermute | solution.py:154
  30.4 3.8 %collective-permute-start.2 = (bf16[16,128,128]{2,1,0:T(8,128)(2,1)S(1)}, bf16[16,128,128]{2,1,0:T(8,128)(2,1)S(1)}, u32[]{:S(2)}, u32[]{:S(2)}) collective-permute-start(bf16[16,128,128]{2,1,0:T(8,128)(2,1)S(1)} %collective-permute-done.1), channel_id=1, source_target_pairs={{0,2},{1,3},{2,4},{3,5},{4,6},{5,7},{8,10},{9,11},{10,12},{11,13},... | collective-permute-start | bytes 1572872 | tf_op jit(solution)/shard_map/ppermute | solution.py:154
  34.3 2.0 %collective-permute-start.5 = (bf16[16,128,128]{2,1,0:T(8,128)(2,1)S(1)}, bf16[16,128,128]{2,1,0:T(8,128)(2,1)S(1)}, u32[]{:S(2)}, u32[]{:S(2)}) collective-permute-start(bf16[16,128,128]{2,1,0:T(8,128)(2,1)S(1)} %collective-permute-done.4), channel_id=1, source_target_pairs={{2,0},{3,1},{4,2},{5,3},{6,4},{7,5},{10,8},{11,9},{12,10},{13,11},... | collective-permute-start | bytes 1572872 | tf_op jit(solution)/shard_map/ppermute | solution.py:155
  36.4 7.9 %collective-permute-done.2 = bf16[16,128,128]{2,1,0:T(8,128)(2,1)S(1)} collective-permute-done((bf16[16,128,128]{2,1,0:T(8,128)(2,1)S(1)}, bf16[16,128,128]{2,1,0:T(8,128)(2,1)S(1)}, u32[]{:S(2)}, u32[]{:S(2)}) %collective-permute-start.2) | collective-permute-done | bytes 524320 | tf_op jit(solution)/shard_map/ppermute | solution.py:154
  44.5 3.6 %collective-permute-done.5 = bf16[16,128,128]{2,1,0:T(8,128)(2,1)S(1)} collective-permute-done((bf16[16,128,128]{2,1,0:T(8,128)(2,1)S(1)}, bf16[16,128,128]{2,1,0:T(8,128)(2,1)S(1)}, u32[]{:S(2)}, u32[]{:S(2)}) %collective-permute-start.5) | collective-permute-done | bytes 524320 | tf_op jit(solution)/shard_map/ppermute | solution.py:155
  48.5 1.6 pad_maximum_fusion.1
  50.3 0.6 gather_fusion
  50.9 0.6 gather_fusion.1
  51.6 0.6 gather_fusion.2
  52.6 2.1 %collective-permute-done.6 = bf16[4,16,128,128]{3,2,1,0:T(8,128)(2,1)} collective-permute-done((bf16[4,16,128,128]{3,2,1,0:T(8,128)(2,1)}, bf16[4,16,128,128]{3,2,1,0:T(8,128)(2,1)}, u32[]{:S(2)}, u32[]{:S(2)}) %collective-permute-start.6) | collective-permute-done | bytes 2097184 | tf_op jit(solution)/shard_map/ppermute | solution.py:173
  54.6 1.8 %select_bitcast_fusion.1 = (bf16[4,1,16,128,128]{4,3,2,0,1:T(8,128)(2,1)S(1)}, bf16[4,1,16,128,128]{4,3,2,0,1:T(8,128)(2,1)S(1)}) fusion(bf16[4,16,128,128]{3,2,1,0:T(8,128)(2,1)} %collective-permute-done.6, pred[]{:T(512)S(6)} %eq.45, bf16[1,16,128,128]{3,2,1,0:T(8,128)(2,1)S(1)} %get-tuple-element.18, bf16[1,16,128,128]{3,2,1,0:T(8,128)(2,1)S(1)} %get-tuple-element.19, ...), kind=kLoop, calls=%fused_computation.6 | loop fusion | flops 5242880 | bytes 8388609 | tf_op jit(solution)/shard_map/stack | solution.py:176
  56.4 0.4 pad_maximum_fusion
  56.8 2.3 %copy.20 = bf16[4,2,16,128,128]{4,3,2,1,0:T(8,128)(2,1)} copy(bf16[4,2,16,128,128]{4,3,2,0,1:T(8,128)(2,1)S(1)} %pad_maximum_fusion) | data formatting | bytes 8388608 | tf_op jit(solution)/shard_map/stack | solution.py:176
  59.1 26.4 %shard_map.46 = (f32[32,128,128]{2,1,0:T(8,128)S(1)}, f32[32,128,128]{2,1,0:T(8,128)S(1)}, f32[32,128,128]{2,1,0:T(8,128)}, f32[32,128,128]{2,1,0:T(8,128)}) custom-call(s32[384]{0:T(512)S(1)} %reshape.88.left_ref, s32[384]{0:T(512)S(1)} %reshape.89.right_ref, s32[384]{0:T(512)S(1)} %reshape.90.target_ref, bf16[128,128,128]{2,1,0:T(8,128)(2,1)} %bitcast.140), custom_call_target="tpu_custom_call" | custom-call | flops 1610612736 | bytes 12582912 | tf_op jit(solution)/shard_map/pallas_call | solution.py:40
  85.5 1.4 copy-done
  86.9 1.9 %dynamic-slice_bitcast_fusion = f32[4,2,128,128]{3,2,1,0:T(8,128)} fusion(f32[4,4,2,128,128]{4,3,2,1,0:T(8,128)} %bitcast.145, s32[]{:T(128)S(6)} %select_n.317), kind=kLoop, calls=%fused_computation.53 | loop fusion | bytes 1048580 | tf_op jit(solution)/shard_map/reshape | solution.py:107
  88.7 3.0 %collective-permute-start.19 = (f32[4,2,128,128]{3,2,1,0:T(8,128)}, f32[4,2,128,128]{3,2,1,0:T(8,128)S(1)}, u32[]{:S(2)}, u32[]{:S(2)}) collective-permute-start(f32[4,2,128,128]{3,2,1,0:T(8,128)} %dynamic-slice_bitcast_fusion), channel_id=1, source_target_pairs={{0,192},{8,200},{16,208},{24,216},{32,224},{40,232},{48,240},{56,2... | collective-permute-start | bytes 1572872 | tf_op jit(solution)/shard_map/ppermute | solution.py:121
  91.7 1.9 %dynamic-slice_bitcast_fusion.1 = f32[4,2,128,128]{3,2,1,0:T(8,128)} fusion(f32[4,4,2,128,128]{4,3,2,1,0:T(8,128)} %bitcast.141, s32[]{:T(128)S(6)} %select_n.323), kind=kLoop, calls=%fused_computation.54 | loop fusion | bytes 1048580 | tf_op jit(solution)/shard_map/reshape | solution.py:107
  93.6 1.2 dynamic-slice_bitcast_fusion.2
  94.9 2.8 %collective-permute-start.10 = (f32[4,2,128,128]{3,2,1,0:T(8,128)S(1)}, f32[4,2,128,128]{3,2,1,0:T(8,128)S(1)}, u32[]{:S(2)}, u32[]{:S(2)}) collective-permute-start(f32[4,2,128,128]{3,2,1,0:T(8,128)S(1)} %dynamic-slice_bitcast_fusion.2), channel_id=1, source_target_pairs={{0,48},{8,56},{16,0},{24,8},{32,16},{40,24},{48,32},{56,40},{64,11... | collective-permute-start | bytes 1572872 | tf_op jit(solution)/shard_map/ppermute | solution.py:121
  97.8 5.7 %collective-permute-done.19 = f32[4,2,128,128]{3,2,1,0:T(8,128)S(1)} collective-permute-done((f32[4,2,128,128]{3,2,1,0:T(8,128)}, f32[4,2,128,128]{3,2,1,0:T(8,128)S(1)}, u32[]{:S(2)}, u32[]{:S(2)}) %collective-permute-start.19) | collective-permute-done | bytes 524320 | tf_op jit(solution)/shard_map/ppermute | solution.py:121
  103.5 1.1 bitcast_add_fusion.2
  104.7 3.7 %collective-permute-start.20 = (f32[4,2,128,128]{3,2,1,0:T(8,128)S(1)}, f32[4,2,128,128]{3,2,1,0:T(8,128)S(1)}, u32[]{:S(2)}, u32[]{:S(2)}) collective-permute-start(f32[4,2,128,128]{3,2,1,0:T(8,128)S(1)} %bitcast_add_fusion.2), channel_id=1, source_target_pairs={{0,192},{8,200},{16,208},{24,216},{32,224},{40,232},{48,240},{56,2... | collective-permute-start | bytes 1572872 | tf_op jit(solution)/shard_map/ppermute | solution.py:121
  108.3 0.4 collective-permute-done.16
  109.0 3.8 %collective-permute-start.11 = (f32[4,2,128,128]{3,2,1,0:T(8,128)S(1)}, f32[4,2,128,128]{3,2,1,0:T(8,128)S(1)}, u32[]{:S(2)}, u32[]{:S(2)}) collective-permute-start(f32[4,2,128,128]{3,2,1,0:T(8,128)S(1)} %bitcast_add_fusion.8), channel_id=1, source_target_pairs={{0,48},{8,56},{16,0},{24,8},{32,16},{40,24},{48,32},{56,40},{64,11... | collective-permute-start | bytes 1572872 | tf_op jit(solution)/shard_map/ppermute | solution.py:121
  112.9 6.1 %collective-permute-done.20 = f32[4,2,128,128]{3,2,1,0:T(8,128)S(1)} collective-permute-done((f32[4,2,128,128]{3,2,1,0:T(8,128)S(1)}, f32[4,2,128,128]{3,2,1,0:T(8,128)S(1)}, u32[]{:S(2)}, u32[]{:S(2)}) %collective-permute-start.20) | collective-permute-done | bytes 524320 | tf_op jit(solution)/shard_map/ppermute | solution.py:121
  119.0 3.8 %collective-permute-start.21 = (f32[4,2,128,128]{3,2,1,0:T(8,128)S(1)}, f32[4,2,128,128]{3,2,1,0:T(8,128)S(1)}, u32[]{:S(2)}, u32[]{:S(2)}) collective-permute-start(f32[4,2,128,128]{3,2,1,0:T(8,128)S(1)} %bitcast_add_fusion.1), channel_id=1, source_target_pairs={{0,192},{8,200},{16,208},{24,216},{32,224},{40,232},{48,240},{56,2... | collective-permute-start | bytes 1572872 | tf_op jit(solution)/shard_map/ppermute | solution.py:121
  123.4 3.6 %collective-permute-start.12 = (f32[4,2,128,128]{3,2,1,0:T(8,128)S(1)}, f32[4,2,128,128]{3,2,1,0:T(8,128)S(1)}, u32[]{:S(2)}, u32[]{:S(2)}) collective-permute-start(f32[4,2,128,128]{3,2,1,0:T(8,128)S(1)} %bitcast_add_fusion.7), channel_id=1, source_target_pairs={{0,48},{8,56},{16,0},{24,8},{32,16},{40,24},{48,32},{56,40},{64,11... | collective-permute-start | bytes 1572872 | tf_op jit(solution)/shard_map/ppermute | solution.py:121
  127.1 5.5 %collective-permute-done.21 = f32[4,2,128,128]{3,2,1,0:T(8,128)S(1)} collective-permute-done((f32[4,2,128,128]{3,2,1,0:T(8,128)S(1)}, f32[4,2,128,128]{3,2,1,0:T(8,128)S(1)}, u32[]{:S(2)}, u32[]{:S(2)}) %collective-permute-start.21) | collective-permute-done | bytes 524320 | tf_op jit(solution)/shard_map/ppermute | solution.py:121
  132.6 3.8 %collective-permute-done.18 = f32[4,2,128,128]{3,2,1,0:T(8,128)S(1)} collective-permute-done((f32[4,2,128,128]{3,2,1,0:T(8,128)S(1)}, f32[4,2,128,128]{3,2,1,0:T(8,128)S(1)}, u32[]{:S(2)}, u32[]{:S(2)}) %collective-permute-start.18) | collective-permute-done | bytes 524320 | tf_op jit(solution)/shard_map/ppermute | solution.py:121
  136.7 1.6 collective-permute-start.22
  138.2 2.8 %collective-permute-start.23 = (f32[2,2,128,128]{3,2,0,1:T(8,128)S(1)}, f32[2,2,128,128]{3,2,0,1:T(8,128)S(1)}, u32[]{:S(2)}, u32[]{:S(2)}) collective-permute-start(f32[2,2,128,128]{3,2,0,1:T(8,128)S(1)} %bitcast.158), channel_id=1, source_target_pairs={{0,32},{8,40},{16,48},{24,56},{32,0},{40,8},{48,16},{56,24},{64,96... | collective-permute-start | bytes 786440 | tf_op jit(solution)/shard_map/ppermute | solution.py:131
  141.0 0.7 copy.37
  141.8 1.4 collective-permute-start.24
  143.6 0.5 collective-permute-start.13
  144.2 3.4 %collective-permute-start.14 = (f32[2,2,128,128]{3,2,0,1:T(8,128)S(1)}, f32[2,2,128,128]{3,2,0,1:T(8,128)S(1)}, u32[]{:S(2)}, u32[]{:S(2)}) collective-permute-start(f32[2,2,128,128]{3,2,0,1:T(8,128)S(1)} %bitcast.161), channel_id=1, source_target_pairs={{0,128},{8,136},{16,144},{24,152},{32,160},{40,168},{48,176},{56,1... | collective-permute-start | bytes 786440 | tf_op jit(solution)/shard_map/ppermute | solution.py:131
  147.6 3.6 %collective-permute-done.22 = f32[2,2,128,128]{3,2,0,1:T(8,128)S(1)} collective-permute-done((f32[2,2,128,128]{3,2,0,1:T(8,128)S(1)}, f32[2,2,128,128]{3,2,0,1:T(8,128)S(1)}, u32[]{:S(2)}, u32[]{:S(2)}) %collective-permute-start.22) | collective-permute-done | bytes 262176 | tf_op jit(solution)/shard_map/ppermute | solution.py:131
  151.2 2.4 %collective-permute-start.15 = (f32[2,2,128,128]{3,2,0,1:T(8,128)S(1)}, f32[2,2,128,128]{3,2,0,1:T(8,128)S(1)}, u32[]{:S(2)}, u32[]{:S(2)}) collective-permute-start(f32[2,2,128,128]{3,2,0,1:T(8,128)S(1)} %bitcast.162), channel_id=1, source_target_pairs={{0,192},{8,200},{16,208},{24,216},{32,224},{40,232},{48,240},{56,2... | collective-permute-start | bytes 786440 | tf_op jit(solution)/shard_map/ppermute | solution.py:131
  153.7 1.4 collective-permute-done.13
  155.0 2.5 %collective-permute-done.15 = f32[2,2,128,128]{3,2,0,1:T(8,128)S(1)} collective-permute-done((f32[2,2,128,128]{3,2,0,1:T(8,128)S(1)}, f32[2,2,128,128]{3,2,0,1:T(8,128)S(1)}, u32[]{:S(2)}, u32[]{:S(2)}) %collective-permute-start.15) | collective-permute-done | bytes 262176 | tf_op jit(solution)/shard_map/ppermute | solution.py:131
  157.7 5.3 %collective-permute-start.25 = (f32[4,128,128]{2,1,0:T(8,128)S(1)}, f32[4,128,128]{2,1,0:T(8,128)S(1)}, u32[]{:S(2)}, u32[]{:S(2)}) collective-permute-start(f32[4,128,128]{2,1,0:T(8,128)S(1)} %fusion.13), channel_id=1, source_target_pairs={{0,8},{8,0},{16,24},{24,16},{32,40},{40,32},{48,56},{56,48},{64,72... | collective-permute-start | bytes 786440 | tf_op jit(solution)/shard_map/ppermute | solution.py:139
  162.9 9.0 %collective-permute-done.25 = f32[4,128,128]{2,1,0:T(8,128)S(1)} collective-permute-done((f32[4,128,128]{2,1,0:T(8,128)S(1)}, f32[4,128,128]{2,1,0:T(8,128)S(1)}, u32[]{:S(2)}, u32[]{:S(2)}) %collective-permute-start.25) | collective-permute-done | bytes 262176 | tf_op jit(solution)/shard_map/ppermute | solution.py:139
  171.9 0.7 fusion.26
  (69 shorter events, 3.4 us)
Async XLA Ops:
  0.0 15.8 %collective-permute-start = (bf16[16,128,128]{2,1,0:T(8,128)(2,1)}, bf16[16,128,128]{2,1,0:T(8,128)(2,1)S(1)}, u32[]{:S(2)}, u32[]{:S(2)}) collective-permute-start(bf16[16,128,128]{2,1,0:T(8,128)(2,1)} %param.6), channel_id=1, source_target_pairs={{0,2},{1,3},{2,4},{3,5},{4,6},{5,7},{8,10},{9,11},{10,12},{11,13},... | collective-permute-start | bytes 1572872 | tf_op jit(solution)/shard_map/ppermute | solution.py:154
  3.8 15.8 %collective-permute-start.3 = (bf16[16,128,128]{2,1,0:T(8,128)(2,1)}, bf16[16,128,128]{2,1,0:T(8,128)(2,1)S(1)}, u32[]{:S(2)}, u32[]{:S(2)}) collective-permute-start(bf16[16,128,128]{2,1,0:T(8,128)(2,1)} %param.6), channel_id=1, source_target_pairs={{2,0},{3,1},{4,2},{5,3},{6,4},{7,5},{10,8},{11,9},{12,10},{13,11},... | collective-permute-start | bytes 1572872 | tf_op jit(solution)/shard_map/ppermute | solution.py:155
  15.8 14.7 %collective-permute-start.1 = (bf16[16,128,128]{2,1,0:T(8,128)(2,1)S(1)}, bf16[16,128,128]{2,1,0:T(8,128)(2,1)S(1)}, u32[]{:S(2)}, u32[]{:S(2)}) collective-permute-start(bf16[16,128,128]{2,1,0:T(8,128)(2,1)S(1)} %collective-permute-done), channel_id=1, source_target_pairs={{0,2},{1,3},{2,4},{3,5},{4,6},{5,7},{8,10},{9,11},{10,12},{11,13},... | collective-permute-start | bytes 1572872 | tf_op jit(solution)/shard_map/ppermute | solution.py:154
  19.6 14.7 %collective-permute-start.4 = (bf16[16,128,128]{2,1,0:T(8,128)(2,1)S(1)}, bf16[16,128,128]{2,1,0:T(8,128)(2,1)S(1)}, u32[]{:S(2)}, u32[]{:S(2)}) collective-permute-start(bf16[16,128,128]{2,1,0:T(8,128)(2,1)S(1)} %collective-permute-done.3), channel_id=1, source_target_pairs={{2,0},{3,1},{4,2},{5,3},{6,4},{7,5},{10,8},{11,9},{12,10},{13,11},... | collective-permute-start | bytes 1572872 | tf_op jit(solution)/shard_map/ppermute | solution.py:155
  30.4 13.8 %collective-permute-start.2 = (bf16[16,128,128]{2,1,0:T(8,128)(2,1)S(1)}, bf16[16,128,128]{2,1,0:T(8,128)(2,1)S(1)}, u32[]{:S(2)}, u32[]{:S(2)}) collective-permute-start(bf16[16,128,128]{2,1,0:T(8,128)(2,1)S(1)} %collective-permute-done.1), channel_id=1, source_target_pairs={{0,2},{1,3},{2,4},{3,5},{4,6},{5,7},{8,10},{9,11},{10,12},{11,13},... | collective-permute-start | bytes 1572872 | tf_op jit(solution)/shard_map/ppermute | solution.py:154
  34.3 13.8 %collective-permute-start.5 = (bf16[16,128,128]{2,1,0:T(8,128)(2,1)S(1)}, bf16[16,128,128]{2,1,0:T(8,128)(2,1)S(1)}, u32[]{:S(2)}, u32[]{:S(2)}) collective-permute-start(bf16[16,128,128]{2,1,0:T(8,128)(2,1)S(1)} %collective-permute-done.4), channel_id=1, source_target_pairs={{2,0},{3,1},{4,2},{5,3},{6,4},{7,5},{10,8},{11,9},{12,10},{13,11},... | collective-permute-start | bytes 1572872 | tf_op jit(solution)/shard_map/ppermute | solution.py:155
  44.5 3.8 %copy-start.4 = (bf16[16,128,128]{2,1,0:T(8,128)(2,1)S(1)}, bf16[16,128,128]{2,1,0:T(8,128)(2,1)}, u32[]{:S(2)}) copy-start(bf16[16,128,128]{2,1,0:T(8,128)(2,1)} %param.6) | copy-start | bytes 1572868
  48.5 1.7 copy-start.5
  48.5 1.7 %copy-start.6 = (s32[1,1,32,12]{2,1,3,0:T(1,128)S(1)}, s32[1,1,32,12]{2,1,3,0:T(1,128)}, u32[]{:S(2)}) copy-start(s32[1,1,32,12]{2,1,3,0:T(1,128)} %param.8) | copy-start | bytes 4612
  48.5 3.0 %copy-start.7 = (s32[1,1,32,12]{2,1,3,0:T(1,128)S(1)}, s32[1,1,32,12]{2,1,3,0:T(1,128)}, u32[]{:S(2)}) copy-start(s32[1,1,32,12]{2,1,3,0:T(1,128)} %param.9) | copy-start | bytes 4612
  50.1 4.5 %collective-permute-start.6 = (bf16[4,16,128,128]{3,2,1,0:T(8,128)(2,1)}, bf16[4,16,128,128]{3,2,1,0:T(8,128)(2,1)}, u32[]{:S(2)}, u32[]{:S(2)}) collective-permute-start(bf16[4,16,128,128]{3,2,1,0:T(8,128)(2,1)} %pad_maximum_fusion.1), channel_id=1, source_target_pairs={{0,1},{1,0},{2,3},{3,2},{4,5},{5,4},{6,7},{7,6},{8,9},{9,8},{10,11... | collective-permute-start | bytes 6291464 | tf_op jit(solution)/shard_map/ppermute | solution.py:173
  85.5 1.4 copy-start
  88.7 14.8 %collective-permute-start.19 = (f32[4,2,128,128]{3,2,1,0:T(8,128)}, f32[4,2,128,128]{3,2,1,0:T(8,128)S(1)}, u32[]{:S(2)}, u32[]{:S(2)}) collective-permute-start(f32[4,2,128,128]{3,2,1,0:T(8,128)} %dynamic-slice_bitcast_fusion), channel_id=1, source_target_pairs={{0,192},{8,200},{16,208},{24,216},{32,224},{40,232},{48,240},{56,2... | collective-permute-start | bytes 1572872 | tf_op jit(solution)/shard_map/ppermute | solution.py:121
  93.6 15.1 %collective-permute-start.16 = (f32[4,2,128,128]{3,2,1,0:T(8,128)}, f32[4,2,128,128]{3,2,1,0:T(8,128)S(1)}, u32[]{:S(2)}, u32[]{:S(2)}) collective-permute-start(f32[4,2,128,128]{3,2,1,0:T(8,128)} %dynamic-slice_bitcast_fusion.1), channel_id=1, source_target_pairs={{0,64},{8,72},{16,80},{24,88},{32,96},{40,104},{48,112},{56,120},{... | collective-permute-start | bytes 1572872 | tf_op jit(solution)/shard_map/ppermute | solution.py:121
  93.6 15.1 %copy-start.2 = (f32[32,128,128]{2,1,0:T(8,128)S(1)}, f32[32,128,128]{2,1,0:T(8,128)}, u32[]{:S(2)}) copy-start(f32[32,128,128]{2,1,0:T(8,128)} %get-tuple-element.12) | copy-start | bytes 6291460
  94.9 14.0 %collective-permute-start.10 = (f32[4,2,128,128]{3,2,1,0:T(8,128)S(1)}, f32[4,2,128,128]{3,2,1,0:T(8,128)S(1)}, u32[]{:S(2)}, u32[]{:S(2)}) collective-permute-start(f32[4,2,128,128]{3,2,1,0:T(8,128)S(1)} %dynamic-slice_bitcast_fusion.2), channel_id=1, source_target_pairs={{0,48},{8,56},{16,0},{24,8},{32,16},{40,24},{48,32},{56,40},{64,11... | collective-permute-start | bytes 1572872 | tf_op jit(solution)/shard_map/ppermute | solution.py:121
  97.7 11.2 %copy-start.1 = (f32[32,128,128]{2,1,0:T(8,128)S(1)}, f32[32,128,128]{2,1,0:T(8,128)}, u32[]{:S(2)}) copy-start(f32[32,128,128]{2,1,0:T(8,128)} %copy-done) | copy-start | bytes 6291460
  97.7 15.0 %collective-permute-start.7 = (f32[4,2,128,128]{3,2,1,0:T(8,128)S(1)}, f32[4,2,128,128]{3,2,1,0:T(8,128)S(1)}, u32[]{:S(2)}, u32[]{:S(2)}) collective-permute-start(f32[4,2,128,128]{3,2,1,0:T(8,128)S(1)} %dynamic-slice_bitcast_fusion.3), channel_id=1, source_target_pairs={{0,16},{8,24},{16,32},{24,40},{32,48},{40,56},{48,0},{56,8},{64,80... | collective-permute-start | bytes 1572872 | tf_op jit(solution)/shard_map/ppermute | solution.py:121
  104.6 14.3 %copy-start.3 = (f32[32,128,128]{2,1,0:T(8,128)S(1)}, f32[32,128,128]{2,1,0:T(8,128)}, u32[]{:S(2)}) copy-start(f32[32,128,128]{2,1,0:T(8,128)} %get-tuple-element.13) | copy-start | bytes 6291460
  104.7 14.3 %collective-permute-start.20 = (f32[4,2,128,128]{3,2,1,0:T(8,128)S(1)}, f32[4,2,128,128]{3,2,1,0:T(8,128)S(1)}, u32[]{:S(2)}, u32[]{:S(2)}) collective-permute-start(f32[4,2,128,128]{3,2,1,0:T(8,128)S(1)} %bitcast_add_fusion.2), channel_id=1, source_target_pairs={{0,192},{8,200},{16,208},{24,216},{32,224},{40,232},{48,240},{56,2... | collective-permute-start | bytes 1572872 | tf_op jit(solution)/shard_map/ppermute | solution.py:121
  108.8 14.1 %collective-permute-start.17 = (f32[4,2,128,128]{3,2,1,0:T(8,128)S(1)}, f32[4,2,128,128]{3,2,1,0:T(8,128)S(1)}, u32[]{:S(2)}, u32[]{:S(2)}) collective-permute-start(f32[4,2,128,128]{3,2,1,0:T(8,128)S(1)} %bitcast_add_fusion.5), channel_id=1, source_target_pairs={{0,64},{8,72},{16,80},{24,88},{32,96},{40,104},{48,112},{56,120},{... | collective-permute-start | bytes 1572872 | tf_op jit(solution)/shard_map/ppermute | solution.py:121
  109.0 14.3 %collective-permute-start.11 = (f32[4,2,128,128]{3,2,1,0:T(8,128)S(1)}, f32[4,2,128,128]{3,2,1,0:T(8,128)S(1)}, u32[]{:S(2)}, u32[]{:S(2)}) collective-permute-start(f32[4,2,128,128]{3,2,1,0:T(8,128)S(1)} %bitcast_add_fusion.8), channel_id=1, source_target_pairs={{0,48},{8,56},{16,0},{24,8},{32,16},{40,24},{48,32},{56,40},{64,11... | collective-permute-start | bytes 1572872 | tf_op jit(solution)/shard_map/ppermute | solution.py:121
  112.8 14.1 %collective-permute-start.8 = (f32[4,2,128,128]{3,2,1,0:T(8,128)S(1)}, f32[4,2,128,128]{3,2,1,0:T(8,128)S(1)}, u32[]{:S(2)}, u32[]{:S(2)}) collective-permute-start(f32[4,2,128,128]{3,2,1,0:T(8,128)S(1)} %bitcast_add_fusion.11), channel_id=1, source_target_pairs={{0,16},{8,24},{16,32},{24,40},{32,48},{40,56},{48,0},{56,8},{64,80... | collective-permute-start | bytes 1572872 | tf_op jit(solution)/shard_map/ppermute | solution.py:121
  119.0 13.5 %collective-permute-start.21 = (f32[4,2,128,128]{3,2,1,0:T(8,128)S(1)}, f32[4,2,128,128]{3,2,1,0:T(8,128)S(1)}, u32[]{:S(2)}, u32[]{:S(2)}) collective-permute-start(f32[4,2,128,128]{3,2,1,0:T(8,128)S(1)} %bitcast_add_fusion.1), channel_id=1, source_target_pairs={{0,192},{8,200},{16,208},{24,216},{32,224},{40,232},{48,240},{56,2... | collective-permute-start | bytes 1572872 | tf_op jit(solution)/shard_map/ppermute | solution.py:121
  123.0 13.4 %collective-permute-start.18 = (f32[4,2,128,128]{3,2,1,0:T(8,128)S(1)}, f32[4,2,128,128]{3,2,1,0:T(8,128)S(1)}, u32[]{:S(2)}, u32[]{:S(2)}) collective-permute-start(f32[4,2,128,128]{3,2,1,0:T(8,128)S(1)} %bitcast_add_fusion.4), channel_id=1, source_target_pairs={{0,64},{8,72},{16,80},{24,88},{32,96},{40,104},{48,112},{56,120},{... | collective-permute-start | bytes 1572872 | tf_op jit(solution)/shard_map/ppermute | solution.py:121
  123.4 19.8 %collective-permute-start.12 = (f32[4,2,128,128]{3,2,1,0:T(8,128)S(1)}, f32[4,2,128,128]{3,2,1,0:T(8,128)S(1)}, u32[]{:S(2)}, u32[]{:S(2)}) collective-permute-start(f32[4,2,128,128]{3,2,1,0:T(8,128)S(1)} %bitcast_add_fusion.7), channel_id=1, source_target_pairs={{0,48},{8,56},{16,0},{24,8},{32,16},{40,24},{48,32},{56,40},{64,11... | collective-permute-start | bytes 1572872 | tf_op jit(solution)/shard_map/ppermute | solution.py:121
  127.0 16.5 %collective-permute-start.9 = (f32[4,2,128,128]{3,2,1,0:T(8,128)S(1)}, f32[4,2,128,128]{3,2,1,0:T(8,128)S(1)}, u32[]{:S(2)}, u32[]{:S(2)}) collective-permute-start(f32[4,2,128,128]{3,2,1,0:T(8,128)S(1)} %bitcast_add_fusion.10), channel_id=1, source_target_pairs={{0,16},{8,24},{16,32},{24,40},{32,48},{40,56},{48,0},{56,8},{64,80... | collective-permute-start | bytes 1572872 | tf_op jit(solution)/shard_map/ppermute | solution.py:121
  136.7 14.5 %collective-permute-start.22 = (f32[2,2,128,128]{3,2,0,1:T(8,128)S(1)}, f32[2,2,128,128]{3,2,0,1:T(8,128)S(1)}, u32[]{:S(2)}, u32[]{:S(2)}) collective-permute-start(f32[2,2,128,128]{3,2,0,1:T(8,128)S(1)} %bitcast.159), channel_id=1, source_target_pairs={{0,16},{8,24},{16,32},{24,40},{32,48},{40,56},{48,0},{56,8},{64,80... | collective-permute-start | bytes 786440 | tf_op jit(solution)/shard_map/ppermute | solution.py:131
  138.2 15.4 %collective-permute-start.23 = (f32[2,2,128,128]{3,2,0,1:T(8,128)S(1)}, f32[2,2,128,128]{3,2,0,1:T(8,128)S(1)}, u32[]{:S(2)}, u32[]{:S(2)}) collective-permute-start(f32[2,2,128,128]{3,2,0,1:T(8,128)S(1)} %bitcast.158), channel_id=1, source_target_pairs={{0,32},{8,40},{16,48},{24,56},{32,0},{40,8},{48,16},{56,24},{64,96... | collective-permute-start | bytes 786440 | tf_op jit(solution)/shard_map/ppermute | solution.py:131
  141.8 11.8 %collective-permute-start.24 = (f32[2,2,128,128]{3,2,0,1:T(8,128)}, f32[2,2,128,128]{3,2,0,1:T(8,128)S(1)}, u32[]{:S(2)}, u32[]{:S(2)}) collective-permute-start(f32[2,2,128,128]{3,2,0,1:T(8,128)} %bitcast.126), channel_id=1, source_target_pairs={{0,48},{8,56},{16,0},{24,8},{32,16},{40,24},{48,32},{56,40},{64,11... | collective-permute-start | bytes 786440 | tf_op jit(solution)/shard_map/ppermute | solution.py:131
  143.6 11.4 %collective-permute-start.13 = (f32[2,2,128,128]{3,2,0,1:T(8,128)S(1)}, f32[2,2,128,128]{3,2,0,1:T(8,128)S(1)}, u32[]{:S(2)}, u32[]{:S(2)}) collective-permute-start(f32[2,2,128,128]{3,2,0,1:T(8,128)S(1)} %bitcast.160), channel_id=1, source_target_pairs={{0,64},{8,72},{16,80},{24,88},{32,96},{40,104},{48,112},{56,120},{... | collective-permute-start | bytes 786440 | tf_op jit(solution)/shard_map/ppermute | solution.py:131
  144.2 10.9 %collective-permute-start.14 = (f32[2,2,128,128]{3,2,0,1:T(8,128)S(1)}, f32[2,2,128,128]{3,2,0,1:T(8,128)S(1)}, u32[]{:S(2)}, u32[]{:S(2)}) collective-permute-start(f32[2,2,128,128]{3,2,0,1:T(8,128)S(1)} %bitcast.161), channel_id=1, source_target_pairs={{0,128},{8,136},{16,144},{24,152},{32,160},{40,168},{48,176},{56,1... | collective-permute-start | bytes 786440 | tf_op jit(solution)/shard_map/ppermute | solution.py:131
  151.2 6.4 %collective-permute-start.15 = (f32[2,2,128,128]{3,2,0,1:T(8,128)S(1)}, f32[2,2,128,128]{3,2,0,1:T(8,128)S(1)}, u32[]{:S(2)}, u32[]{:S(2)}) collective-permute-start(f32[2,2,128,128]{3,2,0,1:T(8,128)S(1)} %bitcast.162), channel_id=1, source_target_pairs={{0,192},{8,200},{16,208},{24,216},{32,224},{40,232},{48,240},{56,2... | collective-permute-start | bytes 786440 | tf_op jit(solution)/shard_map/ppermute | solution.py:131
  157.7 14.3 %collective-permute-start.25 = (f32[4,128,128]{2,1,0:T(8,128)S(1)}, f32[4,128,128]{2,1,0:T(8,128)S(1)}, u32[]{:S(2)}, u32[]{:S(2)}) collective-permute-start(f32[4,128,128]{2,1,0:T(8,128)S(1)} %fusion.13), channel_id=1, source_target_pairs={{0,8},{8,0},{16,24},{24,16},{32,40},{40,32},{48,56},{56,48},{64,72... | collective-permute-start | bytes 786440 | tf_op jit(solution)/shard_map/ppermute | solution.py:139

commit v10 on v9

--- a/solution.py
+++ b/solution.py
@@ -22,7 +22,7 @@
         r = right_ref[flat]
         t = target_ref[flat]
         prod = lax.dot_general(
-            x_ref[l], x_ref[r], (((0,), (0,)), ((), ())), preferred_element_type=jnp.float32
+            x_ref[l], x_ref[r], (((1,), (1,)), ((), ())), preferred_element_type=jnp.float32
         )
         acc_ref[t, k] += prod
         return carry
@@ -179,7 +179,7 @@
 
 def per_device(x_blocks, pair_left, pair_right, pair_target):
     assert lax.axis_size("grp") == LINE * CORES
-    gathered = line_all_gather(x_blocks)
+    gathered = line_all_gather(jnp.swapaxes(x_blocks, 1, 2))
     group_count = lax.axis_size("blk")
     assert group_count == BLK_DIMS[0] * BLK_DIMS[1] * BLK_DIMS[2]
     me = lax.axis_index("blk")

time: 174 us -> 180 us (1.034)
  local copies, waits for them, and re-layouts: 11.8 us -> 15.7 us
  other arithmetic: 7.27 us -> 9.28 us
    another operation x1, local copies, waits for them, and re-layouts: 2.29 us -> 6.23 us  [line_all_gather(): gathered = jnp.stack([first, second], axis=1)]
    another operation x2, other arithmetic: 2.14 us -> 4.15 us  [line_all_gather(): gathered = jnp.stack([first, second], axis=1)]
where the time goes in v10:
time: 180 us; the launch traced here: 178 us
  waiting for transfers between devices  70.4 us (39%)
  starting transfers between devices  56.2 us (31%)
  Pallas kernels  25.9 us (14%)
  local copies, waits for them, and re-layouts  15.7 us (9%)
  other arithmetic  9.28 us (5%)
    ppermute x3, waiting for transfers between devices, line_all_gather(): send_up = lax.ppermute(send_up, 'grp', up)  26.6 us
    pallas_call x1, Pallas kernels, owner_partials(): pl.pallas_call(_products_kernel, out_shape=[jax.ShapeDtypeStruct((owners,...  25.9 us
    ppermute x12, waiting for transfers between devices, ring_reduce_scatter(): arrived = lax.ppermute(send, 'blk', route)  21.9 us
    ppermute x12, starting transfers between devices, ring_reduce_scatter(): arrived = lax.ppermute(send, 'blk', route)  21.2 us
    ppermute x6, starting transfers between devices, direct_reduce_scatter(): total = total + lax.ppermute(piece, 'blk', _shift_route(dim, shift))  12.1 us
    ppermute x3, starting transfers between devices, line_all_gather(): send_up = lax.ppermute(send_up, 'grp', up)  11.4 us
    ppermute x1, waiting for transfers between devices, pair_reduce_scatter(): return lax.ppermute(other, 'blk', route) + mine  8.85 us
    ppermute x6, waiting for transfers between devices, direct_reduce_scatter(): total = total + lax.ppermute(piece, 'blk', _shift_route(dim, shift))  7.52 us
  transfers between devices with their start and end apart: 26, of which 16 were waited for; matrix products, arithmetic and copies ran while one was open for 5% of the time, Pallas kernels for 0%

profile of v10, /device:TPU:32, one launch (start us, length us, event | category | flops | bytes accessed | tf_op | source)
XLA Modules:
  0.0 177.9 jit_solution(8510688495424302330)
XLA Ops:
  0.0 3.8 %collective-permute-start = (bf16[16,128,128]{1,2,0:T(8,128)(2,1)}, bf16[16,128,128]{1,2,0:T(8,128)(2,1)S(1)}, u32[]{:S(2)}, u32[]{:S(2)}) collective-permute-start(bf16[16,128,128]{1,2,0:T(8,128)(2,1)} %bitcast.163), channel_id=1, source_target_pairs={{0,2},{1,3},{2,4},{3,5},{4,6},{5,7},{8,10},{9,11},{10,12},{11,13},... | collective-permute-start | bytes 1572872 | tf_op jit(solution)/shard_map/ppermute | solution.py:154
  3.8 2.0 %collective-permute-start.3 = (bf16[16,128,128]{1,2,0:T(8,128)(2,1)}, bf16[16,128,128]{1,2,0:T(8,128)(2,1)S(1)}, u32[]{:S(2)}, u32[]{:S(2)}) collective-permute-start(bf16[16,128,128]{1,2,0:T(8,128)(2,1)} %bitcast.164), channel_id=1, source_target_pairs={{2,0},{3,1},{4,2},{5,3},{6,4},{7,5},{10,8},{11,9},{12,10},{13,11},... | collective-permute-start | bytes 1572872 | tf_op jit(solution)/shard_map/ppermute | solution.py:155
  5.9 9.9 %collective-permute-done = bf16[16,128,128]{1,2,0:T(8,128)(2,1)S(1)} collective-permute-done((bf16[16,128,128]{1,2,0:T(8,128)(2,1)}, bf16[16,128,128]{1,2,0:T(8,128)(2,1)S(1)}, u32[]{:S(2)}, u32[]{:S(2)}) %collective-permute-start) | collective-permute-done | bytes 524320 | tf_op jit(solution)/shard_map/ppermute | solution.py:154
  15.8 3.8 %collective-permute-start.1 = (bf16[16,128,128]{1,2,0:T(8,128)(2,1)S(1)}, bf16[16,128,128]{1,2,0:T(8,128)(2,1)S(1)}, u32[]{:S(2)}, u32[]{:S(2)}) collective-permute-start(bf16[16,128,128]{1,2,0:T(8,128)(2,1)S(1)} %collective-permute-done), channel_id=1, source_target_pairs={{0,2},{1,3},{2,4},{3,5},{4,6},{5,7},{8,10},{9,11},{10,12},{11,13},... | collective-permute-start | bytes 1572872 | tf_op jit(solution)/shard_map/ppermute | solution.py:154
  19.6 2.0 %collective-permute-start.4 = (bf16[16,128,128]{1,2,0:T(8,128)(2,1)S(1)}, bf16[16,128,128]{1,2,0:T(8,128)(2,1)S(1)}, u32[]{:S(2)}, u32[]{:S(2)}) collective-permute-start(bf16[16,128,128]{1,2,0:T(8,128)(2,1)S(1)} %collective-permute-done.3), channel_id=1, source_target_pairs={{2,0},{3,1},{4,2},{5,3},{6,4},{7,5},{10,8},{11,9},{12,10},{13,11},... | collective-permute-start | bytes 1572872 | tf_op jit(solution)/shard_map/ppermute | solution.py:155
  21.6 8.8 %collective-permute-done.1 = bf16[16,128,128]{1,2,0:T(8,128)(2,1)S(1)} collective-permute-done((bf16[16,128,128]{1,2,0:T(8,128)(2,1)S(1)}, bf16[16,128,128]{1,2,0:T(8,128)(2,1)S(1)}, u32[]{:S(2)}, u32[]{:S(2)}) %collective-permute-start.1) | collective-permute-done | bytes 524320 | tf_op jit(solution)/shard_map/ppermute | solution.py:154
  30.4 3.8 %collective-permute-start.2 = (bf16[16,128,128]{1,2,0:T(8,128)(2,1)S(1)}, bf16[16,128,128]{1,2,0:T(8,128)(2,1)S(1)}, u32[]{:S(2)}, u32[]{:S(2)}) collective-permute-start(bf16[16,128,128]{1,2,0:T(8,128)(2,1)S(1)} %collective-permute-done.1), channel_id=1, source_target_pairs={{0,2},{1,3},{2,4},{3,5},{4,6},{5,7},{8,10},{9,11},{10,12},{11,13},... | collective-permute-start | bytes 1572872 | tf_op jit(solution)/shard_map/ppermute | solution.py:154
  34.3 2.0 %collective-permute-start.5 = (bf16[16,128,128]{1,2,0:T(8,128)(2,1)S(1)}, bf16[16,128,128]{1,2,0:T(8,128)(2,1)S(1)}, u32[]{:S(2)}, u32[]{:S(2)}) collective-permute-start(bf16[16,128,128]{1,2,0:T(8,128)(2,1)S(1)} %collective-permute-done.4), channel_id=1, source_target_pairs={{2,0},{3,1},{4,2},{5,3},{6,4},{7,5},{10,8},{11,9},{12,10},{13,11},... | collective-permute-start | bytes 1572872 | tf_op jit(solution)/shard_map/ppermute | solution.py:155
  36.4 7.9 %collective-permute-done.2 = bf16[16,128,128]{1,2,0:T(8,128)(2,1)S(1)} collective-permute-done((bf16[16,128,128]{1,2,0:T(8,128)(2,1)S(1)}, bf16[16,128,128]{1,2,0:T(8,128)(2,1)S(1)}, u32[]{:S(2)}, u32[]{:S(2)}) %collective-permute-start.2) | collective-permute-done | bytes 524320 | tf_op jit(solution)/shard_map/ppermute | solution.py:154
  44.5 3.6 %collective-permute-done.5 = bf16[16,128,128]{1,2,0:T(8,128)(2,1)S(1)} collective-permute-done((bf16[16,128,128]{1,2,0:T(8,128)(2,1)S(1)}, bf16[16,128,128]{1,2,0:T(8,128)(2,1)S(1)}, u32[]{:S(2)}, u32[]{:S(2)}) %collective-permute-start.5) | collective-permute-done | bytes 524320 | tf_op jit(solution)/shard_map/ppermute | solution.py:155
  48.5 1.6 pad_maximum_fusion.1
  50.3 0.6 gather_fusion
  50.9 0.6 gather_fusion.1
  51.6 0.6 gather_fusion.2
  52.6 2.1 %collective-permute-done.6 = bf16[4,16,128,128]{2,3,1,0:T(8,128)(2,1)} collective-permute-done((bf16[4,16,128,128]{2,3,1,0:T(8,128)(2,1)}, bf16[4,16,128,128]{2,3,1,0:T(8,128)(2,1)}, u32[]{:S(2)}, u32[]{:S(2)}) %collective-permute-start.6) | collective-permute-done | bytes 2097184 | tf_op jit(solution)/shard_map/ppermute | solution.py:173
  54.6 1.8 select_bitcast_fusion.1
  56.4 2.4 %pad_maximum_fusion = bf16[4,2,16,128,128]{3,4,2,0,1:T(8,128)(2,1)} fusion(bf16[4,1,16,128,128]{3,4,2,0,1:T(8,128)(2,1)S(1)} %get-tuple-element.15, bf16[4,1,16,128,128]{3,4,2,0,1:T(8,128)(2,1)S(1)} %get-tuple-element.14), kind=kLoop, calls=%fused_computation.3 | loop fusion | flops 2097152 | bytes 8388608 | tf_op jit(solution)/shard_map/stack | solution.py:176
  58.8 6.2 %copy.20 = bf16[4,2,16,128,128]{4,3,2,1,0:T(8,128)(2,1)} copy(bf16[4,2,16,128,128]{3,4,2,0,1:T(8,128)(2,1)} %pad_maximum_fusion) | data formatting | bytes 8388608 | tf_op jit(solution)/shard_map/stack | solution.py:176
  65.0 25.9 %shard_map.46 = (f32[32,128,128]{2,1,0:T(8,128)S(1)}, f32[32,128,128]{2,1,0:T(8,128)S(1)}, f32[32,128,128]{2,1,0:T(8,128)}, f32[32,128,128]{2,1,0:T(8,128)}) custom-call(s32[384]{0:T(512)S(1)} %reshape.88.left_ref, s32[384]{0:T(512)S(1)} %reshape.89.right_ref, s32[384]{0:T(512)S(1)} %reshape.90.target_ref, bf16[128,128,128]{2,1,0:T(8,128)(2,1)} %bitcast.145), custom_call_target="tpu_custom_call" | custom-call | flops 1610612736 | bytes 12582912 | tf_op jit(solution)/shard_map/pallas_call | solution.py:40
  90.9 1.4 copy-done
  92.3 1.9 %dynamic-slice_bitcast_fusion = f32[4,2,128,128]{3,2,1,0:T(8,128)} fusion(f32[4,4,2,128,128]{4,3,2,1,0:T(8,128)} %bitcast.150, s32[]{:T(128)S(6)} %select_n.317), kind=kLoop, calls=%fused_computation.53 | loop fusion | bytes 1048580 | tf_op jit(solution)/shard_map/reshape | solution.py:107
  94.2 3.0 %collective-permute-start.19 = (f32[4,2,128,128]{3,2,1,0:T(8,128)}, f32[4,2,128,128]{3,2,1,0:T(8,128)S(1)}, u32[]{:S(2)}, u32[]{:S(2)}) collective-permute-start(f32[4,2,128,128]{3,2,1,0:T(8,128)} %dynamic-slice_bitcast_fusion), channel_id=1, source_target_pairs={{0,192},{8,200},{16,208},{24,216},{32,224},{40,232},{48,240},{56,2... | collective-permute-start | bytes 1572872 | tf_op jit(solution)/shard_map/ppermute | solution.py:121
  97.2 1.9 %dynamic-slice_bitcast_fusion.1 = f32[4,2,128,128]{3,2,1,0:T(8,128)} fusion(f32[4,4,2,128,128]{4,3,2,1,0:T(8,128)} %bitcast.146, s32[]{:T(128)S(6)} %select_n.323), kind=kLoop, calls=%fused_computation.54 | loop fusion | bytes 1048580 | tf_op jit(solution)/shard_map/reshape | solution.py:107
  99.1 1.2 dynamic-slice_bitcast_fusion.2
  100.3 2.8 %collective-permute-start.10 = (f32[4,2,128,128]{3,2,1,0:T(8,128)S(1)}, f32[4,2,128,128]{3,2,1,0:T(8,128)S(1)}, u32[]{:S(2)}, u32[]{:S(2)}) collective-permute-start(f32[4,2,128,128]{3,2,1,0:T(8,128)S(1)} %dynamic-slice_bitcast_fusion.2), channel_id=1, source_target_pairs={{0,48},{8,56},{16,0},{24,8},{32,16},{40,24},{48,32},{56,40},{64,11... | collective-permute-start | bytes 1572872 | tf_op jit(solution)/shard_map/ppermute | solution.py:121
  103.3 5.7 %collective-permute-done.19 = f32[4,2,128,128]{3,2,1,0:T(8,128)S(1)} collective-permute-done((f32[4,2,128,128]{3,2,1,0:T(8,128)}, f32[4,2,128,128]{3,2,1,0:T(8,128)S(1)}, u32[]{:S(2)}, u32[]{:S(2)}) %collective-permute-start.19) | collective-permute-done | bytes 524320 | tf_op jit(solution)/shard_map/ppermute | solution.py:121
  109.0 1.1 bitcast_add_fusion.2
  110.1 3.7 %collective-permute-start.20 = (f32[4,2,128,128]{3,2,1,0:T(8,128)S(1)}, f32[4,2,128,128]{3,2,1,0:T(8,128)S(1)}, u32[]{:S(2)}, u32[]{:S(2)}) collective-permute-start(f32[4,2,128,128]{3,2,1,0:T(8,128)S(1)} %bitcast_add_fusion.2), channel_id=1, source_target_pairs={{0,192},{8,200},{16,208},{24,216},{32,224},{40,232},{48,240},{56,2... | collective-permute-start | bytes 1572872 | tf_op jit(solution)/shard_map/ppermute | solution.py:121
  113.8 0.4 collective-permute-done.16
  114.4 3.8 %collective-permute-start.11 = (f32[4,2,128,128]{3,2,1,0:T(8,128)S(1)}, f32[4,2,128,128]{3,2,1,0:T(8,128)S(1)}, u32[]{:S(2)}, u32[]{:S(2)}) collective-permute-start(f32[4,2,128,128]{3,2,1,0:T(8,128)S(1)} %bitcast_add_fusion.8), channel_id=1, source_target_pairs={{0,48},{8,56},{16,0},{24,8},{32,16},{40,24},{48,32},{56,40},{64,11... | collective-permute-start | bytes 1572872 | tf_op jit(solution)/shard_map/ppermute | solution.py:121
  118.3 6.1 %collective-permute-done.20 = f32[4,2,128,128]{3,2,1,0:T(8,128)S(1)} collective-permute-done((f32[4,2,128,128]{3,2,1,0:T(8,128)S(1)}, f32[4,2,128,128]{3,2,1,0:T(8,128)S(1)}, u32[]{:S(2)}, u32[]{:S(2)}) %collective-permute-start.20) | collective-permute-done | bytes 524320 | tf_op jit(solution)/shard_map/ppermute | solution.py:121
  124.5 3.8 %collective-permute-start.21 = (f32[4,2,128,128]{3,2,1,0:T(8,128)S(1)}, f32[4,2,128,128]{3,2,1,0:T(8,128)S(1)}, u32[]{:S(2)}, u32[]{:S(2)}) collective-permute-start(f32[4,2,128,128]{3,2,1,0:T(8,128)S(1)} %bitcast_add_fusion.1), channel_id=1, source_target_pairs={{0,192},{8,200},{16,208},{24,216},{32,224},{40,232},{48,240},{56,2... | collective-permute-start | bytes 1572872 | tf_op jit(solution)/shard_map/ppermute | solution.py:121
  128.8 3.6 %collective-permute-start.12 = (f32[4,2,128,128]{3,2,1,0:T(8,128)S(1)}, f32[4,2,128,128]{3,2,1,0:T(8,128)S(1)}, u32[]{:S(2)}, u32[]{:S(2)}) collective-permute-start(f32[4,2,128,128]{3,2,1,0:T(8,128)S(1)} %bitcast_add_fusion.7), channel_id=1, source_target_pairs={{0,48},{8,56},{16,0},{24,8},{32,16},{40,24},{48,32},{56,40},{64,11... | collective-permute-start | bytes 1572872 | tf_op jit(solution)/shard_map/ppermute | solution.py:121
  132.5 5.5 %collective-permute-done.21 = f32[4,2,128,128]{3,2,1,0:T(8,128)S(1)} collective-permute-done((f32[4,2,128,128]{3,2,1,0:T(8,128)S(1)}, f32[4,2,128,128]{3,2,1,0:T(8,128)S(1)}, u32[]{:S(2)}, u32[]{:S(2)}) %collective-permute-start.21) | collective-permute-done | bytes 524320 | tf_op jit(solution)/shard_map/ppermute | solution.py:121
  138.1 3.8 %collective-permute-done.18 = f32[4,2,128,128]{3,2,1,0:T(8,128)S(1)} collective-permute-done((f32[4,2,128,128]{3,2,1,0:T(8,128)S(1)}, f32[4,2,128,128]{3,2,1,0:T(8,128)S(1)}, u32[]{:S(2)}, u32[]{:S(2)}) %collective-permute-start.18) | collective-permute-done | bytes 524320 | tf_op jit(solution)/shard_map/ppermute | solution.py:121
  142.1 1.6 collective-permute-start.22
  143.7 2.8 %collective-permute-start.23 = (f32[2,2,128,128]{3,2,0,1:T(8,128)S(1)}, f32[2,2,128,128]{3,2,0,1:T(8,128)S(1)}, u32[]{:S(2)}, u32[]{:S(2)}) collective-permute-start(f32[2,2,128,128]{3,2,0,1:T(8,128)S(1)} %bitcast.165), channel_id=1, source_target_pairs={{0,32},{8,40},{16,48},{24,56},{32,0},{40,8},{48,16},{56,24},{64,96... | collective-permute-start | bytes 786440 | tf_op jit(solution)/shard_map/ppermute | solution.py:131
  146.5 0.7 copy.37
  147.2 1.4 collective-permute-start.24
  149.1 0.5 collective-permute-start.13
  149.7 3.4 %collective-permute-start.14 = (f32[2,2,128,128]{3,2,0,1:T(8,128)S(1)}, f32[2,2,128,128]{3,2,0,1:T(8,128)S(1)}, u32[]{:S(2)}, u32[]{:S(2)}) collective-permute-start(f32[2,2,128,128]{3,2,0,1:T(8,128)S(1)} %bitcast.168), channel_id=1, source_target_pairs={{0,128},{8,136},{16,144},{24,152},{32,160},{40,168},{48,176},{56,1... | collective-permute-start | bytes 786440 | tf_op jit(solution)/shard_map/ppermute | solution.py:131
  153.0 3.6 %collective-permute-done.22 = f32[2,2,128,128]{3,2,0,1:T(8,128)S(1)} collective-permute-done((f32[2,2,128,128]{3,2,0,1:T(8,128)S(1)}, f32[2,2,128,128]{3,2,0,1:T(8,128)S(1)}, u32[]{:S(2)}, u32[]{:S(2)}) %collective-permute-start.22) | collective-permute-done | bytes 262176 | tf_op jit(solution)/shard_map/ppermute | solution.py:131
  156.6 2.4 %collective-permute-start.15 = (f32[2,2,128,128]{3,2,0,1:T(8,128)S(1)}, f32[2,2,128,128]{3,2,0,1:T(8,128)S(1)}, u32[]{:S(2)}, u32[]{:S(2)}) collective-permute-start(f32[2,2,128,128]{3,2,0,1:T(8,128)S(1)} %bitcast.169), channel_id=1, source_target_pairs={{0,192},{8,200},{16,208},{24,216},{32,224},{40,232},{48,240},{56,2... | collective-permute-start | bytes 786440 | tf_op jit(solution)/shard_map/ppermute | solution.py:131
  159.1 1.4 collective-permute-done.13
  160.5 2.5 %collective-permute-done.15 = f32[2,2,128,128]{3,2,0,1:T(8,128)S(1)} collective-permute-done((f32[2,2,128,128]{3,2,0,1:T(8,128)S(1)}, f32[2,2,128,128]{3,2,0,1:T(8,128)S(1)}, u32[]{:S(2)}, u32[]{:S(2)}) %collective-permute-start.15) | collective-permute-done | bytes 262176 | tf_op jit(solution)/shard_map/ppermute | solution.py:131
  163.1 5.3 %collective-permute-start.25 = (f32[4,128,128]{2,1,0:T(8,128)S(1)}, f32[4,128,128]{2,1,0:T(8,128)S(1)}, u32[]{:S(2)}, u32[]{:S(2)}) collective-permute-start(f32[4,128,128]{2,1,0:T(8,128)S(1)} %fusion.13), channel_id=1, source_target_pairs={{0,8},{8,0},{16,24},{24,16},{32,40},{40,32},{48,56},{56,48},{64,72... | collective-permute-start | bytes 786440 | tf_op jit(solution)/shard_map/ppermute | solution.py:139
  168.4 8.9 %collective-permute-done.25 = f32[4,128,128]{2,1,0:T(8,128)S(1)} collective-permute-done((f32[4,128,128]{2,1,0:T(8,128)S(1)}, f32[4,128,128]{2,1,0:T(8,128)S(1)}, u32[]{:S(2)}, u32[]{:S(2)}) %collective-permute-start.25) | collective-permute-done | bytes 262176 | tf_op jit(solution)/shard_map/ppermute | solution.py:139
  177.3 0.7 fusion.26
  (69 shorter events, 3.4 us)
Async XLA Ops:
  0.0 15.8 %collective-permute-start = (bf16[16,128,128]{1,2,0:T(8,128)(2,1)}, bf16[16,128,128]{1,2,0:T(8,128)(2,1)S(1)}, u32[]{:S(2)}, u32[]{:S(2)}) collective-permute-start(bf16[16,128,128]{1,2,0:T(8,128)(2,1)} %bitcast.163), channel_id=1, source_target_pairs={{0,2},{1,3},{2,4},{3,5},{4,6},{5,7},{8,10},{9,11},{10,12},{11,13},... | collective-permute-start | bytes 1572872 | tf_op jit(solution)/shard_map/ppermute | solution.py:154
  3.8 15.8 %collective-permute-start.3 = (bf16[16,128,128]{1,2,0:T(8,128)(2,1)}, bf16[16,128,128]{1,2,0:T(8,128)(2,1)S(1)}, u32[]{:S(2)}, u32[]{:S(2)}) collective-permute-start(bf16[16,128,128]{1,2,0:T(8,128)(2,1)} %bitcast.164), channel_id=1, source_target_pairs={{2,0},{3,1},{4,2},{5,3},{6,4},{7,5},{10,8},{11,9},{12,10},{13,11},... | collective-permute-start | bytes 1572872 | tf_op jit(solution)/shard_map/ppermute | solution.py:155
  15.8 14.7 %collective-permute-start.1 = (bf16[16,128,128]{1,2,0:T(8,128)(2,1)S(1)}, bf16[16,128,128]{1,2,0:T(8,128)(2,1)S(1)}, u32[]{:S(2)}, u32[]{:S(2)}) collective-permute-start(bf16[16,128,128]{1,2,0:T(8,128)(2,1)S(1)} %collective-permute-done), channel_id=1, source_target_pairs={{0,2},{1,3},{2,4},{3,5},{4,6},{5,7},{8,10},{9,11},{10,12},{11,13},... | collective-permute-start | bytes 1572872 | tf_op jit(solution)/shard_map/ppermute | solution.py:154
  19.6 14.7 %collective-permute-start.4 = (bf16[16,128,128]{1,2,0:T(8,128)(2,1)S(1)}, bf16[16,128,128]{1,2,0:T(8,128)(2,1)S(1)}, u32[]{:S(2)}, u32[]{:S(2)}) collective-permute-start(bf16[16,128,128]{1,2,0:T(8,128)(2,1)S(1)} %collective-permute-done.3), channel_id=1, source_target_pairs={{2,0},{3,1},{4,2},{5,3},{6,4},{7,5},{10,8},{11,9},{12,10},{13,11},... | collective-permute-start | bytes 1572872 | tf_op jit(solution)/shard_map/ppermute | solution.py:155
  30.4 13.8 %collective-permute-start.2 = (bf16[16,128,128]{1,2,0:T(8,128)(2,1)S(1)}, bf16[16,128,128]{1,2,0:T(8,128)(2,1)S(1)}, u32[]{:S(2)}, u32[]{:S(2)}) collective-permute-start(bf16[16,128,128]{1,2,0:T(8,128)(2,1)S(1)} %collective-permute-done.1), channel_id=1, source_target_pairs={{0,2},{1,3},{2,4},{3,5},{4,6},{5,7},{8,10},{9,11},{10,12},{11,13},... | collective-permute-start | bytes 1572872 | tf_op jit(solution)/shard_map/ppermute | solution.py:154
  34.3 13.8 %collective-permute-start.5 = (bf16[16,128,128]{1,2,0:T(8,128)(2,1)S(1)}, bf16[16,128,128]{1,2,0:T(8,128)(2,1)S(1)}, u32[]{:S(2)}, u32[]{:S(2)}) collective-permute-start(bf16[16,128,128]{1,2,0:T(8,128)(2,1)S(1)} %collective-permute-done.4), channel_id=1, source_target_pairs={{2,0},{3,1},{4,2},{5,3},{6,4},{7,5},{10,8},{11,9},{12,10},{13,11},... | collective-permute-start | bytes 1572872 | tf_op jit(solution)/shard_map/ppermute | solution.py:155
  44.5 3.8 %copy-start.4 = (bf16[16,128,128]{2,1,0:T(8,128)(2,1)S(1)}, bf16[16,128,128]{2,1,0:T(8,128)(2,1)}, u32[]{:S(2)}) copy-start(bf16[16,128,128]{2,1,0:T(8,128)(2,1)} %param.6) | copy-start | bytes 1572868
  48.5 1.7 copy-start.5
  48.5 1.7 copy-start.6
  48.5 3.0 %copy-start.7 = (s32[1,1,32,12]{2,1,3,0:T(1,128)S(1)}, s32[1,1,32,12]{2,1,3,0:T(1,128)}, u32[]{:S(2)}) copy-start(s32[1,1,32,12]{2,1,3,0:T(1,128)} %param.9) | copy-start | bytes 4612
  50.1 4.5 %collective-permute-start.6 = (bf16[4,16,128,128]{2,3,1,0:T(8,128)(2,1)}, bf16[4,16,128,128]{2,3,1,0:T(8,128)(2,1)}, u32[]{:S(2)}, u32[]{:S(2)}) collective-permute-start(bf16[4,16,128,128]{2,3,1,0:T(8,128)(2,1)} %pad_maximum_fusion.1), channel_id=1, source_target_pairs={{0,1},{1,0},{2,3},{3,2},{4,5},{5,4},{6,7},{7,6},{8,9},{9,8},{10,11... | collective-permute-start | bytes 6291464 | tf_op jit(solution)/shard_map/ppermute | solution.py:173
  90.9 1.4 copy-start
  94.2 14.8 %collective-permute-start.19 = (f32[4,2,128,128]{3,2,1,0:T(8,128)}, f32[4,2,128,128]{3,2,1,0:T(8,128)S(1)}, u32[]{:S(2)}, u32[]{:S(2)}) collective-permute-start(f32[4,2,128,128]{3,2,1,0:T(8,128)} %dynamic-slice_bitcast_fusion), channel_id=1, source_target_pairs={{0,192},{8,200},{16,208},{24,216},{32,224},{40,232},{48,240},{56,2... | collective-permute-start | bytes 1572872 | tf_op jit(solution)/shard_map/ppermute | solution.py:121
  99.1 15.1 %collective-permute-start.16 = (f32[4,2,128,128]{3,2,1,0:T(8,128)}, f32[4,2,128,128]{3,2,1,0:T(8,128)S(1)}, u32[]{:S(2)}, u32[]{:S(2)}) collective-permute-start(f32[4,2,128,128]{3,2,1,0:T(8,128)} %dynamic-slice_bitcast_fusion.1), channel_id=1, source_target_pairs={{0,64},{8,72},{16,80},{24,88},{32,96},{40,104},{48,112},{56,120},{... | collective-permute-start | bytes 1572872 | tf_op jit(solution)/shard_map/ppermute | solution.py:121
  99.1 15.1 %copy-start.2 = (f32[32,128,128]{2,1,0:T(8,128)S(1)}, f32[32,128,128]{2,1,0:T(8,128)}, u32[]{:S(2)}) copy-start(f32[32,128,128]{2,1,0:T(8,128)} %get-tuple-element.12) | copy-start | bytes 6291460
  100.3 14.0 %collective-permute-start.10 = (f32[4,2,128,128]{3,2,1,0:T(8,128)S(1)}, f32[4,2,128,128]{3,2,1,0:T(8,128)S(1)}, u32[]{:S(2)}, u32[]{:S(2)}) collective-permute-start(f32[4,2,128,128]{3,2,1,0:T(8,128)S(1)} %dynamic-slice_bitcast_fusion.2), channel_id=1, source_target_pairs={{0,48},{8,56},{16,0},{24,8},{32,16},{40,24},{48,32},{56,40},{64,11... | collective-permute-start | bytes 1572872 | tf_op jit(solution)/shard_map/ppermute | solution.py:121
  103.1 11.2 %copy-start.1 = (f32[32,128,128]{2,1,0:T(8,128)S(1)}, f32[32,128,128]{2,1,0:T(8,128)}, u32[]{:S(2)}) copy-start(f32[32,128,128]{2,1,0:T(8,128)} %copy-done) | copy-start | bytes 6291460
  103.2 15.0 %collective-permute-start.7 = (f32[4,2,128,128]{3,2,1,0:T(8,128)S(1)}, f32[4,2,128,128]{3,2,1,0:T(8,128)S(1)}, u32[]{:S(2)}, u32[]{:S(2)}) collective-permute-start(f32[4,2,128,128]{3,2,1,0:T(8,128)S(1)} %dynamic-slice_bitcast_fusion.3), channel_id=1, source_target_pairs={{0,16},{8,24},{16,32},{24,40},{32,48},{40,56},{48,0},{56,8},{64,80... | collective-permute-start | bytes 1572872 | tf_op jit(solution)/shard_map/ppermute | solution.py:121
  110.1 14.3 %copy-start.3 = (f32[32,128,128]{2,1,0:T(8,128)S(1)}, f32[32,128,128]{2,1,0:T(8,128)}, u32[]{:S(2)}) copy-start(f32[32,128,128]{2,1,0:T(8,128)} %get-tuple-element.13) | copy-start | bytes 6291460
  110.1 14.3 %collective-permute-start.20 = (f32[4,2,128,128]{3,2,1,0:T(8,128)S(1)}, f32[4,2,128,128]{3,2,1,0:T(8,128)S(1)}, u32[]{:S(2)}, u32[]{:S(2)}) collective-permute-start(f32[4,2,128,128]{3,2,1,0:T(8,128)S(1)} %bitcast_add_fusion.2), channel_id=1, source_target_pairs={{0,192},{8,200},{16,208},{24,216},{32,224},{40,232},{48,240},{56,2... | collective-permute-start | bytes 1572872 | tf_op jit(solution)/shard_map/ppermute | solution.py:121
  114.2 14.1 %collective-permute-start.17 = (f32[4,2,128,128]{3,2,1,0:T(8,128)S(1)}, f32[4,2,128,128]{3,2,1,0:T(8,128)S(1)}, u32[]{:S(2)}, u32[]{:S(2)}) collective-permute-start(f32[4,2,128,128]{3,2,1,0:T(8,128)S(1)} %bitcast_add_fusion.5), channel_id=1, source_target_pairs={{0,64},{8,72},{16,80},{24,88},{32,96},{40,104},{48,112},{56,120},{... | collective-permute-start | bytes 1572872 | tf_op jit(solution)/shard_map/ppermute | solution.py:121
  114.4 14.3 %collective-permute-start.11 = (f32[4,2,128,128]{3,2,1,0:T(8,128)S(1)}, f32[4,2,128,128]{3,2,1,0:T(8,128)S(1)}, u32[]{:S(2)}, u32[]{:S(2)}) collective-permute-start(f32[4,2,128,128]{3,2,1,0:T(8,128)S(1)} %bitcast_add_fusion.8), channel_id=1, source_target_pairs={{0,48},{8,56},{16,0},{24,8},{32,16},{40,24},{48,32},{56,40},{64,11... | collective-permute-start | bytes 1572872 | tf_op jit(solution)/shard_map/ppermute | solution.py:121
  118.2 14.1 %collective-permute-start.8 = (f32[4,2,128,128]{3,2,1,0:T(8,128)S(1)}, f32[4,2,128,128]{3,2,1,0:T(8,128)S(1)}, u32[]{:S(2)}, u32[]{:S(2)}) collective-permute-start(f32[4,2,128,128]{3,2,1,0:T(8,128)S(1)} %bitcast_add_fusion.11), channel_id=1, source_target_pairs={{0,16},{8,24},{16,32},{24,40},{32,48},{40,56},{48,0},{56,8},{64,80... | collective-permute-start | bytes 1572872 | tf_op jit(solution)/shard_map/ppermute | solution.py:121
  124.5 13.5 %collective-permute-start.21 = (f32[4,2,128,128]{3,2,1,0:T(8,128)S(1)}, f32[4,2,128,128]{3,2,1,0:T(8,128)S(1)}, u32[]{:S(2)}, u32[]{:S(2)}) collective-permute-start(f32[4,2,128,128]{3,2,1,0:T(8,128)S(1)} %bitcast_add_fusion.1), channel_id=1, source_target_pairs={{0,192},{8,200},{16,208},{24,216},{32,224},{40,232},{48,240},{56,2... | collective-permute-start | bytes 1572872 | tf_op jit(solution)/shard_map/ppermute | solution.py:121
  128.4 13.4 %collective-permute-start.18 = (f32[4,2,128,128]{3,2,1,0:T(8,128)S(1)}, f32[4,2,128,128]{3,2,1,0:T(8,128)S(1)}, u32[]{:S(2)}, u32[]{:S(2)}) collective-permute-start(f32[4,2,128,128]{3,2,1,0:T(8,128)S(1)} %bitcast_add_fusion.4), channel_id=1, source_target_pairs={{0,64},{8,72},{16,80},{24,88},{32,96},{40,104},{48,112},{56,120},{... | collective-permute-start | bytes 1572872 | tf_op jit(solution)/shard_map/ppermute | solution.py:121
  128.8 19.8 %collective-permute-start.12 = (f32[4,2,128,128]{3,2,1,0:T(8,128)S(1)}, f32[4,2,128,128]{3,2,1,0:T(8,128)S(1)}, u32[]{:S(2)}, u32[]{:S(2)}) collective-permute-start(f32[4,2,128,128]{3,2,1,0:T(8,128)S(1)} %bitcast_add_fusion.7), channel_id=1, source_target_pairs={{0,48},{8,56},{16,0},{24,8},{32,16},{40,24},{48,32},{56,40},{64,11... | collective-permute-start | bytes 1572872 | tf_op jit(solution)/shard_map/ppermute | solution.py:121
  132.4 16.5 %collective-permute-start.9 = (f32[4,2,128,128]{3,2,1,0:T(8,128)S(1)}, f32[4,2,128,128]{3,2,1,0:T(8,128)S(1)}, u32[]{:S(2)}, u32[]{:S(2)}) collective-permute-start(f32[4,2,128,128]{3,2,1,0:T(8,128)S(1)} %bitcast_add_fusion.10), channel_id=1, source_target_pairs={{0,16},{8,24},{16,32},{24,40},{32,48},{40,56},{48,0},{56,8},{64,80... | collective-permute-start | bytes 1572872 | tf_op jit(solution)/shard_map/ppermute | solution.py:121
  142.1 14.6 %collective-permute-start.22 = (f32[2,2,128,128]{3,2,0,1:T(8,128)S(1)}, f32[2,2,128,128]{3,2,0,1:T(8,128)S(1)}, u32[]{:S(2)}, u32[]{:S(2)}) collective-permute-start(f32[2,2,128,128]{3,2,0,1:T(8,128)S(1)} %bitcast.166), channel_id=1, source_target_pairs={{0,16},{8,24},{16,32},{24,40},{32,48},{40,56},{48,0},{56,8},{64,80... | collective-permute-start | bytes 786440 | tf_op jit(solution)/shard_map/ppermute | solution.py:131
  143.7 15.4 %collective-permute-start.23 = (f32[2,2,128,128]{3,2,0,1:T(8,128)S(1)}, f32[2,2,128,128]{3,2,0,1:T(8,128)S(1)}, u32[]{:S(2)}, u32[]{:S(2)}) collective-permute-start(f32[2,2,128,128]{3,2,0,1:T(8,128)S(1)} %bitcast.165), channel_id=1, source_target_pairs={{0,32},{8,40},{16,48},{24,56},{32,0},{40,8},{48,16},{56,24},{64,96... | collective-permute-start | bytes 786440 | tf_op jit(solution)/shard_map/ppermute | solution.py:131
  147.2 11.8 %collective-permute-start.24 = (f32[2,2,128,128]{3,2,0,1:T(8,128)}, f32[2,2,128,128]{3,2,0,1:T(8,128)S(1)}, u32[]{:S(2)}, u32[]{:S(2)}) collective-permute-start(f32[2,2,128,128]{3,2,0,1:T(8,128)} %bitcast.131), channel_id=1, source_target_pairs={{0,48},{8,56},{16,0},{24,8},{32,16},{40,24},{48,32},{56,40},{64,11... | collective-permute-start | bytes 786440 | tf_op jit(solution)/shard_map/ppermute | solution.py:131
  149.1 11.3 %collective-permute-start.13 = (f32[2,2,128,128]{3,2,0,1:T(8,128)S(1)}, f32[2,2,128,128]{3,2,0,1:T(8,128)S(1)}, u32[]{:S(2)}, u32[]{:S(2)}) collective-permute-start(f32[2,2,128,128]{3,2,0,1:T(8,128)S(1)} %bitcast.167), channel_id=1, source_target_pairs={{0,64},{8,72},{16,80},{24,88},{32,96},{40,104},{48,112},{56,120},{... | collective-permute-start | bytes 786440 | tf_op jit(solution)/shard_map/ppermute | solution.py:131
  149.7 10.8 %collective-permute-start.14 = (f32[2,2,128,128]{3,2,0,1:T(8,128)S(1)}, f32[2,2,128,128]{3,2,0,1:T(8,128)S(1)}, u32[]{:S(2)}, u32[]{:S(2)}) collective-permute-start(f32[2,2,128,128]{3,2,0,1:T(8,128)S(1)} %bitcast.168), channel_id=1, source_target_pairs={{0,128},{8,136},{16,144},{24,152},{32,160},{40,168},{48,176},{56,1... | collective-permute-start | bytes 786440 | tf_op jit(solution)/shard_map/ppermute | solution.py:131
  156.6 6.4 %collective-permute-start.15 = (f32[2,2,128,128]{3,2,0,1:T(8,128)S(1)}, f32[2,2,128,128]{3,2,0,1:T(8,128)S(1)}, u32[]{:S(2)}, u32[]{:S(2)}) collective-permute-start(f32[2,2,128,128]{3,2,0,1:T(8,128)S(1)} %bitcast.169), channel_id=1, source_target_pairs={{0,192},{8,200},{16,208},{24,216},{32,224},{40,232},{48,240},{56,2... | collective-permute-start | bytes 786440 | tf_op jit(solution)/shard_map/ppermute | solution.py:131
  163.1 14.1 %collective-permute-start.25 = (f32[4,128,128]{2,1,0:T(8,128)S(1)}, f32[4,128,128]{2,1,0:T(8,128)S(1)}, u32[]{:S(2)}, u32[]{:S(2)}) collective-permute-start(f32[4,128,128]{2,1,0:T(8,128)S(1)} %fusion.13), channel_id=1, source_target_pairs={{0,8},{8,0},{16,24},{24,16},{32,40},{40,32},{48,56},{56,48},{64,72... | collective-permute-start | bytes 786440 | tf_op jit(solution)/shard_map/ppermute | solution.py:139

commit v11 on v9

--- a/solution.py
+++ b/solution.py
@@ -146,18 +146,21 @@
     z = lax.axis_index("grp") // CORES
     core = lax.axis_index("grp") % CORES
     members = LINE * CORES
-    up = [(g, g + CORES) for g in range(members) if g // CORES < LINE - 1]
-    down = [(g, g - CORES) for g in range(members) if g // CORES > 0]
-    below, above = [], []
-    send_up, send_down = own, own
+    sibling = [(g, g ^ 1) for g in range(members)]
+    other = lax.ppermute(own, "grp", sibling)
+    chip = jnp.stack([jnp.where(core == 0, own, other), jnp.where(core == 0, other, own)])
+    route = [(g, g + CORES) for g in range(0, members - CORES, CORES)]
+    route += [(g, g - CORES) for g in range(CORES + 1, members, CORES)]
+    carried = []
+    send = chip
     for _ in range(LINE - 1):
-        send_up = lax.ppermute(send_up, "grp", up)
-        send_down = lax.ppermute(send_down, "grp", down)
-        below.append(send_up)
-        above.append(send_down)
-    below = jnp.stack(below)
-    above = jnp.stack(above)
-    mine = []
+        send = lax.ppermute(send, "grp", route)
+        carried.append(send)
+    carried = jnp.stack(carried)
+    swapped = lax.ppermute(carried, "grp", sibling)
+    below = jnp.where(core == 0, carried, swapped)
+    above = jnp.where(core == 0, swapped, carried)
+    rows = []
     for spot in range(LINE):
         from_below = lax.dynamic_index_in_dim(
             below, jnp.clip(z - 1 - spot, 0, LINE - 2), 0, keepdims=False
@@ -165,15 +168,8 @@
         from_above = lax.dynamic_index_in_dim(
             above, jnp.clip(spot - z - 1, 0, LINE - 2), 0, keepdims=False
         )
-        mine.append(
-            jnp.where(spot == z, own, jnp.where(spot < z, from_below, from_above))
-        )
-    mine = jnp.stack(mine)
-    sibling = [(g, g ^ 1) for g in range(members)]
-    theirs = lax.ppermute(mine, "grp", sibling)
-    first = jnp.where(core == 0, mine, theirs)
-    second = jnp.where(core == 0, theirs, mine)
-    gathered = jnp.stack([first, second], axis=1)
+        rows.append(jnp.where(spot == z, chip, jnp.where(spot < z, from_below, from_above)))
+    gathered = jnp.stack(rows)
     return gathered.reshape((members * own.shape[0],) + own.shape[1:])
 
 

time: 174 us -> 181 us (1.040)
  waiting for transfers between devices: 70.6 us -> 80.7 us
  starting transfers between devices: 56.2 us -> 50.4 us
  other arithmetic: 7.27 us -> 12.5 us
  local copies, waits for them, and re-layouts: 11.8 us -> 9.5 us
    ppermute x7 -> x5, waiting for transfers between devices: 32.2 us -> 44.3 us  [the longest x3 38.6 us: line_all_gather(): send = lax.ppermute(send, 'grp', route)]
    ppermute x7 -> x5, starting transfers between devices: 17.6 us -> 11.5 us  [the longest x3 11.5 us: line_all_gather(): send = lax.ppermute(send, 'grp', route)]
    select_n x0 -> x3, other arithmetic: none -> 2.95 us  [the longest x1 2.42 us: line_all_gather(): below = jnp.where(core == 0, carried, swapped)]
    another operation x1 -> x0, local copies, waits for them, and re-layouts: 2.29 us -> none  [line_all_gather(): gathered = jnp.stack([first, second], axis=1)]
    ppermute x1, waiting for transfers between devices: 9 us -> 6.73 us  [pair_reduce_scatter(): return lax.ppermute(other, 'blk', route) + mine]
    another operation x6 -> x4, other arithmetic: 4.36 us -> 5.64 us  [the longest x1 2.32 us: line_all_gather(): gathered = jnp.stack(rows)]
  transfers between devices with their start and end apart: 26 -> 24, of which waited for: 16 -> 15; matrix products, arithmetic and copies ran while one was open for 5% -> 5% of each run, Pallas kernels for 0% -> 0%
where the time goes in v11:
time: 181 us; the launch traced here: 180 us
  waiting for transfers between devices  80.7 us (45%)
  starting transfers between devices  50.4 us (28%)
  Pallas kernels  26.4 us (15%)
  other arithmetic  12.5 us (7%)
  local copies, waits for them, and re-layouts  9.5 us (5%)
    ppermute x3, waiting for transfers between devices, line_all_gather(): send = lax.ppermute(send, 'grp', route)  38.6 us
    pallas_call x1, Pallas kernels, owner_partials(): pl.pallas_call(_products_kernel, out_shape=[jax.ShapeDtypeStruct((owners,...  26.4 us
    ppermute x12, waiting for transfers between devices, ring_reduce_scatter(): arrived = lax.ppermute(send, 'blk', route)  23.3 us
    ppermute x12, starting transfers between devices, ring_reduce_scatter(): arrived = lax.ppermute(send, 'blk', route)  19.5 us
    ppermute x6, starting transfers between devices, direct_reduce_scatter(): total = total + lax.ppermute(piece, 'blk', _shift_route(dim, shift))  13 us
    ppermute x3, starting transfers between devices, line_all_gather(): send = lax.ppermute(send, 'grp', route)  11.5 us
    ppermute x1, waiting for transfers between devices, pair_reduce_scatter(): return lax.ppermute(other, 'blk', route) + mine  6.73 us
    ppermute x6, waiting for transfers between devices, direct_reduce_scatter(): total = total + lax.ppermute(piece, 'blk', _shift_route(dim, shift))  6.46 us
  transfers between devices with their start and end apart: 24, of which 15 were waited for; matrix products, arithmetic and copies ran while one was open for 5% of the time, Pallas kernels for 0%

profile of v11, /device:TPU:32, one launch (start us, length us, event | category | flops | bytes accessed | tf_op | source)
XLA Modules:
  0.0 179.9 jit_solution(10144170808844076282)
XLA Ops:
  0.0 2.1 %collective-permute-done = bf16[16,128,128]{2,1,0:T(8,128)(2,1)S(1)} collective-permute-done((bf16[16,128,128]{2,1,0:T(8,128)(2,1)}, bf16[16,128,128]{2,1,0:T(8,128)(2,1)S(1)}, u32[]{:S(2)}, u32[]{:S(2)}) %collective-permute-start) | collective-permute-done | bytes 524320 | tf_op jit(solution)/shard_map/ppermute | solution.py:150
  2.1 1.2 fusion.23
  3.4 3.8 %collective-permute-start.1 = (bf16[2,16,128,128]{3,2,1,0:T(8,128)(2,1)S(1)}, bf16[2,16,128,128]{3,2,1,0:T(8,128)(2,1)S(1)}, u32[]{:S(2)}, u32[]{:S(2)}) collective-permute-start(bf16[2,16,128,128]{3,2,1,0:T(8,128)(2,1)S(1)} %pad_maximum_fusion.3), channel_id=1, source_target_pairs={{0,2},{2,4},{4,6},{3,1},{5,3},{7,5},{8,10},{10,12},{12,14},{11,9},... | collective-permute-start | bytes 3145736 | tf_op jit(solution)/shard_map/ppermute | solution.py:157
  7.2 12.9 %collective-permute-done.1 = bf16[2,16,128,128]{3,2,1,0:T(8,128)(2,1)S(1)} collective-permute-done((bf16[2,16,128,128]{3,2,1,0:T(8,128)(2,1)S(1)}, bf16[2,16,128,128]{3,2,1,0:T(8,128)(2,1)S(1)}, u32[]{:S(2)}, u32[]{:S(2)}) %collective-permute-start.1) | collective-permute-done | bytes 1048608 | tf_op jit(solution)/shard_map/ppermute | solution.py:157
  20.1 3.8 %collective-permute-start.2 = (bf16[2,16,128,128]{3,2,1,0:T(8,128)(2,1)S(1)}, bf16[2,16,128,128]{3,2,1,0:T(8,128)(2,1)S(1)}, u32[]{:S(2)}, u32[]{:S(2)}) collective-permute-start(bf16[2,16,128,128]{3,2,1,0:T(8,128)(2,1)S(1)} %collective-permute-done.1), channel_id=1, source_target_pairs={{0,2},{2,4},{4,6},{3,1},{5,3},{7,5},{8,10},{10,12},{12,14},{11,9},... | collective-permute-start | bytes 3145736 | tf_op jit(solution)/shard_map/ppermute | solution.py:157
  23.9 12.9 %collective-permute-done.2 = bf16[2,16,128,128]{3,2,1,0:T(8,128)(2,1)S(1)} collective-permute-done((bf16[2,16,128,128]{3,2,1,0:T(8,128)(2,1)S(1)}, bf16[2,16,128,128]{3,2,1,0:T(8,128)(2,1)S(1)}, u32[]{:S(2)}, u32[]{:S(2)}) %collective-permute-start.2) | collective-permute-done | bytes 1048608 | tf_op jit(solution)/shard_map/ppermute | solution.py:157
  36.8 3.8 %collective-permute-start.3 = (bf16[2,16,128,128]{3,2,1,0:T(8,128)(2,1)S(1)}, bf16[2,16,128,128]{3,2,1,0:T(8,128)(2,1)S(1)}, u32[]{:S(2)}, u32[]{:S(2)}) collective-permute-start(bf16[2,16,128,128]{3,2,1,0:T(8,128)(2,1)S(1)} %collective-permute-done.2), channel_id=1, source_target_pairs={{0,2},{2,4},{4,6},{3,1},{5,3},{7,5},{8,10},{10,12},{12,14},{11,9},... | collective-permute-start | bytes 3145736 | tf_op jit(solution)/shard_map/ppermute | solution.py:157
  40.6 12.9 %collective-permute-done.3 = bf16[2,16,128,128]{3,2,1,0:T(8,128)(2,1)S(1)} collective-permute-done((bf16[2,16,128,128]{3,2,1,0:T(8,128)(2,1)S(1)}, bf16[2,16,128,128]{3,2,1,0:T(8,128)(2,1)S(1)}, u32[]{:S(2)}, u32[]{:S(2)}) %collective-permute-start.3) | collective-permute-done | bytes 1048608 | tf_op jit(solution)/shard_map/ppermute | solution.py:157
  53.5 2.0 %pad_maximum_fusion.1 = bf16[3,2,16,128,128]{4,3,2,1,0:T(8,128)(2,1)} fusion(bf16[1,2,16,128,128]{4,3,2,1,0:T(8,128)(2,1)S(1)} %bitcast.122, bf16[1,2,16,128,128]{4,3,2,1,0:T(8,128)(2,1)S(1)} %bitcast.120, bf16[1,2,16,128,128]{4,3,2,1,0:T(8,128)(2,1)S(1)} %bitcast.118), kind=kLoop, calls=%fused_computation.4 | loop fusion | flops 3145728 | bytes 6291456 | tf_op jit(solution)/shard_map/stack | solution.py:159
  55.7 0.6 gather_fusion
  56.3 0.6 gather_fusion.1
  57.0 0.6 gather_fusion.2
  58.0 3.6 %collective-permute-done.4 = bf16[3,2,16,128,128]{4,3,2,1,0:T(8,128)(2,1)} collective-permute-done((bf16[3,2,16,128,128]{4,3,2,1,0:T(8,128)(2,1)}, bf16[3,2,16,128,128]{4,3,2,1,0:T(8,128)(2,1)}, u32[]{:S(2)}, u32[]{:S(2)}) %collective-permute-start.4) | collective-permute-done | bytes 3145760 | tf_op jit(solution)/shard_map/ppermute | solution.py:160
  61.5 2.4 %broadcast_select_fusion.1 = (bf16[3,2,16,128,128]{4,3,2,1,0:T(8,128)(2,1)S(1)}, bf16[3,2,16,128,128]{4,3,2,1,0:T(8,128)(2,1)S(1)}) fusion(bf16[3,2,16,128,128]{4,3,2,1,0:T(8,128)(2,1)} %collective-permute-done.4, pred[]{:T(512)S(6)} %eq.48, bf16[1,2,16,128,128]{4,3,2,1,0:T(8,128)(2,1)} %bitcast.123, bf16[1,2,16,128,128]{4,3,2,1,0:T(8,128)(2,1)S(1)} %bitcast.121, ...), kind=kLoop, calls=%fused_computation.6 | loop fusion | flops 6291456 | bytes 12582913 | tf_op jit(solution)/shard_map/jit(_where)/select_n | solution.py:161
  64.0 0.3 select_select_fusion.2
  64.2 0.3 select_select_fusion.3
  64.5 2.3 %pad_maximum_fusion = bf16[4,2,16,128,128]{4,3,2,1,0:T(8,128)(2,1)} fusion(bf16[1,2,16,128,128]{4,3,2,1,0:T(8,128)(2,1)S(1)} %get-tuple-element.15, bf16[1,2,16,128,128]{4,3,2,1,0:T(8,128)(2,1)S(1)} %get-tuple-element.17, bf16[1,2,16,128,128]{4,3,2,1,0:T(8,128)(2,1)S(1)} %get-tuple-element.16, bf16[1,2,16,128,128]{4,3,2,1,0:T(8,128)(2,1)S(1)} %get-tuple-element.14), kind=kLoop, calls=%fused_computation.3 | loop fusion | flops 6291456 | bytes 8388608 | tf_op jit(solution)/shard_map/stack | solution.py:172
  66.8 26.4 %shard_map.46 = (f32[32,128,128]{2,1,0:T(8,128)S(1)}, f32[32,128,128]{2,1,0:T(8,128)S(1)}, f32[32,128,128]{2,1,0:T(8,128)}, f32[32,128,128]{2,1,0:T(8,128)}) custom-call(s32[384]{0:T(512)S(1)} %reshape.96.left_ref, s32[384]{0:T(512)S(1)} %reshape.97.right_ref, s32[384]{0:T(512)S(1)} %reshape.98.target_ref, bf16[128,128,128]{2,1,0:T(8,128)(2,1)} %bitcast.117), custom_call_target="tpu_custom_call" | custom-call | flops 1610612736 | bytes 12582912 | tf_op jit(solution)/shard_map/pallas_call | solution.py:40
  93.3 1.4 copy-done
  94.6 1.9 %dynamic-slice_bitcast_fusion = f32[4,2,128,128]{3,2,1,0:T(8,128)} fusion(f32[4,4,2,128,128]{4,3,2,1,0:T(8,128)} %bitcast.128, s32[]{:T(128)S(6)} %select_n.324), kind=kLoop, calls=%fused_computation.49 | loop fusion | bytes 1048580 | tf_op jit(solution)/shard_map/reshape | solution.py:107
  96.5 3.0 %collective-permute-start.17 = (f32[4,2,128,128]{3,2,1,0:T(8,128)}, f32[4,2,128,128]{3,2,1,0:T(8,128)S(1)}, u32[]{:S(2)}, u32[]{:S(2)}) collective-permute-start(f32[4,2,128,128]{3,2,1,0:T(8,128)} %dynamic-slice_bitcast_fusion), channel_id=1, source_target_pairs={{0,192},{8,200},{16,208},{24,216},{32,224},{40,232},{48,240},{56,2... | collective-permute-start | bytes 1572872 | tf_op jit(solution)/shard_map/ppermute | solution.py:121
  99.5 1.9 %dynamic-slice_bitcast_fusion.1 = f32[4,2,128,128]{3,2,1,0:T(8,128)} fusion(f32[4,4,2,128,128]{4,3,2,1,0:T(8,128)} %bitcast.124, s32[]{:T(128)S(6)} %select_n.330), kind=kLoop, calls=%fused_computation.50 | loop fusion | bytes 1048580 | tf_op jit(solution)/shard_map/reshape | solution.py:107
  101.4 1.2 dynamic-slice_bitcast_fusion.2
  102.6 2.8 %collective-permute-start.8 = (f32[4,2,128,128]{3,2,1,0:T(8,128)S(1)}, f32[4,2,128,128]{3,2,1,0:T(8,128)S(1)}, u32[]{:S(2)}, u32[]{:S(2)}) collective-permute-start(f32[4,2,128,128]{3,2,1,0:T(8,128)S(1)} %dynamic-slice_bitcast_fusion.2), channel_id=1, source_target_pairs={{0,48},{8,56},{16,0},{24,8},{32,16},{40,24},{48,32},{56,40},{64,11... | collective-permute-start | bytes 1572872 | tf_op jit(solution)/shard_map/ppermute | solution.py:121
  105.6 5.7 %collective-permute-done.17 = f32[4,2,128,128]{3,2,1,0:T(8,128)S(1)} collective-permute-done((f32[4,2,128,128]{3,2,1,0:T(8,128)}, f32[4,2,128,128]{3,2,1,0:T(8,128)S(1)}, u32[]{:S(2)}, u32[]{:S(2)}) %collective-permute-start.17) | collective-permute-done | bytes 524320 | tf_op jit(solution)/shard_map/ppermute | solution.py:121
  111.3 1.1 bitcast_add_fusion.2
  112.4 3.7 %collective-permute-start.18 = (f32[4,2,128,128]{3,2,1,0:T(8,128)S(1)}, f32[4,2,128,128]{3,2,1,0:T(8,128)S(1)}, u32[]{:S(2)}, u32[]{:S(2)}) collective-permute-start(f32[4,2,128,128]{3,2,1,0:T(8,128)S(1)} %bitcast_add_fusion.2), channel_id=1, source_target_pairs={{0,192},{8,200},{16,208},{24,216},{32,224},{40,232},{48,240},{56,2... | collective-permute-start | bytes 1572872 | tf_op jit(solution)/shard_map/ppermute | solution.py:121
  116.1 0.4 collective-permute-done.14
  116.5 1.1 bitcast_add_fusion.5
  117.8 2.8 %collective-permute-start.9 = (f32[4,2,128,128]{3,2,1,0:T(8,128)S(1)}, f32[4,2,128,128]{3,2,1,0:T(8,128)S(1)}, u32[]{:S(2)}, u32[]{:S(2)}) collective-permute-start(f32[4,2,128,128]{3,2,1,0:T(8,128)S(1)} %bitcast_add_fusion.8), channel_id=1, source_target_pairs={{0,48},{8,56},{16,0},{24,8},{32,16},{40,24},{48,32},{56,40},{64,11... | collective-permute-start | bytes 1572872 | tf_op jit(solution)/shard_map/ppermute | solution.py:121
  120.8 5.9 %collective-permute-done.18 = f32[4,2,128,128]{3,2,1,0:T(8,128)S(1)} collective-permute-done((f32[4,2,128,128]{3,2,1,0:T(8,128)S(1)}, f32[4,2,128,128]{3,2,1,0:T(8,128)S(1)}, u32[]{:S(2)}, u32[]{:S(2)}) %collective-permute-start.18) | collective-permute-done | bytes 524320 | tf_op jit(solution)/shard_map/ppermute | solution.py:121
  126.8 3.8 %collective-permute-start.19 = (f32[4,2,128,128]{3,2,1,0:T(8,128)S(1)}, f32[4,2,128,128]{3,2,1,0:T(8,128)S(1)}, u32[]{:S(2)}, u32[]{:S(2)}) collective-permute-start(f32[4,2,128,128]{3,2,1,0:T(8,128)S(1)} %bitcast_add_fusion.1), channel_id=1, source_target_pairs={{0,192},{8,200},{16,208},{24,216},{32,224},{40,232},{48,240},{56,2... | collective-permute-start | bytes 1572872 | tf_op jit(solution)/shard_map/ppermute | solution.py:121
  130.6 1.2 collective-permute-done.15
  132.1 2.8 %collective-permute-start.10 = (f32[4,2,128,128]{3,2,1,0:T(8,128)S(1)}, f32[4,2,128,128]{3,2,1,0:T(8,128)S(1)}, u32[]{:S(2)}, u32[]{:S(2)}) collective-permute-start(f32[4,2,128,128]{3,2,1,0:T(8,128)S(1)} %bitcast_add_fusion.7), channel_id=1, source_target_pairs={{0,48},{8,56},{16,0},{24,8},{32,16},{40,24},{48,32},{56,40},{64,11... | collective-permute-start | bytes 1572872 | tf_op jit(solution)/shard_map/ppermute | solution.py:121
  135.1 5.2 %collective-permute-done.19 = f32[4,2,128,128]{3,2,1,0:T(8,128)S(1)} collective-permute-done((f32[4,2,128,128]{3,2,1,0:T(8,128)S(1)}, f32[4,2,128,128]{3,2,1,0:T(8,128)S(1)}, u32[]{:S(2)}, u32[]{:S(2)}) %collective-permute-start.19) | collective-permute-done | bytes 524320 | tf_op jit(solution)/shard_map/ppermute | solution.py:121
  140.4 4.8 %collective-permute-done.16 = f32[4,2,128,128]{3,2,1,0:T(8,128)S(1)} collective-permute-done((f32[4,2,128,128]{3,2,1,0:T(8,128)S(1)}, f32[4,2,128,128]{3,2,1,0:T(8,128)S(1)}, u32[]{:S(2)}, u32[]{:S(2)}) %collective-permute-start.16) | collective-permute-done | bytes 524320 | tf_op jit(solution)/shard_map/ppermute | solution.py:121
  145.4 1.6 collective-permute-start.20
  147.0 2.8 %collective-permute-start.21 = (f32[2,2,128,128]{3,2,0,1:T(8,128)S(1)}, f32[2,2,128,128]{3,2,0,1:T(8,128)S(1)}, u32[]{:S(2)}, u32[]{:S(2)}) collective-permute-start(f32[2,2,128,128]{3,2,0,1:T(8,128)S(1)} %bitcast.135), channel_id=1, source_target_pairs={{0,32},{8,40},{16,48},{24,56},{32,0},{40,8},{48,16},{56,24},{64,96... | collective-permute-start | bytes 786440 | tf_op jit(solution)/shard_map/ppermute | solution.py:131
  149.8 0.7 copy.35
  150.5 1.4 collective-permute-start.22
  152.4 4.2 %collective-permute-start.12 = (f32[2,2,128,128]{3,2,0,1:T(8,128)S(1)}, f32[2,2,128,128]{3,2,0,1:T(8,128)S(1)}, u32[]{:S(2)}, u32[]{:S(2)}) collective-permute-start(f32[2,2,128,128]{3,2,0,1:T(8,128)S(1)} %bitcast.138), channel_id=1, source_target_pairs={{0,128},{8,136},{16,144},{24,152},{32,160},{40,168},{48,176},{56,1... | collective-permute-start | bytes 786440 | tf_op jit(solution)/shard_map/ppermute | solution.py:131
  156.6 2.6 %collective-permute-done.20 = f32[2,2,128,128]{3,2,0,1:T(8,128)S(1)} collective-permute-done((f32[2,2,128,128]{3,2,0,1:T(8,128)S(1)}, f32[2,2,128,128]{3,2,0,1:T(8,128)S(1)}, u32[]{:S(2)}, u32[]{:S(2)}) %collective-permute-start.20) | collective-permute-done | bytes 262176 | tf_op jit(solution)/shard_map/ppermute | solution.py:131
  159.2 2.9 %collective-permute-start.13 = (f32[2,2,128,128]{3,2,0,1:T(8,128)S(1)}, f32[2,2,128,128]{3,2,0,1:T(8,128)S(1)}, u32[]{:S(2)}, u32[]{:S(2)}) collective-permute-start(f32[2,2,128,128]{3,2,0,1:T(8,128)S(1)} %bitcast.139), channel_id=1, source_target_pairs={{0,192},{8,200},{16,208},{24,216},{32,224},{40,232},{48,240},{56,2... | collective-permute-start | bytes 786440 | tf_op jit(solution)/shard_map/ppermute | solution.py:131
  162.2 1.6 collective-permute-done.11
  163.8 2.2 %collective-permute-done.13 = f32[2,2,128,128]{3,2,0,1:T(8,128)S(1)} collective-permute-done((f32[2,2,128,128]{3,2,0,1:T(8,128)S(1)}, f32[2,2,128,128]{3,2,0,1:T(8,128)S(1)}, u32[]{:S(2)}, u32[]{:S(2)}) %collective-permute-start.13) | collective-permute-done | bytes 262176 | tf_op jit(solution)/shard_map/ppermute | solution.py:131
  166.1 6.4 %collective-permute-start.23 = (f32[4,128,128]{2,1,0:T(8,128)S(1)}, f32[4,128,128]{2,1,0:T(8,128)S(1)}, u32[]{:S(2)}, u32[]{:S(2)}) collective-permute-start(f32[4,128,128]{2,1,0:T(8,128)S(1)} %fusion.9), channel_id=1, source_target_pairs={{0,8},{8,0},{16,24},{24,16},{32,40},{40,32},{48,56},{56,48},{64,72... | collective-permute-start | bytes 786440 | tf_op jit(solution)/shard_map/ppermute | solution.py:139
  172.5 6.7 %collective-permute-done.23 = f32[4,128,128]{2,1,0:T(8,128)S(1)} collective-permute-done((f32[4,128,128]{2,1,0:T(8,128)S(1)}, f32[4,128,128]{2,1,0:T(8,128)S(1)}, u32[]{:S(2)}, u32[]{:S(2)}) %collective-permute-start.23) | collective-permute-done | bytes 262176 | tf_op jit(solution)/shard_map/ppermute | solution.py:139
  179.2 0.7 fusion.26
  (65 shorter events, 2.6 us)
Async XLA Ops:
  0.0 2.1 %collective-permute-start = (bf16[16,128,128]{2,1,0:T(8,128)(2,1)}, bf16[16,128,128]{2,1,0:T(8,128)(2,1)S(1)}, u32[]{:S(2)}, u32[]{:S(2)}) collective-permute-start(bf16[16,128,128]{2,1,0:T(8,128)(2,1)} %param.6), channel_id=1, source_target_pairs={{0,1},{1,0},{2,3},{3,2},{4,5},{5,4},{6,7},{7,6},{8,9},{9,8},{10,11... | collective-permute-start | bytes 1572872 | tf_op jit(solution)/shard_map/ppermute | solution.py:150
  3.4 16.7 %collective-permute-start.1 = (bf16[2,16,128,128]{3,2,1,0:T(8,128)(2,1)S(1)}, bf16[2,16,128,128]{3,2,1,0:T(8,128)(2,1)S(1)}, u32[]{:S(2)}, u32[]{:S(2)}) collective-permute-start(bf16[2,16,128,128]{3,2,1,0:T(8,128)(2,1)S(1)} %pad_maximum_fusion.3), channel_id=1, source_target_pairs={{0,2},{2,4},{4,6},{3,1},{5,3},{7,5},{8,10},{10,12},{12,14},{11,9},... | collective-permute-start | bytes 3145736 | tf_op jit(solution)/shard_map/ppermute | solution.py:157
  20.1 16.7 %collective-permute-start.2 = (bf16[2,16,128,128]{3,2,1,0:T(8,128)(2,1)S(1)}, bf16[2,16,128,128]{3,2,1,0:T(8,128)(2,1)S(1)}, u32[]{:S(2)}, u32[]{:S(2)}) collective-permute-start(bf16[2,16,128,128]{3,2,1,0:T(8,128)(2,1)S(1)} %collective-permute-done.1), channel_id=1, source_target_pairs={{0,2},{2,4},{4,6},{3,1},{5,3},{7,5},{8,10},{10,12},{12,14},{11,9},... | collective-permute-start | bytes 3145736 | tf_op jit(solution)/shard_map/ppermute | solution.py:157
  36.8 16.7 %collective-permute-start.3 = (bf16[2,16,128,128]{3,2,1,0:T(8,128)(2,1)S(1)}, bf16[2,16,128,128]{3,2,1,0:T(8,128)(2,1)S(1)}, u32[]{:S(2)}, u32[]{:S(2)}) collective-permute-start(bf16[2,16,128,128]{3,2,1,0:T(8,128)(2,1)S(1)} %collective-permute-done.2), channel_id=1, source_target_pairs={{0,2},{2,4},{4,6},{3,1},{5,3},{7,5},{8,10},{10,12},{12,14},{11,9},... | collective-permute-start | bytes 3145736 | tf_op jit(solution)/shard_map/ppermute | solution.py:157
  53.5 2.1 %copy-start.2 = (bf16[2,16,128,128]{3,2,1,0:T(8,128)(2,1)}, bf16[2,16,128,128]{3,2,1,0:T(8,128)(2,1)S(1)}, u32[]{:S(2)}) copy-start(bf16[2,16,128,128]{3,2,1,0:T(8,128)(2,1)S(1)} %collective-permute-done.3) | copy-start | bytes 3145732
  53.5 2.1 %copy-start.5 = (s32[1,1,32,12]{2,1,3,0:T(1,128)S(1)}, s32[1,1,32,12]{2,1,3,0:T(1,128)}, u32[]{:S(2)}) copy-start(s32[1,1,32,12]{2,1,3,0:T(1,128)} %param.7) | copy-start | bytes 4612
  53.5 2.1 %copy-start.6 = (s32[1,1,32,12]{2,1,3,0:T(1,128)S(1)}, s32[1,1,32,12]{2,1,3,0:T(1,128)}, u32[]{:S(2)}) copy-start(s32[1,1,32,12]{2,1,3,0:T(1,128)} %param.8) | copy-start | bytes 4612
  53.5 3.4 %copy-start.7 = (s32[1,1,32,12]{2,1,3,0:T(1,128)S(1)}, s32[1,1,32,12]{2,1,3,0:T(1,128)}, u32[]{:S(2)}) copy-start(s32[1,1,32,12]{2,1,3,0:T(1,128)} %param.9) | copy-start | bytes 4612
  55.5 6.0 %collective-permute-start.4 = (bf16[3,2,16,128,128]{4,3,2,1,0:T(8,128)(2,1)}, bf16[3,2,16,128,128]{4,3,2,1,0:T(8,128)(2,1)}, u32[]{:S(2)}, u32[]{:S(2)}) collective-permute-start(bf16[3,2,16,128,128]{4,3,2,1,0:T(8,128)(2,1)} %pad_maximum_fusion.1), channel_id=1, source_target_pairs={{0,1},{1,0},{2,3},{3,2},{4,5},{5,4},{6,7},{7,6},{8,9},{9,8},{10,11... | collective-permute-start | bytes 9437192 | tf_op jit(solution)/shard_map/ppermute | solution.py:160
  93.3 1.4 copy-start
  96.5 14.8 %collective-permute-start.17 = (f32[4,2,128,128]{3,2,1,0:T(8,128)}, f32[4,2,128,128]{3,2,1,0:T(8,128)S(1)}, u32[]{:S(2)}, u32[]{:S(2)}) collective-permute-start(f32[4,2,128,128]{3,2,1,0:T(8,128)} %dynamic-slice_bitcast_fusion), channel_id=1, source_target_pairs={{0,192},{8,200},{16,208},{24,216},{32,224},{40,232},{48,240},{56,2... | collective-permute-start | bytes 1572872 | tf_op jit(solution)/shard_map/ppermute | solution.py:121
  101.4 15.1 %collective-permute-start.14 = (f32[4,2,128,128]{3,2,1,0:T(8,128)}, f32[4,2,128,128]{3,2,1,0:T(8,128)S(1)}, u32[]{:S(2)}, u32[]{:S(2)}) collective-permute-start(f32[4,2,128,128]{3,2,1,0:T(8,128)} %dynamic-slice_bitcast_fusion.1), channel_id=1, source_target_pairs={{0,64},{8,72},{16,80},{24,88},{32,96},{40,104},{48,112},{56,120},{... | collective-permute-start | bytes 1572872 | tf_op jit(solution)/shard_map/ppermute | solution.py:121
  101.4 16.3 %copy-start.1 = (f32[32,128,128]{2,1,0:T(8,128)S(1)}, f32[32,128,128]{2,1,0:T(8,128)}, u32[]{:S(2)}) copy-start(f32[32,128,128]{2,1,0:T(8,128)} %copy-done) | copy-start | bytes 6291460
  102.6 15.1 %collective-permute-start.8 = (f32[4,2,128,128]{3,2,1,0:T(8,128)S(1)}, f32[4,2,128,128]{3,2,1,0:T(8,128)S(1)}, u32[]{:S(2)}, u32[]{:S(2)}) collective-permute-start(f32[4,2,128,128]{3,2,1,0:T(8,128)S(1)} %dynamic-slice_bitcast_fusion.2), channel_id=1, source_target_pairs={{0,48},{8,56},{16,0},{24,8},{32,16},{40,24},{48,32},{56,40},{64,11... | collective-permute-start | bytes 1572872 | tf_op jit(solution)/shard_map/ppermute | solution.py:121
  105.5 21.2 %copy-start.4 = (f32[32,128,128]{2,1,0:T(8,128)S(1)}, f32[32,128,128]{2,1,0:T(8,128)}, u32[]{:S(2)}) copy-start(f32[32,128,128]{2,1,0:T(8,128)} %get-tuple-element.13) | copy-start | bytes 6291460
  105.5 15.1 %collective-permute-start.5 = (f32[4,2,128,128]{3,2,1,0:T(8,128)S(1)}, f32[4,2,128,128]{3,2,1,0:T(8,128)S(1)}, u32[]{:S(2)}, u32[]{:S(2)}) collective-permute-start(f32[4,2,128,128]{3,2,1,0:T(8,128)S(1)} %dynamic-slice_bitcast_fusion.3), channel_id=1, source_target_pairs={{0,16},{8,24},{16,32},{24,40},{32,48},{40,56},{48,0},{56,8},{64,80... | collective-permute-start | bytes 1572872 | tf_op jit(solution)/shard_map/ppermute | solution.py:121
  112.4 19.3 %copy-start.3 = (f32[32,128,128]{2,1,0:T(8,128)S(1)}, f32[32,128,128]{2,1,0:T(8,128)}, u32[]{:S(2)}) copy-start(f32[32,128,128]{2,1,0:T(8,128)} %get-tuple-element.12) | copy-start | bytes 6291460
  112.4 14.3 %collective-permute-start.18 = (f32[4,2,128,128]{3,2,1,0:T(8,128)S(1)}, f32[4,2,128,128]{3,2,1,0:T(8,128)S(1)}, u32[]{:S(2)}, u32[]{:S(2)}) collective-permute-start(f32[4,2,128,128]{3,2,1,0:T(8,128)S(1)} %bitcast_add_fusion.2), channel_id=1, source_target_pairs={{0,192},{8,200},{16,208},{24,216},{32,224},{40,232},{48,240},{56,2... | collective-permute-start | bytes 1572872 | tf_op jit(solution)/shard_map/ppermute | solution.py:121
  117.6 14.1 %collective-permute-start.15 = (f32[4,2,128,128]{3,2,1,0:T(8,128)S(1)}, f32[4,2,128,128]{3,2,1,0:T(8,128)S(1)}, u32[]{:S(2)}, u32[]{:S(2)}) collective-permute-start(f32[4,2,128,128]{3,2,1,0:T(8,128)S(1)} %bitcast_add_fusion.5), channel_id=1, source_target_pairs={{0,64},{8,72},{16,80},{24,88},{32,96},{40,104},{48,112},{56,120},{... | collective-permute-start | bytes 1572872 | tf_op jit(solution)/shard_map/ppermute | solution.py:121
  117.8 14.3 %collective-permute-start.9 = (f32[4,2,128,128]{3,2,1,0:T(8,128)S(1)}, f32[4,2,128,128]{3,2,1,0:T(8,128)S(1)}, u32[]{:S(2)}, u32[]{:S(2)}) collective-permute-start(f32[4,2,128,128]{3,2,1,0:T(8,128)S(1)} %bitcast_add_fusion.8), channel_id=1, source_target_pairs={{0,48},{8,56},{16,0},{24,8},{32,16},{40,24},{48,32},{56,40},{64,11... | collective-permute-start | bytes 1572872 | tf_op jit(solution)/shard_map/ppermute | solution.py:121
  120.7 14.3 %collective-permute-start.6 = (f32[4,2,128,128]{3,2,1,0:T(8,128)S(1)}, f32[4,2,128,128]{3,2,1,0:T(8,128)S(1)}, u32[]{:S(2)}, u32[]{:S(2)}) collective-permute-start(f32[4,2,128,128]{3,2,1,0:T(8,128)S(1)} %bitcast_add_fusion.11), channel_id=1, source_target_pairs={{0,16},{8,24},{16,32},{24,40},{32,48},{40,56},{48,0},{56,8},{64,80... | collective-permute-start | bytes 1572872 | tf_op jit(solution)/shard_map/ppermute | solution.py:121
  126.8 13.5 %collective-permute-start.19 = (f32[4,2,128,128]{3,2,1,0:T(8,128)S(1)}, f32[4,2,128,128]{3,2,1,0:T(8,128)S(1)}, u32[]{:S(2)}, u32[]{:S(2)}) collective-permute-start(f32[4,2,128,128]{3,2,1,0:T(8,128)S(1)} %bitcast_add_fusion.1), channel_id=1, source_target_pairs={{0,192},{8,200},{16,208},{24,216},{32,224},{40,232},{48,240},{56,2... | collective-permute-start | bytes 1572872 | tf_op jit(solution)/shard_map/ppermute | solution.py:121
  131.8 13.4 %collective-permute-start.16 = (f32[4,2,128,128]{3,2,1,0:T(8,128)S(1)}, f32[4,2,128,128]{3,2,1,0:T(8,128)S(1)}, u32[]{:S(2)}, u32[]{:S(2)}) collective-permute-start(f32[4,2,128,128]{3,2,1,0:T(8,128)S(1)} %bitcast_add_fusion.4), channel_id=1, source_target_pairs={{0,64},{8,72},{16,80},{24,88},{32,96},{40,104},{48,112},{56,120},{... | collective-permute-start | bytes 1572872 | tf_op jit(solution)/shard_map/ppermute | solution.py:121
  132.1 19.8 %collective-permute-start.10 = (f32[4,2,128,128]{3,2,1,0:T(8,128)S(1)}, f32[4,2,128,128]{3,2,1,0:T(8,128)S(1)}, u32[]{:S(2)}, u32[]{:S(2)}) collective-permute-start(f32[4,2,128,128]{3,2,1,0:T(8,128)S(1)} %bitcast_add_fusion.7), channel_id=1, source_target_pairs={{0,48},{8,56},{16,0},{24,8},{32,16},{40,24},{48,32},{56,40},{64,11... | collective-permute-start | bytes 1572872 | tf_op jit(solution)/shard_map/ppermute | solution.py:121
  135.0 17.0 %collective-permute-start.7 = (f32[4,2,128,128]{3,2,1,0:T(8,128)S(1)}, f32[4,2,128,128]{3,2,1,0:T(8,128)S(1)}, u32[]{:S(2)}, u32[]{:S(2)}) collective-permute-start(f32[4,2,128,128]{3,2,1,0:T(8,128)S(1)} %bitcast_add_fusion.10), channel_id=1, source_target_pairs={{0,16},{8,24},{16,32},{24,40},{32,48},{40,56},{48,0},{56,8},{64,80... | collective-permute-start | bytes 1572872 | tf_op jit(solution)/shard_map/ppermute | solution.py:121
  145.4 13.8 %collective-permute-start.20 = (f32[2,2,128,128]{3,2,0,1:T(8,128)S(1)}, f32[2,2,128,128]{3,2,0,1:T(8,128)S(1)}, u32[]{:S(2)}, u32[]{:S(2)}) collective-permute-start(f32[2,2,128,128]{3,2,0,1:T(8,128)S(1)} %bitcast.136), channel_id=1, source_target_pairs={{0,16},{8,24},{16,32},{24,40},{32,48},{40,56},{48,0},{56,8},{64,80... | collective-permute-start | bytes 786440 | tf_op jit(solution)/shard_map/ppermute | solution.py:131
  147.0 15.2 %collective-permute-start.21 = (f32[2,2,128,128]{3,2,0,1:T(8,128)S(1)}, f32[2,2,128,128]{3,2,0,1:T(8,128)S(1)}, u32[]{:S(2)}, u32[]{:S(2)}) collective-permute-start(f32[2,2,128,128]{3,2,0,1:T(8,128)S(1)} %bitcast.135), channel_id=1, source_target_pairs={{0,32},{8,40},{16,48},{24,56},{32,0},{40,8},{48,16},{56,24},{64,96... | collective-permute-start | bytes 786440 | tf_op jit(solution)/shard_map/ppermute | solution.py:131
  150.5 11.6 %collective-permute-start.22 = (f32[2,2,128,128]{3,2,0,1:T(8,128)}, f32[2,2,128,128]{3,2,0,1:T(8,128)S(1)}, u32[]{:S(2)}, u32[]{:S(2)}) collective-permute-start(f32[2,2,128,128]{3,2,0,1:T(8,128)} %bitcast.103), channel_id=1, source_target_pairs={{0,48},{8,56},{16,0},{24,8},{32,16},{40,24},{48,32},{56,40},{64,11... | collective-permute-start | bytes 786440 | tf_op jit(solution)/shard_map/ppermute | solution.py:131
  152.2 11.6 %collective-permute-start.11 = (f32[2,2,128,128]{3,2,0,1:T(8,128)S(1)}, f32[2,2,128,128]{3,2,0,1:T(8,128)S(1)}, u32[]{:S(2)}, u32[]{:S(2)}) collective-permute-start(f32[2,2,128,128]{3,2,0,1:T(8,128)S(1)} %bitcast.137), channel_id=1, source_target_pairs={{0,64},{8,72},{16,80},{24,88},{32,96},{40,104},{48,112},{56,120},{... | collective-permute-start | bytes 786440 | tf_op jit(solution)/shard_map/ppermute | solution.py:131
  152.4 11.4 %collective-permute-start.12 = (f32[2,2,128,128]{3,2,0,1:T(8,128)S(1)}, f32[2,2,128,128]{3,2,0,1:T(8,128)S(1)}, u32[]{:S(2)}, u32[]{:S(2)}) collective-permute-start(f32[2,2,128,128]{3,2,0,1:T(8,128)S(1)} %bitcast.138), channel_id=1, source_target_pairs={{0,128},{8,136},{16,144},{24,152},{32,160},{40,168},{48,176},{56,1... | collective-permute-start | bytes 786440 | tf_op jit(solution)/shard_map/ppermute | solution.py:131
  159.2 6.8 %collective-permute-start.13 = (f32[2,2,128,128]{3,2,0,1:T(8,128)S(1)}, f32[2,2,128,128]{3,2,0,1:T(8,128)S(1)}, u32[]{:S(2)}, u32[]{:S(2)}) collective-permute-start(f32[2,2,128,128]{3,2,0,1:T(8,128)S(1)} %bitcast.139), channel_id=1, source_target_pairs={{0,192},{8,200},{16,208},{24,216},{32,224},{40,232},{48,240},{56,2... | collective-permute-start | bytes 786440 | tf_op jit(solution)/shard_map/ppermute | solution.py:131
  166.1 13.1 %collective-permute-start.23 = (f32[4,128,128]{2,1,0:T(8,128)S(1)}, f32[4,128,128]{2,1,0:T(8,128)S(1)}, u32[]{:S(2)}, u32[]{:S(2)}) collective-permute-start(f32[4,128,128]{2,1,0:T(8,128)S(1)} %fusion.9), channel_id=1, source_target_pairs={{0,8},{8,0},{16,24},{24,16},{32,40},{40,32},{48,56},{56,48},{64,72... | collective-permute-start | bytes 786440 | tf_op jit(solution)/shard_map/ppermute | solution.py:139
